TPU v7x, 128 devices: a whole 4x4x4 slice. The times are simulated.
128 devices in a mesh: seq: 16 (over x, z), head: 8 (over y, core).
Axes of the slice: x: 4, y: 4, z: 4, core: 2. Of those that a mesh axis runs over, the one named last changes fastest.
Arguments:
- own_rows: bfloat16 [16384, 2048], P('seq'), may hold values from -400 to 400
- gain: float32 [2048], replicated, may hold values from 0.1 to 1.9
- w_query: bfloat16 [2048, 2048], P(None, 'head'), may hold values from -1 to 1
- w_key: bfloat16 [2048, 2048], P(None, 'head'), may hold values from -1 to 1
- w_value: bfloat16 [2048, 2048], P(None, 'head'), may hold values from -0.125 to 0.125
- grad_context: bfloat16 [16384, 2048], P('seq', 'head'), may hold values from -6 to 6
- send_slot: int32 [16384], P('seq'), may hold values from 0 to 2047, as said below
- recv_slot: int32 [16384], P('seq'), may hold values from 0 to 2047, as said below
- episode_start: int32 [16384], P('seq'), may hold values from 0 to 16256, as said below
Outputs:
- context: bfloat16 [16384, 2048], P('seq', 'head')
- d_rows: bfloat16 [16384, 2048], P(('seq', 'head'))
Inputs may be any that keep to these rules, and one draw needn't show every extreme that they name: `send_slot`: each owner's rows name distinct slots of its send buffer, which holds one bucket of 128 slots for each shard in shard order; slot b * 128 + c sends the row to shard b. At most 128 rows of one owner go to one shard, and in every draw some owner sends exactly 128 rows to some shard. `recv_slot`: A shard receives from each owner o the bucket meant for it at o * 128; each packed row names a distinct received slot that carries a row, so that every owner's row lands in exactly one packed row. `episode_start`: episodes are runs of consecutive packed rows whose starts are multiples of 128; a row's value is its episode's first row, at most the row and more than the row minus 1024. Every shard's first row belongs to an episode that began in the shard before it (the first shard aside). Every draw holds an episode of 8 blocks.
All inputs are finite; a program needn't handle non-finite values.
Results may differ from a plain program's by a relative error of at most 0.02.
The roundings to bfloat16 on the way count: a program that leaves them out, or rounds other values in their place, can miss the bound.
Values may be sent and summed in bfloat16 or wider, within the bound.
No kernel may reach another device: no remote copies, remote signals or barrier semaphores. Data moves between devices by JAX's collectives and lax.ppermute only.
A program may use at most 128 MiB of HBM per device.

v0:
```python
import jax
import jax.numpy as jnp
from jax import lax
from jax.sharding import PartitionSpec as P

HD = 128


neg_large = -1e30
epsilon = 1e-05


def passed_along(array, axis, by):
    count = lax.axis_size(axis)
    pairs = [(i, i + by) for i in range(count) if 0 <= i + by < count]
    return lax.ppermute(array, axis, pairs)


def block_terms(queries, keys_all, values_all, grad_ctx, starts, first_query, first_key):
    score_scale = queries.shape[-1] ** (-0.5)
    query_pos = first_query + jnp.arange(queries.shape[0], dtype=jnp.int32)
    key_pos = first_key + jnp.arange(keys_all.shape[0], dtype=jnp.int32)
    allowed = (key_pos[None, :] >= starts[:, None]) & (key_pos[None, :] <= query_pos[:, None])
    scores = (
        jnp.einsum("bhe,khe->bhk", queries, keys_all, preferred_element_type=jnp.float32)
        * score_scale
    )
    scores = jnp.where(allowed[:, None, :], scores, neg_large)
    row_top = jnp.max(scores, axis=-1, keepdims=True)
    log_total = row_top + jnp.log(jnp.sum(jnp.exp(scores - row_top), axis=-1, keepdims=True))
    probs = jnp.exp(scores - log_total)
    probs_low = probs.astype(jnp.bfloat16)
    context = jnp.einsum("bhk,khe->bhe", probs_low, values_all, preferred_element_type=jnp.float32)
    grad_probs = jnp.einsum(
        "bhe,khe->bhk", grad_ctx, values_all, preferred_element_type=jnp.float32
    )
    weighted = jnp.sum(probs * grad_probs, axis=-1, keepdims=True)
    grad_scores = (probs * (grad_probs - weighted)).astype(jnp.bfloat16)
    grad_q = (
        jnp.einsum("bhk,khe->bhe", grad_scores, keys_all, preferred_element_type=jnp.float32)
        * score_scale
    )
    grad_k = (
        jnp.einsum("bhk,bhe->khe", grad_scores, queries, preferred_element_type=jnp.float32)
        * score_scale
    )
    grad_v = jnp.einsum("bhk,bhe->khe", probs_low, grad_ctx, preferred_element_type=jnp.float32)
    return (context, grad_q, grad_k, grad_v)


def body(
    own_rows, gain, w_query, w_key, w_value, grad_context, send_slot, recv_slot, episode_start
):
    seq_count = lax.axis_size("seq")
    head_count = lax.axis_size("head")
    shard = lax.axis_index("seq")
    head_pos = lax.axis_index("head")
    row_count = own_rows.shape[0]
    capacity = 2 * row_count // seq_count
    outgoing = (
        jnp.zeros((seq_count * capacity, own_rows.shape[1]), own_rows.dtype)
        .at[send_slot]
        .set(own_rows)
    )
    arrived = lax.all_to_all(outgoing, "seq", split_axis=0, concat_axis=0, tiled=True)
    packed = jnp.take(arrived, recv_slot, axis=0)
    rows_float = packed.astype(jnp.float32)
    inv_rms = lax.rsqrt(jnp.mean(rows_float * rows_float, axis=-1, keepdims=True) + epsilon)
    normed = (rows_float * inv_rms * gain).astype(jnp.bfloat16)
    queries = jnp.dot(normed, w_query, preferred_element_type=jnp.float32).astype(jnp.bfloat16)
    keys_own = jnp.dot(normed, w_key, preferred_element_type=jnp.float32).astype(jnp.bfloat16)
    values_own = jnp.dot(normed, w_value, preferred_element_type=jnp.float32).astype(jnp.bfloat16)
    keys_prev, values_prev = passed_along((keys_own, values_own), "seq", 1)
    local_heads = queries.shape[1] // HD

    def split_heads(matrix):
        return matrix.reshape(matrix.shape[0], local_heads, HD)

    keys_all = split_heads(jnp.concatenate([keys_prev, keys_own], axis=0))
    values_all = split_heads(jnp.concatenate([values_prev, values_own], axis=0))
    query_heads = split_heads(queries)
    grad_heads = split_heads(grad_context)
    block_rows = min(512, row_count)
    first_key = (shard - 1) * row_count
    contexts = []
    grad_queries = []
    grad_keys = jnp.zeros(keys_all.shape, jnp.float32)
    grad_values = jnp.zeros(values_all.shape, jnp.float32)
    for block_index in range(row_count // block_rows):
        low = block_index * block_rows
        high = low + block_rows
        context, grad_q, grad_k, grad_v = block_terms(
            query_heads[low:high],
            keys_all,
            values_all,
            grad_heads[low:high],
            episode_start[low:high],
            shard * row_count + low,
            first_key,
        )
        contexts.append(context.astype(jnp.bfloat16))
        grad_queries.append(grad_q.astype(jnp.bfloat16))
        grad_keys = grad_keys + grad_k
        grad_values = grad_values + grad_v
    context_out = jnp.concatenate(contexts, axis=0).reshape(row_count, -1)
    grad_q_all = jnp.concatenate(grad_queries, axis=0).reshape(row_count, -1)
    send_back = (
        grad_keys[:row_count].reshape(row_count, -1).astype(jnp.bfloat16),
        grad_values[:row_count].reshape(row_count, -1).astype(jnp.bfloat16),
    )
    next_keys, next_values = passed_along((send_back[0], send_back[1]), "seq", -1)
    grad_k_all = (
        grad_keys[row_count:].reshape(row_count, -1) + next_keys.astype(jnp.float32)
    ).astype(jnp.bfloat16)
    grad_v_all = (
        grad_values[row_count:].reshape(row_count, -1) + next_values.astype(jnp.float32)
    ).astype(jnp.bfloat16)
    share = row_count // head_count

    def project(grads, weight):
        return jnp.einsum("rc,dc->rd", grads, weight, preferred_element_type=jnp.float32)

    grad_normed = lax.psum_scatter(
        (
            project(grad_q_all, w_query) + project(grad_k_all, w_key) + project(grad_v_all, w_value)
        ).astype(jnp.bfloat16),
        "head",
        scatter_dimension=0,
        tiled=True,
    ).astype(jnp.float32)
    own_start = head_pos * share
    mine = lax.dynamic_slice_in_dim(rows_float, own_start, share, 0)
    mine_inv = lax.dynamic_slice_in_dim(inv_rms, own_start, share, 0)
    gain_grad = gain * grad_normed
    mixed = jnp.mean(gain_grad * mine, axis=-1, keepdims=True)
    d_rows = (mine_inv * gain_grad - mine * mine_inv**3 * mixed).astype(jnp.bfloat16)
    return (context_out, d_rows)


def solution(mesh):
    in_specs = (
        P("seq", None),
        P(),
        P(None, "head"),
        P(None, "head"),
        P(None, "head"),
        P("seq", "head"),
        P("seq"),
        P("seq"),
        P("seq"),
    )
    out_specs = (P("seq", "head"), P(("seq", "head"), None))
    return jax.shard_map(body, mesh=mesh, in_specs=in_specs, out_specs=out_specs, check_vma=False)
```

profile of v0, /device:TPU:0, one launch (start us, length us, event | category | flops | bytes accessed | tf_op | source)
XLA Modules:
  0.0 355.2 jit_solution(410114957804617158)
XLA Ops:
  8.0 12.3 %scatter_custom_fusion = bf16[2048,2048]{1,0:T(8,128)(2,1)} fusion(s32[1024]{0:T(1024)S(1)} %compare_select_fusion, bf16[1024,2048]{1,0:T(8,128)(2,1)} %param.9, bf16[]{:T(256)} %constant.21.clone.1), kind=kCustom, calls=%fused_computation.25 | custom fusion | bytes 8389120 | tf_op jit(solution)/shard_map/scatter | solution.py:63
  20.2 8.2 %all-to-all-start = ((bf16[16,128,2048]{2,1,0:T(8,128)(2,1)}), bf16[16,128,2048]{2,1,0:T(8,128)(2,1)}, u32[]{:S(2)}, u32[]{:S(2)}) async-start(bf16[16,128,2048]{2,1,0:T(8,128)(2,1)} %bitcast.138), calls=%async_computation | async-start | bytes 16777216 | tf_op jit(solution)/shard_map/all_to_all | solution.py:65
  30.8 1.8 compare_and_fusion.1
  32.6 143.4 %all-to-all-done = bf16[16,128,2048]{2,1,0:T(8,128)(2,1)} async-done(((bf16[16,128,2048]{2,1,0:T(8,128)(2,1)}), bf16[16,128,2048]{2,1,0:T(8,128)(2,1)}, u32[]{:S(2)}, u32[]{:S(2)}) %all-to-all-start) | async-done | bytes 8388640 | tf_op jit(solution)/shard_map/all_to_all | solution.py:65
  176.0 13.3 %gather_fusion = bf16[1024,2048]{1,0:T(8,128)(2,1)} fusion(bf16[2048,2048]{1,0:T(8,128)(2,1)} %bitcast.1, s32[1024]{0:T(1024)S(1)} %fusion.33), kind=kCustom, calls=%fused_computation | custom fusion | bytes 8392704 | tf_op jit(solution)/shard_map/jit(_take)/gather | solution.py:66
  189.3 3.3 multiply_reduce_fusion
  192.6 3.2 multiply_convert_fusion
  198.4 2.1 convolution_convert_fusion.2
  200.5 2.1 collective-permute-start
  204.6 6.1 %collective-permute-done.1 = bf16[1024,256]{1,0:T(8,128)(2,1)S(1)} collective-permute-done((bf16[1024,256]{1,0:T(8,128)(2,1)S(1)}, bf16[1024,256]{1,0:T(8,128)(2,1)S(1)}, u32[]{:S(2)}, u32[]{:S(2)}) %collective-permute-start.1) | collective-permute-done | bytes 524320 | tf_op jit(solution)/shard_map/ppermute | solution.py:16
  211.8 2.4 copy.69
  214.2 3.4 fusion.9
  217.6 2.0 exponential_reduce_fusion
  219.7 2.1 fusion.8
  221.7 2.0 exponential_reduce_fusion.1
  223.8 6.6 %fusion = (f32[512,2]{0,1:T(2,128)S(1)}, f32[2,2048,512]{2,1,0:T(8,128)}) fusion(f32[2,2048,512]{2,1,0:T(8,128)S(1)} %get-tuple-element.17, f32[512,2]{0,1:T(2,128)S(1)} %log_add_fusion, pred[512,2048]{0,1:T(8,128)(4,1)S(1)} %get-tuple-element.13, bf16[512,2,128]{0,2,1:T(8,128)(2,1)S(1)} %bitcast.151, bf16[1024,256]{1,0:T(8,128)(2,1)} %convolution_convert_fusion.2, ...), kind=kOutput, calls=%fused_computation.4 | convolution fusion | flops 549452800 | bytes 19144704 | tf_op jit(solution)/shard_map/bhe,khe->bhk/dot_general | solution.py:34
  230.4 5.8 %fusion.3 = (f32[512,2]{0,1:T(2,128)S(1)}, f32[2,2048,512]{2,1,0:T(8,128)}) fusion(f32[2,2048,512]{2,1,0:T(8,128)S(1)} %get-tuple-element.19, f32[512,2]{0,1:T(2,128)S(1)} %log_add_fusion.1, pred[512,2048]{0,1:T(8,128)(4,1)S(1)} %get-tuple-element.12, bf16[512,2,128]{0,2,1:T(8,128)(2,1)S(1)} %bitcast.153, bf16[1024,256]{1,0:T(8,128)(2,1)} %convolution_convert_fusion.2, ...), kind=kOutput, calls=%fused_computation.9 | convolution fusion | flops 549452800 | bytes 19144704 | tf_op jit(solution)/shard_map/bhe,khe->bhk/dot_general | solution.py:34
  236.2 16.8 %fusion.2 = (bf16[512,2,2048]{0,2,1:T(8,128)(2,1)}, bf16[512,2,2048]{0,2,1:T(8,128)(2,1)}) fusion(f32[2,2048,512]{2,1,0:T(8,128)} %get-tuple-element.21, f32[2,2048,512]{2,1,0:T(8,128)} %copy-done.2, f32[512,2]{0,1:T(2,128)S(1)} %get-tuple-element.20, f32[512,2]{0,1:T(2,128)S(1)} %log_add_fusion, pred[512,2048]{0,1:T(8,128)(4,1)S(1)} %get-tuple-element.13, ...), kind=kLoop, calls=%fused_computation.6 | loop fusion | flops 25165824 | bytes 44056576 | tf_op jit(solution)/shard_map/convert_element_type | solution.py:38
  253.0 3.4 fusion.20
  256.4 3.8 %fusion.45 = f32[2,128,2048]{2,1,0:T(8,128)S(1)} fusion(bf16[512,2,128]{0,2,1:T(8,128)(2,1)} %bitcast.147, bf16[512,2,2048]{0,2,1:T(8,128)(2,1)} %get-tuple-element.25), kind=kOutput, calls=%fused_computation.90 | convolution fusion | flops 536870912 | bytes 6553600 | tf_op jit(solution)/shard_map/bhk,bhe->khe/dot_general | solution.py:44
  261.0 1.5 fusion.14
  264.7 3.8 %fusion.37 = f32[2,2048,128]{1,2,0:T(8,128)} fusion(bf16[512,2,128]{0,2,1:T(8,128)(2,1)S(1)} %bitcast.154, f32[2,2048,512]{2,1,0:T(8,128)S(1)} %bitcast.135, f32[512,2]{0,1:T(2,128)S(1)} %log_add_fusion.1, pred[512,2048]{0,1:T(8,128)(4,1)S(1)} %get-tuple-element.12), kind=kOutput, calls=%fused_computation.84 | convolution fusion | flops 545259520 | bytes 11800576 | tf_op jit(solution)/shard_map/bhk,bhe->khe/dot_general | solution.py:47
  268.6 4.2 %fusion.12 = f32[2048,2,128]{0,2,1:T(8,128)S(1)} fusion(f32[2,2048,128]{1,2,0:T(8,128)} %fusion.37, bf16[512,2,128]{0,2,1:T(8,128)(2,1)S(1)} %bitcast.152, f32[2,2048,512]{2,1,0:T(8,128)S(1)} %bitcast.133, f32[512,2]{0,1:T(2,128)S(1)} %log_add_fusion, pred[512,2048]{0,1:T(8,128)(4,1)S(1)} %get-tuple-element.13), kind=kOutput, calls=%fused_computation.31 | convolution fusion | flops 545783808 | bytes 13897728 | tf_op jit(solution)/shard_map/bhk,bhe->khe/dot_general | solution.py:47
  277.1 13.0 %collective-permute-done.2 = bf16[1024,256]{0,1:T(8,128)(2,1)S(1)} collective-permute-done((bf16[1024,256]{0,1:T(8,128)(2,1)S(1)}, bf16[1024,256]{0,1:T(8,128)(2,1)S(1)}, u32[]{:S(2)}, u32[]{:S(2)}) %collective-permute-start.2) | collective-permute-done | bytes 524320 | tf_op jit(solution)/shard_map/ppermute | solution.py:16
  291.6 4.1 %collective-permute-done.3 = bf16[1024,256]{0,1:T(8,128)(2,1)S(1)} collective-permute-done((bf16[1024,256]{0,1:T(8,128)(2,1)S(1)}, bf16[1024,256]{0,1:T(8,128)(2,1)S(1)}, u32[]{:S(2)}, u32[]{:S(2)}) %collective-permute-start.3) | collective-permute-done | bytes 524320 | tf_op jit(solution)/shard_map/ppermute | solution.py:16
  295.9 3.4 add_convert_fusion
  299.3 6.2 %fusion.40 = f32[1024,2048]{1,0:T(8,128)} fusion(bf16[1024,2048]{1,0:T(8,128)(2,1)} %gather_fusion, pred[1024]{0:T(1024)(128)(4,1)S(1)} %compare_and_fusion.2), kind=kLoop, calls=%fused_computation.85 | loop fusion | flops 4194304 | bytes 12583936 | tf_op jit(solution)/shard_map/convert_element_type | solution.py:67
  305.5 6.3 %fusion.18 = bf16[512,2,128]{0,2,1:T(8,128)(2,1)S(1)} fusion(f32[2,2048,512]{2,1,0:T(8,128)} %copy-done.2, f32[512,2]{0,1:T(2,128)S(1)} %log_add_fusion, pred[512,2048]{0,1:T(8,128)(4,1)S(1)} %get-tuple-element.13, bf16[1024,256]{1,0:T(8,128)(2,1)} %convolution_convert_fusion.2, bf16[1024,256]{1,0:T(8,128)(2,1)} %collective-permute-done), kind=kOutput, calls=%fused_computation.45 | convolution fusion | flops 547487744 | bytes 10752000 | tf_op jit(solution)/shard_map/bhk,khe->bhe/dot_general | solution.py:33
  311.9 3.8 %fusion.17 = bf16[512,2,128]{0,2,1:T(8,128)(2,1)S(1)} fusion(f32[2,2048,512]{2,1,0:T(8,128)S(1)} %bitcast.137, f32[512,2]{0,1:T(2,128)S(1)} %log_add_fusion.1, pred[512,2048]{0,1:T(8,128)(4,1)S(1)} %get-tuple-element.12, bf16[1024,256]{1,0:T(8,128)(2,1)} %convolution_convert_fusion.2, bf16[1024,256]{1,0:T(8,128)(2,1)} %collective-permute-done), kind=kOutput, calls=%fused_computation.44 | convolution fusion | flops 547487744 | bytes 10752000 | tf_op jit(solution)/shard_map/bhk,khe->bhe/dot_general | solution.py:33
  316.7 27.3 %reduce-scatter.2.cloned.1.call-done = bf16[128,2048]{1,0:T(8,128)(2,1)} async-done(((bf16[1024,2048]{1,0:T(8,128)(2,1)}), bf16[128,2048]{1,0:T(8,128)(2,1)}) %reduce-scatter.2.cloned.1.call-update) | async-done | bytes 524304 | tf_op jit(solution)/shard_map/reduce_scatter | solution.py:123
  344.0 1.6 multiply_reduce_fusion.1
  345.6 2.5 subtract_convert_fusion
  (95 shorter events, 18.9 us)
Async XLA Ops:
  7.2 195.4 %copy-start = (bf16[2048,256]{1,0:T(8,128)(2,1)S(1)}, bf16[2048,256]{1,0:T(8,128)(2,1)}, u32[]{:S(2)}) copy-start(bf16[2048,256]{1,0:T(8,128)(2,1)} %param.11) | copy-start | bytes 3145732
  20.2 8.7 %copy-start.12 = (bf16[1024,256]{1,0:T(8,128)(2,1)S(1)}, bf16[1024,256]{1,0:T(8,128)(2,1)}, u32[]{:S(2)}) copy-start(bf16[1024,256]{1,0:T(8,128)(2,1)} %param.14) | copy-start | bytes 1572868
  20.2 10.5 %copy-start.19 = (s32[1024]{0:T(1024)S(1)}, s32[1024]{0:T(1024)}, u32[]{:S(2)}) copy-start(s32[1024]{0:T(1024)} %param.16) | copy-start | bytes 12292
  20.2 10.5 %copy-start.20 = (s32[1024]{0:T(1024)S(1)}, s32[1024]{0:T(1024)}, u32[]{:S(2)}) copy-start(s32[1024]{0:T(1024)} %param.17) | copy-start | bytes 12292
  20.2 155.7 %all-to-all-start = ((bf16[16,128,2048]{2,1,0:T(8,128)(2,1)}), bf16[16,128,2048]{2,1,0:T(8,128)(2,1)}, u32[]{:S(2)}, u32[]{:S(2)}) async-start(bf16[16,128,2048]{2,1,0:T(8,128)(2,1)} %bitcast.138), calls=%async_computation | async-start | bytes 16777216 | tf_op jit(solution)/shard_map/all_to_all | solution.py:65
  28.4 315.6 %reduce-scatter.2.cloned.1.call-start = ((), (), s32[]{:S(2)}) async-start(), calls=%async_computation.2 | async-start | bytes 4718592 | tf_op jit(solution)/shard_map/reduce_scatter | solution.py:123
  176.0 16.6 %copy-start.18 = (f32[2048]{0:T(1024)S(1)}, f32[2048]{0:T(1024)}, u32[]{:S(2)}) copy-start(f32[2048]{0:T(1024)} %param.10) | copy-start | bytes 24580
  189.3 6.5 %copy-start.7 = (bf16[2048,256]{1,0:T(8,128)(2,1)S(1)}, bf16[2048,256]{1,0:T(8,128)(2,1)}, u32[]{:S(2)}) copy-start(bf16[2048,256]{1,0:T(8,128)(2,1)} %param.12) | copy-start | bytes 3145732
  192.6 5.9 %copy-start.9 = (bf16[2048,256]{1,0:T(8,128)(2,1)S(1)}, bf16[2048,256]{1,0:T(8,128)(2,1)}, u32[]{:S(2)}) copy-start(bf16[2048,256]{1,0:T(8,128)(2,1)} %param.13) | copy-start | bytes 3145732
  197.1 13.6 %collective-permute-start.1 = (bf16[1024,256]{1,0:T(8,128)(2,1)S(1)}, bf16[1024,256]{1,0:T(8,128)(2,1)S(1)}, u32[]{:S(2)}, u32[]{:S(2)}) collective-permute-start(bf16[1024,256]{1,0:T(8,128)(2,1)S(1)} %convolution_convert_fusion.1), channel_id=1, source_target_pairs={{0,8},{8,16},{16,24},{24,32},{32,40},{40,48},{48,56},{56,64},{64,7... | collective-permute-start | bytes 1572872 | tf_op jit(solution)/shard_map/ppermute | solution.py:16
  200.5 23.3 %collective-permute-start = (bf16[1024,256]{1,0:T(8,128)(2,1)}, bf16[1024,256]{1,0:T(8,128)(2,1)}, u32[]{:S(2)}, u32[]{:S(2)}) collective-permute-start(bf16[1024,256]{1,0:T(8,128)(2,1)} %convolution_convert_fusion.2), channel_id=1, source_target_pairs={{0,8},{8,16},{16,24},{24,32},{32,40},{40,48},{48,56},{56,64},{64,7... | collective-permute-start | bytes 1572872 | tf_op jit(solution)/shard_map/ppermute | solution.py:16
  214.2 5.4 %copy-start.4 = (bf16[2048,256]{0,1:T(8,128)(2,1)S(1)}, bf16[2048,256]{0,1:T(8,128)(2,1)}, u32[]{:S(2)}) copy-start(bf16[2048,256]{0,1:T(8,128)(2,1)} %copy.69) | copy-start | bytes 3145732
  214.2 5.4 %copy-start.11 = (bf16[512,256]{0,1:T(8,128)(2,1)S(1)}, bf16[512,256]{0,1:T(8,128)(2,1)}, u32[]{:S(2)}) copy-start(bf16[512,256]{0,1:T(8,128)(2,1)} %get-tuple-element.10) | copy-start | bytes 786436
  217.6 6.2 %copy-start.2 = (f32[2,2048,512]{2,1,0:T(8,128)}, f32[2,2048,512]{2,1,0:T(8,128)S(1)}, u32[]{:S(2)}) copy-start(f32[2,2048,512]{2,1,0:T(8,128)S(1)} %get-tuple-element.17) | copy-start | bytes 25165828
  219.6 4.2 %copy-start.14 = (bf16[512,256]{0,1:T(8,128)(2,1)S(1)}, bf16[512,256]{0,1:T(8,128)(2,1)}, u32[]{:S(2)}) copy-start(bf16[512,256]{0,1:T(8,128)(2,1)} %copy.68) | copy-start | bytes 786436
  221.7 8.7 %copy-start.3 = (f32[2,2048,512]{2,1,0:T(8,128)}, f32[2,2048,512]{2,1,0:T(8,128)S(1)}, u32[]{:S(2)}) copy-start(f32[2,2048,512]{2,1,0:T(8,128)S(1)} %get-tuple-element.19) | copy-start | bytes 25165828
  223.8 6.6 %copy-start.16 = (bf16[512,256]{0,1:T(8,128)(2,1)S(1)}, bf16[512,256]{0,1:T(8,128)(2,1)}, u32[]{:S(2)}) copy-start(bf16[512,256]{0,1:T(8,128)(2,1)} %copy.67) | copy-start | bytes 786436
  253.0 7.2 %copy-start.1 = (bf16[512,2,2048]{0,2,1:T(8,128)(2,1)S(1)}, bf16[512,2,2048]{0,2,1:T(8,128)(2,1)}, u32[]{:S(2)}) copy-start(bf16[512,2,2048]{0,2,1:T(8,128)(2,1)} %get-tuple-element.24) | copy-start | bytes 12582916
  253.0 7.2 %copy-start.5 = (bf16[2048,256]{0,1:T(8,128)(2,1)S(1)}, bf16[2048,256]{0,1:T(8,128)(2,1)}, u32[]{:S(2)}) copy-start(bf16[2048,256]{0,1:T(8,128)(2,1)} %copy.69) | copy-start | bytes 3145732
  260.2 4.5 %slice-start.2 = ((s8[8388608]{0:T(1024)(128)(4,1)}), s8[4194304]{0:T(1024)(128)(4,1)S(1)}, s32[]{:S(2)}) async-start(s8[8388608]{0:T(1024)(128)(4,1)} %bitcast.134), calls=%async_computation.5 | async-start | bytes 8388608
  260.2 4.5 %copy-start.17 = (bf16[512,256]{0,1:T(8,128)(2,1)S(1)}, bf16[512,256]{0,1:T(8,128)(2,1)}, u32[]{:S(2)}) copy-start(bf16[512,256]{0,1:T(8,128)(2,1)} %copy.67) | copy-start | bytes 786436
  262.5 6.0 %slice-start = ((s8[8388608]{0:T(1024)(128)(4,1)}), s8[4194304]{0:T(1024)(128)(4,1)S(1)}, s32[]{:S(2)}) async-start(s8[8388608]{0:T(1024)(128)(4,1)} %bitcast.132), calls=%async_computation.3 | async-start | bytes 8388608
  262.5 6.0 %copy-start.15 = (bf16[512,256]{0,1:T(8,128)(2,1)S(1)}, bf16[512,256]{0,1:T(8,128)(2,1)}, u32[]{:S(2)}) copy-start(bf16[512,256]{0,1:T(8,128)(2,1)} %copy.68) | copy-start | bytes 786436
  264.7 3.8 %slice-start.1 = ((s8[8388608]{0:T(1024)(128)(4,1)}), s8[4194304]{0:T(1024)(128)(4,1)S(1)}, s32[]{:S(2)}) async-start(s8[8388608]{0:T(1024)(128)(4,1)} %bitcast.132), calls=%async_computation.4 | async-start | bytes 8388608
  268.6 4.4 %copy-start.13 = (bf16[1024,2,128]{0,2,1:T(8,128)(2,1)S(1)}, bf16[1024,2,128]{0,2,1:T(8,128)(2,1)}, u32[]{:S(2)}) copy-start(bf16[1024,2,128]{0,2,1:T(8,128)(2,1)} %slice.69) | copy-start | bytes 1572868
  272.8 17.3 %slice-start.6 = ((f32[2048,2,128]{0,2,1:T(8,128)}), f32[1024,2,128]{0,2,1:T(8,128)S(1)}, s32[]{:S(2)}) async-start(f32[2048,2,128]{0,2,1:T(8,128)} %copy-done.6), calls=%async_computation.9 | async-start | bytes 2097152 | tf_op jit(solution)/shard_map/slice | solution.py:113
  272.9 17.3 %copy-start.8 = (bf16[2048,256]{1,0:T(8,128)(2,1)S(1)}, bf16[2048,256]{1,0:T(8,128)(2,1)}, u32[]{:S(2)}) copy-start(bf16[2048,256]{1,0:T(8,128)(2,1)} %param.12) | copy-start | bytes 3145732
  273.0 17.1 %collective-permute-start.2 = (bf16[1024,256]{0,1:T(8,128)(2,1)S(1)}, bf16[1024,256]{0,1:T(8,128)(2,1)S(1)}, u32[]{:S(2)}, u32[]{:S(2)}) collective-permute-start(bf16[1024,256]{0,1:T(8,128)(2,1)S(1)} %bitcast.150), channel_id=1, source_target_pairs={{8,0},{16,8},{24,16},{32,24},{40,32},{48,40},{56,48},{64,56},{72,6... | collective-permute-start | bytes 1572872 | tf_op jit(solution)/shard_map/ppermute | solution.py:16
  274.4 21.3 %collective-permute-start.3 = (bf16[1024,256]{0,1:T(8,128)(2,1)S(1)}, bf16[1024,256]{0,1:T(8,128)(2,1)S(1)}, u32[]{:S(2)}, u32[]{:S(2)}) collective-permute-start(bf16[1024,256]{0,1:T(8,128)(2,1)S(1)} %bitcast.149), channel_id=1, source_target_pairs={{8,0},{16,8},{24,16},{32,24},{40,32},{48,40},{56,48},{64,56},{72,6... | collective-permute-start | bytes 1572872 | tf_op jit(solution)/shard_map/ppermute | solution.py:16
  277.1 18.7 %copy-start.10 = (bf16[2048,256]{1,0:T(8,128)(2,1)S(1)}, bf16[2048,256]{1,0:T(8,128)(2,1)}, u32[]{:S(2)}) copy-start(bf16[2048,256]{1,0:T(8,128)(2,1)} %param.13) | copy-start | bytes 3145732
  299.3 12.5 %slice-start.4 = ((s8[8388608]{0:T(1024)(128)(4,1)}), s8[4194304]{0:T(1024)(128)(4,1)S(1)}, s32[]{:S(2)}) async-start(s8[8388608]{0:T(1024)(128)(4,1)} %bitcast.136), calls=%async_computation.7 | async-start | bytes 8388608
  305.5 6.3 %slice-start.5 = ((s8[8388608]{0:T(1024)(128)(4,1)}), s8[4194304]{0:T(1024)(128)(4,1)S(1)}, s32[]{:S(2)}) async-start(s8[8388608]{0:T(1024)(128)(4,1)} %bitcast.136), calls=%async_computation.8 | async-start | bytes 8388608
  (2 other events, 5.0 us)
Sparse Core Ops, SparseCore 0:
  299.4 44.6 reduce-scatter.1
where the time goes:
time: 361 us; the launch traced here: 355 us
  waiting for transfers between devices  194 us (54%)
  matrix products  56 us (16%)
  other arithmetic  41.8 us (12%)
  local copies, waits for them, and re-layouts  34 us (9%)
  between operations  14.9 us (4%)
  starting transfers between devices  14.8 us (4%)
    all_to_all x1, waiting for transfers between devices, body(): lax.all_to_all(outgoing, 'seq', split_axis=0, concat_axis=0, tiled=True)  143 us
    reduce_scatter x1, waiting for transfers between devices, body(): lax.psum_scatter((project(grad_q_all, w_query) + project(grad_k_all, w_ke...  27.3 us
    ppermute x4, waiting for transfers between devices, passed_along(): return lax.ppermute(array, axis, pairs)  23.1 us
    convert_element_type x1, other arithmetic, block_terms(): grad_scores = (probs * (grad_probs - weighted)).astype(jnp.bfloat16)  16.8 us
    gather x1, local copies, waits for them, and re-layouts, body(): packed = jnp.take(arrived, recv_slot, axis=0)  13.3 us
    dot_general x2, matrix products, block_terms(): jnp.einsum('bhe,khe->bhk', grad_ctx, values_all, preferred_element_type=j...  12.4 us
    scatter x1, local copies, waits for them, and re-layouts, body(): outgoing = jnp.zeros((seq_count * capacity, own_rows.shape[1]), own_rows....  12.3 us
    dot_general x2, matrix products, block_terms(): jnp.einsum('bhk,khe->bhe', probs_low, values_all, preferred_element_type=...  10.1 us
  transfers between devices with their start and end apart: 6, of which 5 were waited for; matrix products, arithmetic and copies ran while one was open for 12% of the time, Pallas kernels for 0%

commit v1 on v0

--- a/solution.py
+++ b/solution.py
@@ -57,13 +57,16 @@
     head_pos = lax.axis_index("head")
     row_count = own_rows.shape[0]
     capacity = 2 * row_count // seq_count
+    width = own_rows.shape[1] // head_count
+    own_part = lax.dynamic_slice_in_dim(own_rows, head_pos * width, width, 1)
     outgoing = (
-        jnp.zeros((seq_count * capacity, own_rows.shape[1]), own_rows.dtype)
+        jnp.zeros((seq_count * capacity, width), own_rows.dtype)
         .at[send_slot]
-        .set(own_rows)
+        .set(own_part)
     )
     arrived = lax.all_to_all(outgoing, "seq", split_axis=0, concat_axis=0, tiled=True)
-    packed = jnp.take(arrived, recv_slot, axis=0)
+    packed_part = jnp.take(arrived, recv_slot, axis=0)
+    packed = lax.all_gather(packed_part, "head", axis=1, tiled=True)
     rows_float = packed.astype(jnp.float32)
     inv_rms = lax.rsqrt(jnp.mean(rows_float * rows_float, axis=-1, keepdims=True) + epsilon)
     normed = (rows_float * inv_rms * gain).astype(jnp.bfloat16)

time: 361 us -> 262 us (0.73); the launches traced: 355 us -> 260 us
  waiting for transfers between devices: 194 us -> 94 us
  local copies, waits for them, and re-layouts: 34 us -> 17.5 us
  other arithmetic: 41.8 us -> 52.3 us
  matrix products: 56 us -> 62.3 us
  starting transfers between devices: 14.8 us -> 18.8 us
    all_to_all x1, waiting for transfers between devices: 143 us -> 16.3 us  [body(): lax.all_to_all(outgoing, 'seq', split_axis=0, concat_axis=0, tiled=True)]
    all_gather x0 -> x1, waiting for transfers between devices: none -> 29.8 us  [body(): packed = lax.all_gather(packed_part, 'head', axis=1, tiled=True)]
    convert_element_type x1, other arithmetic: 16.8 us -> 27.9 us  [block_terms(): grad_scores = (probs * (grad_probs - weighted)).astype(jnp.bfloat16)]
    gather x1, local copies, waits for them, and re-layouts: 13.3 us -> 3.93 us  [body(): packed_part = jnp.take(arrived, recv_slot, axis=0)]
    scatter x1, local copies, waits for them, and re-layouts: 12.3 us -> 6.42 us  [body(): outgoing = jnp.zeros((seq_count * capacity, width), own_rows.dtype).at[se...]
    ppermute x4, starting transfers between devices: 6.13 us -> 10.6 us  [passed_along(): return lax.ppermute(array, axis, pairs)]
    reduce_scatter x1, waiting for transfers between devices: 27.3 us -> 23.2 us  [body(): lax.psum_scatter((project(grad_q_all, w_query) + project(grad_k_all, w_ke...]
  transfers between devices with their start and end apart: 6 -> 7, of which waited for: 5 -> 6; matrix products, arithmetic and copies ran while one was open for 12% -> 17% of each run, Pallas kernels for 0% -> 0%
where the time goes in v1:
time: 262 us; the launch traced here: 260 us
  waiting for transfers between devices  94 us (36%)
  matrix products  62.3 us (24%)
  other arithmetic  52.3 us (20%)
  starting transfers between devices  18.8 us (7%)
  local copies, waits for them, and re-layouts  17.5 us (7%)
  between operations  14.8 us (6%)
    all_gather x1, waiting for transfers between devices, body(): packed = lax.all_gather(packed_part, 'head', axis=1, tiled=True)  29.8 us
    convert_element_type x1, other arithmetic, block_terms(): grad_scores = (probs * (grad_probs - weighted)).astype(jnp.bfloat16)  27.9 us
    ppermute x4, waiting for transfers between devices, passed_along(): return lax.ppermute(array, axis, pairs)  24.7 us
    reduce_scatter x1, waiting for transfers between devices, body(): lax.psum_scatter((project(grad_q_all, w_query) + project(grad_k_all, w_ke...  23.2 us
    all_to_all x1, waiting for transfers between devices, body(): lax.all_to_all(outgoing, 'seq', split_axis=0, concat_axis=0, tiled=True)  16.3 us
    dot_general x2, matrix products, block_terms(): jnp.einsum('bhe,khe->bhk', grad_ctx, values_all, preferred_element_type=j...  12.4 us
    ppermute x4, starting transfers between devices, passed_along(): return lax.ppermute(array, axis, pairs)  10.6 us
    dot_general x2, matrix products, block_terms(): jnp.einsum('bhk,khe->bhe', probs_low, values_all, preferred_element_type=...  10.1 us
  transfers between devices with their start and end apart: 7, of which 6 were waited for; matrix products, arithmetic and copies ran while one was open for 17% of the time, Pallas kernels for 0%

profile of v1, /device:TPU:0, one launch (start us, length us, event | category | flops | bytes accessed | tf_op | source)
XLA Modules:
  0.0 259.8 jit_solution(6240070213105515635)
XLA Ops:
  8.0 6.4 %scatter_custom_fusion = bf16[2048,256]{1,0:T(8,128)(2,1)} fusion(s32[1024]{0:T(1024)S(1)} %compare_select_fusion, bf16[1024,2048]{1,0:T(8,128)(2,1)} %param.9, s32[]{:T(128)} %constant.19.clone.1, s32[]{:T(128)S(6)} %select_n.28, bf16[]{:T(256)} %constant.22.clone.1), kind=kCustom, calls=%fused_computation.68 | custom fusion | bytes 1573892 | tf_op jit(solution)/shard_map/scatter | solution.py:65
  14.4 8.1 %all-to-all-start = ((bf16[16,128,256]{2,1,0:T(8,128)(2,1)}), bf16[16,128,256]{2,1,0:T(8,128)(2,1)S(1)}, u32[]{:S(2)}, u32[]{:S(2)}) async-start(bf16[16,128,256]{2,1,0:T(8,128)(2,1)} %bitcast), calls=%async_computation | async-start | bytes 2097152 | tf_op jit(solution)/shard_map/all_to_all | solution.py:67
  24.0 16.3 %all-to-all-done = bf16[16,128,256]{2,1,0:T(8,128)(2,1)S(1)} async-done(((bf16[16,128,256]{2,1,0:T(8,128)(2,1)}), bf16[16,128,256]{2,1,0:T(8,128)(2,1)S(1)}, u32[]{:S(2)}, u32[]{:S(2)}) %all-to-all-start) | async-done | bytes 1048608 | tf_op jit(solution)/shard_map/all_to_all | solution.py:67
  40.3 3.9 %gather_fusion = bf16[1024,256]{1,0:T(8,128)(2,1)S(1)} fusion(bf16[2048,256]{1,0:T(8,128)(2,1)S(1)} %bitcast.135, s32[1024]{0:T(1024)S(1)} %fusion.34), kind=kCustom, calls=%fused_computation | custom fusion | bytes 1052672 | tf_op jit(solution)/shard_map/jit(_take)/gather | solution.py:68
  47.1 1.8 compare_and_fusion.1
  48.9 29.8 %all-gather.2.cloned.1.call-done = bf16[1024,2048]{1,0:T(8,128)(2,1)} async-done(((bf16[1024,256]{1,0:T(8,128)(2,1)}), bf16[1024,2048]{1,0:T(8,128)(2,1)}) %all-gather.2.cloned.1.call-update) | async-done | bytes 4194320 | tf_op jit(solution)/shard_map/all_gather | solution.py:69
  78.7 3.2 %multiply_reduce_fusion = f32[1024]{0:T(1024)S(1)} fusion(bf16[1024,2048]{1,0:T(8,128)(2,1)} %all-gather.2.cloned.1.call-done), kind=kLoop, calls=%fused_computation.20 | loop fusion | flops 6290432 | bytes 4198400 | tf_op jit(solution)/shard_map/reduce_sum | solution.py:71
  82.0 3.8 %convolution_convert_fusion.1 = bf16[1024,256]{1,0:T(8,128)(2,1)S(1)} fusion(bf16[2048,256]{1,0:T(8,128)(2,1)} %param.12, f32[2048]{0:T(1024)S(1)} %copy-done.19, f32[1024]{0:T(1024)S(1)} %add_rsqrt_fusion, bf16[1024,2048]{1,0:T(8,128)(2,1)} %all-gather.2.cloned.1.call-done), kind=kOutput, calls=%fused_computation.33 | convolution fusion | flops 1082392576 | bytes 5779456 | tf_op jit(solution)/shard_map/dot_general | solution.py:74
  85.8 3.5 %collective-permute-start.1 = (bf16[1024,256]{1,0:T(8,128)(2,1)S(1)}, bf16[1024,256]{1,0:T(8,128)(2,1)S(1)}, u32[]{:S(2)}, u32[]{:S(2)}) collective-permute-start(bf16[1024,256]{1,0:T(8,128)(2,1)S(1)} %convolution_convert_fusion.1), channel_id=1, source_target_pairs={{0,8},{8,16},{16,24},{24,32},{32,40},{40,48},{48,56},{56,64},{64,7... | collective-permute-start | bytes 1572872 | tf_op jit(solution)/shard_map/ppermute | solution.py:16
  89.3 2.1 convolution_convert_fusion.2
  91.4 4.2 %collective-permute-start = (bf16[1024,256]{1,0:T(8,128)(2,1)}, bf16[1024,256]{1,0:T(8,128)(2,1)}, u32[]{:S(2)}, u32[]{:S(2)}) collective-permute-start(bf16[1024,256]{1,0:T(8,128)(2,1)} %convolution_convert_fusion.2), channel_id=1, source_target_pairs={{0,8},{8,16},{16,24},{24,32},{32,40},{40,48},{48,56},{56,64},{64,7... | collective-permute-start | bytes 1572872 | tf_op jit(solution)/shard_map/ppermute | solution.py:16
  97.9 3.6 %collective-permute-done.1 = bf16[1024,256]{1,0:T(8,128)(2,1)S(1)} collective-permute-done((bf16[1024,256]{1,0:T(8,128)(2,1)S(1)}, bf16[1024,256]{1,0:T(8,128)(2,1)S(1)}, u32[]{:S(2)}, u32[]{:S(2)}) %collective-permute-start.1) | collective-permute-done | bytes 524320 | tf_op jit(solution)/shard_map/ppermute | solution.py:16
  102.6 2.5 copy.69
  105.1 3.4 %fusion.9 = (f32[512,2]{0,1:T(2,128)S(1)}, f32[2,2048,512]{2,1,0:T(8,128)S(1)}) fusion(pred[512,2048]{0,1:T(8,128)(4,1)S(1)} %get-tuple-element.13, bf16[2048,2,128]{0,2,1:T(8,128)(2,1)} %bitcast.136, bf16[512,2,128]{0,2,1:T(8,128)(2,1)S(1)} %bitcast.142), kind=kOutput, calls=%fused_computation.24 | convolution fusion | flops 543161344 | bytes 10752000 | tf_op jit(solution)/shard_map/bhe,khe->bhk/dot_general | solution.py:25
  108.5 2.0 exponential_reduce_fusion
  110.6 2.1 fusion.8
  112.6 2.0 exponential_reduce_fusion.1
  114.7 6.6 %fusion = (f32[512,2]{0,1:T(2,128)S(1)}, f32[2,2048,512]{2,1,0:T(8,128)}) fusion(f32[2,2048,512]{2,1,0:T(8,128)S(1)} %get-tuple-element.17, f32[512,2]{0,1:T(2,128)S(1)} %log_add_fusion, pred[512,2048]{0,1:T(8,128)(4,1)S(1)} %get-tuple-element.13, bf16[512,2,128]{0,2,1:T(8,128)(2,1)S(1)} %bitcast.147, bf16[1024,256]{1,0:T(8,128)(2,1)} %convolution_convert_fusion.2, ...), kind=kOutput, calls=%fused_computation.4 | convolution fusion | flops 549452800 | bytes 19144704 | tf_op jit(solution)/shard_map/bhe,khe->bhk/dot_general | solution.py:34
  121.3 5.8 %fusion.3 = (f32[512,2]{0,1:T(2,128)S(1)}, f32[2,2048,512]{2,1,0:T(8,128)}) fusion(f32[2,2048,512]{2,1,0:T(8,128)S(1)} %get-tuple-element.19, f32[512,2]{0,1:T(2,128)S(1)} %log_add_fusion.1, pred[512,2048]{0,1:T(8,128)(4,1)S(1)} %get-tuple-element.12, bf16[512,2,128]{0,2,1:T(8,128)(2,1)S(1)} %bitcast.150, bf16[1024,256]{1,0:T(8,128)(2,1)} %convolution_convert_fusion.2, ...), kind=kOutput, calls=%fused_computation.9 | convolution fusion | flops 549452800 | bytes 19144704 | tf_op jit(solution)/shard_map/bhe,khe->bhk/dot_general | solution.py:34
  127.1 27.9 %fusion.2 = (bf16[512,2,2048]{0,2,1:T(8,128)(2,1)}, bf16[512,2,2048]{0,2,1:T(8,128)(2,1)}) fusion(f32[2,2048,512]{2,1,0:T(8,128)} %get-tuple-element.21, f32[2,2048,512]{2,1,0:T(8,128)} %copy-done.2, f32[512,2]{0,1:T(2,128)S(1)} %get-tuple-element.20, f32[512,2]{0,1:T(2,128)S(1)} %log_add_fusion, pred[512,2048]{0,1:T(8,128)(4,1)S(1)} %get-tuple-element.13, ...), kind=kLoop, calls=%fused_computation.6 | loop fusion | flops 25165824 | bytes 44056576 | tf_op jit(solution)/shard_map/convert_element_type | solution.py:38
  155.1 4.1 %fusion.18 = bf16[512,2,128]{0,2,1:T(8,128)(2,1)} fusion(bf16[2048,2,128]{0,2,1:T(8,128)(2,1)} %bitcast.137, bf16[512,2,2048]{0,2,1:T(8,128)(2,1)} %get-tuple-element.25), kind=kOutput, calls=%fused_computation.44 | convolution fusion | flops 537133056 | bytes 5505024 | tf_op jit(solution)/shard_map/bhk,khe->bhe/dot_general | solution.py:40
  159.2 3.8 %fusion.45 = f32[2,128,2048]{2,1,0:T(8,128)S(1)} fusion(bf16[512,2,128]{0,2,1:T(8,128)(2,1)} %bitcast.144, bf16[512,2,2048]{0,2,1:T(8,128)(2,1)} %get-tuple-element.25), kind=kOutput, calls=%fused_computation.90 | convolution fusion | flops 536870912 | bytes 6553600 | tf_op jit(solution)/shard_map/bhk,bhe->khe/dot_general | solution.py:44
  166.9 5.9 %fusion.38 = f32[2,2048,128]{1,2,0:T(8,128)} fusion(bf16[512,2,128]{0,2,1:T(8,128)(2,1)} %bitcast.149, f32[2,2048,512]{2,1,0:T(8,128)S(1)} %bitcast.132, f32[512,2]{0,1:T(2,128)S(1)} %log_add_fusion.1, pred[512,2048]{0,1:T(8,128)(4,1)S(1)} %get-tuple-element.12), kind=kOutput, calls=%fused_computation.85 | convolution fusion | flops 545259520 | bytes 11800576 | tf_op jit(solution)/shard_map/bhk,bhe->khe/dot_general | solution.py:47
  172.8 4.2 %fusion.10 = f32[2048,2,128]{0,2,1:T(8,128)S(1)} fusion(f32[2,2048,128]{1,2,0:T(8,128)} %fusion.38, bf16[512,2,128]{0,2,1:T(8,128)(2,1)S(1)} %bitcast.148, f32[2,2048,512]{2,1,0:T(8,128)S(1)} %bitcast.130, f32[512,2]{0,1:T(2,128)S(1)} %log_add_fusion, pred[512,2048]{0,1:T(8,128)(4,1)S(1)} %get-tuple-element.13), kind=kOutput, calls=%fused_computation.28 | convolution fusion | flops 545783808 | bytes 13897728 | tf_op jit(solution)/shard_map/bhk,bhe->khe/dot_general | solution.py:47
  181.4 13.3 %collective-permute-done.2 = bf16[1024,256]{0,1:T(8,128)(2,1)S(1)} collective-permute-done((bf16[1024,256]{0,1:T(8,128)(2,1)}, bf16[1024,256]{0,1:T(8,128)(2,1)S(1)}, u32[]{:S(2)}, u32[]{:S(2)}) %collective-permute-start.2) | collective-permute-done | bytes 524320 | tf_op jit(solution)/shard_map/ppermute | solution.py:16
  196.2 7.8 %collective-permute-done.3 = bf16[1024,256]{0,1:T(8,128)(2,1)S(1)} collective-permute-done((bf16[1024,256]{0,1:T(8,128)(2,1)S(1)}, bf16[1024,256]{0,1:T(8,128)(2,1)S(1)}, u32[]{:S(2)}, u32[]{:S(2)}) %collective-permute-start.3) | collective-permute-done | bytes 524320 | tf_op jit(solution)/shard_map/ppermute | solution.py:16
  204.1 3.4 %add_convert_fusion = bf16[1024,2048]{1,0:T(8,128)(2,1)} fusion(f32[1024,2048]{1,0:T(8,128)S(1)} %fusion.44, f32[1024,2048]{1,0:T(8,128)S(1)} %fusion.46, bf16[1024,256]{0,1:T(8,128)(2,1)S(1)} %fusion.25, bf16[2048,256]{1,0:T(8,128)(2,1)S(1)} %copy-done.11), kind=kOutput, calls=%fused_computation.14 | convolution fusion | flops 1080033280 | bytes 22544384 | tf_op jit(solution)/shard_map/rc,dc->rd/dot_general | solution.py:124
  207.5 6.5 %convert_element_type.80 = f32[1024,2048]{1,0:T(8,128)} convert(bf16[1024,2048]{1,0:T(8,128)(2,1)} %all-gather.2.cloned.1.call-done) | non-fusion elementwise | flops 2097152 | bytes 12582912 | tf_op jit(solution)/shard_map/convert_element_type | solution.py:70
  214.2 6.3 %fusion.16 = bf16[512,2,128]{0,2,1:T(8,128)(2,1)S(1)} fusion(f32[2,2048,512]{2,1,0:T(8,128)} %copy-done.2, f32[512,2]{0,1:T(2,128)S(1)} %log_add_fusion, pred[512,2048]{0,1:T(8,128)(4,1)S(1)} %get-tuple-element.13, bf16[1024,256]{1,0:T(8,128)(2,1)} %convolution_convert_fusion.2, bf16[1024,256]{1,0:T(8,128)(2,1)} %collective-permute-done), kind=kOutput, calls=%fused_computation.42 | convolution fusion | flops 547487744 | bytes 10752000 | tf_op jit(solution)/shard_map/bhk,khe->bhe/dot_general | solution.py:33
  220.6 3.8 %fusion.15 = bf16[512,2,128]{0,2,1:T(8,128)(2,1)S(1)} fusion(f32[2,2048,512]{2,1,0:T(8,128)S(1)} %bitcast.134, f32[512,2]{0,1:T(2,128)S(1)} %log_add_fusion.1, pred[512,2048]{0,1:T(8,128)(4,1)S(1)} %get-tuple-element.12, bf16[1024,256]{1,0:T(8,128)(2,1)} %convolution_convert_fusion.2, bf16[1024,256]{1,0:T(8,128)(2,1)} %collective-permute-done), kind=kOutput, calls=%fused_computation.41 | convolution fusion | flops 547487744 | bytes 10752000 | tf_op jit(solution)/shard_map/bhk,khe->bhe/dot_general | solution.py:33
  225.5 23.2 %reduce-scatter.2.cloned.1.call-done = bf16[128,2048]{1,0:T(8,128)(2,1)} async-done(((bf16[1024,2048]{1,0:T(8,128)(2,1)}), bf16[128,2048]{1,0:T(8,128)(2,1)}) %reduce-scatter.2.cloned.1.call-update) | async-done | bytes 524304 | tf_op jit(solution)/shard_map/reduce_scatter | solution.py:126
  250.3 2.5 subtract_convert_fusion
  (99 shorter events, 21.2 us)
Async XLA Ops:
  7.2 88.4 %copy-start = (bf16[2048,256]{1,0:T(8,128)(2,1)S(1)}, bf16[2048,256]{1,0:T(8,128)(2,1)}, u32[]{:S(2)}) copy-start(bf16[2048,256]{1,0:T(8,128)(2,1)} %param.11) | copy-start | bytes 3145732
  7.2 38.2 %copy-start.15 = (bf16[1024,256]{1,0:T(8,128)(2,1)S(1)}, bf16[1024,256]{1,0:T(8,128)(2,1)}, u32[]{:S(2)}) copy-start(bf16[1024,256]{1,0:T(8,128)(2,1)} %param.14) | copy-start | bytes 1572868
  7.2 39.9 %copy-start.20 = (s32[1024]{0:T(1024)S(1)}, s32[1024]{0:T(1024)}, u32[]{:S(2)}) copy-start(s32[1024]{0:T(1024)} %param.17) | copy-start | bytes 12292
  14.4 67.5 %copy-start.19 = (f32[2048]{0:T(1024)S(1)}, f32[2048]{0:T(1024)}, u32[]{:S(2)}) copy-start(f32[2048]{0:T(1024)} %param.10) | copy-start | bytes 24580
  14.4 25.9 %all-to-all-start = ((bf16[16,128,256]{2,1,0:T(8,128)(2,1)}), bf16[16,128,256]{2,1,0:T(8,128)(2,1)S(1)}, u32[]{:S(2)}, u32[]{:S(2)}) async-start(bf16[16,128,256]{2,1,0:T(8,128)(2,1)} %bitcast), calls=%async_computation | async-start | bytes 2097152 | tf_op jit(solution)/shard_map/all_to_all | solution.py:67
  22.6 56.1 %all-gather.2.cloned.1.call-start = ((), (), s32[]{:S(2)}) async-start(), calls=%async_computation.2 | async-start | bytes 4718592 | tf_op jit(solution)/shard_map/all_gather | solution.py:69
  45.3 203.4 %reduce-scatter.2.cloned.1.call-start = ((), (), s32[]{:S(2)}) async-start(), calls=%async_computation.3 | async-start | bytes 4718592 | tf_op jit(solution)/shard_map/reduce_scatter | solution.py:126
  78.7 10.5 %copy-start.4 = (bf16[1024,2048]{1,0:T(8,128)(2,1)S(1)}, bf16[1024,2048]{1,0:T(8,128)(2,1)}, u32[]{:S(2)}) copy-start(bf16[1024,2048]{1,0:T(8,128)(2,1)} %all-gather.2.cloned.1.call-done) | copy-start | bytes 12582916
  78.7 10.6 %copy-start.10 = (bf16[2048,256]{1,0:T(8,128)(2,1)S(1)}, bf16[2048,256]{1,0:T(8,128)(2,1)}, u32[]{:S(2)}) copy-start(bf16[2048,256]{1,0:T(8,128)(2,1)} %param.13) | copy-start | bytes 3145732
  85.8 15.8 %collective-permute-start.1 = (bf16[1024,256]{1,0:T(8,128)(2,1)S(1)}, bf16[1024,256]{1,0:T(8,128)(2,1)S(1)}, u32[]{:S(2)}, u32[]{:S(2)}) collective-permute-start(bf16[1024,256]{1,0:T(8,128)(2,1)S(1)} %convolution_convert_fusion.1), channel_id=1, source_target_pairs={{0,8},{8,16},{16,24},{24,32},{32,40},{40,48},{48,56},{56,64},{64,7... | collective-permute-start | bytes 1572872 | tf_op jit(solution)/shard_map/ppermute | solution.py:16
  91.4 23.3 %collective-permute-start = (bf16[1024,256]{1,0:T(8,128)(2,1)}, bf16[1024,256]{1,0:T(8,128)(2,1)}, u32[]{:S(2)}, u32[]{:S(2)}) collective-permute-start(bf16[1024,256]{1,0:T(8,128)(2,1)} %convolution_convert_fusion.2), channel_id=1, source_target_pairs={{0,8},{8,16},{16,24},{24,32},{32,40},{40,48},{48,56},{56,64},{64,7... | collective-permute-start | bytes 1572872 | tf_op jit(solution)/shard_map/ppermute | solution.py:16
  105.1 5.4 %copy-start.5 = (bf16[2048,256]{0,1:T(8,128)(2,1)S(1)}, bf16[2048,256]{0,1:T(8,128)(2,1)}, u32[]{:S(2)}) copy-start(bf16[2048,256]{0,1:T(8,128)(2,1)} %copy.69) | copy-start | bytes 3145732
  105.1 5.4 %copy-start.12 = (bf16[512,256]{0,1:T(8,128)(2,1)S(1)}, bf16[512,256]{0,1:T(8,128)(2,1)}, u32[]{:S(2)}) copy-start(bf16[512,256]{0,1:T(8,128)(2,1)} %get-tuple-element.10) | copy-start | bytes 786436
  108.5 6.2 %copy-start.2 = (f32[2,2048,512]{2,1,0:T(8,128)}, f32[2,2048,512]{2,1,0:T(8,128)S(1)}, u32[]{:S(2)}) copy-start(f32[2,2048,512]{2,1,0:T(8,128)S(1)} %get-tuple-element.17) | copy-start | bytes 25165828
  112.6 8.7 %copy-start.3 = (f32[2,2048,512]{2,1,0:T(8,128)}, f32[2,2048,512]{2,1,0:T(8,128)S(1)}, u32[]{:S(2)}) copy-start(f32[2,2048,512]{2,1,0:T(8,128)S(1)} %get-tuple-element.19) | copy-start | bytes 25165828
  114.7 6.6 %copy-start.18 = (bf16[512,256]{0,1:T(8,128)(2,1)S(1)}, bf16[512,256]{0,1:T(8,128)(2,1)}, u32[]{:S(2)}) copy-start(bf16[512,256]{0,1:T(8,128)(2,1)} %copy.67) | copy-start | bytes 786436
  155.0 7.9 %copy-start.1 = (bf16[512,2,2048]{0,2,1:T(8,128)(2,1)S(1)}, bf16[512,2,2048]{0,2,1:T(8,128)(2,1)}, u32[]{:S(2)}) copy-start(bf16[512,2,2048]{0,2,1:T(8,128)(2,1)} %get-tuple-element.24) | copy-start | bytes 12582916
  155.1 7.9 %copy-start.6 = (bf16[2048,256]{0,1:T(8,128)(2,1)S(1)}, bf16[2048,256]{0,1:T(8,128)(2,1)}, u32[]{:S(2)}) copy-start(bf16[2048,256]{0,1:T(8,128)(2,1)} %copy.69) | copy-start | bytes 3145732
  166.0 6.8 %copy-start.7 = (f32[2048,2,128]{0,2,1:T(8,128)}, f32[2048,2,128]{0,2,1:T(8,128)S(1)}, u32[]{:S(2)}) copy-start(f32[2048,2,128]{0,2,1:T(8,128)S(1)} %fusion.12) | copy-start | bytes 6291460
  166.0 6.8 %slice-start = ((s8[8388608]{0:T(1024)(128)(4,1)}), s8[4194304]{0:T(1024)(128)(4,1)S(1)}, s32[]{:S(2)}) async-start(s8[8388608]{0:T(1024)(128)(4,1)} %bitcast.129), calls=%async_computation.4 | async-start | bytes 8388608
  166.0 6.8 %copy-start.17 = (bf16[512,256]{0,1:T(8,128)(2,1)S(1)}, bf16[512,256]{0,1:T(8,128)(2,1)}, u32[]{:S(2)}) copy-start(bf16[512,256]{0,1:T(8,128)(2,1)} %copy.68) | copy-start | bytes 786436
  166.9 5.9 %slice-start.1 = ((s8[8388608]{0:T(1024)(128)(4,1)}), s8[4194304]{0:T(1024)(128)(4,1)S(1)}, s32[]{:S(2)}) async-start(s8[8388608]{0:T(1024)(128)(4,1)} %bitcast.129), calls=%async_computation.5 | async-start | bytes 8388608
  172.8 7.2 %copy-start.13 = (bf16[512,2,128]{0,2,1:T(8,128)(2,1)S(1)}, bf16[512,2,128]{0,2,1:T(8,128)(2,1)}, u32[]{:S(2)}) copy-start(bf16[512,2,128]{0,2,1:T(8,128)(2,1)} %fusion.18) | copy-start | bytes 786436
  172.8 7.2 %copy-start.14 = (bf16[512,2,128]{0,2,1:T(8,128)(2,1)S(1)}, bf16[512,2,128]{0,2,1:T(8,128)(2,1)}, u32[]{:S(2)}) copy-start(bf16[512,2,128]{0,2,1:T(8,128)(2,1)} %fusion.17) | copy-start | bytes 786436
  177.0 17.7 %slice-start.6 = ((f32[2048,2,128]{0,2,1:T(8,128)}), f32[1024,2,128]{0,2,1:T(8,128)S(1)}, s32[]{:S(2)}) async-start(f32[2048,2,128]{0,2,1:T(8,128)} %copy-done.7), calls=%async_computation.10 | async-start | bytes 2097152 | tf_op jit(solution)/shard_map/slice | solution.py:116
  177.0 17.8 %copy-start.9 = (bf16[2048,256]{1,0:T(8,128)(2,1)S(1)}, bf16[2048,256]{1,0:T(8,128)(2,1)}, u32[]{:S(2)}) copy-start(bf16[2048,256]{1,0:T(8,128)(2,1)} %param.12) | copy-start | bytes 3145732
  177.1 17.6 %collective-permute-start.2 = (bf16[1024,256]{0,1:T(8,128)(2,1)}, bf16[1024,256]{0,1:T(8,128)(2,1)S(1)}, u32[]{:S(2)}, u32[]{:S(2)}) collective-permute-start(bf16[1024,256]{0,1:T(8,128)(2,1)} %bitcast.18), channel_id=1, source_target_pairs={{8,0},{16,8},{24,16},{32,24},{40,32},{48,40},{56,48},{64,56},{72,6... | collective-permute-start | bytes 1572872 | tf_op jit(solution)/shard_map/ppermute | solution.py:16
  178.7 25.3 %collective-permute-start.3 = (bf16[1024,256]{0,1:T(8,128)(2,1)S(1)}, bf16[1024,256]{0,1:T(8,128)(2,1)S(1)}, u32[]{:S(2)}, u32[]{:S(2)}) collective-permute-start(bf16[1024,256]{0,1:T(8,128)(2,1)S(1)} %bitcast.146), channel_id=1, source_target_pairs={{8,0},{16,8},{24,16},{32,24},{40,32},{48,40},{56,48},{64,56},{72,6... | collective-permute-start | bytes 1572872 | tf_op jit(solution)/shard_map/ppermute | solution.py:16
  181.4 22.6 %slice-start.7 = ((f32[2048,2,128]{0,2,1:T(8,128)}), f32[1024,2,128]{0,2,1:T(8,128)S(1)}, s32[]{:S(2)}) async-start(f32[2048,2,128]{0,2,1:T(8,128)} %copy-done.8), calls=%async_computation.11 | async-start | bytes 2097152 | tf_op jit(solution)/shard_map/slice | solution.py:119
  181.4 22.7 %copy-start.11 = (bf16[2048,256]{1,0:T(8,128)(2,1)S(1)}, bf16[2048,256]{1,0:T(8,128)(2,1)}, u32[]{:S(2)}) copy-start(bf16[2048,256]{1,0:T(8,128)(2,1)} %param.13) | copy-start | bytes 3145732
  214.1 6.4 %slice-start.4 = ((s8[8388608]{0:T(1024)(128)(4,1)}), s8[4194304]{0:T(1024)(128)(4,1)S(1)}, s32[]{:S(2)}) async-start(s8[8388608]{0:T(1024)(128)(4,1)} %bitcast.133), calls=%async_computation.8 | async-start | bytes 8388608
  214.2 6.5 %slice-start.5 = ((s8[8388608]{0:T(1024)(128)(4,1)}), s8[4194304]{0:T(1024)(128)(4,1)S(1)}, s32[]{:S(2)}) async-start(s8[8388608]{0:T(1024)(128)(4,1)} %bitcast.133), calls=%async_computation.9 | async-start | bytes 8388608
  (4 other events, 13.6 us)
Sparse Core Ops, SparseCore 0:
  45.4 33.2 all-gather.1
  207.7 40.9 reduce-scatter.1

commit v2 on v1

--- a/solution.py
+++ b/solution.py
@@ -1,6 +1,10 @@
+import functools
+
 import jax
 import jax.numpy as jnp
 from jax import lax
+from jax.experimental import pallas as pl
+from jax.experimental.pallas import tpu as pltpu
 from jax.sharding import PartitionSpec as P
 
 HD = 128
@@ -46,6 +50,73 @@
     )
     grad_v = jnp.einsum("bhk,bhe->khe", probs_low, grad_ctx, preferred_element_type=jnp.float32)
     return (context, grad_q, grad_k, grad_v)
+
+
+def attention_kernel(
+    q_ref, k_ref, v_ref, do_ref, st_ref, ctx_ref, dq_ref, dk_ref, dv_ref, *, tq, window, shift, scale
+):
+    qi = pl.program_id(1)
+    a = pl.multiple_of(qi * tq, tq)
+
+    @pl.when(qi == 0)
+    def _():
+        dk_ref[...] = jnp.zeros_like(dk_ref)
+        dv_ref[...] = jnp.zeros_like(dv_ref)
+
+    q = q_ref[...]
+    k = k_ref[pl.ds(a, window), :]
+    v = v_ref[pl.ds(a, window), :]
+    do = do_ref[...]
+    rows_t = (((1,), (1,)), ((), ()))
+    cols_t = (((0,), (0,)), ((), ()))
+    s = lax.dot_general(q, k, rows_t, preferred_element_type=jnp.float32) * scale
+    key_idx = a + lax.broadcasted_iota(jnp.int32, (tq, window), 1)
+    row_idx = a + shift + lax.broadcasted_iota(jnp.int32, (tq, window), 0)
+    allowed = (key_idx >= st_ref[...]) & (key_idx <= row_idx)
+    s = jnp.where(allowed, s, neg_large)
+    row_top = jnp.max(s, axis=1, keepdims=True)
+    log_total = row_top + jnp.log(jnp.sum(jnp.exp(s - row_top), axis=1, keepdims=True))
+    p = jnp.exp(s - log_total)
+    p_low = p.astype(jnp.bfloat16)
+    ctx_ref[...] = jnp.dot(p_low, v, preferred_element_type=jnp.float32).astype(ctx_ref.dtype)
+    dp = lax.dot_general(do, v, rows_t, preferred_element_type=jnp.float32)
+    weighted = jnp.sum(p * dp, axis=1, keepdims=True)
+    ds = (p * (dp - weighted)).astype(jnp.bfloat16)
+    dq_ref[...] = (jnp.dot(ds, k, preferred_element_type=jnp.float32) * scale).astype(dq_ref.dtype)
+    dk_ref[pl.ds(a, window), :] += lax.dot_general(ds, q, cols_t, preferred_element_type=jnp.float32)
+    dv_ref[pl.ds(a, window), :] += lax.dot_general(p_low, do, cols_t, preferred_element_type=jnp.float32)
+
+
+def attention(queries, keys_all, values_all, grad_ctx, rel_start):
+    rows, width = queries.shape
+    heads = width // HD
+    tq = 256
+    window = rows + tq
+    kernel = functools.partial(
+        attention_kernel, tq=tq, window=window, shift=rows, scale=HD ** (-0.5)
+    )
+    q_spec = pl.BlockSpec((tq, HD), lambda h, i: (i, h))
+    kv_spec = pl.BlockSpec((2 * rows, HD), lambda h, i: (0, h))
+    steps = heads * (rows // tq)
+    cost = pl.CostEstimate(
+        flops=steps * 12 * tq * window * HD,
+        transcendentals=steps * 2 * tq * window,
+        bytes_accessed=rows * width * 2 * 4 + 2 * rows * width * (2 * 2 + 4 * 2),
+    )
+    return pl.pallas_call(
+        kernel,
+        grid=(heads, rows // tq),
+        in_specs=[q_spec, kv_spec, kv_spec, q_spec, pl.BlockSpec((tq, 1), lambda h, i: (i, 0))],
+        out_specs=[q_spec, q_spec, kv_spec, kv_spec],
+        out_shape=[
+            jax.ShapeDtypeStruct((rows, width), jnp.bfloat16),
+            jax.ShapeDtypeStruct((rows, width), jnp.bfloat16),
+            jax.ShapeDtypeStruct((2 * rows, width), jnp.float32),
+            jax.ShapeDtypeStruct((2 * rows, width), jnp.float32),
+        ],
+        compiler_params=pltpu.CompilerParams(dimension_semantics=("arbitrary", "arbitrary")),
+        cost_estimate=cost,
+    )(queries, keys_all, values_all, grad_ctx, rel_start)
 
 
 def body(
@@ -74,49 +145,23 @@
     keys_own = jnp.dot(normed, w_key, preferred_element_type=jnp.float32).astype(jnp.bfloat16)
     values_own = jnp.dot(normed, w_value, preferred_element_type=jnp.float32).astype(jnp.bfloat16)
     keys_prev, values_prev = passed_along((keys_own, values_own), "seq", 1)
-    local_heads = queries.shape[1] // HD
-
-    def split_heads(matrix):
-        return matrix.reshape(matrix.shape[0], local_heads, HD)
-
-    keys_all = split_heads(jnp.concatenate([keys_prev, keys_own], axis=0))
-    values_all = split_heads(jnp.concatenate([values_prev, values_own], axis=0))
-    query_heads = split_heads(queries)
-    grad_heads = split_heads(grad_context)
-    block_rows = min(512, row_count)
-    first_key = (shard - 1) * row_count
-    contexts = []
-    grad_queries = []
-    grad_keys = jnp.zeros(keys_all.shape, jnp.float32)
-    grad_values = jnp.zeros(values_all.shape, jnp.float32)
-    for block_index in range(row_count // block_rows):
-        low = block_index * block_rows
-        high = low + block_rows
-        context, grad_q, grad_k, grad_v = block_terms(
-            query_heads[low:high],
-            keys_all,
-            values_all,
-            grad_heads[low:high],
-            episode_start[low:high],
-            shard * row_count + low,
-            first_key,
-        )
-        contexts.append(context.astype(jnp.bfloat16))
-        grad_queries.append(grad_q.astype(jnp.bfloat16))
-        grad_keys = grad_keys + grad_k
-        grad_values = grad_values + grad_v
-    context_out = jnp.concatenate(contexts, axis=0).reshape(row_count, -1)
-    grad_q_all = jnp.concatenate(grad_queries, axis=0).reshape(row_count, -1)
+    keys_all = jnp.concatenate([keys_prev, keys_own], axis=0)
+    values_all = jnp.concatenate([values_prev, values_own], axis=0)
+    rel_start = (episode_start - (shard - 1) * row_count).reshape(row_count, 1)
+    context_out, grad_q_all, grad_keys, grad_values = attention(
+        queries, keys_all, values_all, grad_context, rel_start
+    )
+    grad_keys = grad_keys * HD ** (-0.5)
     send_back = (
-        grad_keys[:row_count].reshape(row_count, -1).astype(jnp.bfloat16),
-        grad_values[:row_count].reshape(row_count, -1).astype(jnp.bfloat16),
+        grad_keys[:row_count].astype(jnp.bfloat16),
+        grad_values[:row_count].astype(jnp.bfloat16),
     )
     next_keys, next_values = passed_along((send_back[0], send_back[1]), "seq", -1)
     grad_k_all = (
-        grad_keys[row_count:].reshape(row_count, -1) + next_keys.astype(jnp.float32)
+        grad_keys[row_count:] + next_keys.astype(jnp.float32)
     ).astype(jnp.bfloat16)
     grad_v_all = (
-        grad_values[row_count:].reshape(row_count, -1) + next_values.astype(jnp.float32)
+        grad_values[row_count:] + next_values.astype(jnp.float32)
     ).astype(jnp.bfloat16)
     share = row_count // head_count
 

time: 262 us -> 216 us (0.82)
  matrix products: 62.3 us -> 11.6 us
  other arithmetic: 52.3 us -> 21.1 us
  waiting for transfers between devices: 94 us -> 120 us
  Pallas kernels: 0 us -> 18.7 us
  local copies, waits for them, and re-layouts: 17.5 us -> 11.7 us
    dot_general x12 -> x0, matrix products: 48.9 us -> none  [the longest x2 12.4 us: block_terms(): jnp.einsum('bhe,khe->bhk', grad_ctx, values_all, preferred_element_type=j...]
    convert_element_type x3 -> x0, other arithmetic: 28.2 us -> none  [the longest x1 27.9 us: block_terms(): grad_scores = (probs * (grad_probs - weighted)).astype(jnp.bfloat16)]
    pallas_call x0 -> x1, Pallas kernels: none -> 18.7 us  [attention(): pl.pallas_call(kernel, grid=(heads, rows // tq), in_specs=[q_spec, kv_spe...]
    ppermute x4, waiting for transfers between devices: 24.7 us -> 36.6 us  [passed_along(): return lax.ppermute(array, axis, pairs)]
    reduce_scatter x1, waiting for transfers between devices: 23.2 us -> 34.6 us  [body(): lax.psum_scatter((project(grad_q_all, w_query) + project(grad_k_all, w_ke...]
    reduce_sum x2 -> x0, other arithmetic: 4.01 us -> none  [block_terms(): jnp.sum(jnp.exp(scores - row_top), axis=-1, keepdims=True)]
    unnamed x57 -> x16, local copies, waits for them, and re-layouts: 2.94 us -> 0.23 us
  transfers between devices with their start and end apart: 7 -> 7, of which waited for: 6 -> 7; matrix products, arithmetic and copies ran while one was open for 17% -> 7% of each run, Pallas kernels for 0% -> 0%
where the time goes in v2:
time: 216 us; the launch traced here: 215 us
  waiting for transfers between devices  120 us (56%)
  other arithmetic  21.1 us (10%)
  Pallas kernels  18.7 us (9%)
  starting transfers between devices  17.9 us (8%)
  between operations  14.2 us (7%)
  local copies, waits for them, and re-layouts  11.7 us (5%)
  matrix products  11.6 us (5%)
    ppermute x4, waiting for transfers between devices, passed_along(): return lax.ppermute(array, axis, pairs)  36.6 us
    reduce_scatter x1, waiting for transfers between devices, body(): lax.psum_scatter((project(grad_q_all, w_query) + project(grad_k_all, w_ke...  34.6 us
    all_gather x1, waiting for transfers between devices, body(): packed = lax.all_gather(packed_part, 'head', axis=1, tiled=True)  32.3 us
    pallas_call x1, Pallas kernels, attention(): pl.pallas_call(kernel, grid=(heads, rows // tq), in_specs=[q_spec, kv_spe...  18.7 us
    all_to_all x1, waiting for transfers between devices, body(): lax.all_to_all(outgoing, 'seq', split_axis=0, concat_axis=0, tiled=True)  16.3 us
    ppermute x4, starting transfers between devices, passed_along(): return lax.ppermute(array, axis, pairs)  9.72 us
    all_to_all x1, starting transfers between devices, body(): lax.all_to_all(outgoing, 'seq', split_axis=0, concat_axis=0, tiled=True)  8.12 us
    dot_general x3, matrix products, project(): jnp.einsum('rc,dc->rd', grads, weight, preferred_element_type=jnp.float32)  6.94 us
  transfers between devices with their start and end apart: 7, of which 7 were waited for; matrix products, arithmetic and copies ran while one was open for 7% of the time, Pallas kernels for 0%

profile of v2, /device:TPU:0, one launch (start us, length us, event | category | flops | bytes accessed | tf_op | source)
XLA Modules:
  0.0 215.1 jit_solution(5574666275536067588)
XLA Ops:
  7.2 0.8 compare_select_fusion
  8.0 6.4 %scatter_custom_fusion = bf16[2048,256]{1,0:T(8,128)(2,1)} fusion(s32[1024]{0:T(1024)S(1)} %compare_select_fusion, bf16[1024,2048]{1,0:T(8,128)(2,1)} %param.9, s32[]{:T(128)} %constant.16.clone.1, s32[]{:T(128)S(6)} %select_n.21, bf16[]{:T(256)} %constant.19.clone.1), kind=kCustom, calls=%fused_computation.20 | custom fusion | bytes 1573892 | tf_op jit(solution)/shard_map/scatter | solution.py:136
  14.4 8.1 %all-to-all-start = ((bf16[16,128,256]{2,1,0:T(8,128)(2,1)}), bf16[16,128,256]{2,1,0:T(8,128)(2,1)S(1)}, u32[]{:S(2)}, u32[]{:S(2)}) async-start(bf16[16,128,256]{2,1,0:T(8,128)(2,1)} %bitcast), calls=%async_computation | async-start | bytes 2097152 | tf_op jit(solution)/shard_map/all_to_all | solution.py:138
  22.5 0.7 compare_and_fusion
  23.9 16.3 %all-to-all-done = bf16[16,128,256]{2,1,0:T(8,128)(2,1)S(1)} async-done(((bf16[16,128,256]{2,1,0:T(8,128)(2,1)}), bf16[16,128,256]{2,1,0:T(8,128)(2,1)S(1)}, u32[]{:S(2)}, u32[]{:S(2)}) %all-to-all-start) | async-done | bytes 1048608 | tf_op jit(solution)/shard_map/all_to_all | solution.py:138
  40.2 3.9 %gather_fusion = bf16[1024,256]{1,0:T(8,128)(2,1)S(1)} fusion(bf16[2048,256]{1,0:T(8,128)(2,1)S(1)} %bitcast.14, s32[1024]{0:T(1024)S(1)} %fusion.6), kind=kCustom, calls=%fused_computation | custom fusion | bytes 1052672 | tf_op jit(solution)/shard_map/jit(_take)/gather | solution.py:139
  44.2 1.0 broadcast_select_fusion
  45.3 1.0 copy.11.st_ref
  46.3 32.3 %all-gather.2.cloned.1.call-done = bf16[1024,2048]{1,0:T(8,128)(2,1)} async-done(((bf16[1024,256]{1,0:T(8,128)(2,1)}), bf16[1024,2048]{1,0:T(8,128)(2,1)}) %all-gather.2.cloned.1.call-update) | async-done | bytes 4194320 | tf_op jit(solution)/shard_map/all_gather | solution.py:140
  78.7 3.2 %multiply_reduce_fusion = f32[1024]{0:T(1024)S(1)} fusion(bf16[1024,2048]{1,0:T(8,128)(2,1)} %all-gather.2.cloned.1.call-done), kind=kLoop, calls=%fused_computation.4 | loop fusion | flops 6290432 | bytes 4198400 | tf_op jit(solution)/shard_map/reduce_sum | solution.py:142
  82.1 1.3 convolution_convert_fusion.1
  83.4 3.5 %collective-permute-start = (bf16[1024,256]{1,0:T(8,128)(2,1)S(1)}, bf16[1024,256]{1,0:T(8,128)(2,1)S(1)}, u32[]{:S(2)}, u32[]{:S(2)}) collective-permute-start(bf16[1024,256]{1,0:T(8,128)(2,1)S(1)} %convolution_convert_fusion.1), channel_id=1, source_target_pairs={{0,8},{8,16},{16,24},{24,32},{32,40},{40,48},{48,56},{56,64},{64,7... | collective-permute-start | bytes 1572872 | tf_op jit(solution)/shard_map/ppermute | solution.py:20
  86.9 1.3 convolution_convert_fusion
  88.2 3.5 %collective-permute-start.1 = (bf16[1024,256]{1,0:T(8,128)(2,1)S(1)}, bf16[1024,256]{1,0:T(8,128)(2,1)S(1)}, u32[]{:S(2)}, u32[]{:S(2)}) collective-permute-start(bf16[1024,256]{1,0:T(8,128)(2,1)S(1)} %convolution_convert_fusion), channel_id=1, source_target_pairs={{0,8},{8,16},{16,24},{24,32},{32,40},{40,48},{48,56},{56,64},{64,7... | collective-permute-start | bytes 1572872 | tf_op jit(solution)/shard_map/ppermute | solution.py:20
  91.7 2.1 convolution_convert_fusion.2.q_ref
  93.8 5.4 %collective-permute-done = bf16[1024,256]{1,0:T(8,128)(2,1)S(1)} collective-permute-done((bf16[1024,256]{1,0:T(8,128)(2,1)S(1)}, bf16[1024,256]{1,0:T(8,128)(2,1)S(1)}, u32[]{:S(2)}, u32[]{:S(2)}) %collective-permute-start) | collective-permute-done | bytes 524320 | tf_op jit(solution)/shard_map/ppermute | solution.py:20
  99.2 1.0 pad_maximum_fusion.k_ref
  100.2 9.5 %collective-permute-done.1 = bf16[1024,256]{1,0:T(8,128)(2,1)S(1)} collective-permute-done((bf16[1024,256]{1,0:T(8,128)(2,1)S(1)}, bf16[1024,256]{1,0:T(8,128)(2,1)S(1)}, u32[]{:S(2)}, u32[]{:S(2)}) %collective-permute-start.1) | collective-permute-done | bytes 524320 | tf_op jit(solution)/shard_map/ppermute | solution.py:20
  109.7 1.1 pad_maximum_fusion.1.v_ref
  110.8 18.7 %shard_map.104 = (bf16[1024,256]{1,0:T(8,128)(2,1)}, bf16[1024,256]{1,0:T(8,128)(2,1)}, f32[2048,256]{1,0:T(8,128)}, f32[2048,256]{1,0:T(8,128)}) custom-call(bf16[1024,256]{1,0:T(8,128)(2,1)} %convolution_convert_fusion.2.q_ref, bf16[2048,256]{1,0:T(8,128)(2,1)} %pad_maximum_fusion.k_ref, bf16[2048,256]{1,0:T(8,128)(2,1)} %pad_maximum_fusion.1.v_ref, ...), custom_call_target="tpu_custom_call" | custom-call | flops 4026531840 | bytes 8388608 | tf_op jit(solution)/shard_map/pallas_call | solution.py:106
  129.4 1.9 broadcast_multiply_fusion
  131.4 1.3 collective-permute-start.2
  132.8 1.5 collective-permute-start.3
  134.3 1.3 fusion.8
  135.6 13.0 %collective-permute-done.2 = bf16[1024,256]{1,0:T(8,128)(2,1)S(1)} collective-permute-done((bf16[1024,256]{1,0:T(8,128)(2,1)S(1)}, bf16[1024,256]{1,0:T(8,128)(2,1)S(1)}, u32[]{:S(2)}, u32[]{:S(2)}) %collective-permute-start.2) | collective-permute-done | bytes 524320 | tf_op jit(solution)/shard_map/ppermute | solution.py:20
  148.6 1.3 fusion.1
  149.9 8.7 %collective-permute-done.3 = bf16[1024,256]{1,0:T(8,128)(2,1)} collective-permute-done((bf16[1024,256]{1,0:T(8,128)(2,1)S(1)}, bf16[1024,256]{1,0:T(8,128)(2,1)}, u32[]{:S(2)}, u32[]{:S(2)}) %collective-permute-start.3) | collective-permute-done | bytes 524320 | tf_op jit(solution)/shard_map/ppermute | solution.py:20
  158.6 4.4 %add_convert_fusion = bf16[1024,2048]{1,0:T(8,128)(2,1)} fusion(f32[1024,2048]{1,0:T(8,128)S(1)} %fusion.8, f32[1024,2048]{1,0:T(8,128)S(1)} %fusion.1, bf16[2048,256]{1,0:T(8,128)(2,1)S(1)} %copy-done.3, bf16[1024,256]{1,0:T(8,128)(2,1)} %collective-permute-done.3, f32[2048,256]{1,0:T(8,128)S(1)} %copy-done.2), kind=kOutput, calls=%fused_computation.2 | convolution fusion | flops 1080819712 | bytes 23592960 | tf_op jit(solution)/shard_map/rc,dc->rd/dot_general | solution.py:169
  163.0 6.5 %convert_element_type.38 = f32[1024,2048]{1,0:T(8,128)} convert(bf16[1024,2048]{1,0:T(8,128)(2,1)} %all-gather.2.cloned.1.call-done) | non-fusion elementwise | flops 2097152 | bytes 12582912 | tf_op jit(solution)/shard_map/convert_element_type | solution.py:141
  169.6 34.6 %reduce-scatter.2.cloned.1.call-done = bf16[128,2048]{1,0:T(8,128)(2,1)} async-done(((bf16[1024,2048]{1,0:T(8,128)(2,1)}), bf16[128,2048]{1,0:T(8,128)(2,1)}) %reduce-scatter.2.cloned.1.call-update) | async-done | bytes 524304 | tf_op jit(solution)/shard_map/reduce_scatter | solution.py:171
  204.1 1.6 multiply_reduce_fusion.1
  205.8 2.5 %subtract_convert_fusion = bf16[128,2048]{1,0:T(8,128)(2,1)} fusion(bf16[128,2048]{1,0:T(8,128)(2,1)} %reduce-scatter.2.cloned.1.call-done, f32[1024,2048]{1,0:T(8,128)} %convert_element_type.38, s32[]{:T(128)S(6)} %select_n.23, f32[128]{0:T(128)S(1)} %broadcast_multiply_fusion.1, f32[128]{0:T(128)S(1)} %get-tuple-element.10, f32[2048]{0:T(1024)S(1)} %copy-done.6, ...), kind=kLoop, calls=%fused_computation.14 | loop fusion | flops 1835008 | bytes 2106884 | tf_op jit(solution)/shard_map/convert_element_type | solution.py:184
  (27 shorter events, 1.2 us)
Async XLA Ops:
  7.2 84.5 %copy-start = (bf16[2048,256]{1,0:T(8,128)(2,1)S(1)}, bf16[2048,256]{1,0:T(8,128)(2,1)}, u32[]{:S(2)}) copy-start(bf16[2048,256]{1,0:T(8,128)(2,1)} %param.11) | copy-start | bytes 3145732
  14.4 30.9 %copy-start.7 = (s32[1024]{0:T(1024)S(1)}, s32[1024]{0:T(1024)}, u32[]{:S(2)}) copy-start(s32[1024]{0:T(1024)} %param.17) | copy-start | bytes 12292
  14.4 25.9 %all-to-all-start = ((bf16[16,128,256]{2,1,0:T(8,128)(2,1)}), bf16[16,128,256]{2,1,0:T(8,128)(2,1)S(1)}, u32[]{:S(2)}, u32[]{:S(2)}) async-start(bf16[16,128,256]{2,1,0:T(8,128)(2,1)} %bitcast), calls=%async_computation | async-start | bytes 2097152 | tf_op jit(solution)/shard_map/all_to_all | solution.py:138
  22.5 56.2 %all-gather.2.cloned.1.call-start = ((), (), s32[]{:S(2)}) async-start(), calls=%async_computation.2 | async-start | bytes 4718592 | tf_op jit(solution)/shard_map/all_gather | solution.py:140
  44.2 37.7 %copy-start.6 = (f32[2048]{0:T(1024)S(1)}, f32[2048]{0:T(1024)}, u32[]{:S(2)}) copy-start(f32[2048]{0:T(1024)} %param.10) | copy-start | bytes 24580
  45.2 36.7 %copy-start.4 = (bf16[2048,256]{1,0:T(8,128)(2,1)S(1)}, bf16[2048,256]{1,0:T(8,128)(2,1)}, u32[]{:S(2)}) copy-start(bf16[2048,256]{1,0:T(8,128)(2,1)} %param.12) | copy-start | bytes 3145732
  45.2 158.9 %reduce-scatter.2.cloned.1.call-start = ((), (), s32[]{:S(2)}) async-start(), calls=%async_computation.3 | async-start | bytes 4718592 | tf_op jit(solution)/shard_map/reduce_scatter | solution.py:171
  78.7 3.4 %copy-start.1 = (bf16[1024,2048]{1,0:T(8,128)(2,1)S(1)}, bf16[1024,2048]{1,0:T(8,128)(2,1)}, u32[]{:S(2)}) copy-start(bf16[1024,2048]{1,0:T(8,128)(2,1)} %all-gather.2.cloned.1.call-done) | copy-start | bytes 12582916
  82.1 4.8 %copy-start.3 = (bf16[2048,256]{1,0:T(8,128)(2,1)S(1)}, bf16[2048,256]{1,0:T(8,128)(2,1)}, u32[]{:S(2)}) copy-start(bf16[2048,256]{1,0:T(8,128)(2,1)} %param.13) | copy-start | bytes 3145732
  83.4 15.8 %collective-permute-start = (bf16[1024,256]{1,0:T(8,128)(2,1)S(1)}, bf16[1024,256]{1,0:T(8,128)(2,1)S(1)}, u32[]{:S(2)}, u32[]{:S(2)}) collective-permute-start(bf16[1024,256]{1,0:T(8,128)(2,1)S(1)} %convolution_convert_fusion.1), channel_id=1, source_target_pairs={{0,8},{8,16},{16,24},{24,32},{32,40},{40,48},{48,56},{56,64},{64,7... | collective-permute-start | bytes 1572872 | tf_op jit(solution)/shard_map/ppermute | solution.py:20
  88.2 21.5 %collective-permute-start.1 = (bf16[1024,256]{1,0:T(8,128)(2,1)S(1)}, bf16[1024,256]{1,0:T(8,128)(2,1)S(1)}, u32[]{:S(2)}, u32[]{:S(2)}) collective-permute-start(bf16[1024,256]{1,0:T(8,128)(2,1)S(1)} %convolution_convert_fusion), channel_id=1, source_target_pairs={{0,8},{8,16},{16,24},{24,32},{32,40},{40,48},{48,56},{56,64},{64,7... | collective-permute-start | bytes 1572872 | tf_op jit(solution)/shard_map/ppermute | solution.py:20
  129.4 3.3 %copy-start.2 = (f32[2048,256]{1,0:T(8,128)S(1)}, f32[2048,256]{1,0:T(8,128)}, u32[]{:S(2)}) copy-start(f32[2048,256]{1,0:T(8,128)} %get-tuple-element.9) | copy-start | bytes 6291460
  129.4 4.8 %copy-start.5 = (bf16[1024,256]{1,0:T(8,128)(2,1)S(1)}, bf16[1024,256]{1,0:T(8,128)(2,1)}, u32[]{:S(2)}) copy-start(bf16[1024,256]{1,0:T(8,128)(2,1)} %get-tuple-element.7) | copy-start | bytes 1572868
  131.4 17.2 %collective-permute-start.2 = (bf16[1024,256]{1,0:T(8,128)(2,1)S(1)}, bf16[1024,256]{1,0:T(8,128)(2,1)S(1)}, u32[]{:S(2)}, u32[]{:S(2)}) collective-permute-start(bf16[1024,256]{1,0:T(8,128)(2,1)S(1)} %slice.32), channel_id=1, source_target_pairs={{8,0},{16,8},{24,16},{32,24},{40,32},{48,40},{56,48},{64,56},{72,6... | collective-permute-start | bytes 1572872 | tf_op jit(solution)/shard_map/ppermute | solution.py:20
  132.8 25.8 %collective-permute-start.3 = (bf16[1024,256]{1,0:T(8,128)(2,1)S(1)}, bf16[1024,256]{1,0:T(8,128)(2,1)}, u32[]{:S(2)}, u32[]{:S(2)}) collective-permute-start(bf16[1024,256]{1,0:T(8,128)(2,1)S(1)} %slice.31), channel_id=1, source_target_pairs={{8,0},{16,8},{24,16},{32,24},{40,32},{48,40},{56,48},{64,56},{72,6... | collective-permute-start | bytes 1572872 | tf_op jit(solution)/shard_map/ppermute | solution.py:20
Sparse Core Ops, SparseCore 0:
  45.4 33.2 all-gather.1
  163.1 40.9 reduce-scatter.1

commit v3 on v2

--- a/solution.py
+++ b/solution.py
@@ -123,9 +123,11 @@
     own_rows, gain, w_query, w_key, w_value, grad_context, send_slot, recv_slot, episode_start
 ):
     seq_count = lax.axis_size("seq")
-    head_count = lax.axis_size("head")
+    chip_count = lax.axis_size("hy")
+    core_count = lax.axis_size("hc")
+    head_count = chip_count * core_count
     shard = lax.axis_index("seq")
-    head_pos = lax.axis_index("head")
+    head_pos = lax.axis_index("hy") * core_count + lax.axis_index("hc")
     row_count = own_rows.shape[0]
     capacity = 2 * row_count // seq_count
     width = own_rows.shape[1] // head_count
@@ -137,7 +139,7 @@
     )
     arrived = lax.all_to_all(outgoing, "seq", split_axis=0, concat_axis=0, tiled=True)
     packed_part = jnp.take(arrived, recv_slot, axis=0)
-    packed = lax.all_gather(packed_part, "head", axis=1, tiled=True)
+    packed = lax.all_gather(packed_part, ("hy", "hc"), axis=1, tiled=True)
     rows_float = packed.astype(jnp.float32)
     inv_rms = lax.rsqrt(jnp.mean(rows_float * rows_float, axis=-1, keepdims=True) + epsilon)
     normed = (rows_float * inv_rms * gain).astype(jnp.bfloat16)
@@ -168,14 +170,13 @@
     def project(grads, weight):
         return jnp.einsum("rc,dc->rd", grads, weight, preferred_element_type=jnp.float32)
 
-    grad_normed = lax.psum_scatter(
-        (
-            project(grad_q_all, w_query) + project(grad_k_all, w_key) + project(grad_v_all, w_value)
-        ).astype(jnp.bfloat16),
-        "head",
-        scatter_dimension=0,
-        tiled=True,
-    ).astype(jnp.float32)
+    term = (
+        project(grad_q_all, w_query) + project(grad_k_all, w_key) + project(grad_v_all, w_value)
+    ).astype(jnp.bfloat16)
+    term = term.reshape(chip_count, core_count, share, -1).transpose(1, 0, 2, 3)
+    term = term.reshape(row_count, -1)
+    term = lax.psum_scatter(term, "hc", scatter_dimension=0, tiled=True)
+    grad_normed = lax.psum_scatter(term, "hy", scatter_dimension=0, tiled=True).astype(jnp.float32)
     own_start = head_pos * share
     mine = lax.dynamic_slice_in_dim(rows_float, own_start, share, 0)
     mine_inv = lax.dynamic_slice_in_dim(inv_rms, own_start, share, 0)
@@ -186,16 +187,24 @@
 
 
 def solution(mesh):
+    seq_count, head_count = mesh.devices.shape
+    core_count = 2
+    split_mesh = jax.sharding.Mesh(
+        mesh.devices.reshape(seq_count, head_count // core_count, core_count), ("seq", "hy", "hc")
+    )
+    head = ("hy", "hc")
     in_specs = (
         P("seq", None),
         P(),
-        P(None, "head"),
-        P(None, "head"),
-        P(None, "head"),
-        P("seq", "head"),
+        P(None, head),
+        P(None, head),
+        P(None, head),
+        P("seq", head),
         P("seq"),
         P("seq"),
         P("seq"),
     )
-    out_specs = (P("seq", "head"), P(("seq", "head"), None))
-    return jax.shard_map(body, mesh=mesh, in_specs=in_specs, out_specs=out_specs, check_vma=False)
+    out_specs = (P("seq", head), P(("seq",) + head, None))
+    return jax.shard_map(
+        body, mesh=split_mesh, in_specs=in_specs, out_specs=out_specs, check_vma=False
+    )

time: 216 us -> 227 us (1.051)
  waiting for transfers between devices: 120 us -> 129 us
  local copies, waits for them, and re-layouts: 11.7 us -> 15.2 us
    reduce_scatter x1 -> x2, waiting for transfers between devices: 34.6 us -> 44.9 us  [the longest x1 27 us: body(): lax.psum_scatter(term, 'hy', scatter_dimension=0, tiled=True)]
  transfers between devices with their start and end apart: 7 -> 8, of which waited for: 7 -> 8; matrix products, arithmetic and copies ran while one was open for 7% -> 8% of each run, Pallas kernels for 0% -> 0%
where the time goes in v3:
time: 227 us; the launch traced here: 226 us
  waiting for transfers between devices  129 us (57%)
  other arithmetic  21 us (9%)
  Pallas kernels  18.7 us (8%)
  starting transfers between devices  18 us (8%)
  local copies, waits for them, and re-layouts  15.2 us (7%)
  between operations  13.9 us (6%)
  matrix products  10.3 us (5%)
    ppermute x4, waiting for transfers between devices, passed_along(): return lax.ppermute(array, axis, pairs)  35.3 us
    all_gather x1, waiting for transfers between devices, body(): packed = lax.all_gather(packed_part, ('hy', 'hc'), axis=1, tiled=True)  32.3 us
    reduce_scatter x1, waiting for transfers between devices, body(): lax.psum_scatter(term, 'hy', scatter_dimension=0, tiled=True)  27 us
    pallas_call x1, Pallas kernels, attention(): pl.pallas_call(kernel, grid=(heads, rows // tq), in_specs=[q_spec, kv_spe...  18.7 us
    reduce_scatter x1, waiting for transfers between devices, body(): term = lax.psum_scatter(term, 'hc', scatter_dimension=0, tiled=True)  17.9 us
    all_to_all x1, waiting for transfers between devices, body(): lax.all_to_all(outgoing, 'seq', split_axis=0, concat_axis=0, tiled=True)  16.3 us
    ppermute x4, starting transfers between devices, passed_along(): return lax.ppermute(array, axis, pairs)  9.72 us
    all_to_all x1, starting transfers between devices, body(): lax.all_to_all(outgoing, 'seq', split_axis=0, concat_axis=0, tiled=True)  8.12 us
  transfers between devices with their start and end apart: 8, of which 8 were waited for; matrix products, arithmetic and copies ran while one was open for 8% of the time, Pallas kernels for 0%

profile of v3, /device:TPU:0, one launch (start us, length us, event | category | flops | bytes accessed | tf_op | source)
XLA Modules:
  0.0 225.9 jit_solution(12501963972790503999)
XLA Ops:
  8.0 6.4 %scatter_custom_fusion = bf16[2048,256]{1,0:T(8,128)(2,1)} fusion(s32[1024]{0:T(1024)S(1)} %compare_select_fusion, bf16[1024,2048]{1,0:T(8,128)(2,1)} %param.9, s32[]{:T(128)} %constant.17.clone.1, s32[]{:T(128)S(6)} %select_n.21, bf16[]{:T(256)} %constant.20.clone.1), kind=kCustom, calls=%fused_computation.20 | custom fusion | bytes 1573892 | tf_op jit(solution)/shard_map/scatter | solution.py:138
  14.4 8.1 %all-to-all-start = ((bf16[16,128,256]{2,1,0:T(8,128)(2,1)}), bf16[16,128,256]{2,1,0:T(8,128)(2,1)S(1)}, u32[]{:S(2)}, u32[]{:S(2)}) async-start(bf16[16,128,256]{2,1,0:T(8,128)(2,1)} %bitcast), calls=%async_computation | async-start | bytes 2097152 | tf_op jit(solution)/shard_map/all_to_all | solution.py:140
  23.9 16.3 %all-to-all-done = bf16[16,128,256]{2,1,0:T(8,128)(2,1)S(1)} async-done(((bf16[16,128,256]{2,1,0:T(8,128)(2,1)}), bf16[16,128,256]{2,1,0:T(8,128)(2,1)S(1)}, u32[]{:S(2)}, u32[]{:S(2)}) %all-to-all-start) | async-done | bytes 1048608 | tf_op jit(solution)/shard_map/all_to_all | solution.py:140
  40.3 3.9 %gather_fusion = bf16[1024,256]{1,0:T(8,128)(2,1)S(1)} fusion(bf16[2048,256]{1,0:T(8,128)(2,1)S(1)} %bitcast.18, s32[1024]{0:T(1024)S(1)} %fusion.6), kind=kCustom, calls=%fused_computation | custom fusion | bytes 1052672 | tf_op jit(solution)/shard_map/jit(_take)/gather | solution.py:141
  45.3 1.1 copy.12.st_ref
  46.4 32.3 %all-gather.2.cloned.1.call-done = bf16[1024,2048]{1,0:T(8,128)(2,1)} async-done(((bf16[1024,256]{1,0:T(8,128)(2,1)}), bf16[1024,2048]{1,0:T(8,128)(2,1)}) %all-gather.2.cloned.1.call-update) | async-done | bytes 4194320 | tf_op jit(solution)/shard_map/all_gather | solution.py:142
  78.7 3.2 %multiply_reduce_fusion = f32[1024]{0:T(1024)S(1)} fusion(bf16[1024,2048]{1,0:T(8,128)(2,1)} %all-gather.2.cloned.1.call-done), kind=kLoop, calls=%fused_computation.4 | loop fusion | flops 6290432 | bytes 4198400 | tf_op jit(solution)/shard_map/reduce_sum | solution.py:144
  82.1 1.3 convolution_convert_fusion.1
  83.4 3.5 %collective-permute-start = (bf16[1024,256]{1,0:T(8,128)(2,1)S(1)}, bf16[1024,256]{1,0:T(8,128)(2,1)S(1)}, u32[]{:S(2)}, u32[]{:S(2)}) collective-permute-start(bf16[1024,256]{1,0:T(8,128)(2,1)S(1)} %convolution_convert_fusion.1), channel_id=1, source_target_pairs={{0,8},{8,16},{16,24},{24,32},{32,40},{40,48},{48,56},{56,64},{64,7... | collective-permute-start | bytes 1572872 | tf_op jit(solution)/shard_map/ppermute | solution.py:20
  86.9 1.3 convolution_convert_fusion
  88.3 3.5 %collective-permute-start.1 = (bf16[1024,256]{1,0:T(8,128)(2,1)S(1)}, bf16[1024,256]{1,0:T(8,128)(2,1)S(1)}, u32[]{:S(2)}, u32[]{:S(2)}) collective-permute-start(bf16[1024,256]{1,0:T(8,128)(2,1)S(1)} %convolution_convert_fusion), channel_id=1, source_target_pairs={{0,8},{8,16},{16,24},{24,32},{32,40},{40,48},{48,56},{56,64},{64,7... | collective-permute-start | bytes 1572872 | tf_op jit(solution)/shard_map/ppermute | solution.py:20
  91.7 2.1 convolution_convert_fusion.2.q_ref
  93.8 5.4 %collective-permute-done = bf16[1024,256]{1,0:T(8,128)(2,1)S(1)} collective-permute-done((bf16[1024,256]{1,0:T(8,128)(2,1)S(1)}, bf16[1024,256]{1,0:T(8,128)(2,1)S(1)}, u32[]{:S(2)}, u32[]{:S(2)}) %collective-permute-start) | collective-permute-done | bytes 524320 | tf_op jit(solution)/shard_map/ppermute | solution.py:20
  99.2 1.0 pad_maximum_fusion.k_ref
  100.2 9.5 %collective-permute-done.1 = bf16[1024,256]{1,0:T(8,128)(2,1)S(1)} collective-permute-done((bf16[1024,256]{1,0:T(8,128)(2,1)S(1)}, bf16[1024,256]{1,0:T(8,128)(2,1)S(1)}, u32[]{:S(2)}, u32[]{:S(2)}) %collective-permute-start.1) | collective-permute-done | bytes 524320 | tf_op jit(solution)/shard_map/ppermute | solution.py:20
  109.7 1.1 pad_maximum_fusion.1.v_ref
  110.8 18.7 %shard_map.104 = (bf16[1024,256]{1,0:T(8,128)(2,1)}, bf16[1024,256]{1,0:T(8,128)(2,1)}, f32[2048,256]{1,0:T(8,128)}, f32[2048,256]{1,0:T(8,128)}) custom-call(bf16[1024,256]{1,0:T(8,128)(2,1)} %convolution_convert_fusion.2.q_ref, bf16[2048,256]{1,0:T(8,128)(2,1)} %pad_maximum_fusion.k_ref, bf16[2048,256]{1,0:T(8,128)(2,1)} %pad_maximum_fusion.1.v_ref, ...), custom_call_target="tpu_custom_call" | custom-call | flops 4026531840 | bytes 8388608 | tf_op jit(solution)/shard_map/pallas_call | solution.py:106
  129.5 1.8 broadcast_multiply_fusion
  131.3 1.3 collective-permute-start.2
  132.6 1.3 slice.31
  133.9 1.5 collective-permute-start.3
  135.4 1.3 fusion.8
  136.7 11.8 %collective-permute-done.2 = bf16[1024,256]{1,0:T(8,128)(2,1)S(1)} collective-permute-done((bf16[1024,256]{1,0:T(8,128)(2,1)S(1)}, bf16[1024,256]{1,0:T(8,128)(2,1)S(1)}, u32[]{:S(2)}, u32[]{:S(2)}) %collective-permute-start.2) | collective-permute-done | bytes 524320 | tf_op jit(solution)/shard_map/ppermute | solution.py:20
  148.5 1.3 fusion.1
  149.8 8.6 %collective-permute-done.3 = bf16[1024,256]{1,0:T(8,128)(2,1)S(1)} collective-permute-done((bf16[1024,256]{1,0:T(8,128)(2,1)S(1)}, bf16[1024,256]{1,0:T(8,128)(2,1)S(1)}, u32[]{:S(2)}, u32[]{:S(2)}) %collective-permute-start.3) | collective-permute-done | bytes 524320 | tf_op jit(solution)/shard_map/ppermute | solution.py:20
  158.4 3.0 %add_convert_fusion = bf16[1024,2048]{1,0:T(8,128)(2,1)S(1)} fusion(f32[1024,2048]{1,0:T(8,128)S(1)} %fusion.8, f32[1024,2048]{1,0:T(8,128)S(1)} %fusion.1, bf16[2048,256]{1,0:T(8,128)(2,1)} %param.13, bf16[1024,256]{1,0:T(8,128)(2,1)S(1)} %collective-permute-done.3, f32[2048,256]{1,0:T(8,128)} %get-tuple-element.9), kind=kOutput, calls=%fused_computation.2 | convolution fusion | flops 1080819712 | bytes 23592960 | tf_op jit(solution)/shard_map/rc,dc->rd/dot_general | solution.py:171
  161.4 2.3 copy.13
  163.8 17.9 %reduce-scatter.3.cloned.1.call-done = bf16[512,2048]{1,0:T(8,128)(2,1)} async-done(((bf16[1024,2048]{1,0:T(8,128)(2,1)}), bf16[512,2048]{1,0:T(8,128)(2,1)}) %reduce-scatter.3.cloned.1.call-update) | async-done | bytes 2097168 | tf_op jit(solution)/shard_map/reduce_scatter | solution.py:178
  181.7 6.5 %convert_element_type.38 = f32[1024,2048]{1,0:T(8,128)} convert(bf16[1024,2048]{1,0:T(8,128)(2,1)} %all-gather.2.cloned.1.call-done) | non-fusion elementwise | flops 2097152 | bytes 12582912 | tf_op jit(solution)/shard_map/convert_element_type | solution.py:143
  188.3 27.0 %reduce-scatter.5.cloned.1.call-done = bf16[128,2048]{1,0:T(8,128)(2,1)} async-done(((bf16[512,2048]{1,0:T(8,128)(2,1)}), bf16[128,2048]{1,0:T(8,128)(2,1)}) %reduce-scatter.5.cloned.1.call-update) | async-done | bytes 524304 | tf_op jit(solution)/shard_map/reduce_scatter | solution.py:179
  215.2 1.6 multiply_reduce_fusion.1
  216.9 2.5 %subtract_convert_fusion = bf16[128,2048]{1,0:T(8,128)(2,1)} fusion(bf16[128,2048]{1,0:T(8,128)(2,1)} %reduce-scatter.5.cloned.1.call-done, f32[1024,2048]{1,0:T(8,128)} %convert_element_type.38, s32[]{:T(128)S(6)} %select_n.23, f32[128]{0:T(128)S(1)} %broadcast_multiply_fusion.1, f32[128]{0:T(128)S(1)} %get-tuple-element.10, f32[2048]{0:T(1024)S(1)} %copy-done.5, ...), kind=kLoop, calls=%fused_computation.14 | loop fusion | flops 1835008 | bytes 2106884 | tf_op jit(solution)/shard_map/convert_element_type | solution.py:185
  (29 shorter events, 3.7 us)
Async XLA Ops:
  7.2 84.6 %copy-start = (bf16[2048,256]{1,0:T(8,128)(2,1)S(1)}, bf16[2048,256]{1,0:T(8,128)(2,1)}, u32[]{:S(2)}) copy-start(bf16[2048,256]{1,0:T(8,128)(2,1)} %param.11) | copy-start | bytes 3145732
  14.4 30.9 %copy-start.6 = (s32[1024]{0:T(1024)S(1)}, s32[1024]{0:T(1024)}, u32[]{:S(2)}) copy-start(s32[1024]{0:T(1024)} %param.17) | copy-start | bytes 12292
  14.4 25.9 %all-to-all-start = ((bf16[16,128,256]{2,1,0:T(8,128)(2,1)}), bf16[16,128,256]{2,1,0:T(8,128)(2,1)S(1)}, u32[]{:S(2)}, u32[]{:S(2)}) async-start(bf16[16,128,256]{2,1,0:T(8,128)(2,1)} %bitcast), calls=%async_computation | async-start | bytes 2097152 | tf_op jit(solution)/shard_map/all_to_all | solution.py:140
  22.5 56.2 %all-gather.2.cloned.1.call-start = ((), (), s32[]{:S(2)}) async-start(), calls=%async_computation.3 | async-start | bytes 4718592 | tf_op jit(solution)/shard_map/all_gather | solution.py:142
  44.2 37.7 %copy-start.3 = (bf16[2048,256]{1,0:T(8,128)(2,1)S(1)}, bf16[2048,256]{1,0:T(8,128)(2,1)}, u32[]{:S(2)}) copy-start(bf16[2048,256]{1,0:T(8,128)(2,1)} %param.12) | copy-start | bytes 3145732
  44.2 37.7 %copy-start.5 = (f32[2048]{0:T(1024)S(1)}, f32[2048]{0:T(1024)}, u32[]{:S(2)}) copy-start(f32[2048]{0:T(1024)} %param.10) | copy-start | bytes 24580
  45.2 136.4 %reduce-scatter.3.cloned.1.call-start = ((), (), s32[]{:S(2)}) async-start(), calls=%async_computation.4 | async-start | bytes 6291456 | tf_op jit(solution)/shard_map/reduce_scatter | solution.py:178
  78.7 3.4 %copy-start.1 = (bf16[1024,2048]{1,0:T(8,128)(2,1)S(1)}, bf16[1024,2048]{1,0:T(8,128)(2,1)}, u32[]{:S(2)}) copy-start(bf16[1024,2048]{1,0:T(8,128)(2,1)} %all-gather.2.cloned.1.call-done) | copy-start | bytes 12582916
  82.1 4.8 %copy-start.2 = (bf16[2048,256]{1,0:T(8,128)(2,1)S(1)}, bf16[2048,256]{1,0:T(8,128)(2,1)}, u32[]{:S(2)}) copy-start(bf16[2048,256]{1,0:T(8,128)(2,1)} %param.13) | copy-start | bytes 3145732
  83.4 15.8 %collective-permute-start = (bf16[1024,256]{1,0:T(8,128)(2,1)S(1)}, bf16[1024,256]{1,0:T(8,128)(2,1)S(1)}, u32[]{:S(2)}, u32[]{:S(2)}) collective-permute-start(bf16[1024,256]{1,0:T(8,128)(2,1)S(1)} %convolution_convert_fusion.1), channel_id=1, source_target_pairs={{0,8},{8,16},{16,24},{24,32},{32,40},{40,48},{48,56},{56,64},{64,7... | collective-permute-start | bytes 1572872 | tf_op jit(solution)/shard_map/ppermute | solution.py:20
  88.3 21.4 %collective-permute-start.1 = (bf16[1024,256]{1,0:T(8,128)(2,1)S(1)}, bf16[1024,256]{1,0:T(8,128)(2,1)S(1)}, u32[]{:S(2)}, u32[]{:S(2)}) collective-permute-start(bf16[1024,256]{1,0:T(8,128)(2,1)S(1)} %convolution_convert_fusion), channel_id=1, source_target_pairs={{0,8},{8,16},{16,24},{24,32},{32,40},{40,48},{48,56},{56,64},{64,7... | collective-permute-start | bytes 1572872 | tf_op jit(solution)/shard_map/ppermute | solution.py:20
  129.5 6.0 %copy-start.4 = (bf16[1024,256]{1,0:T(8,128)(2,1)S(1)}, bf16[1024,256]{1,0:T(8,128)(2,1)}, u32[]{:S(2)}) copy-start(bf16[1024,256]{1,0:T(8,128)(2,1)} %get-tuple-element.7) | copy-start | bytes 1572868
  131.3 17.2 %collective-permute-start.2 = (bf16[1024,256]{1,0:T(8,128)(2,1)S(1)}, bf16[1024,256]{1,0:T(8,128)(2,1)S(1)}, u32[]{:S(2)}, u32[]{:S(2)}) collective-permute-start(bf16[1024,256]{1,0:T(8,128)(2,1)S(1)} %slice.32), channel_id=1, source_target_pairs={{8,0},{16,8},{24,16},{32,24},{40,32},{48,40},{56,48},{64,56},{72,6... | collective-permute-start | bytes 1572872 | tf_op jit(solution)/shard_map/ppermute | solution.py:20
  133.9 24.5 %collective-permute-start.3 = (bf16[1024,256]{1,0:T(8,128)(2,1)S(1)}, bf16[1024,256]{1,0:T(8,128)(2,1)S(1)}, u32[]{:S(2)}, u32[]{:S(2)}) collective-permute-start(bf16[1024,256]{1,0:T(8,128)(2,1)S(1)} %slice.31), channel_id=1, source_target_pairs={{8,0},{16,8},{24,16},{32,24},{40,32},{48,40},{56,48},{64,56},{72,6... | collective-permute-start | bytes 1572872 | tf_op jit(solution)/shard_map/ppermute | solution.py:20
  163.7 51.5 %reduce-scatter.5.cloned.1.call-start = ((), (), s32[]{:S(2)}) async-start(), calls=%async_computation.5 | async-start | bytes 2621440 | tf_op jit(solution)/shard_map/reduce_scatter | solution.py:179
Sparse Core Ops, SparseCore 0:
  45.4 33.2 all-gather.1
  163.8 17.8 reduce-scatter.2
  184.1 31.1 reduce-scatter.4

commit v4 on v2

--- a/solution.py
+++ b/solution.py
@@ -144,25 +144,32 @@
     queries = jnp.dot(normed, w_query, preferred_element_type=jnp.float32).astype(jnp.bfloat16)
     keys_own = jnp.dot(normed, w_key, preferred_element_type=jnp.float32).astype(jnp.bfloat16)
     values_own = jnp.dot(normed, w_value, preferred_element_type=jnp.float32).astype(jnp.bfloat16)
-    keys_prev, values_prev = passed_along((keys_own, values_own), "seq", 1)
-    keys_all = jnp.concatenate([keys_prev, keys_own], axis=0)
-    values_all = jnp.concatenate([values_prev, values_own], axis=0)
     rel_start = (episode_start - (shard - 1) * row_count).reshape(row_count, 1)
-    context_out, grad_q_all, grad_keys, grad_values = attention(
-        queries, keys_all, values_all, grad_context, rel_start
-    )
-    grad_keys = grad_keys * HD ** (-0.5)
-    send_back = (
-        grad_keys[:row_count].astype(jnp.bfloat16),
-        grad_values[:row_count].astype(jnp.bfloat16),
-    )
-    next_keys, next_values = passed_along((send_back[0], send_back[1]), "seq", -1)
-    grad_k_all = (
-        grad_keys[row_count:] + next_keys.astype(jnp.float32)
-    ).astype(jnp.bfloat16)
-    grad_v_all = (
-        grad_values[row_count:] + next_values.astype(jnp.float32)
-    ).astype(jnp.bfloat16)
+    local_heads = queries.shape[1] // HD
+    outs = []
+    for h in range(local_heads):
+        cols = slice(h * HD, (h + 1) * HD)
+        keys_h, values_h = keys_own[:, cols], values_own[:, cols]
+        keys_prev, values_prev = passed_along((keys_h, values_h), "seq", 1)
+        context_h, grad_q_h, grad_k_h, grad_v_h = attention(
+            queries[:, cols],
+            jnp.concatenate([keys_prev, keys_h], axis=0),
+            jnp.concatenate([values_prev, values_h], axis=0),
+            grad_context[:, cols],
+            rel_start,
+        )
+        grad_k_h = grad_k_h * HD ** (-0.5)
+        next_k, next_v = passed_along(
+            (grad_k_h[:row_count].astype(jnp.bfloat16), grad_v_h[:row_count].astype(jnp.bfloat16)),
+            "seq",
+            -1,
+        )
+        grad_k_h = (grad_k_h[row_count:] + next_k.astype(jnp.float32)).astype(jnp.bfloat16)
+        grad_v_h = (grad_v_h[row_count:] + next_v.astype(jnp.float32)).astype(jnp.bfloat16)
+        outs.append((context_h, grad_q_h, grad_k_h, grad_v_h))
+    context_out, grad_q_all, grad_k_all, grad_v_all = (
+        jnp.concatenate(parts, axis=1) for parts in zip(*outs)
+    )
     share = row_count // head_count
 
     def project(grads, weight):

time: 216 us -> 212 us (0.981)
  waiting for transfers between devices: 120 us -> 91 us
  starting transfers between devices: 17.9 us -> 27.4 us
  other arithmetic: 21.1 us -> 27.1 us
  local copies, waits for them, and re-layouts: 11.7 us -> 16.8 us
  Pallas kernels: 18.7 us -> 21.1 us
    ppermute x4 -> x8, waiting for transfers between devices: 36.6 us -> 10.2 us  [passed_along(): return lax.ppermute(array, axis, pairs)]
    ppermute x4 -> x8, starting transfers between devices: 9.72 us -> 19.3 us  [passed_along(): return lax.ppermute(array, axis, pairs)]
    slice x2 -> x8, local copies, waits for them, and re-layouts: 0.11 us -> 5.37 us  [the longest x2 2.14 us: body(): grad_v_h[:row_count].astype(jnp.bfloat16)]
    concatenate x2 -> x5, other arithmetic: 2.1 us -> 6.18 us  [the longest x2 2.73 us: body(): jnp.concatenate([values_prev, values_h], axis=0)]
    dot_general x1, matrix products: 1.3 us -> 3.94 us  [body(): jnp.dot(normed, w_key, preferred_element_type=jnp.float32)]
    pallas_call x1 -> x2, Pallas kernels: 18.7 us -> 21.1 us  [attention(): pl.pallas_call(kernel, grid=(heads, rows // tq), in_specs=[q_spec, kv_spe...]
  transfers between devices with their start and end apart: 7 -> 11, of which waited for: 7 -> 6; matrix products, arithmetic and copies ran while one was open for 7% -> 15% of each run, Pallas kernels for 0% -> 10%
where the time goes in v4:
time: 212 us; the launch traced here: 211 us
  waiting for transfers between devices  91 us (43%)
  starting transfers between devices  27.4 us (13%)
  other arithmetic  27.1 us (13%)
  Pallas kernels  21.1 us (10%)
  local copies, waits for them, and re-layouts  16.8 us (8%)
  between operations  14.4 us (7%)
  matrix products  13.4 us (6%)
    reduce_scatter x1, waiting for transfers between devices, body(): lax.psum_scatter((project(grad_q_all, w_query) + project(grad_k_all, w_ke...  33 us
    all_gather x1, waiting for transfers between devices, body(): packed = lax.all_gather(packed_part, 'head', axis=1, tiled=True)  31.5 us
    pallas_call x2, Pallas kernels, attention(): pl.pallas_call(kernel, grid=(heads, rows // tq), in_specs=[q_spec, kv_spe...  21.1 us
    ppermute x8, starting transfers between devices, passed_along(): return lax.ppermute(array, axis, pairs)  19.3 us
    all_to_all x1, waiting for transfers between devices, body(): lax.all_to_all(outgoing, 'seq', split_axis=0, concat_axis=0, tiled=True)  16.3 us
    ppermute x8, waiting for transfers between devices, passed_along(): return lax.ppermute(array, axis, pairs)  10.2 us
    all_to_all x1, starting transfers between devices, body(): lax.all_to_all(outgoing, 'seq', split_axis=0, concat_axis=0, tiled=True)  7.99 us
    dot_general x3, matrix products, project(): jnp.einsum('rc,dc->rd', grads, weight, preferred_element_type=jnp.float32)  6.81 us
  transfers between devices with their start and end apart: 11, of which 6 were waited for; matrix products, arithmetic and copies ran while one was open for 15% of the time, Pallas kernels for 10%

profile of v4, /device:TPU:0, one launch (start us, length us, event | category | flops | bytes accessed | tf_op | source)
XLA Modules:
  0.0 211.3 jit_solution(8136188009629995265)
XLA Ops:
  8.0 6.4 %scatter_custom_fusion = bf16[2048,256]{1,0:T(8,128)(2,1)} fusion(s32[1024]{0:T(1024)S(1)} %compare_select_fusion, bf16[1024,2048]{1,0:T(8,128)(2,1)} %param.9, s32[]{:T(128)} %constant.16.clone.1, s32[]{:T(128)S(6)} %select_n.21, bf16[]{:T(256)} %constant.19.clone.1), kind=kCustom, calls=%fused_computation.39 | custom fusion | bytes 1573892 | tf_op jit(solution)/shard_map/scatter | solution.py:136
  14.4 8.0 %all-to-all-start = ((bf16[16,128,256]{2,1,0:T(8,128)(2,1)}), bf16[16,128,256]{2,1,0:T(8,128)(2,1)S(1)}, u32[]{:S(2)}, u32[]{:S(2)}) async-start(bf16[16,128,256]{2,1,0:T(8,128)(2,1)} %bitcast), calls=%async_computation | async-start | bytes 2097152 | tf_op jit(solution)/shard_map/all_to_all | solution.py:138
  23.9 16.3 %all-to-all-done = bf16[16,128,256]{2,1,0:T(8,128)(2,1)S(1)} async-done(((bf16[16,128,256]{2,1,0:T(8,128)(2,1)}), bf16[16,128,256]{2,1,0:T(8,128)(2,1)S(1)}, u32[]{:S(2)}, u32[]{:S(2)}) %all-to-all-start) | async-done | bytes 1048608 | tf_op jit(solution)/shard_map/all_to_all | solution.py:138
  40.2 3.9 %gather_fusion = bf16[1024,256]{1,0:T(8,128)(2,1)S(1)} fusion(bf16[2048,256]{1,0:T(8,128)(2,1)S(1)} %bitcast.13, s32[1024]{0:T(1024)S(1)} %fusion.16), kind=kCustom, calls=%fused_computation | custom fusion | bytes 1052672 | tf_op jit(solution)/shard_map/jit(_take)/gather | solution.py:139
  47.1 31.5 %all-gather.2.cloned.1.call-done = bf16[1024,2048]{1,0:T(8,128)(2,1)} async-done(((bf16[1024,256]{1,0:T(8,128)(2,1)}), bf16[1024,2048]{1,0:T(8,128)(2,1)}) %all-gather.2.cloned.1.call-update) | async-done | bytes 4194320 | tf_op jit(solution)/shard_map/all_gather | solution.py:140
  78.6 3.1 %multiply_reduce_fusion = f32[1024]{0:T(1024)S(1)} fusion(bf16[1024,2048]{1,0:T(8,128)(2,1)} %all-gather.2.cloned.1.call-done), kind=kLoop, calls=%fused_computation.4 | loop fusion | flops 6290432 | bytes 4198400 | tf_op jit(solution)/shard_map/reduce_sum | solution.py:142
  81.7 3.9 %convolution_convert_fusion.1 = bf16[1024,256]{1,0:T(8,128)(2,1)S(1)} fusion(bf16[2048,256]{1,0:T(8,128)(2,1)} %param.12, f32[2048]{0:T(1024)S(1)} %copy-done.10, f32[1024]{0:T(1024)S(1)} %add_rsqrt_fusion, bf16[1024,2048]{1,0:T(8,128)(2,1)} %all-gather.2.cloned.1.call-done), kind=kOutput, calls=%fused_computation.6 | convolution fusion | flops 1082392576 | bytes 5779456 | tf_op jit(solution)/shard_map/dot_general | solution.py:145
  85.7 3.5 %collective-permute-start.2 = (bf16[1024,128]{1,0:T(8,128)(2,1)S(1)}, bf16[1024,128]{1,0:T(8,128)(2,1)S(1)}, u32[]{:S(2)}, u32[]{:S(2)}) collective-permute-start(bf16[1024,128]{1,0:T(8,128)(2,1)S(1)} %get-tuple-element.25), channel_id=1, source_target_pairs={{0,8},{8,16},{16,24},{24,32},{32,40},{40,48},{48,56},{56,64},{64,7... | collective-permute-start | bytes 786440 | tf_op jit(solution)/shard_map/ppermute | solution.py:20
  89.2 1.3 convolution_convert_fusion
  91.3 3.4 %collective-permute-start.3 = (bf16[1024,128]{1,0:T(8,128)(2,1)S(1)}, bf16[1024,128]{1,0:T(8,128)(2,1)S(1)}, u32[]{:S(2)}, u32[]{:S(2)}) collective-permute-start(bf16[1024,128]{1,0:T(8,128)(2,1)S(1)} %get-tuple-element.23), channel_id=1, source_target_pairs={{0,8},{8,16},{16,24},{24,32},{32,40},{40,48},{48,56},{56,64},{64,7... | collective-permute-start | bytes 786440 | tf_op jit(solution)/shard_map/ppermute | solution.py:20
  94.7 1.3 convolution_convert_fusion.2
  96.9 3.9 %collective-permute-start = (bf16[1024,128]{1,0:T(8,128)(2,1)S(1)}, bf16[1024,128]{1,0:T(8,128)(2,1)}, u32[]{:S(2)}, u32[]{:S(2)}) collective-permute-start(bf16[1024,128]{1,0:T(8,128)(2,1)S(1)} %get-tuple-element.24), channel_id=1, source_target_pairs={{0,8},{8,16},{16,24},{24,32},{32,40},{40,48},{48,56},{56,64},{64,7... | collective-permute-start | bytes 786440 | tf_op jit(solution)/shard_map/ppermute | solution.py:20
  100.8 3.1 %collective-permute-start.1 = (bf16[1024,128]{1,0:T(8,128)(2,1)}, bf16[1024,128]{1,0:T(8,128)(2,1)}, u32[]{:S(2)}, u32[]{:S(2)}) collective-permute-start(bf16[1024,128]{1,0:T(8,128)(2,1)} %get-tuple-element.22), channel_id=1, source_target_pairs={{0,8},{8,16},{16,24},{24,32},{32,40},{40,48},{48,56},{56,64},{64,7... | collective-permute-start | bytes 786440 | tf_op jit(solution)/shard_map/ppermute | solution.py:20
  105.5 10.6 %shard_map.105 = (bf16[1024,128]{1,0:T(8,128)(2,1)}, bf16[1024,128]{1,0:T(8,128)(2,1)}, f32[2048,128]{1,0:T(8,128)}, f32[2048,128]{1,0:T(8,128)}) custom-call(bf16[1024,128]{1,0:T(8,128)(2,1)} %get-tuple-element.27.q_ref, bf16[2048,128]{1,0:T(8,128)(2,1)} %pad_maximum_fusion.2.k_ref, bf16[2048,128]{1,0:T(8,128)(2,1)} %pad_maximum_fusion.3.v_ref, ...), custom_call_target="tpu_custom_call" | custom-call | flops 2013265920 | bytes 4194304 | tf_op jit(solution)/shard_map/pallas_call | solution.py:106
  116.1 1.3 broadcast_multiply_fusion
  118.2 1.5 collective-permute-start.5
  119.7 1.8 pad_maximum_fusion.k_ref
  121.5 1.9 pad_maximum_fusion.1.v_ref
  123.4 10.6 %shard_map.104 = (bf16[1024,128]{1,0:T(8,128)(2,1)}, bf16[1024,128]{1,0:T(8,128)(2,1)}, f32[2048,128]{1,0:T(8,128)}, f32[2048,128]{1,0:T(8,128)}) custom-call(bf16[1024,128]{1,0:T(8,128)(2,1)} %get-tuple-element.26.q_ref, bf16[2048,128]{1,0:T(8,128)(2,1)} %pad_maximum_fusion.k_ref, bf16[2048,128]{1,0:T(8,128)(2,1)} %pad_maximum_fusion.1.v_ref, ...), custom_call_target="tpu_custom_call" | custom-call | flops 2013265920 | bytes 4194304 | tf_op jit(solution)/shard_map/pallas_call | solution.py:106
  133.9 1.3 broadcast_multiply_fusion.1
  135.3 1.4 collective-permute-start.4
  137.8 1.3 collective-permute-start.7
  140.2 1.3 collective-permute-start.6
  141.5 2.2 %fusion.2 = f32[1024,2048]{1,0:T(8,128)S(1)} fusion(bf16[2048,256]{1,0:T(8,128)(2,1)S(1)} %copy-done, bf16[1024,128]{1,0:T(8,128)(2,1)S(1)} %copy-done.7, bf16[1024,128]{1,0:T(8,128)(2,1)} %get-tuple-element.12), kind=kOutput, calls=%fused_computation.24 | convolution fusion | flops 1074790400 | bytes 9961472 | tf_op jit(solution)/shard_map/rc,dc->rd/dot_general | solution.py:176
  144.9 2.2 %collective-permute-done.4 = bf16[1024,128]{1,0:T(8,128)(2,1)S(1)} collective-permute-done((bf16[1024,128]{1,0:T(8,128)(2,1)S(1)}, bf16[1024,128]{1,0:T(8,128)(2,1)S(1)}, u32[]{:S(2)}, u32[]{:S(2)}) %collective-permute-start.4) | collective-permute-done | bytes 262176 | tf_op jit(solution)/shard_map/ppermute | solution.py:20
  148.5 4.2 %collective-permute-done.7 = bf16[1024,128]{1,0:T(8,128)(2,1)S(1)} collective-permute-done((bf16[1024,128]{1,0:T(8,128)(2,1)S(1)}, bf16[1024,128]{1,0:T(8,128)(2,1)S(1)}, u32[]{:S(2)}, u32[]{:S(2)}) %collective-permute-start.7) | collective-permute-done | bytes 262176 | tf_op jit(solution)/shard_map/ppermute | solution.py:20
  152.8 3.7 %collective-permute-done.6 = bf16[1024,128]{1,0:T(8,128)(2,1)S(1)} collective-permute-done((bf16[1024,128]{1,0:T(8,128)(2,1)S(1)}, bf16[1024,128]{1,0:T(8,128)(2,1)S(1)}, u32[]{:S(2)}, u32[]{:S(2)}) %collective-permute-start.6) | collective-permute-done | bytes 262176 | tf_op jit(solution)/shard_map/ppermute | solution.py:20
  156.6 3.3 %add_convert_fusion = bf16[1024,2048]{1,0:T(8,128)(2,1)} fusion(f32[1024,2048]{1,0:T(8,128)S(1)} %fusion.2, f32[1024,2048]{1,0:T(8,128)S(1)} %fusion.6, bf16[2048,256]{1,0:T(8,128)(2,1)S(1)} %copy-done.3, bf16[1024,128]{1,0:T(8,128)(2,1)S(1)} %add_convert_fusion.1, bf16[1024,128]{1,0:T(8,128)(2,1)S(1)} %add_convert_fusion.2), kind=kOutput, calls=%fused_computation.2 | convolution fusion | flops 1081081856 | bytes 22544384 | tf_op jit(solution)/shard_map/rc,dc->rd/dot_general | solution.py:176
  159.9 6.6 %convert_element_type.52 = f32[1024,2048]{1,0:T(8,128)} convert(bf16[1024,2048]{1,0:T(8,128)(2,1)} %all-gather.2.cloned.1.call-done) | non-fusion elementwise | flops 2097152 | bytes 12582912 | tf_op jit(solution)/shard_map/convert_element_type | solution.py:141
  167.4 33.0 %reduce-scatter.2.cloned.1.call-done = bf16[128,2048]{1,0:T(8,128)(2,1)} async-done(((bf16[1024,2048]{1,0:T(8,128)(2,1)}), bf16[128,2048]{1,0:T(8,128)(2,1)}) %reduce-scatter.2.cloned.1.call-update) | async-done | bytes 524304 | tf_op jit(solution)/shard_map/reduce_scatter | solution.py:178
  200.3 1.6 multiply_reduce_fusion.1
  202.0 2.5 %subtract_convert_fusion = bf16[128,2048]{1,0:T(8,128)(2,1)} fusion(bf16[128,2048]{1,0:T(8,128)(2,1)} %reduce-scatter.2.cloned.1.call-done, f32[1024,2048]{1,0:T(8,128)} %convert_element_type.52, s32[]{:T(128)S(6)} %select_n.23, f32[128]{0:T(128)S(1)} %broadcast_multiply_fusion.2, f32[128]{0:T(128)S(1)} %get-tuple-element.18, f32[2048]{0:T(1024)S(1)} %copy-done.10, ...), kind=kLoop, calls=%fused_computation.8 | loop fusion | flops 1835008 | bytes 2106884 | tf_op jit(solution)/shard_map/convert_element_type | solution.py:191
  (58 shorter events, 15.0 us)
Async XLA Ops:
  7.2 87.6 %copy-start = (bf16[2048,256]{1,0:T(8,128)(2,1)S(1)}, bf16[2048,256]{1,0:T(8,128)(2,1)}, u32[]{:S(2)}) copy-start(bf16[2048,256]{1,0:T(8,128)(2,1)} %param.11) | copy-start | bytes 3145732
  7.2 38.0 %copy-start.11 = (s32[1024]{0:T(1024)S(1)}, s32[1024]{0:T(1024)}, u32[]{:S(2)}) copy-start(s32[1024]{0:T(1024)} %param.17) | copy-start | bytes 12292
  7.2 39.1 %copy-start.6 = (bf16[1024,256]{1,0:T(8,128)(2,1)S(1)}, bf16[1024,256]{1,0:T(8,128)(2,1)}, u32[]{:S(2)}) copy-start(bf16[1024,256]{1,0:T(8,128)(2,1)} %param.14) | copy-start | bytes 1572868
  7.2 74.5 %copy-start.10 = (f32[2048]{0:T(1024)S(1)}, f32[2048]{0:T(1024)}, u32[]{:S(2)}) copy-start(f32[2048]{0:T(1024)} %param.10) | copy-start | bytes 24580
  14.4 25.7 %all-to-all-start = ((bf16[16,128,256]{2,1,0:T(8,128)(2,1)}), bf16[16,128,256]{2,1,0:T(8,128)(2,1)S(1)}, u32[]{:S(2)}, u32[]{:S(2)}) async-start(bf16[16,128,256]{2,1,0:T(8,128)(2,1)} %bitcast), calls=%async_computation | async-start | bytes 2097152 | tf_op jit(solution)/shard_map/all_to_all | solution.py:138
  22.4 56.1 %all-gather.2.cloned.1.call-start = ((), (), s32[]{:S(2)}) async-start(), calls=%async_computation.2 | async-start | bytes 4718592 | tf_op jit(solution)/shard_map/all_gather | solution.py:140
  45.2 155.2 %reduce-scatter.2.cloned.1.call-start = ((), (), s32[]{:S(2)}) async-start(), calls=%async_computation.3 | async-start | bytes 4718592 | tf_op jit(solution)/shard_map/reduce_scatter | solution.py:178
  81.7 7.5 %copy-start.1 = (bf16[1024,2048]{1,0:T(8,128)(2,1)S(1)}, bf16[1024,2048]{1,0:T(8,128)(2,1)}, u32[]{:S(2)}) copy-start(bf16[1024,2048]{1,0:T(8,128)(2,1)} %all-gather.2.cloned.1.call-done) | copy-start | bytes 12582916
  81.7 7.5 %copy-start.3 = (bf16[2048,256]{1,0:T(8,128)(2,1)S(1)}, bf16[2048,256]{1,0:T(8,128)(2,1)}, u32[]{:S(2)}) copy-start(bf16[2048,256]{1,0:T(8,128)(2,1)} %param.13) | copy-start | bytes 3145732
  85.7 18.2 %collective-permute-start.2 = (bf16[1024,128]{1,0:T(8,128)(2,1)S(1)}, bf16[1024,128]{1,0:T(8,128)(2,1)S(1)}, u32[]{:S(2)}, u32[]{:S(2)}) collective-permute-start(bf16[1024,128]{1,0:T(8,128)(2,1)S(1)} %get-tuple-element.25), channel_id=1, source_target_pairs={{0,8},{8,16},{16,24},{24,32},{32,40},{40,48},{48,56},{56,64},{64,7... | collective-permute-start | bytes 786440 | tf_op jit(solution)/shard_map/ppermute | solution.py:20
  91.3 13.4 %collective-permute-start.3 = (bf16[1024,128]{1,0:T(8,128)(2,1)S(1)}, bf16[1024,128]{1,0:T(8,128)(2,1)S(1)}, u32[]{:S(2)}, u32[]{:S(2)}) collective-permute-start(bf16[1024,128]{1,0:T(8,128)(2,1)S(1)} %get-tuple-element.23), channel_id=1, source_target_pairs={{0,8},{8,16},{16,24},{24,32},{32,40},{40,48},{48,56},{56,64},{64,7... | collective-permute-start | bytes 786440 | tf_op jit(solution)/shard_map/ppermute | solution.py:20
  96.9 22.7 %collective-permute-start = (bf16[1024,128]{1,0:T(8,128)(2,1)S(1)}, bf16[1024,128]{1,0:T(8,128)(2,1)}, u32[]{:S(2)}, u32[]{:S(2)}) collective-permute-start(bf16[1024,128]{1,0:T(8,128)(2,1)S(1)} %get-tuple-element.24), channel_id=1, source_target_pairs={{0,8},{8,16},{16,24},{24,32},{32,40},{40,48},{48,56},{56,64},{64,7... | collective-permute-start | bytes 786440 | tf_op jit(solution)/shard_map/ppermute | solution.py:20
  100.8 20.7 %collective-permute-start.1 = (bf16[1024,128]{1,0:T(8,128)(2,1)}, bf16[1024,128]{1,0:T(8,128)(2,1)}, u32[]{:S(2)}, u32[]{:S(2)}) collective-permute-start(bf16[1024,128]{1,0:T(8,128)(2,1)} %get-tuple-element.22), channel_id=1, source_target_pairs={{0,8},{8,16},{16,24},{24,32},{32,40},{40,48},{48,56},{56,64},{64,7... | collective-permute-start | bytes 786440 | tf_op jit(solution)/shard_map/ppermute | solution.py:20
  118.2 25.5 %collective-permute-start.5 = (bf16[1024,128]{1,0:T(8,128)(2,1)}, bf16[1024,128]{1,0:T(8,128)(2,1)}, u32[]{:S(2)}, u32[]{:S(2)}) collective-permute-start(bf16[1024,128]{1,0:T(8,128)(2,1)} %slice.96), channel_id=1, source_target_pairs={{8,0},{16,8},{24,16},{32,24},{40,32},{48,40},{56,48},{64,56},{72,6... | collective-permute-start | bytes 786440 | tf_op jit(solution)/shard_map/ppermute | solution.py:20
  121.5 20.0 %copy-start.7 = (bf16[1024,128]{1,0:T(8,128)(2,1)S(1)}, bf16[1024,128]{1,0:T(8,128)(2,1)}, u32[]{:S(2)}) copy-start(bf16[1024,128]{1,0:T(8,128)(2,1)} %get-tuple-element.13) | copy-start | bytes 786436
  135.2 12.0 %copy-start.2 = (bf16[2048,256]{1,0:T(8,128)(2,1)S(1)}, bf16[2048,256]{1,0:T(8,128)(2,1)}, u32[]{:S(2)}) copy-start(bf16[2048,256]{1,0:T(8,128)(2,1)} %param.12) | copy-start | bytes 3145732
  135.3 11.8 %collective-permute-start.4 = (bf16[1024,128]{1,0:T(8,128)(2,1)S(1)}, bf16[1024,128]{1,0:T(8,128)(2,1)S(1)}, u32[]{:S(2)}, u32[]{:S(2)}) collective-permute-start(bf16[1024,128]{1,0:T(8,128)(2,1)S(1)} %slice.97), channel_id=1, source_target_pairs={{8,0},{16,8},{24,16},{32,24},{40,32},{48,40},{56,48},{64,56},{72,6... | collective-permute-start | bytes 786440 | tf_op jit(solution)/shard_map/ppermute | solution.py:20
  137.8 14.9 %collective-permute-start.7 = (bf16[1024,128]{1,0:T(8,128)(2,1)S(1)}, bf16[1024,128]{1,0:T(8,128)(2,1)S(1)}, u32[]{:S(2)}, u32[]{:S(2)}) collective-permute-start(bf16[1024,128]{1,0:T(8,128)(2,1)S(1)} %slice.94), channel_id=1, source_target_pairs={{8,0},{16,8},{24,16},{32,24},{40,32},{48,40},{56,48},{64,56},{72,6... | collective-permute-start | bytes 786440 | tf_op jit(solution)/shard_map/ppermute | solution.py:20
  140.2 16.4 %collective-permute-start.6 = (bf16[1024,128]{1,0:T(8,128)(2,1)S(1)}, bf16[1024,128]{1,0:T(8,128)(2,1)S(1)}, u32[]{:S(2)}, u32[]{:S(2)}) collective-permute-start(bf16[1024,128]{1,0:T(8,128)(2,1)S(1)} %slice.95), channel_id=1, source_target_pairs={{8,0},{16,8},{24,16},{32,24},{40,32},{48,40},{56,48},{64,56},{72,6... | collective-permute-start | bytes 786440 | tf_op jit(solution)/shard_map/ppermute | solution.py:20
  143.7 9.0 %copy-start.4 = (f32[2048,128]{1,0:T(8,128)S(1)}, f32[2048,128]{1,0:T(8,128)}, u32[]{:S(2)}) copy-start(f32[2048,128]{1,0:T(8,128)} %get-tuple-element.17) | copy-start | bytes 3145732
  143.7 12.8 %copy-start.5 = (f32[2048,128]{1,0:T(8,128)S(1)}, f32[2048,128]{1,0:T(8,128)}, u32[]{:S(2)}) copy-start(f32[2048,128]{1,0:T(8,128)} %get-tuple-element.16) | copy-start | bytes 3145732
  159.9 6.7 %copy-start.8 = (bf16[1024,128]{1,0:T(8,128)(2,1)S(1)}, bf16[1024,128]{1,0:T(8,128)(2,1)}, u32[]{:S(2)}) copy-start(bf16[1024,128]{1,0:T(8,128)(2,1)} %get-tuple-element.11) | copy-start | bytes 786436
  159.9 6.7 %copy-start.9 = (bf16[1024,128]{1,0:T(8,128)(2,1)S(1)}, bf16[1024,128]{1,0:T(8,128)(2,1)}, u32[]{:S(2)}) copy-start(bf16[1024,128]{1,0:T(8,128)(2,1)} %get-tuple-element.10) | copy-start | bytes 786436
Sparse Core Ops, SparseCore 0:
  45.3 33.2 all-gather.1
  160.0 40.2 reduce-scatter.1

commit v5 on v4

--- a/solution.py
+++ b/solution.py
@@ -53,19 +53,26 @@
 
 
 def attention_kernel(
-    q_ref, k_ref, v_ref, do_ref, st_ref, ctx_ref, dq_ref, dk_ref, dv_ref, *, tq, window, shift, scale
+    q_ref, kp_ref, vp_ref, ko_ref, vo_ref, do_ref, st_ref,
+    ctx_ref, dq_ref, send_ref, keep_ref,
+    k_scr, v_scr, dk_scr, dv_scr, *, tq, window, shift, scale
 ):
-    qi = pl.program_id(1)
+    qi = pl.program_id(0)
     a = pl.multiple_of(qi * tq, tq)
+    half = kp_ref.shape[0]
 
     @pl.when(qi == 0)
     def _():
-        dk_ref[...] = jnp.zeros_like(dk_ref)
-        dv_ref[...] = jnp.zeros_like(dv_ref)
+        k_scr[:half, :] = kp_ref[...]
+        k_scr[half:, :] = ko_ref[...]
+        v_scr[:half, :] = vp_ref[...]
+        v_scr[half:, :] = vo_ref[...]
+        dk_scr[...] = jnp.zeros_like(dk_scr)
+        dv_scr[...] = jnp.zeros_like(dv_scr)
 
     q = q_ref[...]
-    k = k_ref[pl.ds(a, window), :]
-    v = v_ref[pl.ds(a, window), :]
+    k = k_scr[pl.ds(a, window), :]
+    v = v_scr[pl.ds(a, window), :]
     do = do_ref[...]
     rows_t = (((1,), (1,)), ((), ()))
     cols_t = (((0,), (0,)), ((), ()))
@@ -83,40 +90,52 @@
     weighted = jnp.sum(p * dp, axis=1, keepdims=True)
     ds = (p * (dp - weighted)).astype(jnp.bfloat16)
     dq_ref[...] = (jnp.dot(ds, k, preferred_element_type=jnp.float32) * scale).astype(dq_ref.dtype)
-    dk_ref[pl.ds(a, window), :] += lax.dot_general(ds, q, cols_t, preferred_element_type=jnp.float32)
-    dv_ref[pl.ds(a, window), :] += lax.dot_general(p_low, do, cols_t, preferred_element_type=jnp.float32)
-
-
-def attention(queries, keys_all, values_all, grad_ctx, rel_start):
-    rows, width = queries.shape
-    heads = width // HD
+    dk_scr[pl.ds(a, window), :] += lax.dot_general(ds, q, cols_t, preferred_element_type=jnp.float32)
+    dv_scr[pl.ds(a, window), :] += lax.dot_general(p_low, do, cols_t, preferred_element_type=jnp.float32)
+
+    @pl.when(qi == pl.num_programs(0) - 1)
+    def _():
+        hd = q_ref.shape[1]
+        send_ref[:, :hd] = (dk_scr[:half, :] * scale).astype(send_ref.dtype)
+        send_ref[:, hd:] = dv_scr[:half, :].astype(send_ref.dtype)
+        keep_ref[:, :hd] = dk_scr[half:, :] * scale
+        keep_ref[:, hd:] = dv_scr[half:, :]
+
+
+def attention(queries, kv_prev, kv_own, grad_ctx, rel_start):
+    rows, hd = queries.shape
     tq = 256
     window = rows + tq
     kernel = functools.partial(
-        attention_kernel, tq=tq, window=window, shift=rows, scale=HD ** (-0.5)
-    )
-    q_spec = pl.BlockSpec((tq, HD), lambda h, i: (i, h))
-    kv_spec = pl.BlockSpec((2 * rows, HD), lambda h, i: (0, h))
-    steps = heads * (rows // tq)
+        attention_kernel, tq=tq, window=window, shift=rows, scale=hd ** (-0.5)
+    )
+    q_spec = pl.BlockSpec((tq, hd), lambda i: (i, 0))
+    k_spec = pl.BlockSpec((rows, hd), lambda i: (0, 0))
+    v_spec = pl.BlockSpec((rows, hd), lambda i: (0, 1))
+    kv_spec = pl.BlockSpec((rows, 2 * hd), lambda i: (0, 0))
+    steps = rows // tq
     cost = pl.CostEstimate(
-        flops=steps * 12 * tq * window * HD,
+        flops=steps * 12 * tq * window * hd,
         transcendentals=steps * 2 * tq * window,
-        bytes_accessed=rows * width * 2 * 4 + 2 * rows * width * (2 * 2 + 4 * 2),
+        bytes_accessed=rows * hd * 2 * 8 + rows * 2 * hd * 6,
     )
     return pl.pallas_call(
         kernel,
-        grid=(heads, rows // tq),
-        in_specs=[q_spec, kv_spec, kv_spec, q_spec, pl.BlockSpec((tq, 1), lambda h, i: (i, 0))],
+        grid=(steps,),
+        in_specs=[q_spec, k_spec, v_spec, k_spec, v_spec, q_spec,
+                  pl.BlockSpec((tq, 1), lambda i: (i, 0))],
         out_specs=[q_spec, q_spec, kv_spec, kv_spec],
         out_shape=[
-            jax.ShapeDtypeStruct((rows, width), jnp.bfloat16),
-            jax.ShapeDtypeStruct((rows, width), jnp.bfloat16),
-            jax.ShapeDtypeStruct((2 * rows, width), jnp.float32),
-            jax.ShapeDtypeStruct((2 * rows, width), jnp.float32),
+            jax.ShapeDtypeStruct((rows, hd), jnp.bfloat16),
+            jax.ShapeDtypeStruct((rows, hd), jnp.bfloat16),
+            jax.ShapeDtypeStruct((rows, 2 * hd), jnp.bfloat16),
+            jax.ShapeDtypeStruct((rows, 2 * hd), jnp.float32),
         ],
-        compiler_params=pltpu.CompilerParams(dimension_semantics=("arbitrary", "arbitrary")),
+        scratch_shapes=[pltpu.VMEM((2 * rows, hd), jnp.bfloat16)] * 2
+        + [pltpu.VMEM((2 * rows, hd), jnp.float32)] * 2,
+        compiler_params=pltpu.CompilerParams(dimension_semantics=("arbitrary",)),
         cost_estimate=cost,
-    )(queries, keys_all, values_all, grad_ctx, rel_start)
+    )(queries, kv_prev, kv_prev, kv_own, kv_own, grad_ctx, rel_start)
 
 
 def body(
@@ -142,49 +161,40 @@
     inv_rms = lax.rsqrt(jnp.mean(rows_float * rows_float, axis=-1, keepdims=True) + epsilon)
     normed = (rows_float * inv_rms * gain).astype(jnp.bfloat16)
     queries = jnp.dot(normed, w_query, preferred_element_type=jnp.float32).astype(jnp.bfloat16)
-    keys_own = jnp.dot(normed, w_key, preferred_element_type=jnp.float32).astype(jnp.bfloat16)
-    values_own = jnp.dot(normed, w_value, preferred_element_type=jnp.float32).astype(jnp.bfloat16)
     rel_start = (episode_start - (shard - 1) * row_count).reshape(row_count, 1)
     local_heads = queries.shape[1] // HD
-    outs = []
+    contexts, grad_queries, kv_parts = [], [], []
     for h in range(local_heads):
         cols = slice(h * HD, (h + 1) * HD)
-        keys_h, values_h = keys_own[:, cols], values_own[:, cols]
-        keys_prev, values_prev = passed_along((keys_h, values_h), "seq", 1)
-        context_h, grad_q_h, grad_k_h, grad_v_h = attention(
-            queries[:, cols],
-            jnp.concatenate([keys_prev, keys_h], axis=0),
-            jnp.concatenate([values_prev, values_h], axis=0),
-            grad_context[:, cols],
-            rel_start,
+        kv_weight = jnp.concatenate([w_key[:, cols], w_value[:, cols]], axis=1)
+        kv_own = jnp.dot(normed, kv_weight, preferred_element_type=jnp.float32).astype(jnp.bfloat16)
+        kv_prev = passed_along(kv_own, "seq", 1)
+        context_h, grad_q_h, kv_send, kv_keep = attention(
+            queries[:, cols], kv_prev, kv_own, grad_context[:, cols], rel_start
         )
-        grad_k_h = grad_k_h * HD ** (-0.5)
-        next_k, next_v = passed_along(
-            (grad_k_h[:row_count].astype(jnp.bfloat16), grad_v_h[:row_count].astype(jnp.bfloat16)),
-            "seq",
-            -1,
-        )
-        grad_k_h = (grad_k_h[row_count:] + next_k.astype(jnp.float32)).astype(jnp.bfloat16)
-        grad_v_h = (grad_v_h[row_count:] + next_v.astype(jnp.float32)).astype(jnp.bfloat16)
-        outs.append((context_h, grad_q_h, grad_k_h, grad_v_h))
-    context_out, grad_q_all, grad_k_all, grad_v_all = (
-        jnp.concatenate(parts, axis=1) for parts in zip(*outs)
-    )
+        kv_next = passed_along(kv_send, "seq", -1)
+        grad_kv = (kv_keep + kv_next.astype(jnp.float32)).astype(jnp.bfloat16)
+        contexts.append(context_h)
+        grad_queries.append(grad_q_h)
+        kv_parts.append((grad_kv, kv_weight))
+    context_out = jnp.concatenate(contexts, axis=1)
+    grad_q_all = jnp.concatenate(grad_queries, axis=1)
     share = row_count // head_count
 
     def project(grads, weight):
         return jnp.einsum("rc,dc->rd", grads, weight, preferred_element_type=jnp.float32)
 
+    term = project(grad_q_all, w_query)
+    for grad_kv, kv_weight in kv_parts:
+        term = term + project(grad_kv, kv_weight)
     grad_normed = lax.psum_scatter(
-        (
-            project(grad_q_all, w_query) + project(grad_k_all, w_key) + project(grad_v_all, w_value)
-        ).astype(jnp.bfloat16),
+        term.astype(jnp.bfloat16),
         "head",
         scatter_dimension=0,
         tiled=True,
     ).astype(jnp.float32)
     own_start = head_pos * share
-    mine = lax.dynamic_slice_in_dim(rows_float, own_start, share, 0)
+    mine = lax.dynamic_slice_in_dim(packed, own_start, share, 0).astype(jnp.float32)
     mine_inv = lax.dynamic_slice_in_dim(inv_rms, own_start, share, 0)
     gain_grad = gain * grad_normed
     mixed = jnp.mean(gain_grad * mine, axis=-1, keepdims=True)

time: 212 us -> 209 us (0.986)
  waiting for transfers between devices: 91 us -> 113 us
  other arithmetic: 27.1 us -> 11.2 us
  starting transfers between devices: 27.4 us -> 18 us
    ppermute x8 -> x4, waiting for transfers between devices: 10.2 us -> 26.7 us  [passed_along(): return lax.ppermute(array, axis, pairs)]
    ppermute x8 -> x4, starting transfers between devices: 19.3 us -> 9.84 us  [passed_along(): return lax.ppermute(array, axis, pairs)]
    convert_element_type x5 -> x0, other arithmetic: 7.88 us -> none  [the longest x1 6.56 us: body(): rows_float = packed.astype(jnp.float32)]
    reduce_scatter x1, waiting for transfers between devices: 33 us -> 39.8 us  [body(): lax.psum_scatter(term.astype(jnp.bfloat16), 'head', scatter_dimension=0,...]
    concatenate x5 -> x1, other arithmetic: 6.18 us -> 0.85 us  [body(): context_out = jnp.concatenate(contexts, axis=1)]
    mul x2 -> x0, other arithmetic: 2.63 us -> none  [body(): grad_k_h = grad_k_h * HD ** (-0.5)]
    dot_general x3, matrix products: 6.81 us -> 9.16 us  [project(): jnp.einsum('rc,dc->rd', grads, weight, preferred_element_type=jnp.float32)]
  transfers between devices with their start and end apart: 11 -> 7, of which waited for: 6 -> 6; matrix products, arithmetic and copies ran while one was open for 15% -> 7% of each run, Pallas kernels for 10% -> 10%
where the time goes in v5:
time: 209 us; the launch traced here: 208 us
  waiting for transfers between devices  113 us (54%)
  Pallas kernels  21.6 us (10%)
  starting transfers between devices  18 us (9%)
  local copies, waits for them, and re-layouts  16.7 us (8%)
  between operations  14.2 us (7%)
  matrix products  13.9 us (7%)
  other arithmetic  11.2 us (5%)
    reduce_scatter x1, waiting for transfers between devices, body(): lax.psum_scatter(term.astype(jnp.bfloat16), 'head', scatter_dimension=0,...  39.8 us
    all_gather x1, waiting for transfers between devices, body(): packed = lax.all_gather(packed_part, 'head', axis=1, tiled=True)  29.8 us
    ppermute x4, waiting for transfers between devices, passed_along(): return lax.ppermute(array, axis, pairs)  26.7 us
    pallas_call x2, Pallas kernels, attention(): pl.pallas_call(kernel, grid=(steps,), in_specs=[q_spec, k_spec, v_spec, k...  21.6 us
    all_to_all x1, waiting for transfers between devices, body(): lax.all_to_all(outgoing, 'seq', split_axis=0, concat_axis=0, tiled=True)  16.3 us
    ppermute x4, starting transfers between devices, passed_along(): return lax.ppermute(array, axis, pairs)  9.84 us
    dot_general x3, matrix products, project(): jnp.einsum('rc,dc->rd', grads, weight, preferred_element_type=jnp.float32)  9.16 us
    all_to_all x1, starting transfers between devices, body(): lax.all_to_all(outgoing, 'seq', split_axis=0, concat_axis=0, tiled=True)  8.12 us
  transfers between devices with their start and end apart: 7, of which 6 were waited for; matrix products, arithmetic and copies ran while one was open for 7% of the time, Pallas kernels for 10%

profile of v5, /device:TPU:0, one launch (start us, length us, event | category | flops | bytes accessed | tf_op | source)
XLA Modules:
  0.0 208.3 jit_solution(9810853456118548591)
XLA Ops:
  7.2 0.8 compare_select_fusion
  8.0 6.4 %scatter_custom_fusion = bf16[2048,256]{1,0:T(8,128)(2,1)} fusion(s32[1024]{0:T(1024)S(1)} %compare_select_fusion, bf16[1024,2048]{1,0:T(8,128)(2,1)} %param.9, s32[]{:T(128)} %constant.15.clone.1, s32[]{:T(128)S(6)} %select_n.21, bf16[]{:T(256)} %constant.18.clone.1), kind=kCustom, calls=%fused_computation.28 | custom fusion | bytes 1573892 | tf_op jit(solution)/shard_map/scatter | solution.py:155
  14.4 8.1 %all-to-all-start = ((bf16[16,128,256]{2,1,0:T(8,128)(2,1)}), bf16[16,128,256]{2,1,0:T(8,128)(2,1)S(1)}, u32[]{:S(2)}, u32[]{:S(2)}) async-start(bf16[16,128,256]{2,1,0:T(8,128)(2,1)} %bitcast), calls=%async_computation | async-start | bytes 2097152 | tf_op jit(solution)/shard_map/all_to_all | solution.py:157
  23.9 16.3 %all-to-all-done = bf16[16,128,256]{2,1,0:T(8,128)(2,1)S(1)} async-done(((bf16[16,128,256]{2,1,0:T(8,128)(2,1)}), bf16[16,128,256]{2,1,0:T(8,128)(2,1)S(1)}, u32[]{:S(2)}, u32[]{:S(2)}) %all-to-all-start) | async-done | bytes 1048608 | tf_op jit(solution)/shard_map/all_to_all | solution.py:157
  40.3 3.9 %gather_fusion = bf16[1024,256]{1,0:T(8,128)(2,1)S(1)} fusion(bf16[2048,256]{1,0:T(8,128)(2,1)S(1)} %bitcast.10, s32[1024]{0:T(1024)S(1)} %fusion.15), kind=kCustom, calls=%fused_computation | custom fusion | bytes 1052672 | tf_op jit(solution)/shard_map/jit(_take)/gather | solution.py:158
  44.2 1.0 broadcast_select_fusion
  45.3 1.0 copy.11.st_ref
  46.3 0.8 fusion.27
  47.2 1.7 fusion.25
  48.9 29.8 %all-gather.2.cloned.1.call-done = bf16[1024,2048]{1,0:T(8,128)(2,1)} async-done(((bf16[1024,256]{1,0:T(8,128)(2,1)}), bf16[1024,2048]{1,0:T(8,128)(2,1)}) %all-gather.2.cloned.1.call-update) | async-done | bytes 4194320 | tf_op jit(solution)/shard_map/all_gather | solution.py:159
  78.7 3.2 %fusion = f32[1024]{0:T(1024)S(1)} fusion(bf16[1024,2048]{1,0:T(8,128)(2,1)} %all-gather.2.cloned.1.call-done), kind=kLoop, calls=%fused_computation.4 | loop fusion | flops 6290432 | bytes 4198400 | tf_op jit(solution)/shard_map/reduce_sum | solution.py:161
  82.1 2.1 %convolution_convert_fusion.ko_ref.vo_ref = bf16[1024,256]{1,0:T(8,128)(2,1)} fusion(bf16[2048,128]{1,0:T(8,128)(2,1)S(1)} %get-tuple-element.28, bf16[2048,128]{1,0:T(8,128)(2,1)S(1)} %get-tuple-element.21, bf16[1024,2048]{1,0:T(8,128)(2,1)S(1)} %copy-done.1, f32[2048]{0:T(1024)S(1)} %copy-done.8, f32[1024]{0:T(1024)S(1)} %add_rsqrt_fusion), kind=kOutput, calls=%fused_computation.10 | convolution fusion | flops 1084489728 | bytes 5779456 | tf_op jit(solution)/shard_map/dot_general | solution.py:170
  84.2 4.2 %collective-permute-start.1 = (bf16[1024,256]{1,0:T(8,128)(2,1)}, bf16[1024,256]{1,0:T(8,128)(2,1)}, u32[]{:S(2)}, u32[]{:S(2)}) collective-permute-start(bf16[1024,256]{1,0:T(8,128)(2,1)} %convolution_convert_fusion.ko_ref.vo_ref), channel_id=1, source_target_pairs={{0,8},{8,16},{16,24},{24,32},{32,40},{40,48},{48,56},{56,64},{64,7... | collective-permute-start | bytes 1572872 | tf_op jit(solution)/shard_map/ppermute | solution.py:20
  88.5 1.3 convolution_convert_fusion.1.ko_ref.vo_ref
  89.8 2.7 %collective-permute-start = (bf16[1024,256]{1,0:T(8,128)(2,1)S(1)}, bf16[1024,256]{1,0:T(8,128)(2,1)S(1)}, u32[]{:S(2)}, u32[]{:S(2)}) collective-permute-start(bf16[1024,256]{1,0:T(8,128)(2,1)S(1)} %convolution_convert_fusion.1.ko_ref.vo_ref), channel_id=1, source_target_pairs={{0,8},{8,16},{16,24},{24,32},{32,40},{40,48},{48,56},{56,64},{64,7... | collective-permute-start | bytes 1572872 | tf_op jit(solution)/shard_map/ppermute | solution.py:20
  92.5 1.3 convolution_convert_fusion.2
  93.8 0.9 fusion.28
  94.7 16.0 %collective-permute-done.kp_ref.vp_ref = bf16[1024,256]{1,0:T(8,128)(2,1)S(1)} collective-permute-done((bf16[1024,256]{1,0:T(8,128)(2,1)S(1)}, bf16[1024,256]{1,0:T(8,128)(2,1)S(1)}, u32[]{:S(2)}, u32[]{:S(2)}) %collective-permute-start) | collective-permute-done | bytes 524320 | tf_op jit(solution)/shard_map/ppermute | solution.py:20
  110.7 0.8 copy-done.11
  111.5 10.7 %shard_map.104 = (bf16[1024,128]{1,0:T(8,128)(2,1)}, bf16[1024,128]{1,0:T(8,128)(2,1)}, bf16[1024,256]{1,0:T(8,128)(2,1)}, f32[1024,256]{1,0:T(8,128)}) custom-call(bf16[1024,128]{1,0:T(8,128)(2,1)} %get-tuple-element.26.q_ref, bf16[1024,256]{1,0:T(8,128)(2,1)} %copy-done.11, bf16[1024,256]{1,0:T(8,128)(2,1)} %copy-done.11, bf16[1024,256]{1,0:T(8,128)(2,1)} %copy-done.10, ...), custom_call_target="tpu_custom_call" | custom-call | flops 2013265920 | bytes 3670016 | tf_op jit(solution)/shard_map/pallas_call | solution.py:122
  122.2 1.6 collective-permute-start.2
  123.8 10.9 %shard_map.105 = (bf16[1024,128]{1,0:T(8,128)(2,1)}, bf16[1024,128]{1,0:T(8,128)(2,1)}, bf16[1024,256]{1,0:T(8,128)(2,1)}, f32[1024,256]{1,0:T(8,128)}) custom-call(bf16[1024,128]{1,0:T(8,128)(2,1)} %get-tuple-element.27.q_ref, bf16[1024,256]{1,0:T(8,128)(2,1)} %collective-permute-done.1.kp_ref.vp_ref, ...), custom_call_target="tpu_custom_call" | custom-call | flops 2013265920 | bytes 3670016 | tf_op jit(solution)/shard_map/pallas_call | solution.py:122
  134.7 1.3 collective-permute-start.3
  136.0 2.3 %fusion.8 = f32[1024,2048]{1,0:T(8,128)S(1)} fusion(bf16[2048,256]{1,0:T(8,128)(2,1)S(1)} %copy-done, bf16[1024,128]{1,0:T(8,128)(2,1)} %get-tuple-element.13, bf16[1024,128]{1,0:T(8,128)(2,1)S(1)} %copy-done.5), kind=kOutput, calls=%fused_computation.24 | convolution fusion | flops 1074790400 | bytes 9961472 | tf_op jit(solution)/shard_map/rc,dc->rd/dot_general | solution.py:185
  138.5 2.4 %fusion.7 = f32[1024,2048]{1,0:T(8,128)S(1)} fusion(bf16[2048,128]{1,0:T(8,128)(2,1)S(1)} %get-tuple-element.29, bf16[2048,128]{1,0:T(8,128)(2,1)S(1)} %get-tuple-element.20, f32[1024,256]{1,0:T(8,128)S(1)} %copy-done.2, bf16[1024,256]{1,0:T(8,128)(2,1)} %collective-permute-done.2), kind=kOutput, calls=%fused_computation.22 | convolution fusion | flops 1076625408 | bytes 11010048 | tf_op jit(solution)/shard_map/rc,dc->rd/dot_general | solution.py:185
  141.0 10.5 %collective-permute-done.3 = bf16[1024,256]{1,0:T(8,128)(2,1)} collective-permute-done((bf16[1024,256]{1,0:T(8,128)(2,1)}, bf16[1024,256]{1,0:T(8,128)(2,1)}, u32[]{:S(2)}, u32[]{:S(2)}) %collective-permute-start.3) | collective-permute-done | bytes 524320 | tf_op jit(solution)/shard_map/ppermute | solution.py:20
  151.5 4.4 %add_convert_fusion = bf16[1024,2048]{1,0:T(8,128)(2,1)} fusion(f32[1024,2048]{1,0:T(8,128)S(1)} %fusion.8, f32[1024,2048]{1,0:T(8,128)S(1)} %fusion.7, bf16[2048,128]{1,0:T(8,128)(2,1)S(1)} %get-tuple-element.28, bf16[2048,128]{1,0:T(8,128)(2,1)S(1)} %get-tuple-element.21, f32[1024,256]{1,0:T(8,128)S(1)} %copy-done.3, ...), kind=kOutput, calls=%fused_computation.7 | convolution fusion | flops 1082916864 | bytes 23592960 | tf_op jit(solution)/shard_map/rc,dc->rd/dot_general | solution.py:185
  156.0 0.8 copy-done.6
  156.9 0.8 pad_maximum_fusion.6
  157.8 39.8 %reduce-scatter.2.cloned.1.call-done = bf16[128,2048]{1,0:T(8,128)(2,1)} async-done(((bf16[1024,2048]{1,0:T(8,128)(2,1)}), bf16[128,2048]{1,0:T(8,128)(2,1)}) %reduce-scatter.2.cloned.1.call-update) | async-done | bytes 524304 | tf_op jit(solution)/shard_map/reduce_scatter | solution.py:190
  197.6 1.5 fusion.6
  199.0 2.4 %fusion.5 = bf16[128,2048]{1,0:T(8,128)(2,1)} fusion(bf16[128,2048]{1,0:T(8,128)(2,1)} %reduce-scatter.2.cloned.1.call-done, f32[128]{0:T(128)S(1)} %broadcast_multiply_fusion, f32[128]{0:T(128)S(1)} %get-tuple-element.18, f32[2048]{0:T(1024)S(1)} %copy-done.8, f32[128]{0:T(128)S(1)} %get-tuple-element.19, ...), kind=kLoop, calls=%fused_computation.15 | loop fusion | flops 2097152 | bytes 1582596 | tf_op jit(solution)/shard_map/convert_element_type | solution.py:201
  (34 shorter events, 2.1 us)
Async XLA Ops:
  7.2 85.3 %copy-start = (bf16[2048,256]{1,0:T(8,128)(2,1)S(1)}, bf16[2048,256]{1,0:T(8,128)(2,1)}, u32[]{:S(2)}) copy-start(bf16[2048,256]{1,0:T(8,128)(2,1)} %param.11) | copy-start | bytes 3145732
  14.4 30.9 %copy-start.9 = (s32[1024]{0:T(1024)S(1)}, s32[1024]{0:T(1024)}, u32[]{:S(2)}) copy-start(s32[1024]{0:T(1024)} %param.17) | copy-start | bytes 12292
  14.4 32.0 %copy-start.4 = (bf16[1024,256]{1,0:T(8,128)(2,1)S(1)}, bf16[1024,256]{1,0:T(8,128)(2,1)}, u32[]{:S(2)}) copy-start(bf16[1024,256]{1,0:T(8,128)(2,1)} %param.14) | copy-start | bytes 1572868
  14.4 25.9 %all-to-all-start = ((bf16[16,128,256]{2,1,0:T(8,128)(2,1)}), bf16[16,128,256]{2,1,0:T(8,128)(2,1)S(1)}, u32[]{:S(2)}, u32[]{:S(2)}) async-start(bf16[16,128,256]{2,1,0:T(8,128)(2,1)} %bitcast), calls=%async_computation | async-start | bytes 2097152 | tf_op jit(solution)/shard_map/all_to_all | solution.py:157
  22.5 56.1 %all-gather.2.cloned.1.call-start = ((), (), s32[]{:S(2)}) async-start(), calls=%async_computation.2 | async-start | bytes 4718592 | tf_op jit(solution)/shard_map/all_gather | solution.py:159
  45.2 152.4 %reduce-scatter.2.cloned.1.call-start = ((), (), s32[]{:S(2)}) async-start(), calls=%async_computation.3 | async-start | bytes 4718592 | tf_op jit(solution)/shard_map/reduce_scatter | solution.py:190
  47.2 34.7 %copy-start.8 = (f32[2048]{0:T(1024)S(1)}, f32[2048]{0:T(1024)}, u32[]{:S(2)}) copy-start(f32[2048]{0:T(1024)} %param.10) | copy-start | bytes 24580
  78.7 3.4 %copy-start.1 = (bf16[1024,2048]{1,0:T(8,128)(2,1)S(1)}, bf16[1024,2048]{1,0:T(8,128)(2,1)}, u32[]{:S(2)}) copy-start(bf16[1024,2048]{1,0:T(8,128)(2,1)} %all-gather.2.cloned.1.call-done) | copy-start | bytes 12582916
  84.2 39.6 %collective-permute-start.1 = (bf16[1024,256]{1,0:T(8,128)(2,1)}, bf16[1024,256]{1,0:T(8,128)(2,1)}, u32[]{:S(2)}, u32[]{:S(2)}) collective-permute-start(bf16[1024,256]{1,0:T(8,128)(2,1)} %convolution_convert_fusion.ko_ref.vo_ref), channel_id=1, source_target_pairs={{0,8},{8,16},{16,24},{24,32},{32,40},{40,48},{48,56},{56,64},{64,7... | collective-permute-start | bytes 1572872 | tf_op jit(solution)/shard_map/ppermute | solution.py:20
  89.8 4.0 %copy-start.10 = (bf16[1024,256]{1,0:T(8,128)(2,1)}, bf16[1024,256]{1,0:T(8,128)(2,1)S(1)}, u32[]{:S(2)}) copy-start(bf16[1024,256]{1,0:T(8,128)(2,1)S(1)} %convolution_convert_fusion.1.ko_ref.vo_ref) | copy-start | bytes 1572868
  89.8 20.9 %collective-permute-start = (bf16[1024,256]{1,0:T(8,128)(2,1)S(1)}, bf16[1024,256]{1,0:T(8,128)(2,1)S(1)}, u32[]{:S(2)}, u32[]{:S(2)}) collective-permute-start(bf16[1024,256]{1,0:T(8,128)(2,1)S(1)} %convolution_convert_fusion.1.ko_ref.vo_ref), channel_id=1, source_target_pairs={{0,8},{8,16},{16,24},{24,32},{32,40},{40,48},{48,56},{56,64},{64,7... | collective-permute-start | bytes 1572872 | tf_op jit(solution)/shard_map/ppermute | solution.py:20
  110.7 0.8 copy-start.11
  122.2 13.8 %copy-start.5 = (bf16[1024,128]{1,0:T(8,128)(2,1)S(1)}, bf16[1024,128]{1,0:T(8,128)(2,1)}, u32[]{:S(2)}) copy-start(bf16[1024,128]{1,0:T(8,128)(2,1)} %get-tuple-element.12) | copy-start | bytes 786436
  122.2 16.3 %collective-permute-start.2 = (bf16[1024,256]{1,0:T(8,128)(2,1)}, bf16[1024,256]{1,0:T(8,128)(2,1)}, u32[]{:S(2)}, u32[]{:S(2)}) collective-permute-start(bf16[1024,256]{1,0:T(8,128)(2,1)} %get-tuple-element.15), channel_id=1, source_target_pairs={{8,0},{16,8},{24,16},{32,24},{40,32},{48,40},{56,48},{64,56},{72,6... | collective-permute-start | bytes 1572872 | tf_op jit(solution)/shard_map/ppermute | solution.py:20
  134.7 16.8 %collective-permute-start.3 = (bf16[1024,256]{1,0:T(8,128)(2,1)}, bf16[1024,256]{1,0:T(8,128)(2,1)}, u32[]{:S(2)}, u32[]{:S(2)}) collective-permute-start(bf16[1024,256]{1,0:T(8,128)(2,1)} %get-tuple-element.17), channel_id=1, source_target_pairs={{8,0},{16,8},{24,16},{32,24},{40,32},{48,40},{56,48},{64,56},{72,6... | collective-permute-start | bytes 1572872 | tf_op jit(solution)/shard_map/ppermute | solution.py:20
  136.0 2.5 %copy-start.2 = (f32[1024,256]{1,0:T(8,128)S(1)}, f32[1024,256]{1,0:T(8,128)}, u32[]{:S(2)}) copy-start(f32[1024,256]{1,0:T(8,128)} %get-tuple-element.14) | copy-start | bytes 3145732
  138.5 13.0 %copy-start.3 = (f32[1024,256]{1,0:T(8,128)S(1)}, f32[1024,256]{1,0:T(8,128)}, u32[]{:S(2)}) copy-start(f32[1024,256]{1,0:T(8,128)} %get-tuple-element.16) | copy-start | bytes 3145732
  155.9 0.9 copy-start.6
  155.9 1.0 copy-start.7
Sparse Core Ops, SparseCore 0:
  45.3 33.2 all-gather.1
  156.1 41.4 reduce-scatter.1

commit v6 on v5

--- a/solution.py
+++ b/solution.py
@@ -52,21 +52,22 @@
     return (context, grad_q, grad_k, grad_v)
 
 
-def attention_kernel(
-    q_ref, kp_ref, vp_ref, ko_ref, vo_ref, do_ref, st_ref,
-    ctx_ref, dq_ref, send_ref, keep_ref,
-    k_scr, v_scr, dk_scr, dv_scr, *, tq, window, shift, scale
-):
+def attention_kernel(*refs, pieces, tq, window, shift, scale):
+    q_ref = refs[0]
+    kv_refs = refs[1 : 1 + 4 * pieces]
+    do_ref, st_ref, ctx_ref, dq_ref, send_ref, keep_ref, k_scr, v_scr, dk_scr, dv_scr = refs[
+        1 + 4 * pieces :
+    ]
     qi = pl.program_id(0)
     a = pl.multiple_of(qi * tq, tq)
-    half = kp_ref.shape[0]
+    piece = kv_refs[0].shape[0]
+    half = piece * pieces
 
     @pl.when(qi == 0)
     def _():
-        k_scr[:half, :] = kp_ref[...]
-        k_scr[half:, :] = ko_ref[...]
-        v_scr[:half, :] = vp_ref[...]
-        v_scr[half:, :] = vo_ref[...]
+        for j in range(2 * pieces):
+            k_scr[j * piece : (j + 1) * piece, :] = kv_refs[2 * j][...]
+            v_scr[j * piece : (j + 1) * piece, :] = kv_refs[2 * j + 1][...]
         dk_scr[...] = jnp.zeros_like(dk_scr)
         dv_scr[...] = jnp.zeros_like(dv_scr)
 
@@ -104,14 +105,16 @@
 
 def attention(queries, kv_prev, kv_own, grad_ctx, rel_start):
     rows, hd = queries.shape
+    pieces = len(kv_prev)
+    piece = rows // pieces
     tq = 256
     window = rows + tq
     kernel = functools.partial(
-        attention_kernel, tq=tq, window=window, shift=rows, scale=hd ** (-0.5)
+        attention_kernel, pieces=pieces, tq=tq, window=window, shift=rows, scale=hd ** (-0.5)
     )
     q_spec = pl.BlockSpec((tq, hd), lambda i: (i, 0))
-    k_spec = pl.BlockSpec((rows, hd), lambda i: (0, 0))
-    v_spec = pl.BlockSpec((rows, hd), lambda i: (0, 1))
+    k_spec = pl.BlockSpec((piece, hd), lambda i: (0, 0))
+    v_spec = pl.BlockSpec((piece, hd), lambda i: (0, 1))
     kv_spec = pl.BlockSpec((rows, 2 * hd), lambda i: (0, 0))
     steps = rows // tq
     cost = pl.CostEstimate(
@@ -119,11 +122,14 @@
         transcendentals=steps * 2 * tq * window,
         bytes_accessed=rows * hd * 2 * 8 + rows * 2 * hd * 6,
     )
+    kv_args = []
+    for part in list(kv_prev) + list(kv_own):
+        kv_args += [part, part]
     return pl.pallas_call(
         kernel,
         grid=(steps,),
-        in_specs=[q_spec, k_spec, v_spec, k_spec, v_spec, q_spec,
-                  pl.BlockSpec((tq, 1), lambda i: (i, 0))],
+        in_specs=[q_spec] + [k_spec, v_spec] * (2 * pieces) + [
+            q_spec, pl.BlockSpec((tq, 1), lambda i: (i, 0))],
         out_specs=[q_spec, q_spec, kv_spec, kv_spec],
         out_shape=[
             jax.ShapeDtypeStruct((rows, hd), jnp.bfloat16),
@@ -135,7 +141,7 @@
         + [pltpu.VMEM((2 * rows, hd), jnp.float32)] * 2,
         compiler_params=pltpu.CompilerParams(dimension_semantics=("arbitrary",)),
         cost_estimate=cost,
-    )(queries, kv_prev, kv_prev, kv_own, kv_own, grad_ctx, rel_start)
+    )(queries, *kv_args, grad_ctx, rel_start)
 
 
 def body(
@@ -156,27 +162,48 @@
     )
     arrived = lax.all_to_all(outgoing, "seq", split_axis=0, concat_axis=0, tiled=True)
     packed_part = jnp.take(arrived, recv_slot, axis=0)
-    packed = lax.all_gather(packed_part, "head", axis=1, tiled=True)
-    rows_float = packed.astype(jnp.float32)
-    inv_rms = lax.rsqrt(jnp.mean(rows_float * rows_float, axis=-1, keepdims=True) + epsilon)
-    normed = (rows_float * inv_rms * gain).astype(jnp.bfloat16)
-    queries = jnp.dot(normed, w_query, preferred_element_type=jnp.float32).astype(jnp.bfloat16)
+    pieces = 2
+    piece = row_count // pieces
     rel_start = (episode_start - (shard - 1) * row_count).reshape(row_count, 1)
-    local_heads = queries.shape[1] // HD
+    local_heads = w_query.shape[1] // HD
+    kv_weights = [
+        jnp.concatenate([w_key[:, h * HD : (h + 1) * HD], w_value[:, h * HD : (h + 1) * HD]], axis=1)
+        for h in range(local_heads)
+    ]
+    packed_pieces, inv_pieces, query_pieces = [], [], []
+    kv_own = [[] for _ in range(local_heads)]
+    kv_prev = [[] for _ in range(local_heads)]
+    for c in range(pieces):
+        part_c = packed_part[c * piece : (c + 1) * piece]
+        if c > 0:
+            part_c, _ = lax.optimization_barrier((part_c, [kv[-1] for kv in kv_own]))
+        packed_c = lax.all_gather(part_c, "head", axis=1, tiled=True)
+        rows_float = packed_c.astype(jnp.float32)
+        inv_rms = lax.rsqrt(jnp.mean(rows_float * rows_float, axis=-1, keepdims=True) + epsilon)
+        normed = (rows_float * inv_rms * gain).astype(jnp.bfloat16)
+        query_pieces.append(
+            jnp.dot(normed, w_query, preferred_element_type=jnp.float32).astype(jnp.bfloat16)
+        )
+        for h in range(local_heads):
+            kv_c = jnp.dot(normed, kv_weights[h], preferred_element_type=jnp.float32).astype(
+                jnp.bfloat16
+            )
+            kv_own[h].append(kv_c)
+            kv_prev[h].append(passed_along(kv_c, "seq", 1))
+        packed_pieces.append(packed_c)
+        inv_pieces.append(inv_rms)
+    queries = jnp.concatenate(query_pieces, axis=0)
     contexts, grad_queries, kv_parts = [], [], []
     for h in range(local_heads):
         cols = slice(h * HD, (h + 1) * HD)
-        kv_weight = jnp.concatenate([w_key[:, cols], w_value[:, cols]], axis=1)
-        kv_own = jnp.dot(normed, kv_weight, preferred_element_type=jnp.float32).astype(jnp.bfloat16)
-        kv_prev = passed_along(kv_own, "seq", 1)
         context_h, grad_q_h, kv_send, kv_keep = attention(
-            queries[:, cols], kv_prev, kv_own, grad_context[:, cols], rel_start
+            queries[:, cols], kv_prev[h], kv_own[h], grad_context[:, cols], rel_start
         )
         kv_next = passed_along(kv_send, "seq", -1)
         grad_kv = (kv_keep + kv_next.astype(jnp.float32)).astype(jnp.bfloat16)
         contexts.append(context_h)
         grad_queries.append(grad_q_h)
-        kv_parts.append((grad_kv, kv_weight))
+        kv_parts.append((grad_kv, kv_weights[h]))
     context_out = jnp.concatenate(contexts, axis=1)
     grad_q_all = jnp.concatenate(grad_queries, axis=1)
     share = row_count // head_count
@@ -193,9 +220,17 @@
         scatter_dimension=0,
         tiled=True,
     ).astype(jnp.float32)
-    own_start = head_pos * share
-    mine = lax.dynamic_slice_in_dim(packed, own_start, share, 0).astype(jnp.float32)
-    mine_inv = lax.dynamic_slice_in_dim(inv_rms, own_start, share, 0)
+    per_piece = piece // share
+    local_start = (head_pos % per_piece) * share
+    mine = lax.dynamic_slice_in_dim(packed_pieces[0], local_start, share, 0)
+    mine_inv = lax.dynamic_slice_in_dim(inv_pieces[0], local_start, share, 0)
+    for c in range(1, pieces):
+        later = head_pos // per_piece == c
+        mine = jnp.where(later, lax.dynamic_slice_in_dim(packed_pieces[c], local_start, share, 0), mine)
+        mine_inv = jnp.where(
+            later, lax.dynamic_slice_in_dim(inv_pieces[c], local_start, share, 0), mine_inv
+        )
+    mine = mine.astype(jnp.float32)
     gain_grad = gain * grad_normed
     mixed = jnp.mean(gain_grad * mine, axis=-1, keepdims=True)
     d_rows = (mine_inv * gain_grad - mine * mine_inv**3 * mixed).astype(jnp.bfloat16)

time: 209 us -> 221 us (1.057)
  starting transfers between devices: 18 us -> 25.5 us
  matrix products: 13.9 us -> 17.6 us
    ppermute x4 -> x6, waiting for transfers between devices: 26.7 us -> 16 us  [passed_along(): return lax.ppermute(array, axis, pairs)]
    all_gather x1 -> x2, waiting for transfers between devices: 29.8 us -> 38.2 us  [body(): packed_c = lax.all_gather(part_c, 'head', axis=1, tiled=True)]
    ppermute x4 -> x6, starting transfers between devices: 9.84 us -> 17.4 us  [passed_along(): return lax.ppermute(array, axis, pairs)]
    dot_general x2 -> x4, matrix products: 3.4 us -> 7.77 us  [body(): jnp.dot(normed, kv_weights[h], preferred_element_type=jnp.float32)]
    reduce_sum x1 -> x2, other arithmetic: 3.22 us -> 4.45 us  [body(): jnp.mean(rows_float * rows_float, axis=-1, keepdims=True) + epsilon]
  transfers between devices with their start and end apart: 7 -> 10, of which waited for: 6 -> 7; matrix products, arithmetic and copies ran while one was open for 7% -> 9% of each run, Pallas kernels for 10% -> 10%
where the time goes in v6:
time: 221 us; the launch traced here: 220 us
  waiting for transfers between devices  111 us (50%)
  starting transfers between devices  25.5 us (12%)
  Pallas kernels  21.7 us (10%)
  local copies, waits for them, and re-layouts  18.6 us (8%)
  matrix products  17.6 us (8%)
  between operations  14.1 us (6%)
  other arithmetic  12.1 us (5%)
    reduce_scatter x1, waiting for transfers between devices, body(): lax.psum_scatter(term.astype(jnp.bfloat16), 'head', scatter_dimension=0,...  38.9 us
    all_gather x2, waiting for transfers between devices, body(): packed_c = lax.all_gather(part_c, 'head', axis=1, tiled=True)  38.2 us
    pallas_call x2, Pallas kernels, attention(): pl.pallas_call(kernel, grid=(steps,), in_specs=[q_spec] + [k_spec, v_spec...  21.7 us
    all_to_all x1, waiting for transfers between devices, body(): lax.all_to_all(outgoing, 'seq', split_axis=0, concat_axis=0, tiled=True)  17.7 us
    ppermute x6, starting transfers between devices, passed_along(): return lax.ppermute(array, axis, pairs)  17.4 us
    ppermute x6, waiting for transfers between devices, passed_along(): return lax.ppermute(array, axis, pairs)  16 us
    dot_general x3, matrix products, project(): jnp.einsum('rc,dc->rd', grads, weight, preferred_element_type=jnp.float32)  8.3 us
    all_to_all x1, starting transfers between devices, body(): lax.all_to_all(outgoing, 'seq', split_axis=0, concat_axis=0, tiled=True)  7.99 us
  transfers between devices with their start and end apart: 10, of which 7 were waited for; matrix products, arithmetic and copies ran while one was open for 9% of the time, Pallas kernels for 10%

profile of v6, /device:TPU:0, one launch (start us, length us, event | category | flops | bytes accessed | tf_op | source)
XLA Modules:
  0.0 220.4 jit_solution(5069623281857749678)
XLA Ops:
  8.0 6.4 %scatter_custom_fusion = bf16[2048,256]{1,0:T(8,128)(2,1)} fusion(s32[1024]{0:T(1024)S(1)} %compare_select_fusion, bf16[1024,2048]{1,0:T(8,128)(2,1)} %param.9, s32[]{:T(128)} %constant.56.clone.1, s32[]{:T(128)S(6)} %select_n.53, bf16[]{:T(256)} %constant.59.clone.1), kind=kCustom, calls=%fused_computation.39 | custom fusion | bytes 1573892 | tf_op jit(solution)/shard_map/scatter | solution.py:161
  14.4 8.0 %all-to-all-start = ((bf16[16,128,256]{2,1,0:T(8,128)(2,1)}), bf16[16,128,256]{2,1,0:T(8,128)(2,1)S(1)}, u32[]{:S(2)}, u32[]{:S(2)}) async-start(bf16[16,128,256]{2,1,0:T(8,128)(2,1)} %bitcast), calls=%async_computation | async-start | bytes 2097152 | tf_op jit(solution)/shard_map/all_to_all | solution.py:163
  22.5 17.7 %all-to-all-done = bf16[16,128,256]{2,1,0:T(8,128)(2,1)S(1)} async-done(((bf16[16,128,256]{2,1,0:T(8,128)(2,1)}), bf16[16,128,256]{2,1,0:T(8,128)(2,1)S(1)}, u32[]{:S(2)}, u32[]{:S(2)}) %all-to-all-start) | async-done | bytes 1048608 | tf_op jit(solution)/shard_map/all_to_all | solution.py:163
  40.1 3.9 %gather_fusion = bf16[1024,256]{1,0:T(8,128)(2,1)S(1)} fusion(bf16[2048,256]{1,0:T(8,128)(2,1)S(1)} %bitcast.11, s32[1024]{0:T(1024)S(1)} %fusion.19), kind=kCustom, calls=%fused_computation | custom fusion | bytes 1052672 | tf_op jit(solution)/shard_map/jit(_take)/gather | solution.py:164
  44.3 0.9 fusion.37
  45.2 2.9 %fusion.34 = (bf16[2048,128]{1,0:T(8,128)(2,1)}, bf16[2048,128]{1,0:T(8,128)(2,1)}, bf16[2048,128]{1,0:T(8,128)(2,1)}, bf16[2048,128]{1,0:T(8,128)(2,1)}) fusion(bf16[2048,256]{1,0:T(8,128)(2,1)} %param.12, bf16[2048,256]{1,0:T(8,128)(2,1)} %param.13), kind=kLoop, calls=%fused_computation.63 | loop fusion | bytes 4194304 | tf_op jit(solution)/shard_map/slice | solution.py:170
  48.1 21.8 %all-gather.3.cloned.1.call-done = bf16[512,2048]{1,0:T(8,128)(2,1)} async-done(((bf16[512,256]{1,0:T(8,128)(2,1)}), bf16[512,2048]{1,0:T(8,128)(2,1)}) %all-gather.3.cloned.1.call-update) | async-done | bytes 2097168 | tf_op jit(solution)/shard_map/all_gather | solution.py:180
  69.9 2.2 %fusion = f32[512]{0:T(512)S(1)} fusion(bf16[512,2048]{1,0:T(8,128)(2,1)} %all-gather.3.cloned.1.call-done), kind=kLoop, calls=%fused_computation.7 | loop fusion | flops 3145216 | bytes 2099200 | tf_op jit(solution)/shard_map/reduce_sum | solution.py:182
  72.1 2.7 %convolution_convert_fusion.3.refs_5_.refs_6_ = bf16[512,256]{1,0:T(8,128)(2,1)} fusion(bf16[2048,128]{1,0:T(8,128)(2,1)} %get-tuple-element.33, bf16[2048,128]{1,0:T(8,128)(2,1)} %get-tuple-element.22, bf16[512,2048]{1,0:T(8,128)(2,1)S(1)} %copy-done.1, f32[2048]{0:T(1024)S(1)} %copy-done.14, f32[512]{0:T(512)S(1)} %add_rsqrt_fusion.1), kind=kOutput, calls=%fused_computation.18 | convolution fusion | flops 543293440 | bytes 3418112 | tf_op jit(solution)/shard_map/dot_general | solution.py:188
  74.9 1.5 convolution_convert_fusion.4.refs_5_.refs_6_
  76.5 1.0 copy.11.refs_10_
  77.5 1.9 fusion.36
  79.4 4.2 %collective-permute-start = (bf16[512,256]{1,0:T(8,128)(2,1)}, bf16[512,256]{1,0:T(8,128)(2,1)}, u32[]{:S(2)}, u32[]{:S(2)}) collective-permute-start(bf16[512,256]{1,0:T(8,128)(2,1)} %convolution_convert_fusion.4.refs_5_.refs_6_), channel_id=1, source_target_pairs={{0,8},{8,16},{16,24},{24,32},{32,40},{40,48},{48,56},{56,64},{64,7... | collective-permute-start | bytes 786440 | tf_op jit(solution)/shard_map/ppermute | solution.py:20
  83.6 3.5 %collective-permute-start.2 = (bf16[512,256]{1,0:T(8,128)(2,1)}, bf16[512,256]{1,0:T(8,128)(2,1)}, u32[]{:S(2)}, u32[]{:S(2)}) collective-permute-start(bf16[512,256]{1,0:T(8,128)(2,1)} %convolution_convert_fusion.3.refs_5_.refs_6_), channel_id=1, source_target_pairs={{0,8},{8,16},{16,24},{24,32},{32,40},{40,48},{48,56},{56,64},{64,7... | collective-permute-start | bytes 786440 | tf_op jit(solution)/shard_map/ppermute | solution.py:20
  87.8 16.5 %all-gather.5.cloned.1.call-done = bf16[512,2048]{1,0:T(8,128)(2,1)} async-done(((bf16[512,256]{1,0:T(8,128)(2,1)}), bf16[512,2048]{1,0:T(8,128)(2,1)}) %all-gather.5.cloned.1.call-update) | async-done | bytes 2097168 | tf_op jit(solution)/shard_map/all_gather | solution.py:180
  104.3 2.2 %fusion.3 = f32[512]{0:T(512)S(1)} fusion(bf16[512,2048]{1,0:T(8,128)(2,1)} %all-gather.5.cloned.1.call-done), kind=kLoop, calls=%fused_computation.10 | loop fusion | flops 3145216 | bytes 2099200 | tf_op jit(solution)/shard_map/reduce_sum | solution.py:182
  106.5 2.8 %convolution_convert_fusion.refs_7_.refs_8_ = bf16[512,256]{1,0:T(8,128)(2,1)} fusion(bf16[2048,128]{1,0:T(8,128)(2,1)} %get-tuple-element.33, bf16[2048,128]{1,0:T(8,128)(2,1)} %get-tuple-element.22, bf16[512,2048]{1,0:T(8,128)(2,1)S(1)} %copy-done.2, f32[512]{0:T(512)S(1)} %add_rsqrt_fusion, f32[2048]{0:T(1024)S(1)} %copy-done.14), kind=kOutput, calls=%fused_computation.15 | convolution fusion | flops 543293440 | bytes 3418112 | tf_op jit(solution)/shard_map/dot_general | solution.py:188
  109.3 4.2 %collective-permute-start.3 = (bf16[512,256]{1,0:T(8,128)(2,1)}, bf16[512,256]{1,0:T(8,128)(2,1)}, u32[]{:S(2)}, u32[]{:S(2)}) collective-permute-start(bf16[512,256]{1,0:T(8,128)(2,1)} %convolution_convert_fusion.refs_7_.refs_8_), channel_id=1, source_target_pairs={{0,8},{8,16},{16,24},{24,32},{32,40},{40,48},{48,56},{56,64},{64,7... | collective-permute-start | bytes 786440 | tf_op jit(solution)/shard_map/ppermute | solution.py:20
  114.3 3.0 %collective-permute-start.1 = (bf16[512,256]{1,0:T(8,128)(2,1)S(1)}, bf16[512,256]{1,0:T(8,128)(2,1)S(1)}, u32[]{:S(2)}, u32[]{:S(2)}) collective-permute-start(bf16[512,256]{1,0:T(8,128)(2,1)S(1)} %convolution_convert_fusion.1.refs_7_.refs_8_), channel_id=1, source_target_pairs={{0,8},{8,16},{16,24},{24,32},{32,40},{40,48},{48,56},{56,64},{64,7... | collective-permute-start | bytes 786440 | tf_op jit(solution)/shard_map/ppermute | solution.py:20
  118.9 5.7 %collective-permute-done.1.refs_3_.refs_4_ = bf16[512,256]{1,0:T(8,128)(2,1)S(1)} collective-permute-done((bf16[512,256]{1,0:T(8,128)(2,1)S(1)}, bf16[512,256]{1,0:T(8,128)(2,1)S(1)}, u32[]{:S(2)}, u32[]{:S(2)}) %collective-permute-start.1) | collective-permute-done | bytes 262176 | tf_op jit(solution)/shard_map/ppermute | solution.py:20
  125.3 10.8 %shard_map.104 = (bf16[1024,128]{1,0:T(8,128)(2,1)}, bf16[1024,128]{1,0:T(8,128)(2,1)}, bf16[1024,256]{1,0:T(8,128)(2,1)}, f32[1024,256]{1,0:T(8,128)}) custom-call(bf16[1024,128]{1,0:T(8,128)(2,1)} %get-tuple-element.28.refs_0_, bf16[512,256]{1,0:T(8,128)(2,1)} %collective-permute-done.refs_1_.refs_2_, ...), custom_call_target="tpu_custom_call" | custom-call | flops 2013265920 | bytes 3670016 | tf_op jit(solution)/shard_map/pallas_call | solution.py:128
  136.1 1.3 collective-permute-start.4
  137.4 10.8 %shard_map.105 = (bf16[1024,128]{1,0:T(8,128)(2,1)}, bf16[1024,128]{1,0:T(8,128)(2,1)}, bf16[1024,256]{1,0:T(8,128)(2,1)}, f32[1024,256]{1,0:T(8,128)}) custom-call(bf16[1024,128]{1,0:T(8,128)(2,1)} %get-tuple-element.29.refs_0_, bf16[512,256]{1,0:T(8,128)(2,1)} %collective-permute-done.2.refs_1_.refs_2_, ...), custom_call_target="tpu_custom_call" | custom-call | flops 2013265920 | bytes 3670016 | tf_op jit(solution)/shard_map/pallas_call | solution.py:128
  148.2 1.3 collective-permute-start.5
  149.6 2.5 %fusion.11 = f32[1024,2048]{1,0:T(8,128)S(1)} fusion(bf16[2048,256]{1,0:T(8,128)(2,1)S(1)} %copy-done, bf16[1024,128]{1,0:T(8,128)(2,1)} %get-tuple-element.15, bf16[1024,128]{1,0:T(8,128)(2,1)} %get-tuple-element.14), kind=kOutput, calls=%fused_computation.34 | convolution fusion | flops 1074790400 | bytes 9961472 | tf_op jit(solution)/shard_map/rc,dc->rd/dot_general | solution.py:212
  152.3 2.5 %fusion.10 = f32[1024,2048]{1,0:T(8,128)S(1)} fusion(f32[1024,256]{1,0:T(8,128)S(1)} %copy-done.11, bf16[1024,256]{1,0:T(8,128)(2,1)} %collective-permute-done.4, bf16[2048,128]{1,0:T(8,128)(2,1)S(1)} %copy-done.10, bf16[2048,128]{1,0:T(8,128)(2,1)S(1)} %copy-done.7), kind=kOutput, calls=%fused_computation.30 | convolution fusion | flops 1076625408 | bytes 11010048 | tf_op jit(solution)/shard_map/rc,dc->rd/dot_general | solution.py:212
  154.8 10.1 %collective-permute-done.5 = bf16[1024,256]{1,0:T(8,128)(2,1)S(1)} collective-permute-done((bf16[1024,256]{1,0:T(8,128)(2,1)}, bf16[1024,256]{1,0:T(8,128)(2,1)S(1)}, u32[]{:S(2)}, u32[]{:S(2)}) %collective-permute-start.5) | collective-permute-done | bytes 524320 | tf_op jit(solution)/shard_map/ppermute | solution.py:20
  165.0 3.4 %add_convert_fusion = bf16[1024,2048]{1,0:T(8,128)(2,1)} fusion(f32[1024,2048]{1,0:T(8,128)S(1)} %fusion.11, f32[1024,2048]{1,0:T(8,128)S(1)} %fusion.10, f32[1024,256]{1,0:T(8,128)S(1)} %copy-done.12, bf16[1024,256]{1,0:T(8,128)(2,1)S(1)} %collective-permute-done.5, bf16[2048,128]{1,0:T(8,128)(2,1)S(1)} %copy-done.4, bf16[2048,128]{1,0:T(8,128)(2,1)S(1)} %copy-done.3), kind=kOutput, calls=%fused_computation.2 | convolution fusion | flops 1082916864 | bytes 23592960 | tf_op jit(solution)/shard_map/rc,dc->rd/dot_general | solution.py:212
  169.3 1.8 pad_maximum_fusion.2
  171.1 38.9 %reduce-scatter.2.cloned.1.call-done = bf16[128,2048]{1,0:T(8,128)(2,1)} async-done(((bf16[1024,2048]{1,0:T(8,128)(2,1)}), bf16[128,2048]{1,0:T(8,128)(2,1)}) %reduce-scatter.2.cloned.1.call-update) | async-done | bytes 524304 | tf_op jit(solution)/shard_map/reduce_scatter | solution.py:217
  210.0 1.5 fusion.9
  211.5 2.4 %fusion.8 = bf16[128,2048]{1,0:T(8,128)(2,1)} fusion(bf16[128,2048]{1,0:T(8,128)(2,1)} %reduce-scatter.2.cloned.1.call-done, f32[128]{0:T(128)S(1)} %broadcast_multiply_fusion, f32[128]{0:T(128)S(1)} %get-tuple-element.20, f32[2048]{0:T(1024)S(1)} %copy-done.14, f32[128]{0:T(128)S(1)} %get-tuple-element.21, bf16[512,2048]{1,0:T(8,128)(2,1)S(1)} %copy-done.1, ...), kind=kLoop, calls=%fused_computation.23 | loop fusion | flops 2359296 | bytes 2106885 | tf_op jit(solution)/shard_map/convert_element_type | solution.py:236
  (61 shorter events, 6.2 us)
Async XLA Ops:
  7.2 79.9 %copy-start = (bf16[2048,256]{1,0:T(8,128)(2,1)S(1)}, bf16[2048,256]{1,0:T(8,128)(2,1)}, u32[]{:S(2)}) copy-start(bf16[2048,256]{1,0:T(8,128)(2,1)} %param.11) | copy-start | bytes 3145732
  7.2 15.3 %copy-start.15 = (s32[1024]{0:T(1024)S(1)}, s32[1024]{0:T(1024)}, u32[]{:S(2)}) copy-start(s32[1024]{0:T(1024)} %param.16) | copy-start | bytes 12292
  14.4 25.7 %all-to-all-start = ((bf16[16,128,256]{2,1,0:T(8,128)(2,1)}), bf16[16,128,256]{2,1,0:T(8,128)(2,1)S(1)}, u32[]{:S(2)}, u32[]{:S(2)}) async-start(bf16[16,128,256]{2,1,0:T(8,128)(2,1)} %bitcast), calls=%async_computation | async-start | bytes 2097152 | tf_op jit(solution)/shard_map/all_to_all | solution.py:163
  22.4 47.5 %all-gather.3.cloned.1.call-start = ((), (), s32[]{:S(2)}) async-start(), calls=%async_computation.2 | async-start | bytes 2359296 | tf_op jit(solution)/shard_map/all_gather | solution.py:180
  45.2 59.1 %all-gather.5.cloned.1.call-start = ((), (), s32[]{:S(2)}) async-start(), calls=%async_computation.3 | async-start | bytes 2359296 | tf_op jit(solution)/shard_map/all_gather | solution.py:180
  48.1 24.0 %copy-start.14 = (f32[2048]{0:T(1024)S(1)}, f32[2048]{0:T(1024)}, u32[]{:S(2)}) copy-start(f32[2048]{0:T(1024)} %param.10) | copy-start | bytes 24580
  69.9 2.2 %copy-start.1 = (bf16[512,2048]{1,0:T(8,128)(2,1)S(1)}, bf16[512,2048]{1,0:T(8,128)(2,1)}, u32[]{:S(2)}) copy-start(bf16[512,2048]{1,0:T(8,128)(2,1)} %all-gather.3.cloned.1.call-done) | copy-start | bytes 6291460
  72.1 2.8 %copy-start.5 = (bf16[2048,128]{1,0:T(8,128)(2,1)S(1)}, bf16[2048,128]{1,0:T(8,128)(2,1)}, u32[]{:S(2)}) copy-start(bf16[2048,128]{1,0:T(8,128)(2,1)} %get-tuple-element.23) | copy-start | bytes 1572868
  72.1 2.8 %copy-start.8 = (bf16[2048,128]{1,0:T(8,128)(2,1)S(1)}, bf16[2048,128]{1,0:T(8,128)(2,1)}, u32[]{:S(2)}) copy-start(bf16[2048,128]{1,0:T(8,128)(2,1)} %get-tuple-element.32) | copy-start | bytes 1572868
  74.9 1.6 copy-start.16
  76.4 133.6 %reduce-scatter.2.cloned.1.call-start = ((), (), s32[]{:S(2)}) async-start(), calls=%async_computation.4 | async-start | bytes 4718592 | tf_op jit(solution)/shard_map/reduce_scatter | solution.py:217
  79.4 39.5 %collective-permute-start = (bf16[512,256]{1,0:T(8,128)(2,1)}, bf16[512,256]{1,0:T(8,128)(2,1)}, u32[]{:S(2)}, u32[]{:S(2)}) collective-permute-start(bf16[512,256]{1,0:T(8,128)(2,1)} %convolution_convert_fusion.4.refs_5_.refs_6_), channel_id=1, source_target_pairs={{0,8},{8,16},{16,24},{24,32},{32,40},{40,48},{48,56},{56,64},{64,7... | collective-permute-start | bytes 786440 | tf_op jit(solution)/shard_map/ppermute | solution.py:20
  83.6 53.8 %collective-permute-start.2 = (bf16[512,256]{1,0:T(8,128)(2,1)}, bf16[512,256]{1,0:T(8,128)(2,1)}, u32[]{:S(2)}, u32[]{:S(2)}) collective-permute-start(bf16[512,256]{1,0:T(8,128)(2,1)} %convolution_convert_fusion.3.refs_5_.refs_6_), channel_id=1, source_target_pairs={{0,8},{8,16},{16,24},{24,32},{32,40},{40,48},{48,56},{56,64},{64,7... | collective-permute-start | bytes 786440 | tf_op jit(solution)/shard_map/ppermute | solution.py:20
  104.3 2.2 %copy-start.2 = (bf16[512,2048]{1,0:T(8,128)(2,1)S(1)}, bf16[512,2048]{1,0:T(8,128)(2,1)}, u32[]{:S(2)}) copy-start(bf16[512,2048]{1,0:T(8,128)(2,1)} %all-gather.5.cloned.1.call-done) | copy-start | bytes 6291460
  106.5 7.0 %copy-start.6 = (bf16[2048,128]{1,0:T(8,128)(2,1)S(1)}, bf16[2048,128]{1,0:T(8,128)(2,1)}, u32[]{:S(2)}) copy-start(bf16[2048,128]{1,0:T(8,128)(2,1)} %get-tuple-element.23) | copy-start | bytes 1572868
  106.5 7.0 %copy-start.9 = (bf16[2048,128]{1,0:T(8,128)(2,1)S(1)}, bf16[2048,128]{1,0:T(8,128)(2,1)}, u32[]{:S(2)}) copy-start(bf16[2048,128]{1,0:T(8,128)(2,1)} %get-tuple-element.32) | copy-start | bytes 1572868
  109.3 28.1 %collective-permute-start.3 = (bf16[512,256]{1,0:T(8,128)(2,1)}, bf16[512,256]{1,0:T(8,128)(2,1)}, u32[]{:S(2)}, u32[]{:S(2)}) collective-permute-start(bf16[512,256]{1,0:T(8,128)(2,1)} %convolution_convert_fusion.refs_7_.refs_8_), channel_id=1, source_target_pairs={{0,8},{8,16},{16,24},{24,32},{32,40},{40,48},{48,56},{56,64},{64,7... | collective-permute-start | bytes 786440 | tf_op jit(solution)/shard_map/ppermute | solution.py:20
  114.3 3.8 %copy-start.17 = (bf16[512,256]{1,0:T(8,128)(2,1)}, bf16[512,256]{1,0:T(8,128)(2,1)S(1)}, u32[]{:S(2)}) copy-start(bf16[512,256]{1,0:T(8,128)(2,1)S(1)} %convolution_convert_fusion.1.refs_7_.refs_8_) | copy-start | bytes 786436
  114.3 10.3 %collective-permute-start.1 = (bf16[512,256]{1,0:T(8,128)(2,1)S(1)}, bf16[512,256]{1,0:T(8,128)(2,1)S(1)}, u32[]{:S(2)}, u32[]{:S(2)}) collective-permute-start(bf16[512,256]{1,0:T(8,128)(2,1)S(1)} %convolution_convert_fusion.1.refs_7_.refs_8_), channel_id=1, source_target_pairs={{0,8},{8,16},{16,24},{24,32},{32,40},{40,48},{48,56},{56,64},{64,7... | collective-permute-start | bytes 786440 | tf_op jit(solution)/shard_map/ppermute | solution.py:20
  124.6 0.7 copy-start.18
  136.1 16.2 %collective-permute-start.4 = (bf16[1024,256]{1,0:T(8,128)(2,1)}, bf16[1024,256]{1,0:T(8,128)(2,1)}, u32[]{:S(2)}, u32[]{:S(2)}) collective-permute-start(bf16[1024,256]{1,0:T(8,128)(2,1)} %get-tuple-element.17), channel_id=1, source_target_pairs={{8,0},{16,8},{24,16},{32,24},{40,32},{48,40},{56,48},{64,56},{72,6... | collective-permute-start | bytes 1572872 | tf_op jit(solution)/shard_map/ppermute | solution.py:20
  148.2 16.7 %collective-permute-start.5 = (bf16[1024,256]{1,0:T(8,128)(2,1)}, bf16[1024,256]{1,0:T(8,128)(2,1)S(1)}, u32[]{:S(2)}, u32[]{:S(2)}) collective-permute-start(bf16[1024,256]{1,0:T(8,128)(2,1)} %get-tuple-element.19), channel_id=1, source_target_pairs={{8,0},{16,8},{24,16},{32,24},{40,32},{48,40},{56,48},{64,56},{72,6... | collective-permute-start | bytes 1572872 | tf_op jit(solution)/shard_map/ppermute | solution.py:20
  149.5 2.7 %copy-start.7 = (bf16[2048,128]{1,0:T(8,128)(2,1)S(1)}, bf16[2048,128]{1,0:T(8,128)(2,1)}, u32[]{:S(2)}) copy-start(bf16[2048,128]{1,0:T(8,128)(2,1)} %get-tuple-element.23) | copy-start | bytes 1572868
  149.6 2.7 %copy-start.10 = (bf16[2048,128]{1,0:T(8,128)(2,1)S(1)}, bf16[2048,128]{1,0:T(8,128)(2,1)}, u32[]{:S(2)}) copy-start(bf16[2048,128]{1,0:T(8,128)(2,1)} %get-tuple-element.32) | copy-start | bytes 1572868
  149.6 2.7 %copy-start.11 = (f32[1024,256]{1,0:T(8,128)S(1)}, f32[1024,256]{1,0:T(8,128)}, u32[]{:S(2)}) copy-start(f32[1024,256]{1,0:T(8,128)} %get-tuple-element.16) | copy-start | bytes 3145732
  152.3 12.7 %copy-start.3 = (bf16[2048,128]{1,0:T(8,128)(2,1)S(1)}, bf16[2048,128]{1,0:T(8,128)(2,1)}, u32[]{:S(2)}) copy-start(bf16[2048,128]{1,0:T(8,128)(2,1)} %get-tuple-element.22) | copy-start | bytes 1572868
  152.3 12.7 %copy-start.4 = (bf16[2048,128]{1,0:T(8,128)(2,1)S(1)}, bf16[2048,128]{1,0:T(8,128)(2,1)}, u32[]{:S(2)}) copy-start(bf16[2048,128]{1,0:T(8,128)(2,1)} %get-tuple-element.33) | copy-start | bytes 1572868
  152.3 12.7 %copy-start.12 = (f32[1024,256]{1,0:T(8,128)S(1)}, f32[1024,256]{1,0:T(8,128)}, u32[]{:S(2)}) copy-start(f32[1024,256]{1,0:T(8,128)} %get-tuple-element.18) | copy-start | bytes 3145732
  168.3 0.9 copy-start.13
Sparse Core Ops, SparseCore 0:
  45.3 24.5 all-gather.2
  76.5 27.7 all-gather.4
  168.5 41.4 reduce-scatter.1

commit v7 on v5

--- a/solution.py
+++ b/solution.py
@@ -149,13 +149,20 @@
     capacity = 2 * row_count // seq_count
     width = own_rows.shape[1] // head_count
     own_part = lax.dynamic_slice_in_dim(own_rows, head_pos * width, width, 1)
-    outgoing = (
-        jnp.zeros((seq_count * capacity, width), own_rows.dtype)
-        .at[send_slot]
-        .set(own_part)
+    slots = seq_count * capacity
+    send_pick = (
+        lax.broadcasted_iota(jnp.int32, (slots, row_count), 0) == send_slot[None, :]
+    ).astype(own_rows.dtype)
+    outgoing = jnp.dot(send_pick, own_part, preferred_element_type=jnp.float32).astype(
+        own_rows.dtype
     )
     arrived = lax.all_to_all(outgoing, "seq", split_axis=0, concat_axis=0, tiled=True)
-    packed_part = jnp.take(arrived, recv_slot, axis=0)
+    recv_pick = (
+        lax.broadcasted_iota(jnp.int32, (row_count, slots), 1) == recv_slot[:, None]
+    ).astype(own_rows.dtype)
+    packed_part = jnp.dot(recv_pick, arrived, preferred_element_type=jnp.float32).astype(
+        own_rows.dtype
+    )
     packed = lax.all_gather(packed_part, "head", axis=1, tiled=True)
     rows_float = packed.astype(jnp.float32)
     inv_rms = lax.rsqrt(jnp.mean(rows_float * rows_float, axis=-1, keepdims=True) + epsilon)

time: 209 us -> 200 us (0.957)
  blocking collectives: 0 us -> 24.6 us
  waiting for transfers between devices: 113 us -> 96.8 us
  local copies, waits for them, and re-layouts: 16.7 us -> 6.37 us
  starting transfers between devices: 18 us -> 9.94 us
  matrix products: 13.9 us -> 17.9 us
  other arithmetic: 11.2 us -> 8.05 us
    all_to_all x0 -> x1, blocking collectives: none -> 24.6 us  [body(): lax.all_to_all(outgoing, 'seq', split_axis=0, concat_axis=0, tiled=True)]
    all_to_all x1 -> x0, waiting for transfers between devices: 16.3 us -> none  [body(): lax.all_to_all(outgoing, 'seq', split_axis=0, concat_axis=0, tiled=True)]
    all_to_all x1 -> x0, starting transfers between devices: 8.12 us -> none  [body(): lax.all_to_all(outgoing, 'seq', split_axis=0, concat_axis=0, tiled=True)]
    scatter x1 -> x0, local copies, waits for them, and re-layouts: 6.41 us -> none  [body(): outgoing = jnp.zeros((seq_count * capacity, width), own_rows.dtype).at[se...]
    dot_general x0 -> x2, matrix products: none -> 5.06 us  [the longest x1 2.76 us: body(): jnp.dot(send_pick, own_part, preferred_element_type=jnp.float32)]
    gather x1 -> x0, local copies, waits for them, and re-layouts: 3.93 us -> none  [body(): packed_part = jnp.take(arrived, recv_slot, axis=0)]
  transfers between devices with their start and end apart: 7 -> 6, of which waited for: 6 -> 5; matrix products, arithmetic and copies ran while one was open for 7% -> 6% of each run, Pallas kernels for 10% -> 11%
where the time goes in v7:
time: 200 us; the launch traced here: 199 us
  waiting for transfers between devices  96.8 us (48%)
  blocking collectives  24.6 us (12%)
  Pallas kernels  21.6 us (11%)
  matrix products  17.9 us (9%)
  between operations  14.2 us (7%)
  starting transfers between devices  9.94 us (5%)
  other arithmetic  8.05 us (4%)
  local copies, waits for them, and re-layouts  6.37 us (3%)
    reduce_scatter x1, waiting for transfers between devices, body(): lax.psum_scatter(term.astype(jnp.bfloat16), 'head', scatter_dimension=0,...  39.7 us
    all_gather x1, waiting for transfers between devices, body(): packed = lax.all_gather(packed_part, 'head', axis=1, tiled=True)  30.4 us
    ppermute x4, waiting for transfers between devices, passed_along(): return lax.ppermute(array, axis, pairs)  26.6 us
    all_to_all x1, blocking collectives, body(): lax.all_to_all(outgoing, 'seq', split_axis=0, concat_axis=0, tiled=True)  24.6 us
    pallas_call x2, Pallas kernels, attention(): pl.pallas_call(kernel, grid=(steps,), in_specs=[q_spec, k_spec, v_spec, k...  21.6 us
    ppermute x4, starting transfers between devices, passed_along(): return lax.ppermute(array, axis, pairs)  9.86 us
    dot_general x3, matrix products, project(): jnp.einsum('rc,dc->rd', grads, weight, preferred_element_type=jnp.float32)  8.15 us
  transfers between devices with their start and end apart: 6, of which 5 were waited for; matrix products, arithmetic and copies ran while one was open for 6% of the time, Pallas kernels for 11%

profile of v7, /device:TPU:0, one launch (start us, length us, event | category | flops | bytes accessed | tf_op | source)
XLA Modules:
  0.0 199.5 jit_solution(15657233587713830523)
XLA Ops:
  7.2 2.8 %fusion.7 = bf16[2048,256]{1,0:T(8,128)(2,1)S(1)} fusion(s32[1024]{0:T(1024)} %param.15, bf16[1024,2048]{1,0:T(8,128)(2,1)} %param.9, s32[]{:T(128)S(6)} %select_n.7), kind=kOutput, calls=%fused_computation.12 | convolution fusion | flops 1076363264 | bytes 1576964 | tf_op jit(solution)/shard_map/dot_general | solution.py:156
  10.0 24.6 %all_to_all.12 = bf16[16,128,256]{2,1,0:T(8,128)(2,1)S(1)} all-to-all(bf16[16,128,256]{2,1,0:T(8,128)(2,1)S(1)} %bitcast.10), channel_id=1, replica_groups=mesh['seq'=16,'head'=8] {'seq'}, dimensions={0} | all-to-all | bytes 2097152 | tf_op jit(solution)/shard_map/all_to_all | solution.py:159
  34.6 2.3 %fusion.8 = bf16[1024,256]{1,0:T(8,128)(2,1)} fusion(bf16[2048,256]{1,0:T(8,128)(2,1)S(1)} %bitcast.11, s32[1024]{0:T(1024)S(1)} %copy-done.12), kind=kOutput, calls=%fused_computation.15 | convolution fusion | flops 1076101120 | bytes 1576960 | tf_op jit(solution)/shard_map/dot_general | solution.py:163
  37.0 1.0 copy.11.st_ref
  38.1 0.8 fusion.31
  38.9 1.7 fusion.29
  40.6 30.4 %all-gather.2.cloned.1.call-done = bf16[1024,2048]{1,0:T(8,128)(2,1)} async-done(((bf16[1024,256]{1,0:T(8,128)(2,1)}), bf16[1024,2048]{1,0:T(8,128)(2,1)}) %all-gather.2.cloned.1.call-update) | async-done | bytes 4194320 | tf_op jit(solution)/shard_map/all_gather | solution.py:166
  71.0 3.2 %fusion = f32[1024]{0:T(1024)S(1)} fusion(bf16[1024,2048]{1,0:T(8,128)(2,1)} %all-gather.2.cloned.1.call-done), kind=kLoop, calls=%fused_computation.2 | loop fusion | flops 6290432 | bytes 4198400 | tf_op jit(solution)/shard_map/reduce_sum | solution.py:168
  74.2 0.2 copy-done.1
  74.5 2.1 %convolution_convert_fusion.ko_ref.vo_ref = bf16[1024,256]{1,0:T(8,128)(2,1)} fusion(bf16[2048,128]{1,0:T(8,128)(2,1)S(1)} %get-tuple-element.28, bf16[2048,128]{1,0:T(8,128)(2,1)S(1)} %get-tuple-element.21, bf16[1024,2048]{1,0:T(8,128)(2,1)S(1)} %copy-done.1, f32[2048]{0:T(1024)S(1)} %copy-done.8, f32[1024]{0:T(1024)S(1)} %add_rsqrt_fusion), kind=kOutput, calls=%fused_computation.16 | convolution fusion | flops 1084489728 | bytes 5779456 | tf_op jit(solution)/shard_map/dot_general | solution.py:177
  76.5 4.3 %collective-permute-start.1 = (bf16[1024,256]{1,0:T(8,128)(2,1)}, bf16[1024,256]{1,0:T(8,128)(2,1)}, u32[]{:S(2)}, u32[]{:S(2)}) collective-permute-start(bf16[1024,256]{1,0:T(8,128)(2,1)} %convolution_convert_fusion.ko_ref.vo_ref), channel_id=1, source_target_pairs={{0,8},{8,16},{16,24},{24,32},{32,40},{40,48},{48,56},{56,64},{64,7... | collective-permute-start | bytes 1572872 | tf_op jit(solution)/shard_map/ppermute | solution.py:20
  80.8 1.3 convolution_convert_fusion.1.ko_ref.vo_ref
  82.1 2.7 %collective-permute-start = (bf16[1024,256]{1,0:T(8,128)(2,1)S(1)}, bf16[1024,256]{1,0:T(8,128)(2,1)S(1)}, u32[]{:S(2)}, u32[]{:S(2)}) collective-permute-start(bf16[1024,256]{1,0:T(8,128)(2,1)S(1)} %convolution_convert_fusion.1.ko_ref.vo_ref), channel_id=1, source_target_pairs={{0,8},{8,16},{16,24},{24,32},{32,40},{40,48},{48,56},{56,64},{64,7... | collective-permute-start | bytes 1572872 | tf_op jit(solution)/shard_map/ppermute | solution.py:20
  84.8 1.3 convolution_convert_fusion.2
  86.2 0.9 fusion.32
  87.0 16.0 %collective-permute-done.kp_ref.vp_ref = bf16[1024,256]{1,0:T(8,128)(2,1)S(1)} collective-permute-done((bf16[1024,256]{1,0:T(8,128)(2,1)S(1)}, bf16[1024,256]{1,0:T(8,128)(2,1)S(1)}, u32[]{:S(2)}, u32[]{:S(2)}) %collective-permute-start) | collective-permute-done | bytes 524320 | tf_op jit(solution)/shard_map/ppermute | solution.py:20
  103.0 0.8 copy-done.11
  103.8 10.7 %shard_map.104 = (bf16[1024,128]{1,0:T(8,128)(2,1)}, bf16[1024,128]{1,0:T(8,128)(2,1)}, bf16[1024,256]{1,0:T(8,128)(2,1)}, f32[1024,256]{1,0:T(8,128)}) custom-call(bf16[1024,128]{1,0:T(8,128)(2,1)} %get-tuple-element.26.q_ref, bf16[1024,256]{1,0:T(8,128)(2,1)} %copy-done.11, bf16[1024,256]{1,0:T(8,128)(2,1)} %copy-done.11, bf16[1024,256]{1,0:T(8,128)(2,1)} %copy-done.10, ...), custom_call_target="tpu_custom_call" | custom-call | flops 2013265920 | bytes 3670016 | tf_op jit(solution)/shard_map/pallas_call | solution.py:122
  114.6 1.6 collective-permute-start.2
  116.2 10.8 %shard_map.105 = (bf16[1024,128]{1,0:T(8,128)(2,1)}, bf16[1024,128]{1,0:T(8,128)(2,1)}, bf16[1024,256]{1,0:T(8,128)(2,1)}, f32[1024,256]{1,0:T(8,128)}) custom-call(bf16[1024,128]{1,0:T(8,128)(2,1)} %get-tuple-element.27.q_ref, bf16[1024,256]{1,0:T(8,128)(2,1)} %collective-permute-done.1.kp_ref.vp_ref, ...), custom_call_target="tpu_custom_call" | custom-call | flops 2013265920 | bytes 3670016 | tf_op jit(solution)/shard_map/pallas_call | solution.py:122
  127.0 1.3 collective-permute-start.3
  128.4 2.3 %fusion.14 = f32[1024,2048]{1,0:T(8,128)S(1)} fusion(bf16[2048,256]{1,0:T(8,128)(2,1)S(1)} %copy-done, bf16[1024,128]{1,0:T(8,128)(2,1)} %get-tuple-element.13, bf16[1024,128]{1,0:T(8,128)(2,1)S(1)} %copy-done.5), kind=kOutput, calls=%fused_computation.30 | convolution fusion | flops 1074790400 | bytes 9961472 | tf_op jit(solution)/shard_map/rc,dc->rd/dot_general | solution.py:192
  130.7 0.2 collective-permute-done.2
  130.9 2.4 %fusion.13 = f32[1024,2048]{1,0:T(8,128)S(1)} fusion(bf16[2048,128]{1,0:T(8,128)(2,1)S(1)} %get-tuple-element.29, bf16[2048,128]{1,0:T(8,128)(2,1)S(1)} %get-tuple-element.20, f32[1024,256]{1,0:T(8,128)S(1)} %copy-done.2, bf16[1024,256]{1,0:T(8,128)(2,1)} %collective-permute-done.2), kind=kOutput, calls=%fused_computation.28 | convolution fusion | flops 1076625408 | bytes 11010048 | tf_op jit(solution)/shard_map/rc,dc->rd/dot_general | solution.py:192
  133.3 10.4 %collective-permute-done.3 = bf16[1024,256]{1,0:T(8,128)(2,1)S(1)} collective-permute-done((bf16[1024,256]{1,0:T(8,128)(2,1)}, bf16[1024,256]{1,0:T(8,128)(2,1)S(1)}, u32[]{:S(2)}, u32[]{:S(2)}) %collective-permute-start.3) | collective-permute-done | bytes 524320 | tf_op jit(solution)/shard_map/ppermute | solution.py:20
  143.7 3.4 %add_convert_fusion = bf16[1024,2048]{1,0:T(8,128)(2,1)} fusion(f32[1024,2048]{1,0:T(8,128)S(1)} %fusion.14, f32[1024,2048]{1,0:T(8,128)S(1)} %fusion.13, bf16[2048,128]{1,0:T(8,128)(2,1)S(1)} %get-tuple-element.28, bf16[2048,128]{1,0:T(8,128)(2,1)S(1)} %get-tuple-element.21, f32[1024,256]{1,0:T(8,128)S(1)} %copy-done.3, ...), kind=kOutput, calls=%fused_computation.5 | convolution fusion | flops 1082916864 | bytes 23592960 | tf_op jit(solution)/shard_map/rc,dc->rd/dot_general | solution.py:192
  147.2 0.1 fusion.19
  147.3 0.8 copy-done.6
  148.2 0.8 pad_maximum_fusion.6
  149.0 39.7 %reduce-scatter.2.cloned.1.call-done = bf16[128,2048]{1,0:T(8,128)(2,1)} async-done(((bf16[1024,2048]{1,0:T(8,128)(2,1)}), bf16[128,2048]{1,0:T(8,128)(2,1)}) %reduce-scatter.2.cloned.1.call-update) | async-done | bytes 524304 | tf_op jit(solution)/shard_map/reduce_scatter | solution.py:197
  188.7 1.5 fusion.12
  190.2 2.4 %fusion.11 = bf16[128,2048]{1,0:T(8,128)(2,1)} fusion(bf16[128,2048]{1,0:T(8,128)(2,1)} %reduce-scatter.2.cloned.1.call-done, f32[128]{0:T(128)S(1)} %broadcast_multiply_fusion, f32[128]{0:T(128)S(1)} %get-tuple-element.18, f32[2048]{0:T(1024)S(1)} %copy-done.8, f32[128]{0:T(128)S(1)} %get-tuple-element.19, ...), kind=kLoop, calls=%fused_computation.21 | loop fusion | flops 2097152 | bytes 1582596 | tf_op jit(solution)/shard_map/convert_element_type | solution.py:208
  (31 shorter events, 0.3 us)
Async XLA Ops:
  7.2 77.7 %copy-start = (bf16[2048,256]{1,0:T(8,128)(2,1)S(1)}, bf16[2048,256]{1,0:T(8,128)(2,1)}, u32[]{:S(2)}) copy-start(bf16[2048,256]{1,0:T(8,128)(2,1)} %param.11) | copy-start | bytes 3145732
  7.2 63.8 %all-gather.2.cloned.1.call-start = ((), (), s32[]{:S(2)}) async-start(), calls=%async_computation.2 | async-start | bytes 4718592 | tf_op jit(solution)/shard_map/all_gather | solution.py:166
  7.2 27.4 %copy-start.12 = (s32[1024]{0:T(1024)S(1)}, s32[1024]{0:T(1024)}, u32[]{:S(2)}) copy-start(s32[1024]{0:T(1024)} %param.16) | copy-start | bytes 12292
  34.6 2.4 %copy-start.9 = (s32[1024]{0:T(1024)S(1)}, s32[1024]{0:T(1024)}, u32[]{:S(2)}) copy-start(s32[1024]{0:T(1024)} %param.17) | copy-start | bytes 12292
  34.6 3.4 %copy-start.4 = (bf16[1024,256]{1,0:T(8,128)(2,1)S(1)}, bf16[1024,256]{1,0:T(8,128)(2,1)}, u32[]{:S(2)}) copy-start(bf16[1024,256]{1,0:T(8,128)(2,1)} %param.14) | copy-start | bytes 1572868
  37.0 151.8 %reduce-scatter.2.cloned.1.call-start = ((), (), s32[]{:S(2)}) async-start(), calls=%async_computation.3 | async-start | bytes 4718592 | tf_op jit(solution)/shard_map/reduce_scatter | solution.py:197
  38.9 35.3 %copy-start.8 = (f32[2048]{0:T(1024)S(1)}, f32[2048]{0:T(1024)}, u32[]{:S(2)}) copy-start(f32[2048]{0:T(1024)} %param.10) | copy-start | bytes 24580
  71.0 3.4 %copy-start.1 = (bf16[1024,2048]{1,0:T(8,128)(2,1)S(1)}, bf16[1024,2048]{1,0:T(8,128)(2,1)}, u32[]{:S(2)}) copy-start(bf16[1024,2048]{1,0:T(8,128)(2,1)} %all-gather.2.cloned.1.call-done) | copy-start | bytes 12582916
  76.5 39.6 %collective-permute-start.1 = (bf16[1024,256]{1,0:T(8,128)(2,1)}, bf16[1024,256]{1,0:T(8,128)(2,1)}, u32[]{:S(2)}, u32[]{:S(2)}) collective-permute-start(bf16[1024,256]{1,0:T(8,128)(2,1)} %convolution_convert_fusion.ko_ref.vo_ref), channel_id=1, source_target_pairs={{0,8},{8,16},{16,24},{24,32},{32,40},{40,48},{48,56},{56,64},{64,7... | collective-permute-start | bytes 1572872 | tf_op jit(solution)/shard_map/ppermute | solution.py:20
  82.1 4.1 %copy-start.10 = (bf16[1024,256]{1,0:T(8,128)(2,1)}, bf16[1024,256]{1,0:T(8,128)(2,1)S(1)}, u32[]{:S(2)}) copy-start(bf16[1024,256]{1,0:T(8,128)(2,1)S(1)} %convolution_convert_fusion.1.ko_ref.vo_ref) | copy-start | bytes 1572868
  82.1 20.9 %collective-permute-start = (bf16[1024,256]{1,0:T(8,128)(2,1)S(1)}, bf16[1024,256]{1,0:T(8,128)(2,1)S(1)}, u32[]{:S(2)}, u32[]{:S(2)}) collective-permute-start(bf16[1024,256]{1,0:T(8,128)(2,1)S(1)} %convolution_convert_fusion.1.ko_ref.vo_ref), channel_id=1, source_target_pairs={{0,8},{8,16},{16,24},{24,32},{32,40},{40,48},{48,56},{56,64},{64,7... | collective-permute-start | bytes 1572872 | tf_op jit(solution)/shard_map/ppermute | solution.py:20
  103.0 0.8 copy-start.11
  114.6 13.8 %copy-start.5 = (bf16[1024,128]{1,0:T(8,128)(2,1)S(1)}, bf16[1024,128]{1,0:T(8,128)(2,1)}, u32[]{:S(2)}) copy-start(bf16[1024,128]{1,0:T(8,128)(2,1)} %get-tuple-element.12) | copy-start | bytes 786436
  114.6 16.3 %collective-permute-start.2 = (bf16[1024,256]{1,0:T(8,128)(2,1)}, bf16[1024,256]{1,0:T(8,128)(2,1)}, u32[]{:S(2)}, u32[]{:S(2)}) collective-permute-start(bf16[1024,256]{1,0:T(8,128)(2,1)} %get-tuple-element.15), channel_id=1, source_target_pairs={{8,0},{16,8},{24,16},{32,24},{40,32},{48,40},{56,48},{64,56},{72,6... | collective-permute-start | bytes 1572872 | tf_op jit(solution)/shard_map/ppermute | solution.py:20
  127.0 16.7 %collective-permute-start.3 = (bf16[1024,256]{1,0:T(8,128)(2,1)}, bf16[1024,256]{1,0:T(8,128)(2,1)S(1)}, u32[]{:S(2)}, u32[]{:S(2)}) collective-permute-start(bf16[1024,256]{1,0:T(8,128)(2,1)} %get-tuple-element.17), channel_id=1, source_target_pairs={{8,0},{16,8},{24,16},{32,24},{40,32},{48,40},{56,48},{64,56},{72,6... | collective-permute-start | bytes 1572872 | tf_op jit(solution)/shard_map/ppermute | solution.py:20
  128.3 2.5 %copy-start.2 = (f32[1024,256]{1,0:T(8,128)S(1)}, f32[1024,256]{1,0:T(8,128)}, u32[]{:S(2)}) copy-start(f32[1024,256]{1,0:T(8,128)} %get-tuple-element.14) | copy-start | bytes 3145732
  130.9 12.9 %copy-start.3 = (f32[1024,256]{1,0:T(8,128)S(1)}, f32[1024,256]{1,0:T(8,128)}, u32[]{:S(2)}) copy-start(f32[1024,256]{1,0:T(8,128)} %get-tuple-element.16) | copy-start | bytes 3145732
  147.2 0.9 copy-start.6
  147.2 1.0 copy-start.7
Sparse Core Ops, SparseCore 0:
  37.1 33.8 all-gather.1
  147.3 41.3 reduce-scatter.1

commit v8 on v7

--- a/solution.py
+++ b/solution.py
@@ -175,7 +175,10 @@
         cols = slice(h * HD, (h + 1) * HD)
         kv_weight = jnp.concatenate([w_key[:, cols], w_value[:, cols]], axis=1)
         kv_own = jnp.dot(normed, kv_weight, preferred_element_type=jnp.float32).astype(jnp.bfloat16)
-        kv_prev = passed_along(kv_own, "seq", 1)
+        kv_sent = kv_own
+        if h > 0:
+            kv_sent, _ = lax.optimization_barrier((kv_own, kv_prev))
+        kv_prev = passed_along(kv_sent, "seq", 1)
         context_h, grad_q_h, kv_send, kv_keep = attention(
             queries[:, cols], kv_prev, kv_own, grad_context[:, cols], rel_start
         )

time: 200 us -> 193 us (0.965)
  waiting for transfers between devices: 96.8 us -> 89.3 us
    ppermute x4, waiting for transfers between devices: 26.6 us -> 19 us  [passed_along(): return lax.ppermute(array, axis, pairs)]
  transfers between devices with their start and end apart: 6 -> 6, of which waited for: 5 -> 4; matrix products, arithmetic and copies ran while one was open for 6% -> 7% of each run, Pallas kernels for 11% -> 11%
where the time goes in v8:
time: 193 us
  waiting for transfers between devices  89.3 us (46%)
  blocking collectives  24.6 us (13%)
  Pallas kernels  21.6 us (11%)
  matrix products  17.9 us (9%)
  between operations  14.2 us (7%)
  starting transfers between devices  11.6 us (6%)
  other arithmetic  8.05 us (4%)
  local copies, waits for them, and re-layouts  5.57 us (3%)
    reduce_scatter x1, waiting for transfers between devices, body(): lax.psum_scatter(term.astype(jnp.bfloat16), 'head', scatter_dimension=0,...  39.8 us
    all_gather x1, waiting for transfers between devices, body(): packed = lax.all_gather(packed_part, 'head', axis=1, tiled=True)  30.4 us
    all_to_all x1, blocking collectives, body(): lax.all_to_all(outgoing, 'seq', split_axis=0, concat_axis=0, tiled=True)  24.6 us
    pallas_call x2, Pallas kernels, attention(): pl.pallas_call(kernel, grid=(steps,), in_specs=[q_spec, k_spec, v_spec, k...  21.6 us
    ppermute x4, waiting for transfers between devices, passed_along(): return lax.ppermute(array, axis, pairs)  19 us
    ppermute x4, starting transfers between devices, passed_along(): return lax.ppermute(array, axis, pairs)  11.6 us
    dot_general x3, matrix products, project(): jnp.einsum('rc,dc->rd', grads, weight, preferred_element_type=jnp.float32)  8.15 us
  transfers between devices with their start and end apart: 6, of which 4 were waited for; matrix products, arithmetic and copies ran while one was open for 7% of the time, Pallas kernels for 11%

profile of v8, /device:TPU:0, one launch (start us, length us, event | category | flops | bytes accessed | tf_op | source)
XLA Modules:
  0.0 192.9 jit_solution(9750825930801540271)
XLA Ops:
  7.2 2.8 %fusion.7 = bf16[2048,256]{1,0:T(8,128)(2,1)S(1)} fusion(s32[1024]{0:T(1024)} %param.15, bf16[1024,2048]{1,0:T(8,128)(2,1)} %param.9, s32[]{:T(128)S(6)} %select_n.7), kind=kOutput, calls=%fused_computation.12 | convolution fusion | flops 1076363264 | bytes 1576964 | tf_op jit(solution)/shard_map/dot_general | solution.py:156
  10.0 24.6 %all_to_all.12 = bf16[16,128,256]{2,1,0:T(8,128)(2,1)S(1)} all-to-all(bf16[16,128,256]{2,1,0:T(8,128)(2,1)S(1)} %bitcast.10), channel_id=1, replica_groups=mesh['seq'=16,'head'=8] {'seq'}, dimensions={0} | all-to-all | bytes 2097152 | tf_op jit(solution)/shard_map/all_to_all | solution.py:159
  34.6 2.3 %fusion.8 = bf16[1024,256]{1,0:T(8,128)(2,1)} fusion(bf16[2048,256]{1,0:T(8,128)(2,1)S(1)} %bitcast.11, s32[1024]{0:T(1024)S(1)} %copy-done.12), kind=kOutput, calls=%fused_computation.15 | convolution fusion | flops 1076101120 | bytes 1576960 | tf_op jit(solution)/shard_map/dot_general | solution.py:163
  37.0 0.0 reduce-scatter.2.cloned.1.call-start
  37.0 1.0 copy.11.st_ref
  38.1 0.8 fusion.31
  38.9 1.7 fusion.29
  40.6 30.4 %all-gather.2.cloned.1.call-done = bf16[1024,2048]{1,0:T(8,128)(2,1)} async-done(((bf16[1024,256]{1,0:T(8,128)(2,1)}), bf16[1024,2048]{1,0:T(8,128)(2,1)}) %all-gather.2.cloned.1.call-update) | async-done | bytes 4194320 | tf_op jit(solution)/shard_map/all_gather | solution.py:166
  71.0 3.2 %fusion = f32[1024]{0:T(1024)S(1)} fusion(bf16[1024,2048]{1,0:T(8,128)(2,1)} %all-gather.2.cloned.1.call-done), kind=kLoop, calls=%fused_computation.2 | loop fusion | flops 6290432 | bytes 4198400 | tf_op jit(solution)/shard_map/reduce_sum | solution.py:168
  74.2 0.2 copy-done.1
  74.5 1.3 convolution_convert_fusion.1.ko_ref.vo_ref
  75.8 3.5 %collective-permute-start = (bf16[1024,256]{1,0:T(8,128)(2,1)S(1)}, bf16[1024,256]{1,0:T(8,128)(2,1)S(1)}, u32[]{:S(2)}, u32[]{:S(2)}) collective-permute-start(bf16[1024,256]{1,0:T(8,128)(2,1)S(1)} %convolution_convert_fusion.1.ko_ref.vo_ref), channel_id=1, source_target_pairs={{0,8},{8,16},{16,24},{24,32},{32,40},{40,48},{48,56},{56,64},{64,7... | collective-permute-start | bytes 1572872 | tf_op jit(solution)/shard_map/ppermute | solution.py:20
  79.3 2.1 %convolution_convert_fusion.ko_ref.vo_ref = bf16[1024,256]{1,0:T(8,128)(2,1)} fusion(bf16[2048,128]{1,0:T(8,128)(2,1)S(1)} %get-tuple-element.30, bf16[2048,128]{1,0:T(8,128)(2,1)S(1)} %get-tuple-element.23, bf16[1024,2048]{1,0:T(8,128)(2,1)S(1)} %copy-done.1, f32[2048]{0:T(1024)S(1)} %copy-done.8, f32[1024]{0:T(1024)S(1)} %add_rsqrt_fusion), kind=kOutput, calls=%fused_computation.16 | convolution fusion | flops 1084489728 | bytes 5779456 | tf_op jit(solution)/shard_map/dot_general | solution.py:177
  81.4 9.4 %collective-permute-done.kp_ref.vp_ref = bf16[1024,256]{1,0:T(8,128)(2,1)S(1)} collective-permute-done((bf16[1024,256]{1,0:T(8,128)(2,1)S(1)}, bf16[1024,256]{1,0:T(8,128)(2,1)S(1)}, u32[]{:S(2)}, u32[]{:S(2)}) %collective-permute-start) | collective-permute-done | bytes 524320 | tf_op jit(solution)/shard_map/ppermute | solution.py:20
  90.8 5.2 %collective-permute-start.1 = (bf16[1024,256]{1,0:T(8,128)(2,1)}, bf16[1024,256]{1,0:T(8,128)(2,1)}, u32[]{:S(2)}, u32[]{:S(2)}) collective-permute-start(bf16[1024,256]{1,0:T(8,128)(2,1)} %convolution_convert_fusion.ko_ref.vo_ref), channel_id=1, source_target_pairs={{0,8},{8,16},{16,24},{24,32},{32,40},{40,48},{48,56},{56,64},{64,7... | collective-permute-start | bytes 1572872 | tf_op jit(solution)/shard_map/ppermute | solution.py:20
  96.0 1.3 convolution_convert_fusion.2
  97.3 0.9 fusion.32
  98.2 10.7 %shard_map.104 = (bf16[1024,128]{1,0:T(8,128)(2,1)}, bf16[1024,128]{1,0:T(8,128)(2,1)}, bf16[1024,256]{1,0:T(8,128)(2,1)}, f32[1024,256]{1,0:T(8,128)}) custom-call(bf16[1024,128]{1,0:T(8,128)(2,1)} %get-tuple-element.28.q_ref, bf16[1024,256]{1,0:T(8,128)(2,1)} %copy-done.11, bf16[1024,256]{1,0:T(8,128)(2,1)} %copy-done.11, bf16[1024,256]{1,0:T(8,128)(2,1)} %copy-done.10, ...), custom_call_target="tpu_custom_call" | custom-call | flops 2013265920 | bytes 3670016 | tf_op jit(solution)/shard_map/pallas_call | solution.py:122
  108.9 1.6 collective-permute-start.2
  110.5 10.8 %shard_map.105 = (bf16[1024,128]{1,0:T(8,128)(2,1)}, bf16[1024,128]{1,0:T(8,128)(2,1)}, bf16[1024,256]{1,0:T(8,128)(2,1)}, f32[1024,256]{1,0:T(8,128)}) custom-call(bf16[1024,128]{1,0:T(8,128)(2,1)} %get-tuple-element.29.q_ref, bf16[1024,256]{1,0:T(8,128)(2,1)} %collective-permute-done.1.kp_ref.vp_ref, ...), custom_call_target="tpu_custom_call" | custom-call | flops 2013265920 | bytes 3670016 | tf_op jit(solution)/shard_map/pallas_call | solution.py:122
  121.4 1.3 collective-permute-start.3
  122.7 2.3 %fusion.14 = f32[1024,2048]{1,0:T(8,128)S(1)} fusion(bf16[2048,256]{1,0:T(8,128)(2,1)S(1)} %copy-done, bf16[1024,128]{1,0:T(8,128)(2,1)} %get-tuple-element.15, bf16[1024,128]{1,0:T(8,128)(2,1)S(1)} %copy-done.5), kind=kOutput, calls=%fused_computation.30 | convolution fusion | flops 1074790400 | bytes 9961472 | tf_op jit(solution)/shard_map/rc,dc->rd/dot_general | solution.py:195
  125.1 2.4 %fusion.13 = f32[1024,2048]{1,0:T(8,128)S(1)} fusion(bf16[2048,128]{1,0:T(8,128)(2,1)S(1)} %get-tuple-element.31, bf16[2048,128]{1,0:T(8,128)(2,1)S(1)} %get-tuple-element.22, f32[1024,256]{1,0:T(8,128)S(1)} %copy-done.2, bf16[1024,256]{1,0:T(8,128)(2,1)} %collective-permute-done.2), kind=kOutput, calls=%fused_computation.28 | convolution fusion | flops 1076625408 | bytes 11010048 | tf_op jit(solution)/shard_map/rc,dc->rd/dot_general | solution.py:195
  127.5 9.6 %collective-permute-done.3 = bf16[1024,256]{1,0:T(8,128)(2,1)S(1)} collective-permute-done((bf16[1024,256]{1,0:T(8,128)(2,1)}, bf16[1024,256]{1,0:T(8,128)(2,1)S(1)}, u32[]{:S(2)}, u32[]{:S(2)}) %collective-permute-start.3) | collective-permute-done | bytes 524320 | tf_op jit(solution)/shard_map/ppermute | solution.py:20
  137.1 3.4 %add_convert_fusion = bf16[1024,2048]{1,0:T(8,128)(2,1)} fusion(f32[1024,2048]{1,0:T(8,128)S(1)} %fusion.14, f32[1024,2048]{1,0:T(8,128)S(1)} %fusion.13, bf16[2048,128]{1,0:T(8,128)(2,1)S(1)} %get-tuple-element.30, bf16[2048,128]{1,0:T(8,128)(2,1)S(1)} %get-tuple-element.23, f32[1024,256]{1,0:T(8,128)S(1)} %copy-done.3, ...), kind=kOutput, calls=%fused_computation.5 | convolution fusion | flops 1082916864 | bytes 23592960 | tf_op jit(solution)/shard_map/rc,dc->rd/dot_general | solution.py:195
  140.5 0.1 fusion.19
  140.6 0.8 copy-done.6
  141.4 0.1 copy-done.7
  141.5 0.8 pad_maximum_fusion.6
  142.3 39.8 %reduce-scatter.2.cloned.1.call-done = bf16[128,2048]{1,0:T(8,128)(2,1)} async-done(((bf16[1024,2048]{1,0:T(8,128)(2,1)}), bf16[128,2048]{1,0:T(8,128)(2,1)}) %reduce-scatter.2.cloned.1.call-update) | async-done | bytes 524304 | tf_op jit(solution)/shard_map/reduce_scatter | solution.py:200
  182.2 1.5 fusion.12
  183.6 2.4 %fusion.11 = bf16[128,2048]{1,0:T(8,128)(2,1)} fusion(bf16[128,2048]{1,0:T(8,128)(2,1)} %reduce-scatter.2.cloned.1.call-done, f32[128]{0:T(128)S(1)} %broadcast_multiply_fusion, f32[128]{0:T(128)S(1)} %get-tuple-element.20, f32[2048]{0:T(1024)S(1)} %copy-done.8, f32[128]{0:T(128)S(1)} %get-tuple-element.21, ...), kind=kLoop, calls=%fused_computation.21 | loop fusion | flops 2097152 | bytes 1582596 | tf_op jit(solution)/shard_map/convert_element_type | solution.py:211
  (31 shorter events, 0.1 us)
Async XLA Ops:
  7.2 88.8 %copy-start = (bf16[2048,256]{1,0:T(8,128)(2,1)S(1)}, bf16[2048,256]{1,0:T(8,128)(2,1)}, u32[]{:S(2)}) copy-start(bf16[2048,256]{1,0:T(8,128)(2,1)} %param.11) | copy-start | bytes 3145732
  7.2 63.8 %all-gather.2.cloned.1.call-start = ((), (), s32[]{:S(2)}) async-start(), calls=%async_computation.2 | async-start | bytes 4718592 | tf_op jit(solution)/shard_map/all_gather | solution.py:166
  7.2 27.4 %copy-start.12 = (s32[1024]{0:T(1024)S(1)}, s32[1024]{0:T(1024)}, u32[]{:S(2)}) copy-start(s32[1024]{0:T(1024)} %param.16) | copy-start | bytes 12292
  34.6 2.4 %copy-start.9 = (s32[1024]{0:T(1024)S(1)}, s32[1024]{0:T(1024)}, u32[]{:S(2)}) copy-start(s32[1024]{0:T(1024)} %param.17) | copy-start | bytes 12292
  34.6 3.4 %copy-start.4 = (bf16[1024,256]{1,0:T(8,128)(2,1)S(1)}, bf16[1024,256]{1,0:T(8,128)(2,1)}, u32[]{:S(2)}) copy-start(bf16[1024,256]{1,0:T(8,128)(2,1)} %param.14) | copy-start | bytes 1572868
  37.0 145.2 %reduce-scatter.2.cloned.1.call-start = ((), (), s32[]{:S(2)}) async-start(), calls=%async_computation.3 | async-start | bytes 4718592 | tf_op jit(solution)/shard_map/reduce_scatter | solution.py:200
  38.9 35.3 %copy-start.8 = (f32[2048]{0:T(1024)S(1)}, f32[2048]{0:T(1024)}, u32[]{:S(2)}) copy-start(f32[2048]{0:T(1024)} %param.10) | copy-start | bytes 24580
  71.0 3.4 %copy-start.1 = (bf16[1024,2048]{1,0:T(8,128)(2,1)S(1)}, bf16[1024,2048]{1,0:T(8,128)(2,1)}, u32[]{:S(2)}) copy-start(bf16[1024,2048]{1,0:T(8,128)(2,1)} %all-gather.2.cloned.1.call-done) | copy-start | bytes 12582916
  75.8 5.6 %copy-start.10 = (bf16[1024,256]{1,0:T(8,128)(2,1)}, bf16[1024,256]{1,0:T(8,128)(2,1)S(1)}, u32[]{:S(2)}) copy-start(bf16[1024,256]{1,0:T(8,128)(2,1)S(1)} %convolution_convert_fusion.1.ko_ref.vo_ref) | copy-start | bytes 1572868
  75.8 15.0 %collective-permute-start = (bf16[1024,256]{1,0:T(8,128)(2,1)S(1)}, bf16[1024,256]{1,0:T(8,128)(2,1)S(1)}, u32[]{:S(2)}, u32[]{:S(2)}) collective-permute-start(bf16[1024,256]{1,0:T(8,128)(2,1)S(1)} %convolution_convert_fusion.1.ko_ref.vo_ref), channel_id=1, source_target_pairs={{0,8},{8,16},{16,24},{24,32},{32,40},{40,48},{48,56},{56,64},{64,7... | collective-permute-start | bytes 1572872 | tf_op jit(solution)/shard_map/ppermute | solution.py:20
  90.8 6.5 %copy-start.11 = (bf16[1024,256]{1,0:T(8,128)(2,1)}, bf16[1024,256]{1,0:T(8,128)(2,1)S(1)}, u32[]{:S(2)}) copy-start(bf16[1024,256]{1,0:T(8,128)(2,1)S(1)} %collective-permute-done.kp_ref.vp_ref) | copy-start | bytes 1572868
  90.8 19.7 %collective-permute-start.1 = (bf16[1024,256]{1,0:T(8,128)(2,1)}, bf16[1024,256]{1,0:T(8,128)(2,1)}, u32[]{:S(2)}, u32[]{:S(2)}) collective-permute-start(bf16[1024,256]{1,0:T(8,128)(2,1)} %convolution_convert_fusion.ko_ref.vo_ref), channel_id=1, source_target_pairs={{0,8},{8,16},{16,24},{24,32},{32,40},{40,48},{48,56},{56,64},{64,7... | collective-permute-start | bytes 1572872 | tf_op jit(solution)/shard_map/ppermute | solution.py:20
  108.9 13.8 %copy-start.5 = (bf16[1024,128]{1,0:T(8,128)(2,1)S(1)}, bf16[1024,128]{1,0:T(8,128)(2,1)}, u32[]{:S(2)}) copy-start(bf16[1024,128]{1,0:T(8,128)(2,1)} %get-tuple-element.14) | copy-start | bytes 786436
  108.9 16.1 %collective-permute-start.2 = (bf16[1024,256]{1,0:T(8,128)(2,1)}, bf16[1024,256]{1,0:T(8,128)(2,1)}, u32[]{:S(2)}, u32[]{:S(2)}) collective-permute-start(bf16[1024,256]{1,0:T(8,128)(2,1)} %get-tuple-element.17), channel_id=1, source_target_pairs={{8,0},{16,8},{24,16},{32,24},{40,32},{48,40},{56,48},{64,56},{72,6... | collective-permute-start | bytes 1572872 | tf_op jit(solution)/shard_map/ppermute | solution.py:20
  121.4 15.7 %collective-permute-start.3 = (bf16[1024,256]{1,0:T(8,128)(2,1)}, bf16[1024,256]{1,0:T(8,128)(2,1)S(1)}, u32[]{:S(2)}, u32[]{:S(2)}) collective-permute-start(bf16[1024,256]{1,0:T(8,128)(2,1)} %get-tuple-element.19), channel_id=1, source_target_pairs={{8,0},{16,8},{24,16},{32,24},{40,32},{48,40},{56,48},{64,56},{72,6... | collective-permute-start | bytes 1572872 | tf_op jit(solution)/shard_map/ppermute | solution.py:20
  122.7 2.3 %copy-start.2 = (f32[1024,256]{1,0:T(8,128)S(1)}, f32[1024,256]{1,0:T(8,128)}, u32[]{:S(2)}) copy-start(f32[1024,256]{1,0:T(8,128)} %get-tuple-element.16) | copy-start | bytes 3145732
  125.1 12.0 %copy-start.3 = (f32[1024,256]{1,0:T(8,128)S(1)}, f32[1024,256]{1,0:T(8,128)}, u32[]{:S(2)}) copy-start(f32[1024,256]{1,0:T(8,128)} %get-tuple-element.18) | copy-start | bytes 3145732
  140.5 0.9 copy-start.6
  140.5 1.0 copy-start.7
Sparse Core Ops, SparseCore 0:
  37.1 33.8 all-gather.1
  140.6 41.4 reduce-scatter.1

commit v9 on v8

--- a/solution.py
+++ b/solution.py
@@ -82,8 +82,8 @@
     allowed = (key_idx >= st_ref[...]) & (key_idx <= row_idx)
     s = jnp.where(allowed, s, neg_large)
     row_top = jnp.max(s, axis=1, keepdims=True)
-    log_total = row_top + jnp.log(jnp.sum(jnp.exp(s - row_top), axis=1, keepdims=True))
-    p = jnp.exp(s - log_total)
+    e = jnp.exp(s - row_top)
+    p = e * (1.0 / jnp.sum(e, axis=1, keepdims=True))
     p_low = p.astype(jnp.bfloat16)
     ctx_ref[...] = jnp.dot(p_low, v, preferred_element_type=jnp.float32).astype(ctx_ref.dtype)
     dp = lax.dot_general(do, v, rows_t, preferred_element_type=jnp.float32)

time: 193 us -> 193 us (level)
  no operation moved by 1% of the time
where the time goes in v9:
time: 193 us
  waiting for transfers between devices  89.1 us (46%)
  blocking collectives  24.6 us (13%)
  Pallas kernels  21.3 us (11%)
  matrix products  17.9 us (9%)
  between operations  14.2 us (7%)
  starting transfers between devices  11.6 us (6%)
  other arithmetic  8.05 us (4%)
  local copies, waits for them, and re-layouts  5.57 us (3%)
    reduce_scatter x1, waiting for transfers between devices, body(): lax.psum_scatter(term.astype(jnp.bfloat16), 'head', scatter_dimension=0,...  39.7 us
    all_gather x1, waiting for transfers between devices, body(): packed = lax.all_gather(packed_part, 'head', axis=1, tiled=True)  30.4 us
    all_to_all x1, blocking collectives, body(): lax.all_to_all(outgoing, 'seq', split_axis=0, concat_axis=0, tiled=True)  24.6 us
    pallas_call x2, Pallas kernels, attention(): pl.pallas_call(kernel, grid=(steps,), in_specs=[q_spec, k_spec, v_spec, k...  21.3 us
    ppermute x4, waiting for transfers between devices, passed_along(): return lax.ppermute(array, axis, pairs)  19 us
    ppermute x4, starting transfers between devices, passed_along(): return lax.ppermute(array, axis, pairs)  11.6 us
    dot_general x3, matrix products, project(): jnp.einsum('rc,dc->rd', grads, weight, preferred_element_type=jnp.float32)  8.15 us
  transfers between devices with their start and end apart: 6, of which 4 were waited for; matrix products, arithmetic and copies ran while one was open for 7% of the time, Pallas kernels for 11%

profile of v9, /device:TPU:0, one launch (start us, length us, event | category | flops | bytes accessed | tf_op | source)
XLA Modules:
  0.0 192.5 jit_solution(17321228127900428849)
XLA Ops:
  7.2 2.8 %fusion.7 = bf16[2048,256]{1,0:T(8,128)(2,1)S(1)} fusion(s32[1024]{0:T(1024)} %param.15, bf16[1024,2048]{1,0:T(8,128)(2,1)} %param.9, s32[]{:T(128)S(6)} %select_n.7), kind=kOutput, calls=%fused_computation.12 | convolution fusion | flops 1076363264 | bytes 1576964 | tf_op jit(solution)/shard_map/dot_general | solution.py:156
  10.0 24.6 %all_to_all.12 = bf16[16,128,256]{2,1,0:T(8,128)(2,1)S(1)} all-to-all(bf16[16,128,256]{2,1,0:T(8,128)(2,1)S(1)} %bitcast.10), channel_id=1, replica_groups=mesh['seq'=16,'head'=8] {'seq'}, dimensions={0} | all-to-all | bytes 2097152 | tf_op jit(solution)/shard_map/all_to_all | solution.py:159
  34.6 2.3 %fusion.8 = bf16[1024,256]{1,0:T(8,128)(2,1)} fusion(bf16[2048,256]{1,0:T(8,128)(2,1)S(1)} %bitcast.11, s32[1024]{0:T(1024)S(1)} %copy-done.12), kind=kOutput, calls=%fused_computation.15 | convolution fusion | flops 1076101120 | bytes 1576960 | tf_op jit(solution)/shard_map/dot_general | solution.py:163
  37.0 0.0 reduce-scatter.2.cloned.1.call-start
  37.0 1.0 copy.11.st_ref
  38.1 0.8 fusion.31
  38.9 1.7 fusion.29
  40.6 30.4 %all-gather.2.cloned.1.call-done = bf16[1024,2048]{1,0:T(8,128)(2,1)} async-done(((bf16[1024,256]{1,0:T(8,128)(2,1)}), bf16[1024,2048]{1,0:T(8,128)(2,1)}) %all-gather.2.cloned.1.call-update) | async-done | bytes 4194320 | tf_op jit(solution)/shard_map/all_gather | solution.py:166
  71.0 3.2 %fusion = f32[1024]{0:T(1024)S(1)} fusion(bf16[1024,2048]{1,0:T(8,128)(2,1)} %all-gather.2.cloned.1.call-done), kind=kLoop, calls=%fused_computation.2 | loop fusion | flops 6290432 | bytes 4198400 | tf_op jit(solution)/shard_map/reduce_sum | solution.py:168
  74.2 0.2 copy-done.1
  74.5 1.3 convolution_convert_fusion.1.ko_ref.vo_ref
  75.8 3.5 %collective-permute-start = (bf16[1024,256]{1,0:T(8,128)(2,1)S(1)}, bf16[1024,256]{1,0:T(8,128)(2,1)S(1)}, u32[]{:S(2)}, u32[]{:S(2)}) collective-permute-start(bf16[1024,256]{1,0:T(8,128)(2,1)S(1)} %convolution_convert_fusion.1.ko_ref.vo_ref), channel_id=1, source_target_pairs={{0,8},{8,16},{16,24},{24,32},{32,40},{40,48},{48,56},{56,64},{64,7... | collective-permute-start | bytes 1572872 | tf_op jit(solution)/shard_map/ppermute | solution.py:20
  79.3 2.1 %convolution_convert_fusion.ko_ref.vo_ref = bf16[1024,256]{1,0:T(8,128)(2,1)} fusion(bf16[2048,128]{1,0:T(8,128)(2,1)S(1)} %get-tuple-element.30, bf16[2048,128]{1,0:T(8,128)(2,1)S(1)} %get-tuple-element.23, bf16[1024,2048]{1,0:T(8,128)(2,1)S(1)} %copy-done.1, f32[2048]{0:T(1024)S(1)} %copy-done.8, f32[1024]{0:T(1024)S(1)} %add_rsqrt_fusion), kind=kOutput, calls=%fused_computation.16 | convolution fusion | flops 1084489728 | bytes 5779456 | tf_op jit(solution)/shard_map/dot_general | solution.py:177
  81.4 9.4 %collective-permute-done.kp_ref.vp_ref = bf16[1024,256]{1,0:T(8,128)(2,1)S(1)} collective-permute-done((bf16[1024,256]{1,0:T(8,128)(2,1)S(1)}, bf16[1024,256]{1,0:T(8,128)(2,1)S(1)}, u32[]{:S(2)}, u32[]{:S(2)}) %collective-permute-start) | collective-permute-done | bytes 524320 | tf_op jit(solution)/shard_map/ppermute | solution.py:20
  90.8 5.2 %collective-permute-start.1 = (bf16[1024,256]{1,0:T(8,128)(2,1)}, bf16[1024,256]{1,0:T(8,128)(2,1)}, u32[]{:S(2)}, u32[]{:S(2)}) collective-permute-start(bf16[1024,256]{1,0:T(8,128)(2,1)} %convolution_convert_fusion.ko_ref.vo_ref), channel_id=1, source_target_pairs={{0,8},{8,16},{16,24},{24,32},{32,40},{40,48},{48,56},{56,64},{64,7... | collective-permute-start | bytes 1572872 | tf_op jit(solution)/shard_map/ppermute | solution.py:20
  96.0 1.3 convolution_convert_fusion.2
  97.3 0.9 fusion.32
  98.2 10.6 %shard_map.104 = (bf16[1024,128]{1,0:T(8,128)(2,1)}, bf16[1024,128]{1,0:T(8,128)(2,1)}, bf16[1024,256]{1,0:T(8,128)(2,1)}, f32[1024,256]{1,0:T(8,128)}) custom-call(bf16[1024,128]{1,0:T(8,128)(2,1)} %get-tuple-element.28.q_ref, bf16[1024,256]{1,0:T(8,128)(2,1)} %copy-done.11, bf16[1024,256]{1,0:T(8,128)(2,1)} %copy-done.11, bf16[1024,256]{1,0:T(8,128)(2,1)} %copy-done.10, ...), custom_call_target="tpu_custom_call" | custom-call | flops 2013265920 | bytes 3670016 | tf_op jit(solution)/shard_map/pallas_call | solution.py:122
  108.8 1.6 collective-permute-start.2
  110.4 10.7 %shard_map.105 = (bf16[1024,128]{1,0:T(8,128)(2,1)}, bf16[1024,128]{1,0:T(8,128)(2,1)}, bf16[1024,256]{1,0:T(8,128)(2,1)}, f32[1024,256]{1,0:T(8,128)}) custom-call(bf16[1024,128]{1,0:T(8,128)(2,1)} %get-tuple-element.29.q_ref, bf16[1024,256]{1,0:T(8,128)(2,1)} %collective-permute-done.1.kp_ref.vp_ref, ...), custom_call_target="tpu_custom_call" | custom-call | flops 2013265920 | bytes 3670016 | tf_op jit(solution)/shard_map/pallas_call | solution.py:122
  121.1 1.3 collective-permute-start.3
  122.5 2.3 %fusion.14 = f32[1024,2048]{1,0:T(8,128)S(1)} fusion(bf16[2048,256]{1,0:T(8,128)(2,1)S(1)} %copy-done, bf16[1024,128]{1,0:T(8,128)(2,1)} %get-tuple-element.15, bf16[1024,128]{1,0:T(8,128)(2,1)S(1)} %copy-done.5), kind=kOutput, calls=%fused_computation.30 | convolution fusion | flops 1074790400 | bytes 9961472 | tf_op jit(solution)/shard_map/rc,dc->rd/dot_general | solution.py:195
  124.8 2.4 %fusion.13 = f32[1024,2048]{1,0:T(8,128)S(1)} fusion(bf16[2048,128]{1,0:T(8,128)(2,1)S(1)} %get-tuple-element.31, bf16[2048,128]{1,0:T(8,128)(2,1)S(1)} %get-tuple-element.22, f32[1024,256]{1,0:T(8,128)S(1)} %copy-done.2, bf16[1024,256]{1,0:T(8,128)(2,1)} %collective-permute-done.2), kind=kOutput, calls=%fused_computation.28 | convolution fusion | flops 1076625408 | bytes 11010048 | tf_op jit(solution)/shard_map/rc,dc->rd/dot_general | solution.py:195
  127.2 9.6 %collective-permute-done.3 = bf16[1024,256]{1,0:T(8,128)(2,1)S(1)} collective-permute-done((bf16[1024,256]{1,0:T(8,128)(2,1)}, bf16[1024,256]{1,0:T(8,128)(2,1)S(1)}, u32[]{:S(2)}, u32[]{:S(2)}) %collective-permute-start.3) | collective-permute-done | bytes 524320 | tf_op jit(solution)/shard_map/ppermute | solution.py:20
  136.8 3.4 %add_convert_fusion = bf16[1024,2048]{1,0:T(8,128)(2,1)} fusion(f32[1024,2048]{1,0:T(8,128)S(1)} %fusion.14, f32[1024,2048]{1,0:T(8,128)S(1)} %fusion.13, bf16[2048,128]{1,0:T(8,128)(2,1)S(1)} %get-tuple-element.30, bf16[2048,128]{1,0:T(8,128)(2,1)S(1)} %get-tuple-element.23, f32[1024,256]{1,0:T(8,128)S(1)} %copy-done.3, ...), kind=kOutput, calls=%fused_computation.5 | convolution fusion | flops 1082916864 | bytes 23592960 | tf_op jit(solution)/shard_map/rc,dc->rd/dot_general | solution.py:195
  140.3 0.1 fusion.19
  140.3 0.8 copy-done.6
  141.2 0.1 copy-done.7
  141.2 0.8 pad_maximum_fusion.6
  142.1 39.7 %reduce-scatter.2.cloned.1.call-done = bf16[128,2048]{1,0:T(8,128)(2,1)} async-done(((bf16[1024,2048]{1,0:T(8,128)(2,1)}), bf16[128,2048]{1,0:T(8,128)(2,1)}) %reduce-scatter.2.cloned.1.call-update) | async-done | bytes 524304 | tf_op jit(solution)/shard_map/reduce_scatter | solution.py:200
  181.8 1.5 fusion.12
  183.3 2.4 %fusion.11 = bf16[128,2048]{1,0:T(8,128)(2,1)} fusion(bf16[128,2048]{1,0:T(8,128)(2,1)} %reduce-scatter.2.cloned.1.call-done, f32[128]{0:T(128)S(1)} %broadcast_multiply_fusion, f32[128]{0:T(128)S(1)} %get-tuple-element.20, f32[2048]{0:T(1024)S(1)} %copy-done.8, f32[128]{0:T(128)S(1)} %get-tuple-element.21, ...), kind=kLoop, calls=%fused_computation.21 | loop fusion | flops 2097152 | bytes 1582596 | tf_op jit(solution)/shard_map/convert_element_type | solution.py:211
  (31 shorter events, 0.1 us)
Async XLA Ops:
  7.2 88.8 %copy-start = (bf16[2048,256]{1,0:T(8,128)(2,1)S(1)}, bf16[2048,256]{1,0:T(8,128)(2,1)}, u32[]{:S(2)}) copy-start(bf16[2048,256]{1,0:T(8,128)(2,1)} %param.11) | copy-start | bytes 3145732
  7.2 63.8 %all-gather.2.cloned.1.call-start = ((), (), s32[]{:S(2)}) async-start(), calls=%async_computation.2 | async-start | bytes 4718592 | tf_op jit(solution)/shard_map/all_gather | solution.py:166
  7.2 27.4 %copy-start.12 = (s32[1024]{0:T(1024)S(1)}, s32[1024]{0:T(1024)}, u32[]{:S(2)}) copy-start(s32[1024]{0:T(1024)} %param.16) | copy-start | bytes 12292
  34.6 2.4 %copy-start.9 = (s32[1024]{0:T(1024)S(1)}, s32[1024]{0:T(1024)}, u32[]{:S(2)}) copy-start(s32[1024]{0:T(1024)} %param.17) | copy-start | bytes 12292
  34.6 3.4 %copy-start.4 = (bf16[1024,256]{1,0:T(8,128)(2,1)S(1)}, bf16[1024,256]{1,0:T(8,128)(2,1)}, u32[]{:S(2)}) copy-start(bf16[1024,256]{1,0:T(8,128)(2,1)} %param.14) | copy-start | bytes 1572868
  37.0 144.8 %reduce-scatter.2.cloned.1.call-start = ((), (), s32[]{:S(2)}) async-start(), calls=%async_computation.3 | async-start | bytes 4718592 | tf_op jit(solution)/shard_map/reduce_scatter | solution.py:200
  38.9 35.3 %copy-start.8 = (f32[2048]{0:T(1024)S(1)}, f32[2048]{0:T(1024)}, u32[]{:S(2)}) copy-start(f32[2048]{0:T(1024)} %param.10) | copy-start | bytes 24580
  71.0 3.4 %copy-start.1 = (bf16[1024,2048]{1,0:T(8,128)(2,1)S(1)}, bf16[1024,2048]{1,0:T(8,128)(2,1)}, u32[]{:S(2)}) copy-start(bf16[1024,2048]{1,0:T(8,128)(2,1)} %all-gather.2.cloned.1.call-done) | copy-start | bytes 12582916
  75.8 5.6 %copy-start.10 = (bf16[1024,256]{1,0:T(8,128)(2,1)}, bf16[1024,256]{1,0:T(8,128)(2,1)S(1)}, u32[]{:S(2)}) copy-start(bf16[1024,256]{1,0:T(8,128)(2,1)S(1)} %convolution_convert_fusion.1.ko_ref.vo_ref) | copy-start | bytes 1572868
  75.8 15.0 %collective-permute-start = (bf16[1024,256]{1,0:T(8,128)(2,1)S(1)}, bf16[1024,256]{1,0:T(8,128)(2,1)S(1)}, u32[]{:S(2)}, u32[]{:S(2)}) collective-permute-start(bf16[1024,256]{1,0:T(8,128)(2,1)S(1)} %convolution_convert_fusion.1.ko_ref.vo_ref), channel_id=1, source_target_pairs={{0,8},{8,16},{16,24},{24,32},{32,40},{40,48},{48,56},{56,64},{64,7... | collective-permute-start | bytes 1572872 | tf_op jit(solution)/shard_map/ppermute | solution.py:20
  90.8 6.5 %copy-start.11 = (bf16[1024,256]{1,0:T(8,128)(2,1)}, bf16[1024,256]{1,0:T(8,128)(2,1)S(1)}, u32[]{:S(2)}) copy-start(bf16[1024,256]{1,0:T(8,128)(2,1)S(1)} %collective-permute-done.kp_ref.vp_ref) | copy-start | bytes 1572868
  90.8 19.6 %collective-permute-start.1 = (bf16[1024,256]{1,0:T(8,128)(2,1)}, bf16[1024,256]{1,0:T(8,128)(2,1)}, u32[]{:S(2)}, u32[]{:S(2)}) collective-permute-start(bf16[1024,256]{1,0:T(8,128)(2,1)} %convolution_convert_fusion.ko_ref.vo_ref), channel_id=1, source_target_pairs={{0,8},{8,16},{16,24},{24,32},{32,40},{40,48},{48,56},{56,64},{64,7... | collective-permute-start | bytes 1572872 | tf_op jit(solution)/shard_map/ppermute | solution.py:20
  108.8 13.7 %copy-start.5 = (bf16[1024,128]{1,0:T(8,128)(2,1)S(1)}, bf16[1024,128]{1,0:T(8,128)(2,1)}, u32[]{:S(2)}) copy-start(bf16[1024,128]{1,0:T(8,128)(2,1)} %get-tuple-element.14) | copy-start | bytes 786436
  108.8 16.0 %collective-permute-start.2 = (bf16[1024,256]{1,0:T(8,128)(2,1)}, bf16[1024,256]{1,0:T(8,128)(2,1)}, u32[]{:S(2)}, u32[]{:S(2)}) collective-permute-start(bf16[1024,256]{1,0:T(8,128)(2,1)} %get-tuple-element.17), channel_id=1, source_target_pairs={{8,0},{16,8},{24,16},{32,24},{40,32},{48,40},{56,48},{64,56},{72,6... | collective-permute-start | bytes 1572872 | tf_op jit(solution)/shard_map/ppermute | solution.py:20
  121.1 15.7 %collective-permute-start.3 = (bf16[1024,256]{1,0:T(8,128)(2,1)}, bf16[1024,256]{1,0:T(8,128)(2,1)S(1)}, u32[]{:S(2)}, u32[]{:S(2)}) collective-permute-start(bf16[1024,256]{1,0:T(8,128)(2,1)} %get-tuple-element.19), channel_id=1, source_target_pairs={{8,0},{16,8},{24,16},{32,24},{40,32},{48,40},{56,48},{64,56},{72,6... | collective-permute-start | bytes 1572872 | tf_op jit(solution)/shard_map/ppermute | solution.py:20
  122.5 2.4 %copy-start.2 = (f32[1024,256]{1,0:T(8,128)S(1)}, f32[1024,256]{1,0:T(8,128)}, u32[]{:S(2)}) copy-start(f32[1024,256]{1,0:T(8,128)} %get-tuple-element.16) | copy-start | bytes 3145732
  124.8 12.0 %copy-start.3 = (f32[1024,256]{1,0:T(8,128)S(1)}, f32[1024,256]{1,0:T(8,128)}, u32[]{:S(2)}) copy-start(f32[1024,256]{1,0:T(8,128)} %get-tuple-element.18) | copy-start | bytes 3145732
  140.2 0.9 copy-start.6
  140.2 1.0 copy-start.7
Sparse Core Ops, SparseCore 0:
  37.1 33.8 all-gather.1
  140.4 41.3 reduce-scatter.1

commit v10 on v8

--- a/solution.py
+++ b/solution.py
@@ -104,7 +104,7 @@
 
 def attention(queries, kv_prev, kv_own, grad_ctx, rel_start):
     rows, hd = queries.shape
-    tq = 256
+    tq = 128
     window = rows + tq
     kernel = functools.partial(
         attention_kernel, tq=tq, window=window, shift=rows, scale=hd ** (-0.5)

time: 193 us -> 197 us (1.021)
  Pallas kernels: 21.6 us -> 25.8 us
    pallas_call x2, Pallas kernels: 21.6 us -> 25.8 us  [attention(): pl.pallas_call(kernel, grid=(steps,), in_specs=[q_spec, k_spec, v_spec, k...]
  transfers between devices with their start and end apart: 6 -> 6, of which waited for: 4 -> 4; matrix products, arithmetic and copies ran while one was open for 7% -> 7% of each run, Pallas kernels for 11% -> 13%
where the time goes in v10:
time: 197 us
  waiting for transfers between devices  89.1 us (45%)
  Pallas kernels  25.8 us (13%)
  blocking collectives  24.6 us (12%)
  matrix products  17.9 us (9%)
  between operations  14.2 us (7%)
  starting transfers between devices  11.6 us (6%)
  other arithmetic  8.05 us (4%)
  local copies, waits for them, and re-layouts  5.57 us (3%)
    reduce_scatter x1, waiting for transfers between devices, body(): lax.psum_scatter(term.astype(jnp.bfloat16), 'head', scatter_dimension=0,...  39.7 us
    all_gather x1, waiting for transfers between devices, body(): packed = lax.all_gather(packed_part, 'head', axis=1, tiled=True)  30.4 us
    pallas_call x2, Pallas kernels, attention(): pl.pallas_call(kernel, grid=(steps,), in_specs=[q_spec, k_spec, v_spec, k...  25.8 us
    all_to_all x1, blocking collectives, body(): lax.all_to_all(outgoing, 'seq', split_axis=0, concat_axis=0, tiled=True)  24.6 us
    ppermute x4, waiting for transfers between devices, passed_along(): return lax.ppermute(array, axis, pairs)  19 us
    ppermute x4, starting transfers between devices, passed_along(): return lax.ppermute(array, axis, pairs)  11.6 us
    dot_general x3, matrix products, project(): jnp.einsum('rc,dc->rd', grads, weight, preferred_element_type=jnp.float32)  8.14 us
  transfers between devices with their start and end apart: 6, of which 4 were waited for; matrix products, arithmetic and copies ran while one was open for 7% of the time, Pallas kernels for 13%

profile of v10, /device:TPU:0, one launch (start us, length us, event | category | flops | bytes accessed | tf_op | source)
XLA Modules:
  0.0 197.0 jit_solution(12461783963052060092)
XLA Ops:
  7.2 2.8 %fusion.7 = bf16[2048,256]{1,0:T(8,128)(2,1)S(1)} fusion(s32[1024]{0:T(1024)} %param.15, bf16[1024,2048]{1,0:T(8,128)(2,1)} %param.9, s32[]{:T(128)S(6)} %select_n.7), kind=kOutput, calls=%fused_computation.12 | convolution fusion | flops 1076363264 | bytes 1576964 | tf_op jit(solution)/shard_map/dot_general | solution.py:156
  10.0 24.6 %all_to_all.12 = bf16[16,128,256]{2,1,0:T(8,128)(2,1)S(1)} all-to-all(bf16[16,128,256]{2,1,0:T(8,128)(2,1)S(1)} %bitcast.10), channel_id=1, replica_groups=mesh['seq'=16,'head'=8] {'seq'}, dimensions={0} | all-to-all | bytes 2097152 | tf_op jit(solution)/shard_map/all_to_all | solution.py:159
  34.6 2.3 %fusion.8 = bf16[1024,256]{1,0:T(8,128)(2,1)} fusion(bf16[2048,256]{1,0:T(8,128)(2,1)S(1)} %bitcast.11, s32[1024]{0:T(1024)S(1)} %copy-done.12), kind=kOutput, calls=%fused_computation.15 | convolution fusion | flops 1076101120 | bytes 1576960 | tf_op jit(solution)/shard_map/dot_general | solution.py:163
  37.0 0.0 reduce-scatter.2.cloned.1.call-start
  37.0 1.0 copy.11.st_ref
  38.1 0.8 fusion.31
  38.9 1.7 fusion.29
  40.6 30.4 %all-gather.2.cloned.1.call-done = bf16[1024,2048]{1,0:T(8,128)(2,1)} async-done(((bf16[1024,256]{1,0:T(8,128)(2,1)}), bf16[1024,2048]{1,0:T(8,128)(2,1)}) %all-gather.2.cloned.1.call-update) | async-done | bytes 4194320 | tf_op jit(solution)/shard_map/all_gather | solution.py:166
  71.0 3.2 %fusion = f32[1024]{0:T(1024)S(1)} fusion(bf16[1024,2048]{1,0:T(8,128)(2,1)} %all-gather.2.cloned.1.call-done), kind=kLoop, calls=%fused_computation.2 | loop fusion | flops 6290432 | bytes 4198400 | tf_op jit(solution)/shard_map/reduce_sum | solution.py:168
  74.2 0.2 copy-done.1
  74.5 1.3 convolution_convert_fusion.1.ko_ref.vo_ref
  75.8 3.5 %collective-permute-start = (bf16[1024,256]{1,0:T(8,128)(2,1)S(1)}, bf16[1024,256]{1,0:T(8,128)(2,1)S(1)}, u32[]{:S(2)}, u32[]{:S(2)}) collective-permute-start(bf16[1024,256]{1,0:T(8,128)(2,1)S(1)} %convolution_convert_fusion.1.ko_ref.vo_ref), channel_id=1, source_target_pairs={{0,8},{8,16},{16,24},{24,32},{32,40},{40,48},{48,56},{56,64},{64,7... | collective-permute-start | bytes 1572872 | tf_op jit(solution)/shard_map/ppermute | solution.py:20
  79.3 2.1 %convolution_convert_fusion.ko_ref.vo_ref = bf16[1024,256]{1,0:T(8,128)(2,1)} fusion(bf16[2048,128]{1,0:T(8,128)(2,1)S(1)} %get-tuple-element.30, bf16[2048,128]{1,0:T(8,128)(2,1)S(1)} %get-tuple-element.23, bf16[1024,2048]{1,0:T(8,128)(2,1)S(1)} %copy-done.1, f32[2048]{0:T(1024)S(1)} %copy-done.8, f32[1024]{0:T(1024)S(1)} %add_rsqrt_fusion), kind=kOutput, calls=%fused_computation.16 | convolution fusion | flops 1084489728 | bytes 5779456 | tf_op jit(solution)/shard_map/dot_general | solution.py:177
  81.4 9.4 %collective-permute-done.kp_ref.vp_ref = bf16[1024,256]{1,0:T(8,128)(2,1)S(1)} collective-permute-done((bf16[1024,256]{1,0:T(8,128)(2,1)S(1)}, bf16[1024,256]{1,0:T(8,128)(2,1)S(1)}, u32[]{:S(2)}, u32[]{:S(2)}) %collective-permute-start) | collective-permute-done | bytes 524320 | tf_op jit(solution)/shard_map/ppermute | solution.py:20
  90.8 5.2 %collective-permute-start.1 = (bf16[1024,256]{1,0:T(8,128)(2,1)}, bf16[1024,256]{1,0:T(8,128)(2,1)}, u32[]{:S(2)}, u32[]{:S(2)}) collective-permute-start(bf16[1024,256]{1,0:T(8,128)(2,1)} %convolution_convert_fusion.ko_ref.vo_ref), channel_id=1, source_target_pairs={{0,8},{8,16},{16,24},{24,32},{32,40},{40,48},{48,56},{56,64},{64,7... | collective-permute-start | bytes 1572872 | tf_op jit(solution)/shard_map/ppermute | solution.py:20
  96.0 1.3 convolution_convert_fusion.2
  97.3 0.9 fusion.32
  98.2 12.8 %shard_map.104 = (bf16[1024,128]{1,0:T(8,128)(2,1)}, bf16[1024,128]{1,0:T(8,128)(2,1)}, bf16[1024,256]{1,0:T(8,128)(2,1)}, f32[1024,256]{1,0:T(8,128)}) custom-call(bf16[1024,128]{1,0:T(8,128)(2,1)} %get-tuple-element.28.q_ref, bf16[1024,256]{1,0:T(8,128)(2,1)} %copy-done.11, bf16[1024,256]{1,0:T(8,128)(2,1)} %copy-done.11, bf16[1024,256]{1,0:T(8,128)(2,1)} %copy-done.10, ...), custom_call_target="tpu_custom_call" | custom-call | flops 1811939328 | bytes 3670016 | tf_op jit(solution)/shard_map/pallas_call | solution.py:122
  111.0 1.6 collective-permute-start.2
  112.6 12.9 %shard_map.105 = (bf16[1024,128]{1,0:T(8,128)(2,1)}, bf16[1024,128]{1,0:T(8,128)(2,1)}, bf16[1024,256]{1,0:T(8,128)(2,1)}, f32[1024,256]{1,0:T(8,128)}) custom-call(bf16[1024,128]{1,0:T(8,128)(2,1)} %get-tuple-element.29.q_ref, bf16[1024,256]{1,0:T(8,128)(2,1)} %collective-permute-done.1.kp_ref.vp_ref, ...), custom_call_target="tpu_custom_call" | custom-call | flops 1811939328 | bytes 3670016 | tf_op jit(solution)/shard_map/pallas_call | solution.py:122
  125.6 1.3 collective-permute-start.3
  126.9 2.3 %fusion.14 = f32[1024,2048]{1,0:T(8,128)S(1)} fusion(bf16[2048,256]{1,0:T(8,128)(2,1)S(1)} %copy-done, bf16[1024,128]{1,0:T(8,128)(2,1)} %get-tuple-element.15, bf16[1024,128]{1,0:T(8,128)(2,1)S(1)} %copy-done.5), kind=kOutput, calls=%fused_computation.30 | convolution fusion | flops 1074790400 | bytes 9961472 | tf_op jit(solution)/shard_map/rc,dc->rd/dot_general | solution.py:195
  129.3 2.4 %fusion.13 = f32[1024,2048]{1,0:T(8,128)S(1)} fusion(bf16[2048,128]{1,0:T(8,128)(2,1)S(1)} %get-tuple-element.31, bf16[2048,128]{1,0:T(8,128)(2,1)S(1)} %get-tuple-element.22, f32[1024,256]{1,0:T(8,128)S(1)} %copy-done.2, bf16[1024,256]{1,0:T(8,128)(2,1)} %collective-permute-done.2), kind=kOutput, calls=%fused_computation.28 | convolution fusion | flops 1076625408 | bytes 11010048 | tf_op jit(solution)/shard_map/rc,dc->rd/dot_general | solution.py:195
  131.7 9.6 %collective-permute-done.3 = bf16[1024,256]{1,0:T(8,128)(2,1)S(1)} collective-permute-done((bf16[1024,256]{1,0:T(8,128)(2,1)}, bf16[1024,256]{1,0:T(8,128)(2,1)S(1)}, u32[]{:S(2)}, u32[]{:S(2)}) %collective-permute-start.3) | collective-permute-done | bytes 524320 | tf_op jit(solution)/shard_map/ppermute | solution.py:20
  141.3 3.4 %add_convert_fusion = bf16[1024,2048]{1,0:T(8,128)(2,1)} fusion(f32[1024,2048]{1,0:T(8,128)S(1)} %fusion.14, f32[1024,2048]{1,0:T(8,128)S(1)} %fusion.13, bf16[2048,128]{1,0:T(8,128)(2,1)S(1)} %get-tuple-element.30, bf16[2048,128]{1,0:T(8,128)(2,1)S(1)} %get-tuple-element.23, f32[1024,256]{1,0:T(8,128)S(1)} %copy-done.3, ...), kind=kOutput, calls=%fused_computation.5 | convolution fusion | flops 1082916864 | bytes 23592960 | tf_op jit(solution)/shard_map/rc,dc->rd/dot_general | solution.py:195
  144.7 0.1 fusion.19
  144.8 0.8 copy-done.6
  145.6 0.1 copy-done.7
  145.7 0.8 pad_maximum_fusion.6
  146.5 39.7 %reduce-scatter.2.cloned.1.call-done = bf16[128,2048]{1,0:T(8,128)(2,1)} async-done(((bf16[1024,2048]{1,0:T(8,128)(2,1)}), bf16[128,2048]{1,0:T(8,128)(2,1)}) %reduce-scatter.2.cloned.1.call-update) | async-done | bytes 524304 | tf_op jit(solution)/shard_map/reduce_scatter | solution.py:200
  186.2 1.5 fusion.12
  187.7 2.4 %fusion.11 = bf16[128,2048]{1,0:T(8,128)(2,1)} fusion(bf16[128,2048]{1,0:T(8,128)(2,1)} %reduce-scatter.2.cloned.1.call-done, f32[128]{0:T(128)S(1)} %broadcast_multiply_fusion, f32[128]{0:T(128)S(1)} %get-tuple-element.20, f32[2048]{0:T(1024)S(1)} %copy-done.8, f32[128]{0:T(128)S(1)} %get-tuple-element.21, ...), kind=kLoop, calls=%fused_computation.21 | loop fusion | flops 2097152 | bytes 1582596 | tf_op jit(solution)/shard_map/convert_element_type | solution.py:211
  (31 shorter events, 0.1 us)
Async XLA Ops:
  7.2 88.8 %copy-start = (bf16[2048,256]{1,0:T(8,128)(2,1)S(1)}, bf16[2048,256]{1,0:T(8,128)(2,1)}, u32[]{:S(2)}) copy-start(bf16[2048,256]{1,0:T(8,128)(2,1)} %param.11) | copy-start | bytes 3145732
  7.2 63.8 %all-gather.2.cloned.1.call-start = ((), (), s32[]{:S(2)}) async-start(), calls=%async_computation.2 | async-start | bytes 4718592 | tf_op jit(solution)/shard_map/all_gather | solution.py:166
  7.2 27.4 %copy-start.12 = (s32[1024]{0:T(1024)S(1)}, s32[1024]{0:T(1024)}, u32[]{:S(2)}) copy-start(s32[1024]{0:T(1024)} %param.16) | copy-start | bytes 12292
  34.6 2.4 %copy-start.9 = (s32[1024]{0:T(1024)S(1)}, s32[1024]{0:T(1024)}, u32[]{:S(2)}) copy-start(s32[1024]{0:T(1024)} %param.17) | copy-start | bytes 12292
  34.6 3.4 %copy-start.4 = (bf16[1024,256]{1,0:T(8,128)(2,1)S(1)}, bf16[1024,256]{1,0:T(8,128)(2,1)}, u32[]{:S(2)}) copy-start(bf16[1024,256]{1,0:T(8,128)(2,1)} %param.14) | copy-start | bytes 1572868
  37.0 149.3 %reduce-scatter.2.cloned.1.call-start = ((), (), s32[]{:S(2)}) async-start(), calls=%async_computation.3 | async-start | bytes 4718592 | tf_op jit(solution)/shard_map/reduce_scatter | solution.py:200
  38.9 35.3 %copy-start.8 = (f32[2048]{0:T(1024)S(1)}, f32[2048]{0:T(1024)}, u32[]{:S(2)}) copy-start(f32[2048]{0:T(1024)} %param.10) | copy-start | bytes 24580
  71.0 3.4 %copy-start.1 = (bf16[1024,2048]{1,0:T(8,128)(2,1)S(1)}, bf16[1024,2048]{1,0:T(8,128)(2,1)}, u32[]{:S(2)}) copy-start(bf16[1024,2048]{1,0:T(8,128)(2,1)} %all-gather.2.cloned.1.call-done) | copy-start | bytes 12582916
  75.8 5.6 %copy-start.10 = (bf16[1024,256]{1,0:T(8,128)(2,1)}, bf16[1024,256]{1,0:T(8,128)(2,1)S(1)}, u32[]{:S(2)}) copy-start(bf16[1024,256]{1,0:T(8,128)(2,1)S(1)} %convolution_convert_fusion.1.ko_ref.vo_ref) | copy-start | bytes 1572868
  75.8 15.0 %collective-permute-start = (bf16[1024,256]{1,0:T(8,128)(2,1)S(1)}, bf16[1024,256]{1,0:T(8,128)(2,1)S(1)}, u32[]{:S(2)}, u32[]{:S(2)}) collective-permute-start(bf16[1024,256]{1,0:T(8,128)(2,1)S(1)} %convolution_convert_fusion.1.ko_ref.vo_ref), channel_id=1, source_target_pairs={{0,8},{8,16},{16,24},{24,32},{32,40},{40,48},{48,56},{56,64},{64,7... | collective-permute-start | bytes 1572872 | tf_op jit(solution)/shard_map/ppermute | solution.py:20
  90.8 6.5 %copy-start.11 = (bf16[1024,256]{1,0:T(8,128)(2,1)}, bf16[1024,256]{1,0:T(8,128)(2,1)S(1)}, u32[]{:S(2)}) copy-start(bf16[1024,256]{1,0:T(8,128)(2,1)S(1)} %collective-permute-done.kp_ref.vp_ref) | copy-start | bytes 1572868
  90.8 21.8 %collective-permute-start.1 = (bf16[1024,256]{1,0:T(8,128)(2,1)}, bf16[1024,256]{1,0:T(8,128)(2,1)}, u32[]{:S(2)}, u32[]{:S(2)}) collective-permute-start(bf16[1024,256]{1,0:T(8,128)(2,1)} %convolution_convert_fusion.ko_ref.vo_ref), channel_id=1, source_target_pairs={{0,8},{8,16},{16,24},{24,32},{32,40},{40,48},{48,56},{56,64},{64,7... | collective-permute-start | bytes 1572872 | tf_op jit(solution)/shard_map/ppermute | solution.py:20
  111.0 15.9 %copy-start.5 = (bf16[1024,128]{1,0:T(8,128)(2,1)S(1)}, bf16[1024,128]{1,0:T(8,128)(2,1)}, u32[]{:S(2)}) copy-start(bf16[1024,128]{1,0:T(8,128)(2,1)} %get-tuple-element.14) | copy-start | bytes 786436
  111.0 18.2 %collective-permute-start.2 = (bf16[1024,256]{1,0:T(8,128)(2,1)}, bf16[1024,256]{1,0:T(8,128)(2,1)}, u32[]{:S(2)}, u32[]{:S(2)}) collective-permute-start(bf16[1024,256]{1,0:T(8,128)(2,1)} %get-tuple-element.17), channel_id=1, source_target_pairs={{8,0},{16,8},{24,16},{32,24},{40,32},{48,40},{56,48},{64,56},{72,6... | collective-permute-start | bytes 1572872 | tf_op jit(solution)/shard_map/ppermute | solution.py:20
  125.6 15.7 %collective-permute-start.3 = (bf16[1024,256]{1,0:T(8,128)(2,1)}, bf16[1024,256]{1,0:T(8,128)(2,1)S(1)}, u32[]{:S(2)}, u32[]{:S(2)}) collective-permute-start(bf16[1024,256]{1,0:T(8,128)(2,1)} %get-tuple-element.19), channel_id=1, source_target_pairs={{8,0},{16,8},{24,16},{32,24},{40,32},{48,40},{56,48},{64,56},{72,6... | collective-permute-start | bytes 1572872 | tf_op jit(solution)/shard_map/ppermute | solution.py:20
  126.9 2.4 %copy-start.2 = (f32[1024,256]{1,0:T(8,128)S(1)}, f32[1024,256]{1,0:T(8,128)}, u32[]{:S(2)}) copy-start(f32[1024,256]{1,0:T(8,128)} %get-tuple-element.16) | copy-start | bytes 3145732
  129.3 12.0 %copy-start.3 = (f32[1024,256]{1,0:T(8,128)S(1)}, f32[1024,256]{1,0:T(8,128)}, u32[]{:S(2)}) copy-start(f32[1024,256]{1,0:T(8,128)} %get-tuple-element.18) | copy-start | bytes 3145732
  144.7 0.9 copy-start.6
  144.7 1.0 copy-start.7
Sparse Core Ops, SparseCore 0:
  37.1 33.8 all-gather.1
  144.8 41.3 reduce-scatter.1

commit v11 on v8

--- a/solution.py
+++ b/solution.py
@@ -77,9 +77,9 @@
     rows_t = (((1,), (1,)), ((), ()))
     cols_t = (((0,), (0,)), ((), ()))
     s = lax.dot_general(q, k, rows_t, preferred_element_type=jnp.float32) * scale
-    key_idx = a + lax.broadcasted_iota(jnp.int32, (tq, window), 1)
-    row_idx = a + shift + lax.broadcasted_iota(jnp.int32, (tq, window), 0)
-    allowed = (key_idx >= st_ref[...]) & (key_idx <= row_idx)
+    key_off = lax.broadcasted_iota(jnp.int32, (tq, window), 1)
+    row_off = lax.broadcasted_iota(jnp.int32, (tq, window), 0)
+    allowed = (key_off >= st_ref[...] - a) & (key_off - row_off <= shift)
     s = jnp.where(allowed, s, neg_large)
     row_top = jnp.max(s, axis=1, keepdims=True)
     log_total = row_top + jnp.log(jnp.sum(jnp.exp(s - row_top), axis=1, keepdims=True))

time: 193 us -> 193 us (level)
  no operation moved by 1% of the time
where the time goes in v11:
time: 193 us
  waiting for transfers between devices  89.2 us (46%)
  blocking collectives  24.6 us (13%)
  Pallas kernels  21.7 us (11%)
  matrix products  17.9 us (9%)
  between operations  14.2 us (7%)
  starting transfers between devices  11.6 us (6%)
  other arithmetic  8.05 us (4%)
  local copies, waits for them, and re-layouts  5.57 us (3%)
    reduce_scatter x1, waiting for transfers between devices, body(): lax.psum_scatter(term.astype(jnp.bfloat16), 'head', scatter_dimension=0,...  39.8 us
    all_gather x1, waiting for transfers between devices, body(): packed = lax.all_gather(packed_part, 'head', axis=1, tiled=True)  30.4 us
    all_to_all x1, blocking collectives, body(): lax.all_to_all(outgoing, 'seq', split_axis=0, concat_axis=0, tiled=True)  24.6 us
    pallas_call x2, Pallas kernels, attention(): pl.pallas_call(kernel, grid=(steps,), in_specs=[q_spec, k_spec, v_spec, k...  21.7 us
    ppermute x4, waiting for transfers between devices, passed_along(): return lax.ppermute(array, axis, pairs)  19 us
    ppermute x4, starting transfers between devices, passed_along(): return lax.ppermute(array, axis, pairs)  11.6 us
    dot_general x3, matrix products, project(): jnp.einsum('rc,dc->rd', grads, weight, preferred_element_type=jnp.float32)  8.15 us
  transfers between devices with their start and end apart: 6, of which 4 were waited for; matrix products, arithmetic and copies ran while one was open for 7% of the time, Pallas kernels for 11%

profile of v11, /device:TPU:0, one launch (start us, length us, event | category | flops | bytes accessed | tf_op | source)
XLA Modules:
  0.0 193.0 jit_solution(12028400691378467349)
XLA Ops:
  7.2 2.8 %fusion.7 = bf16[2048,256]{1,0:T(8,128)(2,1)S(1)} fusion(s32[1024]{0:T(1024)} %param.15, bf16[1024,2048]{1,0:T(8,128)(2,1)} %param.9, s32[]{:T(128)S(6)} %select_n.7), kind=kOutput, calls=%fused_computation.12 | convolution fusion | flops 1076363264 | bytes 1576964 | tf_op jit(solution)/shard_map/dot_general | solution.py:156
  10.0 24.6 %all_to_all.12 = bf16[16,128,256]{2,1,0:T(8,128)(2,1)S(1)} all-to-all(bf16[16,128,256]{2,1,0:T(8,128)(2,1)S(1)} %bitcast.10), channel_id=1, replica_groups=mesh['seq'=16,'head'=8] {'seq'}, dimensions={0} | all-to-all | bytes 2097152 | tf_op jit(solution)/shard_map/all_to_all | solution.py:159
  34.6 2.3 %fusion.8 = bf16[1024,256]{1,0:T(8,128)(2,1)} fusion(bf16[2048,256]{1,0:T(8,128)(2,1)S(1)} %bitcast.11, s32[1024]{0:T(1024)S(1)} %copy-done.12), kind=kOutput, calls=%fused_computation.15 | convolution fusion | flops 1076101120 | bytes 1576960 | tf_op jit(solution)/shard_map/dot_general | solution.py:163
  37.0 0.0 reduce-scatter.2.cloned.1.call-start
  37.0 1.0 copy.11.st_ref
  38.1 0.8 fusion.31
  38.9 1.7 fusion.29
  40.6 30.4 %all-gather.2.cloned.1.call-done = bf16[1024,2048]{1,0:T(8,128)(2,1)} async-done(((bf16[1024,256]{1,0:T(8,128)(2,1)}), bf16[1024,2048]{1,0:T(8,128)(2,1)}) %all-gather.2.cloned.1.call-update) | async-done | bytes 4194320 | tf_op jit(solution)/shard_map/all_gather | solution.py:166
  71.0 3.2 %fusion = f32[1024]{0:T(1024)S(1)} fusion(bf16[1024,2048]{1,0:T(8,128)(2,1)} %all-gather.2.cloned.1.call-done), kind=kLoop, calls=%fused_computation.2 | loop fusion | flops 6290432 | bytes 4198400 | tf_op jit(solution)/shard_map/reduce_sum | solution.py:168
  74.2 0.2 copy-done.1
  74.5 1.3 convolution_convert_fusion.1.ko_ref.vo_ref
  75.8 3.5 %collective-permute-start = (bf16[1024,256]{1,0:T(8,128)(2,1)S(1)}, bf16[1024,256]{1,0:T(8,128)(2,1)S(1)}, u32[]{:S(2)}, u32[]{:S(2)}) collective-permute-start(bf16[1024,256]{1,0:T(8,128)(2,1)S(1)} %convolution_convert_fusion.1.ko_ref.vo_ref), channel_id=1, source_target_pairs={{0,8},{8,16},{16,24},{24,32},{32,40},{40,48},{48,56},{56,64},{64,7... | collective-permute-start | bytes 1572872 | tf_op jit(solution)/shard_map/ppermute | solution.py:20
  79.3 2.1 %convolution_convert_fusion.ko_ref.vo_ref = bf16[1024,256]{1,0:T(8,128)(2,1)} fusion(bf16[2048,128]{1,0:T(8,128)(2,1)S(1)} %get-tuple-element.30, bf16[2048,128]{1,0:T(8,128)(2,1)S(1)} %get-tuple-element.23, bf16[1024,2048]{1,0:T(8,128)(2,1)S(1)} %copy-done.1, f32[2048]{0:T(1024)S(1)} %copy-done.8, f32[1024]{0:T(1024)S(1)} %add_rsqrt_fusion), kind=kOutput, calls=%fused_computation.16 | convolution fusion | flops 1084489728 | bytes 5779456 | tf_op jit(solution)/shard_map/dot_general | solution.py:177
  81.4 9.4 %collective-permute-done.kp_ref.vp_ref = bf16[1024,256]{1,0:T(8,128)(2,1)S(1)} collective-permute-done((bf16[1024,256]{1,0:T(8,128)(2,1)S(1)}, bf16[1024,256]{1,0:T(8,128)(2,1)S(1)}, u32[]{:S(2)}, u32[]{:S(2)}) %collective-permute-start) | collective-permute-done | bytes 524320 | tf_op jit(solution)/shard_map/ppermute | solution.py:20
  90.8 5.2 %collective-permute-start.1 = (bf16[1024,256]{1,0:T(8,128)(2,1)}, bf16[1024,256]{1,0:T(8,128)(2,1)}, u32[]{:S(2)}, u32[]{:S(2)}) collective-permute-start(bf16[1024,256]{1,0:T(8,128)(2,1)} %convolution_convert_fusion.ko_ref.vo_ref), channel_id=1, source_target_pairs={{0,8},{8,16},{16,24},{24,32},{32,40},{40,48},{48,56},{56,64},{64,7... | collective-permute-start | bytes 1572872 | tf_op jit(solution)/shard_map/ppermute | solution.py:20
  96.0 1.3 convolution_convert_fusion.2
  97.3 0.9 fusion.32
  98.2 10.8 %shard_map.104 = (bf16[1024,128]{1,0:T(8,128)(2,1)}, bf16[1024,128]{1,0:T(8,128)(2,1)}, bf16[1024,256]{1,0:T(8,128)(2,1)}, f32[1024,256]{1,0:T(8,128)}) custom-call(bf16[1024,128]{1,0:T(8,128)(2,1)} %get-tuple-element.28.q_ref, bf16[1024,256]{1,0:T(8,128)(2,1)} %copy-done.11, bf16[1024,256]{1,0:T(8,128)(2,1)} %copy-done.11, bf16[1024,256]{1,0:T(8,128)(2,1)} %copy-done.10, ...), custom_call_target="tpu_custom_call" | custom-call | flops 2013265920 | bytes 3670016 | tf_op jit(solution)/shard_map/pallas_call | solution.py:122
  109.0 1.6 collective-permute-start.2
  110.6 10.9 %shard_map.105 = (bf16[1024,128]{1,0:T(8,128)(2,1)}, bf16[1024,128]{1,0:T(8,128)(2,1)}, bf16[1024,256]{1,0:T(8,128)(2,1)}, f32[1024,256]{1,0:T(8,128)}) custom-call(bf16[1024,128]{1,0:T(8,128)(2,1)} %get-tuple-element.29.q_ref, bf16[1024,256]{1,0:T(8,128)(2,1)} %collective-permute-done.1.kp_ref.vp_ref, ...), custom_call_target="tpu_custom_call" | custom-call | flops 2013265920 | bytes 3670016 | tf_op jit(solution)/shard_map/pallas_call | solution.py:122
  121.5 1.3 collective-permute-start.3
  122.9 2.3 %fusion.14 = f32[1024,2048]{1,0:T(8,128)S(1)} fusion(bf16[2048,256]{1,0:T(8,128)(2,1)S(1)} %copy-done, bf16[1024,128]{1,0:T(8,128)(2,1)} %get-tuple-element.15, bf16[1024,128]{1,0:T(8,128)(2,1)S(1)} %copy-done.5), kind=kOutput, calls=%fused_computation.30 | convolution fusion | flops 1074790400 | bytes 9961472 | tf_op jit(solution)/shard_map/rc,dc->rd/dot_general | solution.py:195
  125.2 2.4 %fusion.13 = f32[1024,2048]{1,0:T(8,128)S(1)} fusion(bf16[2048,128]{1,0:T(8,128)(2,1)S(1)} %get-tuple-element.31, bf16[2048,128]{1,0:T(8,128)(2,1)S(1)} %get-tuple-element.22, f32[1024,256]{1,0:T(8,128)S(1)} %copy-done.2, bf16[1024,256]{1,0:T(8,128)(2,1)} %collective-permute-done.2), kind=kOutput, calls=%fused_computation.28 | convolution fusion | flops 1076625408 | bytes 11010048 | tf_op jit(solution)/shard_map/rc,dc->rd/dot_general | solution.py:195
  127.7 9.6 %collective-permute-done.3 = bf16[1024,256]{1,0:T(8,128)(2,1)S(1)} collective-permute-done((bf16[1024,256]{1,0:T(8,128)(2,1)}, bf16[1024,256]{1,0:T(8,128)(2,1)S(1)}, u32[]{:S(2)}, u32[]{:S(2)}) %collective-permute-start.3) | collective-permute-done | bytes 524320 | tf_op jit(solution)/shard_map/ppermute | solution.py:20
  137.2 3.4 %add_convert_fusion = bf16[1024,2048]{1,0:T(8,128)(2,1)} fusion(f32[1024,2048]{1,0:T(8,128)S(1)} %fusion.14, f32[1024,2048]{1,0:T(8,128)S(1)} %fusion.13, bf16[2048,128]{1,0:T(8,128)(2,1)S(1)} %get-tuple-element.30, bf16[2048,128]{1,0:T(8,128)(2,1)S(1)} %get-tuple-element.23, f32[1024,256]{1,0:T(8,128)S(1)} %copy-done.3, ...), kind=kOutput, calls=%fused_computation.5 | convolution fusion | flops 1082916864 | bytes 23592960 | tf_op jit(solution)/shard_map/rc,dc->rd/dot_general | solution.py:195
  140.7 0.1 fusion.19
  140.7 0.8 copy-done.6
  141.6 0.1 copy-done.7
  141.6 0.8 pad_maximum_fusion.6
  142.5 39.8 %reduce-scatter.2.cloned.1.call-done = bf16[128,2048]{1,0:T(8,128)(2,1)} async-done(((bf16[1024,2048]{1,0:T(8,128)(2,1)}), bf16[128,2048]{1,0:T(8,128)(2,1)}) %reduce-scatter.2.cloned.1.call-update) | async-done | bytes 524304 | tf_op jit(solution)/shard_map/reduce_scatter | solution.py:200
  182.3 1.5 fusion.12
  183.7 2.4 %fusion.11 = bf16[128,2048]{1,0:T(8,128)(2,1)} fusion(bf16[128,2048]{1,0:T(8,128)(2,1)} %reduce-scatter.2.cloned.1.call-done, f32[128]{0:T(128)S(1)} %broadcast_multiply_fusion, f32[128]{0:T(128)S(1)} %get-tuple-element.20, f32[2048]{0:T(1024)S(1)} %copy-done.8, f32[128]{0:T(128)S(1)} %get-tuple-element.21, ...), kind=kLoop, calls=%fused_computation.21 | loop fusion | flops 2097152 | bytes 1582596 | tf_op jit(solution)/shard_map/convert_element_type | solution.py:211
  (31 shorter events, 0.1 us)
Async XLA Ops:
  7.2 88.8 %copy-start = (bf16[2048,256]{1,0:T(8,128)(2,1)S(1)}, bf16[2048,256]{1,0:T(8,128)(2,1)}, u32[]{:S(2)}) copy-start(bf16[2048,256]{1,0:T(8,128)(2,1)} %param.11) | copy-start | bytes 3145732
  7.2 63.8 %all-gather.2.cloned.1.call-start = ((), (), s32[]{:S(2)}) async-start(), calls=%async_computation.2 | async-start | bytes 4718592 | tf_op jit(solution)/shard_map/all_gather | solution.py:166
  7.2 27.4 %copy-start.12 = (s32[1024]{0:T(1024)S(1)}, s32[1024]{0:T(1024)}, u32[]{:S(2)}) copy-start(s32[1024]{0:T(1024)} %param.16) | copy-start | bytes 12292
  34.6 2.4 %copy-start.9 = (s32[1024]{0:T(1024)S(1)}, s32[1024]{0:T(1024)}, u32[]{:S(2)}) copy-start(s32[1024]{0:T(1024)} %param.17) | copy-start | bytes 12292
  34.6 3.4 %copy-start.4 = (bf16[1024,256]{1,0:T(8,128)(2,1)S(1)}, bf16[1024,256]{1,0:T(8,128)(2,1)}, u32[]{:S(2)}) copy-start(bf16[1024,256]{1,0:T(8,128)(2,1)} %param.14) | copy-start | bytes 1572868
  37.0 145.3 %reduce-scatter.2.cloned.1.call-start = ((), (), s32[]{:S(2)}) async-start(), calls=%async_computation.3 | async-start | bytes 4718592 | tf_op jit(solution)/shard_map/reduce_scatter | solution.py:200
  38.9 35.3 %copy-start.8 = (f32[2048]{0:T(1024)S(1)}, f32[2048]{0:T(1024)}, u32[]{:S(2)}) copy-start(f32[2048]{0:T(1024)} %param.10) | copy-start | bytes 24580
  71.0 3.4 %copy-start.1 = (bf16[1024,2048]{1,0:T(8,128)(2,1)S(1)}, bf16[1024,2048]{1,0:T(8,128)(2,1)}, u32[]{:S(2)}) copy-start(bf16[1024,2048]{1,0:T(8,128)(2,1)} %all-gather.2.cloned.1.call-done) | copy-start | bytes 12582916
  75.8 5.6 %copy-start.10 = (bf16[1024,256]{1,0:T(8,128)(2,1)}, bf16[1024,256]{1,0:T(8,128)(2,1)S(1)}, u32[]{:S(2)}) copy-start(bf16[1024,256]{1,0:T(8,128)(2,1)S(1)} %convolution_convert_fusion.1.ko_ref.vo_ref) | copy-start | bytes 1572868
  75.8 15.0 %collective-permute-start = (bf16[1024,256]{1,0:T(8,128)(2,1)S(1)}, bf16[1024,256]{1,0:T(8,128)(2,1)S(1)}, u32[]{:S(2)}, u32[]{:S(2)}) collective-permute-start(bf16[1024,256]{1,0:T(8,128)(2,1)S(1)} %convolution_convert_fusion.1.ko_ref.vo_ref), channel_id=1, source_target_pairs={{0,8},{8,16},{16,24},{24,32},{32,40},{40,48},{48,56},{56,64},{64,7... | collective-permute-start | bytes 1572872 | tf_op jit(solution)/shard_map/ppermute | solution.py:20
  90.8 6.5 %copy-start.11 = (bf16[1024,256]{1,0:T(8,128)(2,1)}, bf16[1024,256]{1,0:T(8,128)(2,1)S(1)}, u32[]{:S(2)}) copy-start(bf16[1024,256]{1,0:T(8,128)(2,1)S(1)} %collective-permute-done.kp_ref.vp_ref) | copy-start | bytes 1572868
  90.8 19.8 %collective-permute-start.1 = (bf16[1024,256]{1,0:T(8,128)(2,1)}, bf16[1024,256]{1,0:T(8,128)(2,1)}, u32[]{:S(2)}, u32[]{:S(2)}) collective-permute-start(bf16[1024,256]{1,0:T(8,128)(2,1)} %convolution_convert_fusion.ko_ref.vo_ref), channel_id=1, source_target_pairs={{0,8},{8,16},{16,24},{24,32},{32,40},{40,48},{48,56},{56,64},{64,7... | collective-permute-start | bytes 1572872 | tf_op jit(solution)/shard_map/ppermute | solution.py:20
  109.0 13.9 %copy-start.5 = (bf16[1024,128]{1,0:T(8,128)(2,1)S(1)}, bf16[1024,128]{1,0:T(8,128)(2,1)}, u32[]{:S(2)}) copy-start(bf16[1024,128]{1,0:T(8,128)(2,1)} %get-tuple-element.14) | copy-start | bytes 786436
  109.0 16.2 %collective-permute-start.2 = (bf16[1024,256]{1,0:T(8,128)(2,1)}, bf16[1024,256]{1,0:T(8,128)(2,1)}, u32[]{:S(2)}, u32[]{:S(2)}) collective-permute-start(bf16[1024,256]{1,0:T(8,128)(2,1)} %get-tuple-element.17), channel_id=1, source_target_pairs={{8,0},{16,8},{24,16},{32,24},{40,32},{48,40},{56,48},{64,56},{72,6... | collective-permute-start | bytes 1572872 | tf_op jit(solution)/shard_map/ppermute | solution.py:20
  121.5 15.7 %collective-permute-start.3 = (bf16[1024,256]{1,0:T(8,128)(2,1)}, bf16[1024,256]{1,0:T(8,128)(2,1)S(1)}, u32[]{:S(2)}, u32[]{:S(2)}) collective-permute-start(bf16[1024,256]{1,0:T(8,128)(2,1)} %get-tuple-element.19), channel_id=1, source_target_pairs={{8,0},{16,8},{24,16},{32,24},{40,32},{48,40},{56,48},{64,56},{72,6... | collective-permute-start | bytes 1572872 | tf_op jit(solution)/shard_map/ppermute | solution.py:20
  122.9 2.4 %copy-start.2 = (f32[1024,256]{1,0:T(8,128)S(1)}, f32[1024,256]{1,0:T(8,128)}, u32[]{:S(2)}) copy-start(f32[1024,256]{1,0:T(8,128)} %get-tuple-element.16) | copy-start | bytes 3145732
  125.2 12.0 %copy-start.3 = (f32[1024,256]{1,0:T(8,128)S(1)}, f32[1024,256]{1,0:T(8,128)}, u32[]{:S(2)}) copy-start(f32[1024,256]{1,0:T(8,128)} %get-tuple-element.18) | copy-start | bytes 3145732
  140.6 0.9 copy-start.6
  140.6 1.0 copy-start.7
Sparse Core Ops, SparseCore 0:
  37.1 33.8 all-gather.1
  140.8 41.4 reduce-scatter.1

commit v12 on v11

--- a/solution.py
+++ b/solution.py
@@ -55,7 +55,7 @@
 def attention_kernel(
     q_ref, kp_ref, vp_ref, ko_ref, vo_ref, do_ref, st_ref,
     ctx_ref, dq_ref, send_ref, keep_ref,
-    k_scr, v_scr, dk_scr, dv_scr, *, tq, window, shift, scale
+    k_scr, kt_scr, vt_scr, dk_scr, dv_scr, *, tq, window, shift, scale
 ):
     qi = pl.program_id(0)
     a = pl.multiple_of(qi * tq, tq)
@@ -65,18 +65,19 @@
     def _():
         k_scr[:half, :] = kp_ref[...]
         k_scr[half:, :] = ko_ref[...]
-        v_scr[:half, :] = vp_ref[...]
-        v_scr[half:, :] = vo_ref[...]
+        kt_scr[:, :half] = kp_ref[...].T
+        kt_scr[:, half:] = ko_ref[...].T
+        vt_scr[:, :half] = vp_ref[...].T
+        vt_scr[:, half:] = vo_ref[...].T
         dk_scr[...] = jnp.zeros_like(dk_scr)
         dv_scr[...] = jnp.zeros_like(dv_scr)
 
     q = q_ref[...]
     k = k_scr[pl.ds(a, window), :]
-    v = v_scr[pl.ds(a, window), :]
+    kt = kt_scr[:, pl.ds(a, window)]
+    vt = vt_scr[:, pl.ds(a, window)]
     do = do_ref[...]
-    rows_t = (((1,), (1,)), ((), ()))
-    cols_t = (((0,), (0,)), ((), ()))
-    s = lax.dot_general(q, k, rows_t, preferred_element_type=jnp.float32) * scale
+    s = jnp.dot(q, kt, preferred_element_type=jnp.float32) * scale
     key_off = lax.broadcasted_iota(jnp.int32, (tq, window), 1)
     row_off = lax.broadcasted_iota(jnp.int32, (tq, window), 0)
     allowed = (key_off >= st_ref[...] - a) & (key_off - row_off <= shift)
@@ -85,21 +86,23 @@
     log_total = row_top + jnp.log(jnp.sum(jnp.exp(s - row_top), axis=1, keepdims=True))
     p = jnp.exp(s - log_total)
     p_low = p.astype(jnp.bfloat16)
-    ctx_ref[...] = jnp.dot(p_low, v, preferred_element_type=jnp.float32).astype(ctx_ref.dtype)
-    dp = lax.dot_general(do, v, rows_t, preferred_element_type=jnp.float32)
+    ctx_ref[...] = lax.dot_general(
+        p_low, vt, (((1,), (1,)), ((), ())), preferred_element_type=jnp.float32
+    ).astype(ctx_ref.dtype)
+    dp = jnp.dot(do, vt, preferred_element_type=jnp.float32)
     weighted = jnp.sum(p * dp, axis=1, keepdims=True)
     ds = (p * (dp - weighted)).astype(jnp.bfloat16)
     dq_ref[...] = (jnp.dot(ds, k, preferred_element_type=jnp.float32) * scale).astype(dq_ref.dtype)
-    dk_scr[pl.ds(a, window), :] += lax.dot_general(ds, q, cols_t, preferred_element_type=jnp.float32)
-    dv_scr[pl.ds(a, window), :] += lax.dot_general(p_low, do, cols_t, preferred_element_type=jnp.float32)
+    dk_scr[:, pl.ds(a, window)] += jnp.dot(q.T, ds, preferred_element_type=jnp.float32)
+    dv_scr[:, pl.ds(a, window)] += jnp.dot(do.T, p_low, preferred_element_type=jnp.float32)
 
     @pl.when(qi == pl.num_programs(0) - 1)
     def _():
         hd = q_ref.shape[1]
-        send_ref[:, :hd] = (dk_scr[:half, :] * scale).astype(send_ref.dtype)
-        send_ref[:, hd:] = dv_scr[:half, :].astype(send_ref.dtype)
-        keep_ref[:, :hd] = dk_scr[half:, :] * scale
-        keep_ref[:, hd:] = dv_scr[half:, :]
+        send_ref[:, :hd] = (dk_scr[:, :half].T * scale).astype(send_ref.dtype)
+        send_ref[:, hd:] = dv_scr[:, :half].T.astype(send_ref.dtype)
+        keep_ref[:, :hd] = dk_scr[:, half:].T * scale
+        keep_ref[:, hd:] = dv_scr[:, half:].T
 
 
 def attention(queries, kv_prev, kv_own, grad_ctx, rel_start):
@@ -131,8 +134,9 @@
             jax.ShapeDtypeStruct((rows, 2 * hd), jnp.bfloat16),
             jax.ShapeDtypeStruct((rows, 2 * hd), jnp.float32),
         ],
-        scratch_shapes=[pltpu.VMEM((2 * rows, hd), jnp.bfloat16)] * 2
-        + [pltpu.VMEM((2 * rows, hd), jnp.float32)] * 2,
+        scratch_shapes=[pltpu.VMEM((2 * rows, hd), jnp.bfloat16)]
+        + [pltpu.VMEM((hd, 2 * rows), jnp.bfloat16)] * 2
+        + [pltpu.VMEM((hd, 2 * rows), jnp.float32)] * 2,
         compiler_params=pltpu.CompilerParams(dimension_semantics=("arbitrary",)),
         cost_estimate=cost,
     )(queries, kv_prev, kv_prev, kv_own, kv_own, grad_ctx, rel_start)

time: 193 us -> 192 us (level)
  no operation moved by 1% of the time
where the time goes in v12:
time: 192 us
  waiting for transfers between devices  89.2 us (46%)
  blocking collectives  24.6 us (13%)
  Pallas kernels  20.3 us (11%)
  matrix products  17.9 us (9%)
  between operations  14.2 us (7%)
  starting transfers between devices  11.6 us (6%)
  other arithmetic  8.05 us (4%)
  local copies, waits for them, and re-layouts  5.57 us (3%)
    reduce_scatter x1, waiting for transfers between devices, body(): lax.psum_scatter(term.astype(jnp.bfloat16), 'head', scatter_dimension=0,...  39.7 us
    all_gather x1, waiting for transfers between devices, body(): packed = lax.all_gather(packed_part, 'head', axis=1, tiled=True)  30.4 us
    all_to_all x1, blocking collectives, body(): lax.all_to_all(outgoing, 'seq', split_axis=0, concat_axis=0, tiled=True)  24.6 us
    pallas_call x2, Pallas kernels, attention(): pl.pallas_call(kernel, grid=(steps,), in_specs=[q_spec, k_spec, v_spec, k...  20.3 us
    ppermute x4, waiting for transfers between devices, passed_along(): return lax.ppermute(array, axis, pairs)  19 us
    ppermute x4, starting transfers between devices, passed_along(): return lax.ppermute(array, axis, pairs)  11.6 us
    dot_general x3, matrix products, project(): jnp.einsum('rc,dc->rd', grads, weight, preferred_element_type=jnp.float32)  8.15 us
  transfers between devices with their start and end apart: 6, of which 4 were waited for; matrix products, arithmetic and copies ran while one was open for 7% of the time, Pallas kernels for 11%

profile of v12, /device:TPU:0, one launch (start us, length us, event | category | flops | bytes accessed | tf_op | source)
XLA Modules:
  0.0 191.6 jit_solution(76483208881881041)
XLA Ops:
  7.2 2.8 %fusion.7 = bf16[2048,256]{1,0:T(8,128)(2,1)S(1)} fusion(s32[1024]{0:T(1024)} %param.15, bf16[1024,2048]{1,0:T(8,128)(2,1)} %param.9, s32[]{:T(128)S(6)} %select_n.7), kind=kOutput, calls=%fused_computation.12 | convolution fusion | flops 1076363264 | bytes 1576964 | tf_op jit(solution)/shard_map/dot_general | solution.py:160
  10.0 24.6 %all_to_all.12 = bf16[16,128,256]{2,1,0:T(8,128)(2,1)S(1)} all-to-all(bf16[16,128,256]{2,1,0:T(8,128)(2,1)S(1)} %bitcast.10), channel_id=1, replica_groups=mesh['seq'=16,'head'=8] {'seq'}, dimensions={0} | all-to-all | bytes 2097152 | tf_op jit(solution)/shard_map/all_to_all | solution.py:163
  34.6 2.3 %fusion.8 = bf16[1024,256]{1,0:T(8,128)(2,1)} fusion(bf16[2048,256]{1,0:T(8,128)(2,1)S(1)} %bitcast.11, s32[1024]{0:T(1024)S(1)} %copy-done.12), kind=kOutput, calls=%fused_computation.15 | convolution fusion | flops 1076101120 | bytes 1576960 | tf_op jit(solution)/shard_map/dot_general | solution.py:167
  37.0 0.0 reduce-scatter.2.cloned.1.call-start
  37.0 1.0 copy.11.st_ref
  38.1 0.8 fusion.31
  38.9 1.7 fusion.29
  40.6 30.4 %all-gather.2.cloned.1.call-done = bf16[1024,2048]{1,0:T(8,128)(2,1)} async-done(((bf16[1024,256]{1,0:T(8,128)(2,1)}), bf16[1024,2048]{1,0:T(8,128)(2,1)}) %all-gather.2.cloned.1.call-update) | async-done | bytes 4194320 | tf_op jit(solution)/shard_map/all_gather | solution.py:170
  71.0 3.2 %fusion = f32[1024]{0:T(1024)S(1)} fusion(bf16[1024,2048]{1,0:T(8,128)(2,1)} %all-gather.2.cloned.1.call-done), kind=kLoop, calls=%fused_computation.2 | loop fusion | flops 6290432 | bytes 4198400 | tf_op jit(solution)/shard_map/reduce_sum | solution.py:172
  74.2 0.2 copy-done.1
  74.5 1.3 convolution_convert_fusion.1.ko_ref.vo_ref
  75.8 3.5 %collective-permute-start = (bf16[1024,256]{1,0:T(8,128)(2,1)S(1)}, bf16[1024,256]{1,0:T(8,128)(2,1)S(1)}, u32[]{:S(2)}, u32[]{:S(2)}) collective-permute-start(bf16[1024,256]{1,0:T(8,128)(2,1)S(1)} %convolution_convert_fusion.1.ko_ref.vo_ref), channel_id=1, source_target_pairs={{0,8},{8,16},{16,24},{24,32},{32,40},{40,48},{48,56},{56,64},{64,7... | collective-permute-start | bytes 1572872 | tf_op jit(solution)/shard_map/ppermute | solution.py:20
  79.3 2.1 %convolution_convert_fusion.ko_ref.vo_ref = bf16[1024,256]{1,0:T(8,128)(2,1)} fusion(bf16[2048,128]{1,0:T(8,128)(2,1)S(1)} %get-tuple-element.30, bf16[2048,128]{1,0:T(8,128)(2,1)S(1)} %get-tuple-element.23, bf16[1024,2048]{1,0:T(8,128)(2,1)S(1)} %copy-done.1, f32[2048]{0:T(1024)S(1)} %copy-done.8, f32[1024]{0:T(1024)S(1)} %add_rsqrt_fusion), kind=kOutput, calls=%fused_computation.16 | convolution fusion | flops 1084489728 | bytes 5779456 | tf_op jit(solution)/shard_map/dot_general | solution.py:181
  81.4 9.4 %collective-permute-done.kp_ref.vp_ref = bf16[1024,256]{1,0:T(8,128)(2,1)S(1)} collective-permute-done((bf16[1024,256]{1,0:T(8,128)(2,1)S(1)}, bf16[1024,256]{1,0:T(8,128)(2,1)S(1)}, u32[]{:S(2)}, u32[]{:S(2)}) %collective-permute-start) | collective-permute-done | bytes 524320 | tf_op jit(solution)/shard_map/ppermute | solution.py:20
  90.8 5.2 %collective-permute-start.1 = (bf16[1024,256]{1,0:T(8,128)(2,1)}, bf16[1024,256]{1,0:T(8,128)(2,1)}, u32[]{:S(2)}, u32[]{:S(2)}) collective-permute-start(bf16[1024,256]{1,0:T(8,128)(2,1)} %convolution_convert_fusion.ko_ref.vo_ref), channel_id=1, source_target_pairs={{0,8},{8,16},{16,24},{24,32},{32,40},{40,48},{48,56},{56,64},{64,7... | collective-permute-start | bytes 1572872 | tf_op jit(solution)/shard_map/ppermute | solution.py:20
  96.0 1.3 convolution_convert_fusion.2
  97.3 0.9 fusion.32
  98.2 10.1 %shard_map.104 = (bf16[1024,128]{1,0:T(8,128)(2,1)}, bf16[1024,128]{1,0:T(8,128)(2,1)}, bf16[1024,256]{1,0:T(8,128)(2,1)}, f32[1024,256]{1,0:T(8,128)}) custom-call(bf16[1024,128]{1,0:T(8,128)(2,1)} %get-tuple-element.28.q_ref, bf16[1024,256]{1,0:T(8,128)(2,1)} %copy-done.11, bf16[1024,256]{1,0:T(8,128)(2,1)} %copy-done.11, bf16[1024,256]{1,0:T(8,128)(2,1)} %copy-done.10, ...), custom_call_target="tpu_custom_call" | custom-call | flops 2013265920 | bytes 3670016 | tf_op jit(solution)/shard_map/pallas_call | solution.py:125
  108.3 1.6 collective-permute-start.2
  109.9 10.2 %shard_map.105 = (bf16[1024,128]{1,0:T(8,128)(2,1)}, bf16[1024,128]{1,0:T(8,128)(2,1)}, bf16[1024,256]{1,0:T(8,128)(2,1)}, f32[1024,256]{1,0:T(8,128)}) custom-call(bf16[1024,128]{1,0:T(8,128)(2,1)} %get-tuple-element.29.q_ref, bf16[1024,256]{1,0:T(8,128)(2,1)} %collective-permute-done.1.kp_ref.vp_ref, ...), custom_call_target="tpu_custom_call" | custom-call | flops 2013265920 | bytes 3670016 | tf_op jit(solution)/shard_map/pallas_call | solution.py:125
  120.2 1.3 collective-permute-start.3
  121.5 2.3 %fusion.14 = f32[1024,2048]{1,0:T(8,128)S(1)} fusion(bf16[2048,256]{1,0:T(8,128)(2,1)S(1)} %copy-done, bf16[1024,128]{1,0:T(8,128)(2,1)} %get-tuple-element.15, bf16[1024,128]{1,0:T(8,128)(2,1)S(1)} %copy-done.5), kind=kOutput, calls=%fused_computation.30 | convolution fusion | flops 1074790400 | bytes 9961472 | tf_op jit(solution)/shard_map/rc,dc->rd/dot_general | solution.py:199
  123.8 2.4 %fusion.13 = f32[1024,2048]{1,0:T(8,128)S(1)} fusion(bf16[2048,128]{1,0:T(8,128)(2,1)S(1)} %get-tuple-element.31, bf16[2048,128]{1,0:T(8,128)(2,1)S(1)} %get-tuple-element.22, f32[1024,256]{1,0:T(8,128)S(1)} %copy-done.2, bf16[1024,256]{1,0:T(8,128)(2,1)} %collective-permute-done.2), kind=kOutput, calls=%fused_computation.28 | convolution fusion | flops 1076625408 | bytes 11010048 | tf_op jit(solution)/shard_map/rc,dc->rd/dot_general | solution.py:199
  126.3 9.6 %collective-permute-done.3 = bf16[1024,256]{1,0:T(8,128)(2,1)S(1)} collective-permute-done((bf16[1024,256]{1,0:T(8,128)(2,1)}, bf16[1024,256]{1,0:T(8,128)(2,1)S(1)}, u32[]{:S(2)}, u32[]{:S(2)}) %collective-permute-start.3) | collective-permute-done | bytes 524320 | tf_op jit(solution)/shard_map/ppermute | solution.py:20
  135.9 3.4 %add_convert_fusion = bf16[1024,2048]{1,0:T(8,128)(2,1)} fusion(f32[1024,2048]{1,0:T(8,128)S(1)} %fusion.14, f32[1024,2048]{1,0:T(8,128)S(1)} %fusion.13, bf16[2048,128]{1,0:T(8,128)(2,1)S(1)} %get-tuple-element.30, bf16[2048,128]{1,0:T(8,128)(2,1)S(1)} %get-tuple-element.23, f32[1024,256]{1,0:T(8,128)S(1)} %copy-done.3, ...), kind=kOutput, calls=%fused_computation.5 | convolution fusion | flops 1082916864 | bytes 23592960 | tf_op jit(solution)/shard_map/rc,dc->rd/dot_general | solution.py:199
  139.3 0.1 fusion.19
  139.4 0.8 copy-done.6
  140.2 0.1 copy-done.7
  140.3 0.8 pad_maximum_fusion.6
  141.1 39.7 %reduce-scatter.2.cloned.1.call-done = bf16[128,2048]{1,0:T(8,128)(2,1)} async-done(((bf16[1024,2048]{1,0:T(8,128)(2,1)}), bf16[128,2048]{1,0:T(8,128)(2,1)}) %reduce-scatter.2.cloned.1.call-update) | async-done | bytes 524304 | tf_op jit(solution)/shard_map/reduce_scatter | solution.py:204
  180.8 1.5 fusion.12
  182.3 2.4 %fusion.11 = bf16[128,2048]{1,0:T(8,128)(2,1)} fusion(bf16[128,2048]{1,0:T(8,128)(2,1)} %reduce-scatter.2.cloned.1.call-done, f32[128]{0:T(128)S(1)} %broadcast_multiply_fusion, f32[128]{0:T(128)S(1)} %get-tuple-element.20, f32[2048]{0:T(1024)S(1)} %copy-done.8, f32[128]{0:T(128)S(1)} %get-tuple-element.21, ...), kind=kLoop, calls=%fused_computation.21 | loop fusion | flops 2097152 | bytes 1582596 | tf_op jit(solution)/shard_map/convert_element_type | solution.py:215
  (31 shorter events, 0.1 us)
Async XLA Ops:
  7.2 88.8 %copy-start = (bf16[2048,256]{1,0:T(8,128)(2,1)S(1)}, bf16[2048,256]{1,0:T(8,128)(2,1)}, u32[]{:S(2)}) copy-start(bf16[2048,256]{1,0:T(8,128)(2,1)} %param.11) | copy-start | bytes 3145732
  7.2 63.8 %all-gather.2.cloned.1.call-start = ((), (), s32[]{:S(2)}) async-start(), calls=%async_computation.2 | async-start | bytes 4718592 | tf_op jit(solution)/shard_map/all_gather | solution.py:170
  7.2 27.4 %copy-start.12 = (s32[1024]{0:T(1024)S(1)}, s32[1024]{0:T(1024)}, u32[]{:S(2)}) copy-start(s32[1024]{0:T(1024)} %param.16) | copy-start | bytes 12292
  34.6 2.4 %copy-start.9 = (s32[1024]{0:T(1024)S(1)}, s32[1024]{0:T(1024)}, u32[]{:S(2)}) copy-start(s32[1024]{0:T(1024)} %param.17) | copy-start | bytes 12292
  34.6 3.4 %copy-start.4 = (bf16[1024,256]{1,0:T(8,128)(2,1)S(1)}, bf16[1024,256]{1,0:T(8,128)(2,1)}, u32[]{:S(2)}) copy-start(bf16[1024,256]{1,0:T(8,128)(2,1)} %param.14) | copy-start | bytes 1572868
  37.0 143.9 %reduce-scatter.2.cloned.1.call-start = ((), (), s32[]{:S(2)}) async-start(), calls=%async_computation.3 | async-start | bytes 4718592 | tf_op jit(solution)/shard_map/reduce_scatter | solution.py:204
  38.9 35.3 %copy-start.8 = (f32[2048]{0:T(1024)S(1)}, f32[2048]{0:T(1024)}, u32[]{:S(2)}) copy-start(f32[2048]{0:T(1024)} %param.10) | copy-start | bytes 24580
  71.0 3.4 %copy-start.1 = (bf16[1024,2048]{1,0:T(8,128)(2,1)S(1)}, bf16[1024,2048]{1,0:T(8,128)(2,1)}, u32[]{:S(2)}) copy-start(bf16[1024,2048]{1,0:T(8,128)(2,1)} %all-gather.2.cloned.1.call-done) | copy-start | bytes 12582916
  75.8 5.6 %copy-start.10 = (bf16[1024,256]{1,0:T(8,128)(2,1)}, bf16[1024,256]{1,0:T(8,128)(2,1)S(1)}, u32[]{:S(2)}) copy-start(bf16[1024,256]{1,0:T(8,128)(2,1)S(1)} %convolution_convert_fusion.1.ko_ref.vo_ref) | copy-start | bytes 1572868
  75.8 15.0 %collective-permute-start = (bf16[1024,256]{1,0:T(8,128)(2,1)S(1)}, bf16[1024,256]{1,0:T(8,128)(2,1)S(1)}, u32[]{:S(2)}, u32[]{:S(2)}) collective-permute-start(bf16[1024,256]{1,0:T(8,128)(2,1)S(1)} %convolution_convert_fusion.1.ko_ref.vo_ref), channel_id=1, source_target_pairs={{0,8},{8,16},{16,24},{24,32},{32,40},{40,48},{48,56},{56,64},{64,7... | collective-permute-start | bytes 1572872 | tf_op jit(solution)/shard_map/ppermute | solution.py:20
  90.8 6.5 %copy-start.11 = (bf16[1024,256]{1,0:T(8,128)(2,1)}, bf16[1024,256]{1,0:T(8,128)(2,1)S(1)}, u32[]{:S(2)}) copy-start(bf16[1024,256]{1,0:T(8,128)(2,1)S(1)} %collective-permute-done.kp_ref.vp_ref) | copy-start | bytes 1572868
  90.8 19.1 %collective-permute-start.1 = (bf16[1024,256]{1,0:T(8,128)(2,1)}, bf16[1024,256]{1,0:T(8,128)(2,1)}, u32[]{:S(2)}, u32[]{:S(2)}) collective-permute-start(bf16[1024,256]{1,0:T(8,128)(2,1)} %convolution_convert_fusion.ko_ref.vo_ref), channel_id=1, source_target_pairs={{0,8},{8,16},{16,24},{24,32},{32,40},{40,48},{48,56},{56,64},{64,7... | collective-permute-start | bytes 1572872 | tf_op jit(solution)/shard_map/ppermute | solution.py:20
  108.3 13.2 %copy-start.5 = (bf16[1024,128]{1,0:T(8,128)(2,1)S(1)}, bf16[1024,128]{1,0:T(8,128)(2,1)}, u32[]{:S(2)}) copy-start(bf16[1024,128]{1,0:T(8,128)(2,1)} %get-tuple-element.14) | copy-start | bytes 786436
  108.3 15.5 %collective-permute-start.2 = (bf16[1024,256]{1,0:T(8,128)(2,1)}, bf16[1024,256]{1,0:T(8,128)(2,1)}, u32[]{:S(2)}, u32[]{:S(2)}) collective-permute-start(bf16[1024,256]{1,0:T(8,128)(2,1)} %get-tuple-element.17), channel_id=1, source_target_pairs={{8,0},{16,8},{24,16},{32,24},{40,32},{48,40},{56,48},{64,56},{72,6... | collective-permute-start | bytes 1572872 | tf_op jit(solution)/shard_map/ppermute | solution.py:20
  120.2 15.7 %collective-permute-start.3 = (bf16[1024,256]{1,0:T(8,128)(2,1)}, bf16[1024,256]{1,0:T(8,128)(2,1)S(1)}, u32[]{:S(2)}, u32[]{:S(2)}) collective-permute-start(bf16[1024,256]{1,0:T(8,128)(2,1)} %get-tuple-element.19), channel_id=1, source_target_pairs={{8,0},{16,8},{24,16},{32,24},{40,32},{48,40},{56,48},{64,56},{72,6... | collective-permute-start | bytes 1572872 | tf_op jit(solution)/shard_map/ppermute | solution.py:20
  121.5 2.4 %copy-start.2 = (f32[1024,256]{1,0:T(8,128)S(1)}, f32[1024,256]{1,0:T(8,128)}, u32[]{:S(2)}) copy-start(f32[1024,256]{1,0:T(8,128)} %get-tuple-element.16) | copy-start | bytes 3145732
  123.8 12.0 %copy-start.3 = (f32[1024,256]{1,0:T(8,128)S(1)}, f32[1024,256]{1,0:T(8,128)}, u32[]{:S(2)}) copy-start(f32[1024,256]{1,0:T(8,128)} %get-tuple-element.18) | copy-start | bytes 3145732
  139.3 0.9 copy-start.6
  139.3 1.0 copy-start.7
Sparse Core Ops, SparseCore 0:
  37.1 33.8 all-gather.1
  139.4 41.3 reduce-scatter.1

commit v13 on v12

--- a/solution.py
+++ b/solution.py
@@ -210,9 +210,10 @@
     own_start = head_pos * share
     mine = lax.dynamic_slice_in_dim(packed, own_start, share, 0).astype(jnp.float32)
     mine_inv = lax.dynamic_slice_in_dim(inv_rms, own_start, share, 0)
+    mine, mine_inv, mine_cubed = lax.optimization_barrier((mine, mine_inv, mine * mine_inv**3))
     gain_grad = gain * grad_normed
     mixed = jnp.mean(gain_grad * mine, axis=-1, keepdims=True)
-    d_rows = (mine_inv * gain_grad - mine * mine_inv**3 * mixed).astype(jnp.bfloat16)
+    d_rows = (mine_inv * gain_grad - mine_cubed * mixed).astype(jnp.bfloat16)
     return (context_out, d_rows)
 
 

time: 192 us -> 193 us (level)
  other arithmetic: 8.05 us -> 10.8 us
  waiting for transfers between devices: 89.2 us -> 87 us
    reduce_scatter x1, waiting for transfers between devices: 39.7 us -> 37.4 us  [body(): lax.psum_scatter(term.astype(jnp.bfloat16), 'head', scatter_dimension=0,...]
  transfers between devices with their start and end apart: 6 -> 6, of which waited for: 4 -> 4; matrix products, arithmetic and copies ran while one was open for 7% -> 9% of each run, Pallas kernels for 11% -> 11%
where the time goes in v13:
time: 193 us; the launch traced here: 192 us
  waiting for transfers between devices  87 us (45%)
  blocking collectives  24.6 us (13%)
  Pallas kernels  20.4 us (11%)
  matrix products  18.9 us (10%)
  between operations  14.3 us (7%)
  starting transfers between devices  11.6 us (6%)
  other arithmetic  10.8 us (6%)
  local copies, waits for them, and re-layouts  4.63 us (2%)
    reduce_scatter x1, waiting for transfers between devices, body(): lax.psum_scatter(term.astype(jnp.bfloat16), 'head', scatter_dimension=0,...  37.4 us
    all_gather x1, waiting for transfers between devices, body(): packed = lax.all_gather(packed_part, 'head', axis=1, tiled=True)  30.4 us
    all_to_all x1, blocking collectives, body(): lax.all_to_all(outgoing, 'seq', split_axis=0, concat_axis=0, tiled=True)  24.6 us
    pallas_call x2, Pallas kernels, attention(): pl.pallas_call(kernel, grid=(steps,), in_specs=[q_spec, k_spec, v_spec, k...  20.4 us
    ppermute x4, waiting for transfers between devices, passed_along(): return lax.ppermute(array, axis, pairs)  19.1 us
    ppermute x4, starting transfers between devices, passed_along(): return lax.ppermute(array, axis, pairs)  11.6 us
    dot_general x3, matrix products, project(): jnp.einsum('rc,dc->rd', grads, weight, preferred_element_type=jnp.float32)  9.16 us
  transfers between devices with their start and end apart: 6, of which 4 were waited for; matrix products, arithmetic and copies ran while one was open for 9% of the time, Pallas kernels for 11%

profile of v13, /device:TPU:0, one launch (start us, length us, event | category | flops | bytes accessed | tf_op | source)
XLA Modules:
  0.0 192.2 jit_solution(2831959677292701138)
XLA Ops:
  7.2 2.8 %fusion.7 = bf16[2048,256]{1,0:T(8,128)(2,1)S(1)} fusion(s32[1024]{0:T(1024)} %param.15, bf16[1024,2048]{1,0:T(8,128)(2,1)} %param.9, s32[]{:T(128)S(6)} %select_n.7), kind=kOutput, calls=%fused_computation.12 | convolution fusion | flops 1076363264 | bytes 1576964 | tf_op jit(solution)/shard_map/dot_general | solution.py:160
  10.0 24.6 %all_to_all.12 = bf16[16,128,256]{2,1,0:T(8,128)(2,1)S(1)} all-to-all(bf16[16,128,256]{2,1,0:T(8,128)(2,1)S(1)} %bitcast.12), channel_id=1, replica_groups=mesh['seq'=16,'head'=8] {'seq'}, dimensions={0} | all-to-all | bytes 2097152 | tf_op jit(solution)/shard_map/all_to_all | solution.py:163
  34.6 2.3 %fusion.8 = bf16[1024,256]{1,0:T(8,128)(2,1)} fusion(bf16[2048,256]{1,0:T(8,128)(2,1)S(1)} %bitcast.13, s32[1024]{0:T(1024)S(1)} %copy-done.11), kind=kOutput, calls=%fused_computation.13 | convolution fusion | flops 1076101120 | bytes 1576960 | tf_op jit(solution)/shard_map/dot_general | solution.py:167
  37.0 0.0 reduce-scatter.2.cloned.1.call-start
  37.0 1.0 copy.11.st_ref
  38.1 0.8 fusion.27
  38.9 1.7 fusion.25
  40.6 30.4 %all-gather.2.cloned.1.call-done = bf16[1024,2048]{1,0:T(8,128)(2,1)} async-done(((bf16[1024,256]{1,0:T(8,128)(2,1)}), bf16[1024,2048]{1,0:T(8,128)(2,1)}) %all-gather.2.cloned.1.call-update) | async-done | bytes 4194320 | tf_op jit(solution)/shard_map/all_gather | solution.py:170
  71.0 3.2 %fusion = f32[1024]{0:T(1024)S(1)} fusion(bf16[1024,2048]{1,0:T(8,128)(2,1)} %all-gather.2.cloned.1.call-done), kind=kLoop, calls=%fused_computation.2 | loop fusion | flops 6290432 | bytes 4198400 | tf_op jit(solution)/shard_map/reduce_sum | solution.py:172
  74.3 0.2 copy-done.1
  74.5 1.3 convolution_convert_fusion.1.ko_ref.vo_ref
  75.8 3.5 %collective-permute-start = (bf16[1024,256]{1,0:T(8,128)(2,1)S(1)}, bf16[1024,256]{1,0:T(8,128)(2,1)S(1)}, u32[]{:S(2)}, u32[]{:S(2)}) collective-permute-start(bf16[1024,256]{1,0:T(8,128)(2,1)S(1)} %convolution_convert_fusion.1.ko_ref.vo_ref), channel_id=1, source_target_pairs={{0,8},{8,16},{16,24},{24,32},{32,40},{40,48},{48,56},{56,64},{64,7... | collective-permute-start | bytes 1572872 | tf_op jit(solution)/shard_map/ppermute | solution.py:20
  79.3 2.1 %convolution_convert_fusion.ko_ref.vo_ref = bf16[1024,256]{1,0:T(8,128)(2,1)} fusion(bf16[2048,128]{1,0:T(8,128)(2,1)S(1)} %get-tuple-element.36, bf16[2048,128]{1,0:T(8,128)(2,1)S(1)} %get-tuple-element.29, bf16[1024,2048]{1,0:T(8,128)(2,1)S(1)} %copy-done.1, f32[2048]{0:T(1024)S(1)} %copy-done.7, f32[1024]{0:T(1024)S(1)} %add_rsqrt_fusion), kind=kOutput, calls=%fused_computation.14 | convolution fusion | flops 1084489728 | bytes 5779456 | tf_op jit(solution)/shard_map/dot_general | solution.py:181
  81.4 9.4 %collective-permute-done.kp_ref.vp_ref = bf16[1024,256]{1,0:T(8,128)(2,1)S(1)} collective-permute-done((bf16[1024,256]{1,0:T(8,128)(2,1)S(1)}, bf16[1024,256]{1,0:T(8,128)(2,1)S(1)}, u32[]{:S(2)}, u32[]{:S(2)}) %collective-permute-start) | collective-permute-done | bytes 524320 | tf_op jit(solution)/shard_map/ppermute | solution.py:20
  90.8 5.2 %collective-permute-start.1 = (bf16[1024,256]{1,0:T(8,128)(2,1)}, bf16[1024,256]{1,0:T(8,128)(2,1)}, u32[]{:S(2)}, u32[]{:S(2)}) collective-permute-start(bf16[1024,256]{1,0:T(8,128)(2,1)} %convolution_convert_fusion.ko_ref.vo_ref), channel_id=1, source_target_pairs={{0,8},{8,16},{16,24},{24,32},{32,40},{40,48},{48,56},{56,64},{64,7... | collective-permute-start | bytes 1572872 | tf_op jit(solution)/shard_map/ppermute | solution.py:20
  96.0 1.3 convolution_convert_fusion.2
  97.3 0.8 fusion.28
  98.1 10.1 %shard_map.104 = (bf16[1024,128]{1,0:T(8,128)(2,1)}, bf16[1024,128]{1,0:T(8,128)(2,1)}, bf16[1024,256]{1,0:T(8,128)(2,1)}, f32[1024,256]{1,0:T(8,128)}) custom-call(bf16[1024,128]{1,0:T(8,128)(2,1)} %get-tuple-element.34.q_ref, bf16[1024,256]{1,0:T(8,128)(2,1)} %copy-done.10, bf16[1024,256]{1,0:T(8,128)(2,1)} %copy-done.10, bf16[1024,256]{1,0:T(8,128)(2,1)} %copy-done.9, ...), custom_call_target="tpu_custom_call" | custom-call | flops 2013265920 | bytes 3670016 | tf_op jit(solution)/shard_map/pallas_call | solution.py:125
  108.3 1.6 collective-permute-start.2
  109.9 10.2 %shard_map.105 = (bf16[1024,128]{1,0:T(8,128)(2,1)}, bf16[1024,128]{1,0:T(8,128)(2,1)}, bf16[1024,256]{1,0:T(8,128)(2,1)}, f32[1024,256]{1,0:T(8,128)}) custom-call(bf16[1024,128]{1,0:T(8,128)(2,1)} %get-tuple-element.35.q_ref, bf16[1024,256]{1,0:T(8,128)(2,1)} %collective-permute-done.1.kp_ref.vp_ref, ...), custom_call_target="tpu_custom_call" | custom-call | flops 2013265920 | bytes 3670016 | tf_op jit(solution)/shard_map/pallas_call | solution.py:125
  120.2 1.3 collective-permute-start.3
  121.5 2.3 %fusion.10 = f32[1024,2048]{1,0:T(8,128)S(1)} fusion(bf16[2048,256]{1,0:T(8,128)(2,1)S(1)} %copy-done, bf16[1024,128]{1,0:T(8,128)(2,1)} %get-tuple-element.19, bf16[1024,128]{1,0:T(8,128)(2,1)S(1)} %copy-done.5), kind=kOutput, calls=%fused_computation.26 | convolution fusion | flops 1074790400 | bytes 9961472 | tf_op jit(solution)/shard_map/rc,dc->rd/dot_general | solution.py:199
  123.8 2.4 %fusion.9 = f32[1024,2048]{1,0:T(8,128)S(1)} fusion(bf16[2048,128]{1,0:T(8,128)(2,1)S(1)} %get-tuple-element.37, bf16[2048,128]{1,0:T(8,128)(2,1)S(1)} %get-tuple-element.28, f32[1024,256]{1,0:T(8,128)S(1)} %copy-done.2, bf16[1024,256]{1,0:T(8,128)(2,1)} %collective-permute-done.2), kind=kOutput, calls=%fused_computation.24 | convolution fusion | flops 1076625408 | bytes 11010048 | tf_op jit(solution)/shard_map/rc,dc->rd/dot_general | solution.py:199
  126.3 9.7 %collective-permute-done.3 = bf16[1024,256]{1,0:T(8,128)(2,1)} collective-permute-done((bf16[1024,256]{1,0:T(8,128)(2,1)}, bf16[1024,256]{1,0:T(8,128)(2,1)}, u32[]{:S(2)}, u32[]{:S(2)}) %collective-permute-start.3) | collective-permute-done | bytes 524320 | tf_op jit(solution)/shard_map/ppermute | solution.py:20
  136.0 4.4 %add_convert_fusion = bf16[1024,2048]{1,0:T(8,128)(2,1)} fusion(f32[1024,2048]{1,0:T(8,128)S(1)} %fusion.10, f32[1024,2048]{1,0:T(8,128)S(1)} %fusion.9, bf16[2048,128]{1,0:T(8,128)(2,1)S(1)} %get-tuple-element.36, bf16[2048,128]{1,0:T(8,128)(2,1)S(1)} %get-tuple-element.29, f32[1024,256]{1,0:T(8,128)S(1)} %copy-done.3, ...), kind=kOutput, calls=%fused_computation.5 | convolution fusion | flops 1082916864 | bytes 23592960 | tf_op jit(solution)/shard_map/rc,dc->rd/dot_general | solution.py:199
  140.4 0.1 fusion.15
  140.5 1.1 dynamic-slice_convert_fusion
  141.6 1.2 broadcast_multiply_fusion
  142.8 1.8 pad_maximum_fusion.6
  144.6 37.4 %reduce-scatter.2.cloned.1.call-done = bf16[128,2048]{1,0:T(8,128)(2,1)} async-done(((bf16[1024,2048]{1,0:T(8,128)(2,1)}), bf16[128,2048]{1,0:T(8,128)(2,1)}) %reduce-scatter.2.cloned.1.call-update) | async-done | bytes 524304 | tf_op jit(solution)/shard_map/reduce_scatter | solution.py:204
  182.0 1.3 multiply_reduce_fusion
  183.3 2.1 %subtract_convert_fusion = bf16[128,2048]{1,0:T(8,128)(2,1)} fusion(f32[128,2048]{1,0:T(8,128)S(1)} %broadcast_multiply_fusion, bf16[128,2048]{1,0:T(8,128)(2,1)} %reduce-scatter.2.cloned.1.call-done, f32[128]{0:T(128)S(1)} %broadcast_multiply_fusion.1, f32[2048]{0:T(1024)S(1)} %copy-done.7, f32[128]{0:T(128)S(1)} %bitcast.15), kind=kLoop, calls=%fused_computation.19 | loop fusion | flops 1572864 | bytes 2106368 | tf_op jit(solution)/shard_map/convert_element_type | solution.py:216
  (31 shorter events, 0.1 us)
Async XLA Ops:
  7.2 88.8 %copy-start = (bf16[2048,256]{1,0:T(8,128)(2,1)S(1)}, bf16[2048,256]{1,0:T(8,128)(2,1)}, u32[]{:S(2)}) copy-start(bf16[2048,256]{1,0:T(8,128)(2,1)} %param.11) | copy-start | bytes 3145732
  7.2 63.8 %all-gather.2.cloned.1.call-start = ((), (), s32[]{:S(2)}) async-start(), calls=%async_computation.2 | async-start | bytes 4718592 | tf_op jit(solution)/shard_map/all_gather | solution.py:170
  7.2 27.4 %copy-start.11 = (s32[1024]{0:T(1024)S(1)}, s32[1024]{0:T(1024)}, u32[]{:S(2)}) copy-start(s32[1024]{0:T(1024)} %param.16) | copy-start | bytes 12292
  34.6 2.4 %copy-start.8 = (s32[1024]{0:T(1024)S(1)}, s32[1024]{0:T(1024)}, u32[]{:S(2)}) copy-start(s32[1024]{0:T(1024)} %param.17) | copy-start | bytes 12292
  34.6 3.4 %copy-start.4 = (bf16[1024,256]{1,0:T(8,128)(2,1)S(1)}, bf16[1024,256]{1,0:T(8,128)(2,1)}, u32[]{:S(2)}) copy-start(bf16[1024,256]{1,0:T(8,128)(2,1)} %param.14) | copy-start | bytes 1572868
  37.0 145.1 %reduce-scatter.2.cloned.1.call-start = ((), (), s32[]{:S(2)}) async-start(), calls=%async_computation.3 | async-start | bytes 4718592 | tf_op jit(solution)/shard_map/reduce_scatter | solution.py:204
  38.9 35.3 %copy-start.7 = (f32[2048]{0:T(1024)S(1)}, f32[2048]{0:T(1024)}, u32[]{:S(2)}) copy-start(f32[2048]{0:T(1024)} %param.10) | copy-start | bytes 24580
  71.0 3.4 %copy-start.1 = (bf16[1024,2048]{1,0:T(8,128)(2,1)S(1)}, bf16[1024,2048]{1,0:T(8,128)(2,1)}, u32[]{:S(2)}) copy-start(bf16[1024,2048]{1,0:T(8,128)(2,1)} %all-gather.2.cloned.1.call-done) | copy-start | bytes 12582916
  75.8 5.6 %copy-start.9 = (bf16[1024,256]{1,0:T(8,128)(2,1)}, bf16[1024,256]{1,0:T(8,128)(2,1)S(1)}, u32[]{:S(2)}) copy-start(bf16[1024,256]{1,0:T(8,128)(2,1)S(1)} %convolution_convert_fusion.1.ko_ref.vo_ref) | copy-start | bytes 1572868
  75.8 15.0 %collective-permute-start = (bf16[1024,256]{1,0:T(8,128)(2,1)S(1)}, bf16[1024,256]{1,0:T(8,128)(2,1)S(1)}, u32[]{:S(2)}, u32[]{:S(2)}) collective-permute-start(bf16[1024,256]{1,0:T(8,128)(2,1)S(1)} %convolution_convert_fusion.1.ko_ref.vo_ref), channel_id=1, source_target_pairs={{0,8},{8,16},{16,24},{24,32},{32,40},{40,48},{48,56},{56,64},{64,7... | collective-permute-start | bytes 1572872 | tf_op jit(solution)/shard_map/ppermute | solution.py:20
  90.8 6.5 %copy-start.10 = (bf16[1024,256]{1,0:T(8,128)(2,1)}, bf16[1024,256]{1,0:T(8,128)(2,1)S(1)}, u32[]{:S(2)}) copy-start(bf16[1024,256]{1,0:T(8,128)(2,1)S(1)} %collective-permute-done.kp_ref.vp_ref) | copy-start | bytes 1572868
  90.8 19.1 %collective-permute-start.1 = (bf16[1024,256]{1,0:T(8,128)(2,1)}, bf16[1024,256]{1,0:T(8,128)(2,1)}, u32[]{:S(2)}, u32[]{:S(2)}) collective-permute-start(bf16[1024,256]{1,0:T(8,128)(2,1)} %convolution_convert_fusion.ko_ref.vo_ref), channel_id=1, source_target_pairs={{0,8},{8,16},{16,24},{24,32},{32,40},{40,48},{48,56},{56,64},{64,7... | collective-permute-start | bytes 1572872 | tf_op jit(solution)/shard_map/ppermute | solution.py:20
  108.3 13.2 %copy-start.5 = (bf16[1024,128]{1,0:T(8,128)(2,1)S(1)}, bf16[1024,128]{1,0:T(8,128)(2,1)}, u32[]{:S(2)}) copy-start(bf16[1024,128]{1,0:T(8,128)(2,1)} %get-tuple-element.18) | copy-start | bytes 786436
  108.3 15.5 %collective-permute-start.2 = (bf16[1024,256]{1,0:T(8,128)(2,1)}, bf16[1024,256]{1,0:T(8,128)(2,1)}, u32[]{:S(2)}, u32[]{:S(2)}) collective-permute-start(bf16[1024,256]{1,0:T(8,128)(2,1)} %get-tuple-element.21), channel_id=1, source_target_pairs={{8,0},{16,8},{24,16},{32,24},{40,32},{48,40},{56,48},{64,56},{72,6... | collective-permute-start | bytes 1572872 | tf_op jit(solution)/shard_map/ppermute | solution.py:20
  120.2 15.8 %collective-permute-start.3 = (bf16[1024,256]{1,0:T(8,128)(2,1)}, bf16[1024,256]{1,0:T(8,128)(2,1)}, u32[]{:S(2)}, u32[]{:S(2)}) collective-permute-start(bf16[1024,256]{1,0:T(8,128)(2,1)} %get-tuple-element.23), channel_id=1, source_target_pairs={{8,0},{16,8},{24,16},{32,24},{40,32},{48,40},{56,48},{64,56},{72,6... | collective-permute-start | bytes 1572872 | tf_op jit(solution)/shard_map/ppermute | solution.py:20
  121.5 2.3 %copy-start.2 = (f32[1024,256]{1,0:T(8,128)S(1)}, f32[1024,256]{1,0:T(8,128)}, u32[]{:S(2)}) copy-start(f32[1024,256]{1,0:T(8,128)} %get-tuple-element.20) | copy-start | bytes 3145732
  123.8 12.1 %copy-start.3 = (f32[1024,256]{1,0:T(8,128)S(1)}, f32[1024,256]{1,0:T(8,128)}, u32[]{:S(2)}) copy-start(f32[1024,256]{1,0:T(8,128)} %get-tuple-element.22) | copy-start | bytes 3145732
  140.4 2.4 %copy-start.6 = (bf16[1024,128]{1,0:T(8,128)(2,1)S(1)}, bf16[1024,128]{1,0:T(8,128)(2,1)}, u32[]{:S(2)}) copy-start(bf16[1024,128]{1,0:T(8,128)(2,1)} %get-tuple-element.14) | copy-start | bytes 786436
Sparse Core Ops, SparseCore 0:
  37.1 33.8 all-gather.1
  140.5 41.4 reduce-scatter.1

commit v14 on v12

--- a/solution.py
+++ b/solution.py
@@ -107,7 +107,7 @@
 
 def attention(queries, kv_prev, kv_own, grad_ctx, rel_start):
     rows, hd = queries.shape
-    tq = 256
+    tq = 512
     window = rows + tq
     kernel = functools.partial(
         attention_kernel, tq=tq, window=window, shift=rows, scale=hd ** (-0.5)

time: 192 us -> 192 us (level)
  no operation moved by 1% of the time
where the time goes in v14:
time: 192 us; the launch traced here: 191 us
  waiting for transfers between devices  89.1 us (46%)
  blocking collectives  24.6 us (13%)
  Pallas kernels  20.3 us (11%)
  matrix products  17.9 us (9%)
  between operations  14.2 us (7%)
  starting transfers between devices  11.6 us (6%)
  other arithmetic  8.05 us (4%)
  local copies, waits for them, and re-layouts  5.57 us (3%)
    reduce_scatter x1, waiting for transfers between devices, body(): lax.psum_scatter(term.astype(jnp.bfloat16), 'head', scatter_dimension=0,...  39.9 us
    all_gather x1, waiting for transfers between devices, body(): packed = lax.all_gather(packed_part, 'head', axis=1, tiled=True)  30.4 us
    all_to_all x1, blocking collectives, body(): lax.all_to_all(outgoing, 'seq', split_axis=0, concat_axis=0, tiled=True)  24.6 us
    pallas_call x2, Pallas kernels, attention(): pl.pallas_call(kernel, grid=(steps,), in_specs=[q_spec, k_spec, v_spec, k...  20.3 us
    ppermute x4, waiting for transfers between devices, passed_along(): return lax.ppermute(array, axis, pairs)  18.8 us
    ppermute x4, starting transfers between devices, passed_along(): return lax.ppermute(array, axis, pairs)  11.5 us
    dot_general x3, matrix products, project(): jnp.einsum('rc,dc->rd', grads, weight, preferred_element_type=jnp.float32)  8.14 us
  transfers between devices with their start and end apart: 6, of which 4 were waited for; matrix products, arithmetic and copies ran while one was open for 7% of the time, Pallas kernels for 11%

profile of v14, /device:TPU:0, one launch (start us, length us, event | category | flops | bytes accessed | tf_op | source)
XLA Modules:
  0.0 191.4 jit_solution(8709037584027724824)
XLA Ops:
  7.2 2.8 %fusion.7 = bf16[2048,256]{1,0:T(8,128)(2,1)S(1)} fusion(s32[1024]{0:T(1024)} %param.15, bf16[1024,2048]{1,0:T(8,128)(2,1)} %param.9, s32[]{:T(128)S(6)} %select_n.7), kind=kOutput, calls=%fused_computation.12 | convolution fusion | flops 1076363264 | bytes 1576964 | tf_op jit(solution)/shard_map/dot_general | solution.py:160
  10.0 24.6 %all_to_all.12 = bf16[16,128,256]{2,1,0:T(8,128)(2,1)S(1)} all-to-all(bf16[16,128,256]{2,1,0:T(8,128)(2,1)S(1)} %bitcast.10), channel_id=1, replica_groups=mesh['seq'=16,'head'=8] {'seq'}, dimensions={0} | all-to-all | bytes 2097152 | tf_op jit(solution)/shard_map/all_to_all | solution.py:163
  34.6 2.3 %fusion.8 = bf16[1024,256]{1,0:T(8,128)(2,1)} fusion(bf16[2048,256]{1,0:T(8,128)(2,1)S(1)} %bitcast.11, s32[1024]{0:T(1024)S(1)} %copy-done.12), kind=kOutput, calls=%fused_computation.15 | convolution fusion | flops 1076101120 | bytes 1576960 | tf_op jit(solution)/shard_map/dot_general | solution.py:167
  37.0 0.0 reduce-scatter.2.cloned.1.call-start
  37.0 1.0 copy.11.st_ref
  38.1 0.8 fusion.31
  38.9 1.7 fusion.29
  40.6 30.4 %all-gather.2.cloned.1.call-done = bf16[1024,2048]{1,0:T(8,128)(2,1)} async-done(((bf16[1024,256]{1,0:T(8,128)(2,1)}), bf16[1024,2048]{1,0:T(8,128)(2,1)}) %all-gather.2.cloned.1.call-update) | async-done | bytes 4194320 | tf_op jit(solution)/shard_map/all_gather | solution.py:170
  71.0 3.2 %fusion = f32[1024]{0:T(1024)S(1)} fusion(bf16[1024,2048]{1,0:T(8,128)(2,1)} %all-gather.2.cloned.1.call-done), kind=kLoop, calls=%fused_computation.2 | loop fusion | flops 6290432 | bytes 4198400 | tf_op jit(solution)/shard_map/reduce_sum | solution.py:172
  74.2 0.2 copy-done.1
  74.5 1.3 convolution_convert_fusion.1.ko_ref.vo_ref
  75.8 3.5 %collective-permute-start = (bf16[1024,256]{1,0:T(8,128)(2,1)S(1)}, bf16[1024,256]{1,0:T(8,128)(2,1)S(1)}, u32[]{:S(2)}, u32[]{:S(2)}) collective-permute-start(bf16[1024,256]{1,0:T(8,128)(2,1)S(1)} %convolution_convert_fusion.1.ko_ref.vo_ref), channel_id=1, source_target_pairs={{0,8},{8,16},{16,24},{24,32},{32,40},{40,48},{48,56},{56,64},{64,7... | collective-permute-start | bytes 1572872 | tf_op jit(solution)/shard_map/ppermute | solution.py:20
  79.3 2.1 %convolution_convert_fusion.ko_ref.vo_ref = bf16[1024,256]{1,0:T(8,128)(2,1)} fusion(bf16[2048,128]{1,0:T(8,128)(2,1)S(1)} %get-tuple-element.30, bf16[2048,128]{1,0:T(8,128)(2,1)S(1)} %get-tuple-element.23, bf16[1024,2048]{1,0:T(8,128)(2,1)S(1)} %copy-done.1, f32[2048]{0:T(1024)S(1)} %copy-done.8, f32[1024]{0:T(1024)S(1)} %add_rsqrt_fusion), kind=kOutput, calls=%fused_computation.16 | convolution fusion | flops 1084489728 | bytes 5779456 | tf_op jit(solution)/shard_map/dot_general | solution.py:181
  81.4 9.4 %collective-permute-done.kp_ref.vp_ref = bf16[1024,256]{1,0:T(8,128)(2,1)S(1)} collective-permute-done((bf16[1024,256]{1,0:T(8,128)(2,1)S(1)}, bf16[1024,256]{1,0:T(8,128)(2,1)S(1)}, u32[]{:S(2)}, u32[]{:S(2)}) %collective-permute-start) | collective-permute-done | bytes 524320 | tf_op jit(solution)/shard_map/ppermute | solution.py:20
  90.8 5.2 %collective-permute-start.1 = (bf16[1024,256]{1,0:T(8,128)(2,1)}, bf16[1024,256]{1,0:T(8,128)(2,1)}, u32[]{:S(2)}, u32[]{:S(2)}) collective-permute-start(bf16[1024,256]{1,0:T(8,128)(2,1)} %convolution_convert_fusion.ko_ref.vo_ref), channel_id=1, source_target_pairs={{0,8},{8,16},{16,24},{24,32},{32,40},{40,48},{48,56},{56,64},{64,7... | collective-permute-start | bytes 1572872 | tf_op jit(solution)/shard_map/ppermute | solution.py:20
  96.0 1.3 convolution_convert_fusion.2
  97.3 0.9 fusion.32
  98.2 10.1 %shard_map.104 = (bf16[1024,128]{1,0:T(8,128)(2,1)}, bf16[1024,128]{1,0:T(8,128)(2,1)}, bf16[1024,256]{1,0:T(8,128)(2,1)}, f32[1024,256]{1,0:T(8,128)}) custom-call(bf16[1024,128]{1,0:T(8,128)(2,1)} %get-tuple-element.28.q_ref, bf16[1024,256]{1,0:T(8,128)(2,1)} %copy-done.11, bf16[1024,256]{1,0:T(8,128)(2,1)} %copy-done.11, bf16[1024,256]{1,0:T(8,128)(2,1)} %copy-done.10, ...), custom_call_target="tpu_custom_call" | custom-call | flops 2415919104 | bytes 3670016 | tf_op jit(solution)/shard_map/pallas_call | solution.py:125
  108.3 1.3 collective-permute-start.2
  109.6 10.3 %shard_map.105 = (bf16[1024,128]{1,0:T(8,128)(2,1)}, bf16[1024,128]{1,0:T(8,128)(2,1)}, bf16[1024,256]{1,0:T(8,128)(2,1)}, f32[1024,256]{1,0:T(8,128)}) custom-call(bf16[1024,128]{1,0:T(8,128)(2,1)} %get-tuple-element.29.q_ref, bf16[1024,256]{1,0:T(8,128)(2,1)} %collective-permute-done.1.kp_ref.vp_ref, ...), custom_call_target="tpu_custom_call" | custom-call | flops 2415919104 | bytes 3670016 | tf_op jit(solution)/shard_map/pallas_call | solution.py:125
  119.8 1.5 collective-permute-start.3
  121.4 2.3 %fusion.14 = f32[1024,2048]{1,0:T(8,128)S(1)} fusion(bf16[2048,256]{1,0:T(8,128)(2,1)S(1)} %copy-done, bf16[1024,128]{1,0:T(8,128)(2,1)} %get-tuple-element.15, bf16[1024,128]{1,0:T(8,128)(2,1)S(1)} %copy-done.5), kind=kOutput, calls=%fused_computation.30 | convolution fusion | flops 1074790400 | bytes 9961472 | tf_op jit(solution)/shard_map/rc,dc->rd/dot_general | solution.py:199
  123.7 2.4 %fusion.13 = f32[1024,2048]{1,0:T(8,128)S(1)} fusion(bf16[2048,128]{1,0:T(8,128)(2,1)S(1)} %get-tuple-element.31, bf16[2048,128]{1,0:T(8,128)(2,1)S(1)} %get-tuple-element.22, f32[1024,256]{1,0:T(8,128)S(1)} %copy-done.2, bf16[1024,256]{1,0:T(8,128)(2,1)} %collective-permute-done.2), kind=kOutput, calls=%fused_computation.28 | convolution fusion | flops 1076625408 | bytes 11010048 | tf_op jit(solution)/shard_map/rc,dc->rd/dot_general | solution.py:199
  126.2 9.4 %collective-permute-done.3 = bf16[1024,256]{1,0:T(8,128)(2,1)S(1)} collective-permute-done((bf16[1024,256]{1,0:T(8,128)(2,1)}, bf16[1024,256]{1,0:T(8,128)(2,1)S(1)}, u32[]{:S(2)}, u32[]{:S(2)}) %collective-permute-start.3) | collective-permute-done | bytes 524320 | tf_op jit(solution)/shard_map/ppermute | solution.py:20
  135.5 3.4 %add_convert_fusion = bf16[1024,2048]{1,0:T(8,128)(2,1)} fusion(f32[1024,2048]{1,0:T(8,128)S(1)} %fusion.14, f32[1024,2048]{1,0:T(8,128)S(1)} %fusion.13, bf16[2048,128]{1,0:T(8,128)(2,1)S(1)} %get-tuple-element.30, bf16[2048,128]{1,0:T(8,128)(2,1)S(1)} %get-tuple-element.23, f32[1024,256]{1,0:T(8,128)S(1)} %copy-done.3, ...), kind=kOutput, calls=%fused_computation.5 | convolution fusion | flops 1082916864 | bytes 23592960 | tf_op jit(solution)/shard_map/rc,dc->rd/dot_general | solution.py:199
  139.0 0.1 fusion.19
  139.0 0.8 copy-done.6
  139.9 0.1 copy-done.7
  140.0 0.8 pad_maximum_fusion.6
  140.8 39.9 %reduce-scatter.2.cloned.1.call-done = bf16[128,2048]{1,0:T(8,128)(2,1)} async-done(((bf16[1024,2048]{1,0:T(8,128)(2,1)}), bf16[128,2048]{1,0:T(8,128)(2,1)}) %reduce-scatter.2.cloned.1.call-update) | async-done | bytes 524304 | tf_op jit(solution)/shard_map/reduce_scatter | solution.py:204
  180.7 1.5 fusion.12
  182.2 2.4 %fusion.11 = bf16[128,2048]{1,0:T(8,128)(2,1)} fusion(bf16[128,2048]{1,0:T(8,128)(2,1)} %reduce-scatter.2.cloned.1.call-done, f32[128]{0:T(128)S(1)} %broadcast_multiply_fusion, f32[128]{0:T(128)S(1)} %get-tuple-element.20, f32[2048]{0:T(1024)S(1)} %copy-done.8, f32[128]{0:T(128)S(1)} %get-tuple-element.21, ...), kind=kLoop, calls=%fused_computation.21 | loop fusion | flops 2097152 | bytes 1582596 | tf_op jit(solution)/shard_map/convert_element_type | solution.py:215
  (31 shorter events, 0.1 us)
Async XLA Ops:
  7.2 88.8 %copy-start = (bf16[2048,256]{1,0:T(8,128)(2,1)S(1)}, bf16[2048,256]{1,0:T(8,128)(2,1)}, u32[]{:S(2)}) copy-start(bf16[2048,256]{1,0:T(8,128)(2,1)} %param.11) | copy-start | bytes 3145732
  7.2 63.8 %all-gather.2.cloned.1.call-start = ((), (), s32[]{:S(2)}) async-start(), calls=%async_computation.2 | async-start | bytes 4718592 | tf_op jit(solution)/shard_map/all_gather | solution.py:170
  7.2 27.4 %copy-start.12 = (s32[1024]{0:T(1024)S(1)}, s32[1024]{0:T(1024)}, u32[]{:S(2)}) copy-start(s32[1024]{0:T(1024)} %param.16) | copy-start | bytes 12292
  34.6 2.4 %copy-start.9 = (s32[1024]{0:T(1024)S(1)}, s32[1024]{0:T(1024)}, u32[]{:S(2)}) copy-start(s32[1024]{0:T(1024)} %param.17) | copy-start | bytes 12292
  34.6 3.4 %copy-start.4 = (bf16[1024,256]{1,0:T(8,128)(2,1)S(1)}, bf16[1024,256]{1,0:T(8,128)(2,1)}, u32[]{:S(2)}) copy-start(bf16[1024,256]{1,0:T(8,128)(2,1)} %param.14) | copy-start | bytes 1572868
  37.0 143.7 %reduce-scatter.2.cloned.1.call-start = ((), (), s32[]{:S(2)}) async-start(), calls=%async_computation.3 | async-start | bytes 4718592 | tf_op jit(solution)/shard_map/reduce_scatter | solution.py:204
  38.9 35.3 %copy-start.8 = (f32[2048]{0:T(1024)S(1)}, f32[2048]{0:T(1024)}, u32[]{:S(2)}) copy-start(f32[2048]{0:T(1024)} %param.10) | copy-start | bytes 24580
  71.0 3.4 %copy-start.1 = (bf16[1024,2048]{1,0:T(8,128)(2,1)S(1)}, bf16[1024,2048]{1,0:T(8,128)(2,1)}, u32[]{:S(2)}) copy-start(bf16[1024,2048]{1,0:T(8,128)(2,1)} %all-gather.2.cloned.1.call-done) | copy-start | bytes 12582916
  75.8 5.6 %copy-start.10 = (bf16[1024,256]{1,0:T(8,128)(2,1)}, bf16[1024,256]{1,0:T(8,128)(2,1)S(1)}, u32[]{:S(2)}) copy-start(bf16[1024,256]{1,0:T(8,128)(2,1)S(1)} %convolution_convert_fusion.1.ko_ref.vo_ref) | copy-start | bytes 1572868
  75.8 15.0 %collective-permute-start = (bf16[1024,256]{1,0:T(8,128)(2,1)S(1)}, bf16[1024,256]{1,0:T(8,128)(2,1)S(1)}, u32[]{:S(2)}, u32[]{:S(2)}) collective-permute-start(bf16[1024,256]{1,0:T(8,128)(2,1)S(1)} %convolution_convert_fusion.1.ko_ref.vo_ref), channel_id=1, source_target_pairs={{0,8},{8,16},{16,24},{24,32},{32,40},{40,48},{48,56},{56,64},{64,7... | collective-permute-start | bytes 1572872 | tf_op jit(solution)/shard_map/ppermute | solution.py:20
  90.8 6.5 %copy-start.11 = (bf16[1024,256]{1,0:T(8,128)(2,1)}, bf16[1024,256]{1,0:T(8,128)(2,1)S(1)}, u32[]{:S(2)}) copy-start(bf16[1024,256]{1,0:T(8,128)(2,1)S(1)} %collective-permute-done.kp_ref.vp_ref) | copy-start | bytes 1572868
  90.8 18.8 %collective-permute-start.1 = (bf16[1024,256]{1,0:T(8,128)(2,1)}, bf16[1024,256]{1,0:T(8,128)(2,1)}, u32[]{:S(2)}, u32[]{:S(2)}) collective-permute-start(bf16[1024,256]{1,0:T(8,128)(2,1)} %convolution_convert_fusion.ko_ref.vo_ref), channel_id=1, source_target_pairs={{0,8},{8,16},{16,24},{24,32},{32,40},{40,48},{48,56},{56,64},{64,7... | collective-permute-start | bytes 1572872 | tf_op jit(solution)/shard_map/ppermute | solution.py:20
  108.3 15.4 %collective-permute-start.2 = (bf16[1024,256]{1,0:T(8,128)(2,1)}, bf16[1024,256]{1,0:T(8,128)(2,1)}, u32[]{:S(2)}, u32[]{:S(2)}) collective-permute-start(bf16[1024,256]{1,0:T(8,128)(2,1)} %get-tuple-element.17), channel_id=1, source_target_pairs={{8,0},{16,8},{24,16},{32,24},{40,32},{48,40},{56,48},{64,56},{72,6... | collective-permute-start | bytes 1572872 | tf_op jit(solution)/shard_map/ppermute | solution.py:20
  109.6 11.8 %copy-start.5 = (bf16[1024,128]{1,0:T(8,128)(2,1)S(1)}, bf16[1024,128]{1,0:T(8,128)(2,1)}, u32[]{:S(2)}) copy-start(bf16[1024,128]{1,0:T(8,128)(2,1)} %get-tuple-element.14) | copy-start | bytes 786436
  119.8 15.7 %collective-permute-start.3 = (bf16[1024,256]{1,0:T(8,128)(2,1)}, bf16[1024,256]{1,0:T(8,128)(2,1)S(1)}, u32[]{:S(2)}, u32[]{:S(2)}) collective-permute-start(bf16[1024,256]{1,0:T(8,128)(2,1)} %get-tuple-element.19), channel_id=1, source_target_pairs={{8,0},{16,8},{24,16},{32,24},{40,32},{48,40},{56,48},{64,56},{72,6... | collective-permute-start | bytes 1572872 | tf_op jit(solution)/shard_map/ppermute | solution.py:20
  121.4 2.3 %copy-start.2 = (f32[1024,256]{1,0:T(8,128)S(1)}, f32[1024,256]{1,0:T(8,128)}, u32[]{:S(2)}) copy-start(f32[1024,256]{1,0:T(8,128)} %get-tuple-element.16) | copy-start | bytes 3145732
  123.7 11.8 %copy-start.3 = (f32[1024,256]{1,0:T(8,128)S(1)}, f32[1024,256]{1,0:T(8,128)}, u32[]{:S(2)}) copy-start(f32[1024,256]{1,0:T(8,128)} %get-tuple-element.18) | copy-start | bytes 3145732
  138.9 0.9 copy-start.6
  138.9 1.0 copy-start.7
Sparse Core Ops, SparseCore 0:
  37.1 33.8 all-gather.1
  139.1 41.5 reduce-scatter.1

commit v15 on v14

--- a/solution.py
+++ b/solution.py
@@ -199,8 +199,10 @@
         return jnp.einsum("rc,dc->rd", grads, weight, preferred_element_type=jnp.float32)
 
     term = project(grad_q_all, w_query)
-    for grad_kv, kv_weight in kv_parts:
+    for grad_kv, kv_weight in kv_parts[:-1]:
         term = term + project(grad_kv, kv_weight)
+    term = lax.optimization_barrier(term)
+    term = term + project(kv_parts[-1][0], kv_parts[-1][1])
     grad_normed = lax.psum_scatter(
         term.astype(jnp.bfloat16),
         "head",

time: 192 us -> 190 us (0.990)
  transfers between devices with their start and end apart: 6 -> 6, of which waited for: 4 -> 5; matrix products, arithmetic and copies ran while one was open for 7% -> 7% of each run, Pallas kernels for 11% -> 11%
where the time goes in v15:
time: 190 us
  waiting for transfers between devices  88.6 us (47%)
  blocking collectives  24.6 us (13%)
  Pallas kernels  20.2 us (11%)
  matrix products  17.1 us (9%)
  between operations  14.2 us (7%)
  starting transfers between devices  11.6 us (6%)
  other arithmetic  8.05 us (4%)
  local copies, waits for them, and re-layouts  5.56 us (3%)
    reduce_scatter x1, waiting for transfers between devices, body(): lax.psum_scatter(term.astype(jnp.bfloat16), 'head', scatter_dimension=0,...  40 us
    all_gather x1, waiting for transfers between devices, body(): packed = lax.all_gather(packed_part, 'head', axis=1, tiled=True)  30.4 us
    all_to_all x1, blocking collectives, body(): lax.all_to_all(outgoing, 'seq', split_axis=0, concat_axis=0, tiled=True)  24.6 us
    pallas_call x2, Pallas kernels, attention(): pl.pallas_call(kernel, grid=(steps,), in_specs=[q_spec, k_spec, v_spec, k...  20.2 us
    ppermute x4, waiting for transfers between devices, passed_along(): return lax.ppermute(array, axis, pairs)  18.2 us
    ppermute x4, starting transfers between devices, passed_along(): return lax.ppermute(array, axis, pairs)  11.5 us
    dot_general x3, matrix products, project(): jnp.einsum('rc,dc->rd', grads, weight, preferred_element_type=jnp.float32)  7.33 us
  transfers between devices with their start and end apart: 6, of which 5 were waited for; matrix products, arithmetic and copies ran while one was open for 7% of the time, Pallas kernels for 11%

profile of v15, /device:TPU:0, one launch (start us, length us, event | category | flops | bytes accessed | tf_op | source)
XLA Modules:
  0.0 190.0 jit_solution(14881033294132004258)
XLA Ops:
  7.2 2.8 %fusion.7 = bf16[2048,256]{1,0:T(8,128)(2,1)S(1)} fusion(s32[1024]{0:T(1024)} %param.15, bf16[1024,2048]{1,0:T(8,128)(2,1)} %param.9, s32[]{:T(128)S(6)} %select_n.7), kind=kOutput, calls=%fused_computation.13 | convolution fusion | flops 1076363264 | bytes 1576964 | tf_op jit(solution)/shard_map/dot_general | solution.py:160
  10.0 24.6 %all_to_all.12 = bf16[16,128,256]{2,1,0:T(8,128)(2,1)S(1)} all-to-all(bf16[16,128,256]{2,1,0:T(8,128)(2,1)S(1)} %bitcast.10), channel_id=1, replica_groups=mesh['seq'=16,'head'=8] {'seq'}, dimensions={0} | all-to-all | bytes 2097152 | tf_op jit(solution)/shard_map/all_to_all | solution.py:163
  34.6 2.3 %fusion.8 = bf16[1024,256]{1,0:T(8,128)(2,1)} fusion(bf16[2048,256]{1,0:T(8,128)(2,1)S(1)} %bitcast.11, s32[1024]{0:T(1024)S(1)} %copy-done.12), kind=kOutput, calls=%fused_computation.16 | convolution fusion | flops 1076101120 | bytes 1576960 | tf_op jit(solution)/shard_map/dot_general | solution.py:167
  37.0 1.0 copy.11.st_ref
  38.1 0.8 fusion.30
  38.9 1.7 fusion.28
  40.6 30.4 %all-gather.2.cloned.1.call-done = bf16[1024,2048]{1,0:T(8,128)(2,1)} async-done(((bf16[1024,256]{1,0:T(8,128)(2,1)}), bf16[1024,2048]{1,0:T(8,128)(2,1)}) %all-gather.2.cloned.1.call-update) | async-done | bytes 4194320 | tf_op jit(solution)/shard_map/all_gather | solution.py:170
  71.0 3.2 %fusion = f32[1024]{0:T(1024)S(1)} fusion(bf16[1024,2048]{1,0:T(8,128)(2,1)} %all-gather.2.cloned.1.call-done), kind=kLoop, calls=%fused_computation.2 | loop fusion | flops 6290432 | bytes 4198400 | tf_op jit(solution)/shard_map/reduce_sum | solution.py:172
  74.2 0.2 copy-done.1
  74.5 1.3 convolution_convert_fusion.1.ko_ref.vo_ref
  75.8 3.5 %collective-permute-start = (bf16[1024,256]{1,0:T(8,128)(2,1)S(1)}, bf16[1024,256]{1,0:T(8,128)(2,1)S(1)}, u32[]{:S(2)}, u32[]{:S(2)}) collective-permute-start(bf16[1024,256]{1,0:T(8,128)(2,1)S(1)} %convolution_convert_fusion.1.ko_ref.vo_ref), channel_id=1, source_target_pairs={{0,8},{8,16},{16,24},{24,32},{32,40},{40,48},{48,56},{56,64},{64,7... | collective-permute-start | bytes 1572872 | tf_op jit(solution)/shard_map/ppermute | solution.py:20
  79.3 1.3 convolution_convert_fusion.2
  80.6 2.1 %convolution_convert_fusion.ko_ref.vo_ref = bf16[1024,256]{1,0:T(8,128)(2,1)} fusion(bf16[2048,128]{1,0:T(8,128)(2,1)S(1)} %get-tuple-element.30, bf16[2048,128]{1,0:T(8,128)(2,1)S(1)} %get-tuple-element.23, bf16[1024,2048]{1,0:T(8,128)(2,1)S(1)} %copy-done.1, f32[2048]{0:T(1024)S(1)} %copy-done.8, f32[1024]{0:T(1024)S(1)} %add_rsqrt_fusion), kind=kOutput, calls=%fused_computation.17 | convolution fusion | flops 1084489728 | bytes 5779456 | tf_op jit(solution)/shard_map/dot_general | solution.py:181
  82.7 8.1 %collective-permute-done.kp_ref.vp_ref = bf16[1024,256]{1,0:T(8,128)(2,1)S(1)} collective-permute-done((bf16[1024,256]{1,0:T(8,128)(2,1)S(1)}, bf16[1024,256]{1,0:T(8,128)(2,1)S(1)}, u32[]{:S(2)}, u32[]{:S(2)}) %collective-permute-start) | collective-permute-done | bytes 524320 | tf_op jit(solution)/shard_map/ppermute | solution.py:20
  90.8 5.2 %collective-permute-start.1 = (bf16[1024,256]{1,0:T(8,128)(2,1)}, bf16[1024,256]{1,0:T(8,128)(2,1)}, u32[]{:S(2)}, u32[]{:S(2)}) collective-permute-start(bf16[1024,256]{1,0:T(8,128)(2,1)} %convolution_convert_fusion.ko_ref.vo_ref), channel_id=1, source_target_pairs={{0,8},{8,16},{16,24},{24,32},{32,40},{40,48},{48,56},{56,64},{64,7... | collective-permute-start | bytes 1572872 | tf_op jit(solution)/shard_map/ppermute | solution.py:20
  96.0 0.9 fusion.31
  96.8 10.1 %shard_map.104 = (bf16[1024,128]{1,0:T(8,128)(2,1)}, bf16[1024,128]{1,0:T(8,128)(2,1)}, bf16[1024,256]{1,0:T(8,128)(2,1)}, f32[1024,256]{1,0:T(8,128)}) custom-call(bf16[1024,128]{1,0:T(8,128)(2,1)} %get-tuple-element.28.q_ref, bf16[1024,256]{1,0:T(8,128)(2,1)} %copy-done.11, bf16[1024,256]{1,0:T(8,128)(2,1)} %copy-done.11, bf16[1024,256]{1,0:T(8,128)(2,1)} %copy-done.10, ...), custom_call_target="tpu_custom_call" | custom-call | flops 2415919104 | bytes 3670016 | tf_op jit(solution)/shard_map/pallas_call | solution.py:125
  106.9 1.3 collective-permute-start.2
  108.3 10.1 %shard_map.105 = (bf16[1024,128]{1,0:T(8,128)(2,1)}, bf16[1024,128]{1,0:T(8,128)(2,1)}, bf16[1024,256]{1,0:T(8,128)(2,1)}, f32[1024,256]{1,0:T(8,128)}) custom-call(bf16[1024,128]{1,0:T(8,128)(2,1)} %get-tuple-element.29.q_ref, bf16[1024,256]{1,0:T(8,128)(2,1)} %collective-permute-done.1.kp_ref.vp_ref, ...), custom_call_target="tpu_custom_call" | custom-call | flops 2415919104 | bytes 3670016 | tf_op jit(solution)/shard_map/pallas_call | solution.py:125
  118.4 1.5 collective-permute-start.3
  119.9 2.2 %collective-permute-done.2 = bf16[1024,256]{1,0:T(8,128)(2,1)} collective-permute-done((bf16[1024,256]{1,0:T(8,128)(2,1)}, bf16[1024,256]{1,0:T(8,128)(2,1)}, u32[]{:S(2)}, u32[]{:S(2)}) %collective-permute-start.2) | collective-permute-done | bytes 524320 | tf_op jit(solution)/shard_map/ppermute | solution.py:20
  122.1 2.7 %fusion.13 = f32[1024,2048]{1,0:T(8,128)S(1)} fusion(bf16[2048,128]{1,0:T(8,128)(2,1)S(1)} %get-tuple-element.31, bf16[2048,128]{1,0:T(8,128)(2,1)S(1)} %get-tuple-element.22, f32[1024,256]{1,0:T(8,128)} %get-tuple-element.16, bf16[1024,256]{1,0:T(8,128)(2,1)} %collective-permute-done.2), kind=kOutput, calls=%fused_computation.29 | convolution fusion | flops 1076625408 | bytes 11010048 | tf_op jit(solution)/shard_map/rc,dc->rd/dot_general | solution.py:199
  124.8 1.3 convolution_add_fusion
  126.1 7.9 %collective-permute-done.3 = bf16[1024,256]{1,0:T(8,128)(2,1)S(1)} collective-permute-done((bf16[1024,256]{1,0:T(8,128)(2,1)}, bf16[1024,256]{1,0:T(8,128)(2,1)S(1)}, u32[]{:S(2)}, u32[]{:S(2)}) %collective-permute-start.3) | collective-permute-done | bytes 524320 | tf_op jit(solution)/shard_map/ppermute | solution.py:20
  134.1 3.3 %add_convert_fusion = bf16[1024,2048]{1,0:T(8,128)(2,1)} fusion(f32[1024,2048]{1,0:T(8,128)S(1)} %convolution_add_fusion, bf16[2048,128]{1,0:T(8,128)(2,1)S(1)} %get-tuple-element.30, bf16[2048,128]{1,0:T(8,128)(2,1)S(1)} %get-tuple-element.23, f32[1024,256]{1,0:T(8,128)S(1)} %copy-done.2, bf16[1024,256]{1,0:T(8,128)(2,1)S(1)} %collective-permute-done.3), kind=kOutput, calls=%fused_computation.5 | convolution fusion | flops 1080819712 | bytes 15204352 | tf_op jit(solution)/shard_map/rc,dc->rd/dot_general | solution.py:199
  137.5 0.1 fusion.18
  137.5 0.8 copy-done.6
  138.4 0.1 copy-done.7
  138.4 0.8 pad_maximum_fusion.6
  139.3 40.0 %reduce-scatter.2.cloned.1.call-done = bf16[128,2048]{1,0:T(8,128)(2,1)} async-done(((bf16[1024,2048]{1,0:T(8,128)(2,1)}), bf16[128,2048]{1,0:T(8,128)(2,1)}) %reduce-scatter.2.cloned.1.call-update) | async-done | bytes 524304 | tf_op jit(solution)/shard_map/reduce_scatter | solution.py:206
  179.3 1.5 fusion.12
  180.7 2.4 %fusion.11 = bf16[128,2048]{1,0:T(8,128)(2,1)} fusion(bf16[128,2048]{1,0:T(8,128)(2,1)} %reduce-scatter.2.cloned.1.call-done, f32[128]{0:T(128)S(1)} %broadcast_multiply_fusion, f32[128]{0:T(128)S(1)} %get-tuple-element.20, f32[2048]{0:T(1024)S(1)} %copy-done.8, f32[128]{0:T(128)S(1)} %get-tuple-element.21, ...), kind=kLoop, calls=%fused_computation.22 | loop fusion | flops 2097152 | bytes 1582596 | tf_op jit(solution)/shard_map/convert_element_type | solution.py:217
  (31 shorter events, 0.2 us)
Async XLA Ops:
  7.2 72.1 %copy-start = (bf16[2048,256]{1,0:T(8,128)(2,1)S(1)}, bf16[2048,256]{1,0:T(8,128)(2,1)}, u32[]{:S(2)}) copy-start(bf16[2048,256]{1,0:T(8,128)(2,1)} %param.11) | copy-start | bytes 3145732
  7.2 63.8 %all-gather.2.cloned.1.call-start = ((), (), s32[]{:S(2)}) async-start(), calls=%async_computation.2 | async-start | bytes 4718592 | tf_op jit(solution)/shard_map/all_gather | solution.py:170
  7.2 27.4 %copy-start.12 = (s32[1024]{0:T(1024)S(1)}, s32[1024]{0:T(1024)}, u32[]{:S(2)}) copy-start(s32[1024]{0:T(1024)} %param.16) | copy-start | bytes 12292
  34.6 2.4 %copy-start.9 = (s32[1024]{0:T(1024)S(1)}, s32[1024]{0:T(1024)}, u32[]{:S(2)}) copy-start(s32[1024]{0:T(1024)} %param.17) | copy-start | bytes 12292
  34.6 3.4 %copy-start.3 = (bf16[1024,256]{1,0:T(8,128)(2,1)S(1)}, bf16[1024,256]{1,0:T(8,128)(2,1)}, u32[]{:S(2)}) copy-start(bf16[1024,256]{1,0:T(8,128)(2,1)} %param.14) | copy-start | bytes 1572868
  37.0 142.3 %reduce-scatter.2.cloned.1.call-start = ((), (), s32[]{:S(2)}) async-start(), calls=%async_computation.3 | async-start | bytes 4718592 | tf_op jit(solution)/shard_map/reduce_scatter | solution.py:206
  38.9 35.3 %copy-start.8 = (f32[2048]{0:T(1024)S(1)}, f32[2048]{0:T(1024)}, u32[]{:S(2)}) copy-start(f32[2048]{0:T(1024)} %param.10) | copy-start | bytes 24580
  71.0 3.4 %copy-start.1 = (bf16[1024,2048]{1,0:T(8,128)(2,1)S(1)}, bf16[1024,2048]{1,0:T(8,128)(2,1)}, u32[]{:S(2)}) copy-start(bf16[1024,2048]{1,0:T(8,128)(2,1)} %all-gather.2.cloned.1.call-done) | copy-start | bytes 12582916
  75.8 4.8 %copy-start.10 = (bf16[1024,256]{1,0:T(8,128)(2,1)}, bf16[1024,256]{1,0:T(8,128)(2,1)S(1)}, u32[]{:S(2)}) copy-start(bf16[1024,256]{1,0:T(8,128)(2,1)S(1)} %convolution_convert_fusion.1.ko_ref.vo_ref) | copy-start | bytes 1572868
  75.8 15.0 %collective-permute-start = (bf16[1024,256]{1,0:T(8,128)(2,1)S(1)}, bf16[1024,256]{1,0:T(8,128)(2,1)S(1)}, u32[]{:S(2)}, u32[]{:S(2)}) collective-permute-start(bf16[1024,256]{1,0:T(8,128)(2,1)S(1)} %convolution_convert_fusion.1.ko_ref.vo_ref), channel_id=1, source_target_pairs={{0,8},{8,16},{16,24},{24,32},{32,40},{40,48},{48,56},{56,64},{64,7... | collective-permute-start | bytes 1572872 | tf_op jit(solution)/shard_map/ppermute | solution.py:20
  90.8 6.0 %copy-start.11 = (bf16[1024,256]{1,0:T(8,128)(2,1)}, bf16[1024,256]{1,0:T(8,128)(2,1)S(1)}, u32[]{:S(2)}) copy-start(bf16[1024,256]{1,0:T(8,128)(2,1)S(1)} %collective-permute-done.kp_ref.vp_ref) | copy-start | bytes 1572868
  90.8 17.4 %collective-permute-start.1 = (bf16[1024,256]{1,0:T(8,128)(2,1)}, bf16[1024,256]{1,0:T(8,128)(2,1)}, u32[]{:S(2)}, u32[]{:S(2)}) collective-permute-start(bf16[1024,256]{1,0:T(8,128)(2,1)} %convolution_convert_fusion.ko_ref.vo_ref), channel_id=1, source_target_pairs={{0,8},{8,16},{16,24},{24,32},{32,40},{40,48},{48,56},{56,64},{64,7... | collective-permute-start | bytes 1572872 | tf_op jit(solution)/shard_map/ppermute | solution.py:20
  106.9 15.2 %collective-permute-start.2 = (bf16[1024,256]{1,0:T(8,128)(2,1)}, bf16[1024,256]{1,0:T(8,128)(2,1)}, u32[]{:S(2)}, u32[]{:S(2)}) collective-permute-start(bf16[1024,256]{1,0:T(8,128)(2,1)} %get-tuple-element.17), channel_id=1, source_target_pairs={{8,0},{16,8},{24,16},{32,24},{40,32},{48,40},{56,48},{64,56},{72,6... | collective-permute-start | bytes 1572872 | tf_op jit(solution)/shard_map/ppermute | solution.py:20
  118.4 15.7 %collective-permute-start.3 = (bf16[1024,256]{1,0:T(8,128)(2,1)}, bf16[1024,256]{1,0:T(8,128)(2,1)S(1)}, u32[]{:S(2)}, u32[]{:S(2)}) collective-permute-start(bf16[1024,256]{1,0:T(8,128)(2,1)} %get-tuple-element.19), channel_id=1, source_target_pairs={{8,0},{16,8},{24,16},{32,24},{40,32},{48,40},{56,48},{64,56},{72,6... | collective-permute-start | bytes 1572872 | tf_op jit(solution)/shard_map/ppermute | solution.py:20
  122.1 2.7 %copy-start.4 = (bf16[1024,128]{1,0:T(8,128)(2,1)S(1)}, bf16[1024,128]{1,0:T(8,128)(2,1)}, u32[]{:S(2)}) copy-start(bf16[1024,128]{1,0:T(8,128)(2,1)} %get-tuple-element.14) | copy-start | bytes 786436
  122.1 2.7 %copy-start.5 = (bf16[1024,128]{1,0:T(8,128)(2,1)S(1)}, bf16[1024,128]{1,0:T(8,128)(2,1)}, u32[]{:S(2)}) copy-start(bf16[1024,128]{1,0:T(8,128)(2,1)} %get-tuple-element.15) | copy-start | bytes 786436
  124.8 9.3 %copy-start.2 = (f32[1024,256]{1,0:T(8,128)S(1)}, f32[1024,256]{1,0:T(8,128)}, u32[]{:S(2)}) copy-start(f32[1024,256]{1,0:T(8,128)} %get-tuple-element.18) | copy-start | bytes 3145732
  137.4 0.9 copy-start.6
  137.4 1.0 copy-start.7
Sparse Core Ops, SparseCore 0:
  37.1 33.8 all-gather.1
  137.6 41.6 reduce-scatter.1

commit v16 on v15

--- a/solution.py
+++ b/solution.py
@@ -83,8 +83,8 @@
     allowed = (key_off >= st_ref[...] - a) & (key_off - row_off <= shift)
     s = jnp.where(allowed, s, neg_large)
     row_top = jnp.max(s, axis=1, keepdims=True)
-    log_total = row_top + jnp.log(jnp.sum(jnp.exp(s - row_top), axis=1, keepdims=True))
-    p = jnp.exp(s - log_total)
+    e = jnp.exp(s - row_top)
+    p = e * (1.0 / jnp.sum(e, axis=1, keepdims=True))
     p_low = p.astype(jnp.bfloat16)
     ctx_ref[...] = lax.dot_general(
         p_low, vt, (((1,), (1,)), ((), ())), preferred_element_type=jnp.float32

time: 190 us -> 190 us (level)
  no operation moved by 1% of the time
where the time goes in v16:
time: 190 us
  waiting for transfers between devices  88.6 us (47%)
  blocking collectives  24.6 us (13%)
  Pallas kernels  20.3 us (11%)
  matrix products  17.1 us (9%)
  between operations  14.2 us (7%)
  starting transfers between devices  11.6 us (6%)
  other arithmetic  8.05 us (4%)
  local copies, waits for them, and re-layouts  5.56 us (3%)
    reduce_scatter x1, waiting for transfers between devices, body(): lax.psum_scatter(term.astype(jnp.bfloat16), 'head', scatter_dimension=0,...  40 us
    all_gather x1, waiting for transfers between devices, body(): packed = lax.all_gather(packed_part, 'head', axis=1, tiled=True)  30.4 us
    all_to_all x1, blocking collectives, body(): lax.all_to_all(outgoing, 'seq', split_axis=0, concat_axis=0, tiled=True)  24.6 us
    pallas_call x2, Pallas kernels, attention(): pl.pallas_call(kernel, grid=(steps,), in_specs=[q_spec, k_spec, v_spec, k...  20.3 us
    ppermute x4, waiting for transfers between devices, passed_along(): return lax.ppermute(array, axis, pairs)  18.2 us
    ppermute x4, starting transfers between devices, passed_along(): return lax.ppermute(array, axis, pairs)  11.5 us
    dot_general x3, matrix products, project(): jnp.einsum('rc,dc->rd', grads, weight, preferred_element_type=jnp.float32)  7.33 us
  transfers between devices with their start and end apart: 6, of which 5 were waited for; matrix products, arithmetic and copies ran while one was open for 7% of the time, Pallas kernels for 11%

profile of v16, /device:TPU:0, one launch (start us, length us, event | category | flops | bytes accessed | tf_op | source)
XLA Modules:
  0.0 190.0 jit_solution(15157536185932490592)
XLA Ops:
  7.2 2.8 %fusion.7 = bf16[2048,256]{1,0:T(8,128)(2,1)S(1)} fusion(s32[1024]{0:T(1024)} %param.15, bf16[1024,2048]{1,0:T(8,128)(2,1)} %param.9, s32[]{:T(128)S(6)} %select_n.7), kind=kOutput, calls=%fused_computation.13 | convolution fusion | flops 1076363264 | bytes 1576964 | tf_op jit(solution)/shard_map/dot_general | solution.py:160
  10.0 24.6 %all_to_all.12 = bf16[16,128,256]{2,1,0:T(8,128)(2,1)S(1)} all-to-all(bf16[16,128,256]{2,1,0:T(8,128)(2,1)S(1)} %bitcast.10), channel_id=1, replica_groups=mesh['seq'=16,'head'=8] {'seq'}, dimensions={0} | all-to-all | bytes 2097152 | tf_op jit(solution)/shard_map/all_to_all | solution.py:163
  34.6 2.3 %fusion.8 = bf16[1024,256]{1,0:T(8,128)(2,1)} fusion(bf16[2048,256]{1,0:T(8,128)(2,1)S(1)} %bitcast.11, s32[1024]{0:T(1024)S(1)} %copy-done.12), kind=kOutput, calls=%fused_computation.16 | convolution fusion | flops 1076101120 | bytes 1576960 | tf_op jit(solution)/shard_map/dot_general | solution.py:167
  37.0 1.0 copy.11.st_ref
  38.1 0.8 fusion.30
  38.9 1.7 fusion.28
  40.6 30.4 %all-gather.2.cloned.1.call-done = bf16[1024,2048]{1,0:T(8,128)(2,1)} async-done(((bf16[1024,256]{1,0:T(8,128)(2,1)}), bf16[1024,2048]{1,0:T(8,128)(2,1)}) %all-gather.2.cloned.1.call-update) | async-done | bytes 4194320 | tf_op jit(solution)/shard_map/all_gather | solution.py:170
  71.0 3.2 %fusion = f32[1024]{0:T(1024)S(1)} fusion(bf16[1024,2048]{1,0:T(8,128)(2,1)} %all-gather.2.cloned.1.call-done), kind=kLoop, calls=%fused_computation.2 | loop fusion | flops 6290432 | bytes 4198400 | tf_op jit(solution)/shard_map/reduce_sum | solution.py:172
  74.2 0.2 copy-done.1
  74.5 1.3 convolution_convert_fusion.1.ko_ref.vo_ref
  75.8 3.5 %collective-permute-start = (bf16[1024,256]{1,0:T(8,128)(2,1)S(1)}, bf16[1024,256]{1,0:T(8,128)(2,1)S(1)}, u32[]{:S(2)}, u32[]{:S(2)}) collective-permute-start(bf16[1024,256]{1,0:T(8,128)(2,1)S(1)} %convolution_convert_fusion.1.ko_ref.vo_ref), channel_id=1, source_target_pairs={{0,8},{8,16},{16,24},{24,32},{32,40},{40,48},{48,56},{56,64},{64,7... | collective-permute-start | bytes 1572872 | tf_op jit(solution)/shard_map/ppermute | solution.py:20
  79.3 1.3 convolution_convert_fusion.2
  80.6 2.1 %convolution_convert_fusion.ko_ref.vo_ref = bf16[1024,256]{1,0:T(8,128)(2,1)} fusion(bf16[2048,128]{1,0:T(8,128)(2,1)S(1)} %get-tuple-element.30, bf16[2048,128]{1,0:T(8,128)(2,1)S(1)} %get-tuple-element.23, bf16[1024,2048]{1,0:T(8,128)(2,1)S(1)} %copy-done.1, f32[2048]{0:T(1024)S(1)} %copy-done.8, f32[1024]{0:T(1024)S(1)} %add_rsqrt_fusion), kind=kOutput, calls=%fused_computation.17 | convolution fusion | flops 1084489728 | bytes 5779456 | tf_op jit(solution)/shard_map/dot_general | solution.py:181
  82.7 8.1 %collective-permute-done.kp_ref.vp_ref = bf16[1024,256]{1,0:T(8,128)(2,1)S(1)} collective-permute-done((bf16[1024,256]{1,0:T(8,128)(2,1)S(1)}, bf16[1024,256]{1,0:T(8,128)(2,1)S(1)}, u32[]{:S(2)}, u32[]{:S(2)}) %collective-permute-start) | collective-permute-done | bytes 524320 | tf_op jit(solution)/shard_map/ppermute | solution.py:20
  90.8 5.2 %collective-permute-start.1 = (bf16[1024,256]{1,0:T(8,128)(2,1)}, bf16[1024,256]{1,0:T(8,128)(2,1)}, u32[]{:S(2)}, u32[]{:S(2)}) collective-permute-start(bf16[1024,256]{1,0:T(8,128)(2,1)} %convolution_convert_fusion.ko_ref.vo_ref), channel_id=1, source_target_pairs={{0,8},{8,16},{16,24},{24,32},{32,40},{40,48},{48,56},{56,64},{64,7... | collective-permute-start | bytes 1572872 | tf_op jit(solution)/shard_map/ppermute | solution.py:20
  96.0 0.9 fusion.31
  96.8 10.1 %shard_map.104 = (bf16[1024,128]{1,0:T(8,128)(2,1)}, bf16[1024,128]{1,0:T(8,128)(2,1)}, bf16[1024,256]{1,0:T(8,128)(2,1)}, f32[1024,256]{1,0:T(8,128)}) custom-call(bf16[1024,128]{1,0:T(8,128)(2,1)} %get-tuple-element.28.q_ref, bf16[1024,256]{1,0:T(8,128)(2,1)} %copy-done.11, bf16[1024,256]{1,0:T(8,128)(2,1)} %copy-done.11, bf16[1024,256]{1,0:T(8,128)(2,1)} %copy-done.10, ...), custom_call_target="tpu_custom_call" | custom-call | flops 2415919104 | bytes 3670016 | tf_op jit(solution)/shard_map/pallas_call | solution.py:125
  107.0 1.3 collective-permute-start.2
  108.3 10.2 %shard_map.105 = (bf16[1024,128]{1,0:T(8,128)(2,1)}, bf16[1024,128]{1,0:T(8,128)(2,1)}, bf16[1024,256]{1,0:T(8,128)(2,1)}, f32[1024,256]{1,0:T(8,128)}) custom-call(bf16[1024,128]{1,0:T(8,128)(2,1)} %get-tuple-element.29.q_ref, bf16[1024,256]{1,0:T(8,128)(2,1)} %collective-permute-done.1.kp_ref.vp_ref, ...), custom_call_target="tpu_custom_call" | custom-call | flops 2415919104 | bytes 3670016 | tf_op jit(solution)/shard_map/pallas_call | solution.py:125
  118.4 1.5 collective-permute-start.3
  119.9 2.2 %collective-permute-done.2 = bf16[1024,256]{1,0:T(8,128)(2,1)} collective-permute-done((bf16[1024,256]{1,0:T(8,128)(2,1)}, bf16[1024,256]{1,0:T(8,128)(2,1)}, u32[]{:S(2)}, u32[]{:S(2)}) %collective-permute-start.2) | collective-permute-done | bytes 524320 | tf_op jit(solution)/shard_map/ppermute | solution.py:20
  122.1 2.7 %fusion.13 = f32[1024,2048]{1,0:T(8,128)S(1)} fusion(bf16[2048,128]{1,0:T(8,128)(2,1)S(1)} %get-tuple-element.31, bf16[2048,128]{1,0:T(8,128)(2,1)S(1)} %get-tuple-element.22, f32[1024,256]{1,0:T(8,128)} %get-tuple-element.16, bf16[1024,256]{1,0:T(8,128)(2,1)} %collective-permute-done.2), kind=kOutput, calls=%fused_computation.29 | convolution fusion | flops 1076625408 | bytes 11010048 | tf_op jit(solution)/shard_map/rc,dc->rd/dot_general | solution.py:199
  124.8 1.3 convolution_add_fusion
  126.1 7.9 %collective-permute-done.3 = bf16[1024,256]{1,0:T(8,128)(2,1)S(1)} collective-permute-done((bf16[1024,256]{1,0:T(8,128)(2,1)}, bf16[1024,256]{1,0:T(8,128)(2,1)S(1)}, u32[]{:S(2)}, u32[]{:S(2)}) %collective-permute-start.3) | collective-permute-done | bytes 524320 | tf_op jit(solution)/shard_map/ppermute | solution.py:20
  134.1 3.3 %add_convert_fusion = bf16[1024,2048]{1,0:T(8,128)(2,1)} fusion(f32[1024,2048]{1,0:T(8,128)S(1)} %convolution_add_fusion, bf16[2048,128]{1,0:T(8,128)(2,1)S(1)} %get-tuple-element.30, bf16[2048,128]{1,0:T(8,128)(2,1)S(1)} %get-tuple-element.23, f32[1024,256]{1,0:T(8,128)S(1)} %copy-done.2, bf16[1024,256]{1,0:T(8,128)(2,1)S(1)} %collective-permute-done.3), kind=kOutput, calls=%fused_computation.5 | convolution fusion | flops 1080819712 | bytes 15204352 | tf_op jit(solution)/shard_map/rc,dc->rd/dot_general | solution.py:199
  137.5 0.1 fusion.18
  137.5 0.8 copy-done.6
  138.4 0.1 copy-done.7
  138.5 0.8 pad_maximum_fusion.6
  139.3 40.0 %reduce-scatter.2.cloned.1.call-done = bf16[128,2048]{1,0:T(8,128)(2,1)} async-done(((bf16[1024,2048]{1,0:T(8,128)(2,1)}), bf16[128,2048]{1,0:T(8,128)(2,1)}) %reduce-scatter.2.cloned.1.call-update) | async-done | bytes 524304 | tf_op jit(solution)/shard_map/reduce_scatter | solution.py:206
  179.3 1.5 fusion.12
  180.7 2.4 %fusion.11 = bf16[128,2048]{1,0:T(8,128)(2,1)} fusion(bf16[128,2048]{1,0:T(8,128)(2,1)} %reduce-scatter.2.cloned.1.call-done, f32[128]{0:T(128)S(1)} %broadcast_multiply_fusion, f32[128]{0:T(128)S(1)} %get-tuple-element.20, f32[2048]{0:T(1024)S(1)} %copy-done.8, f32[128]{0:T(128)S(1)} %get-tuple-element.21, ...), kind=kLoop, calls=%fused_computation.22 | loop fusion | flops 2097152 | bytes 1582596 | tf_op jit(solution)/shard_map/convert_element_type | solution.py:217
  (31 shorter events, 0.2 us)
Async XLA Ops:
  7.2 72.1 %copy-start = (bf16[2048,256]{1,0:T(8,128)(2,1)S(1)}, bf16[2048,256]{1,0:T(8,128)(2,1)}, u32[]{:S(2)}) copy-start(bf16[2048,256]{1,0:T(8,128)(2,1)} %param.11) | copy-start | bytes 3145732
  7.2 63.8 %all-gather.2.cloned.1.call-start = ((), (), s32[]{:S(2)}) async-start(), calls=%async_computation.2 | async-start | bytes 4718592 | tf_op jit(solution)/shard_map/all_gather | solution.py:170
  7.2 27.4 %copy-start.12 = (s32[1024]{0:T(1024)S(1)}, s32[1024]{0:T(1024)}, u32[]{:S(2)}) copy-start(s32[1024]{0:T(1024)} %param.16) | copy-start | bytes 12292
  34.6 2.4 %copy-start.9 = (s32[1024]{0:T(1024)S(1)}, s32[1024]{0:T(1024)}, u32[]{:S(2)}) copy-start(s32[1024]{0:T(1024)} %param.17) | copy-start | bytes 12292
  34.6 3.4 %copy-start.3 = (bf16[1024,256]{1,0:T(8,128)(2,1)S(1)}, bf16[1024,256]{1,0:T(8,128)(2,1)}, u32[]{:S(2)}) copy-start(bf16[1024,256]{1,0:T(8,128)(2,1)} %param.14) | copy-start | bytes 1572868
  37.0 142.3 %reduce-scatter.2.cloned.1.call-start = ((), (), s32[]{:S(2)}) async-start(), calls=%async_computation.3 | async-start | bytes 4718592 | tf_op jit(solution)/shard_map/reduce_scatter | solution.py:206
  38.9 35.3 %copy-start.8 = (f32[2048]{0:T(1024)S(1)}, f32[2048]{0:T(1024)}, u32[]{:S(2)}) copy-start(f32[2048]{0:T(1024)} %param.10) | copy-start | bytes 24580
  71.0 3.4 %copy-start.1 = (bf16[1024,2048]{1,0:T(8,128)(2,1)S(1)}, bf16[1024,2048]{1,0:T(8,128)(2,1)}, u32[]{:S(2)}) copy-start(bf16[1024,2048]{1,0:T(8,128)(2,1)} %all-gather.2.cloned.1.call-done) | copy-start | bytes 12582916
  75.8 4.8 %copy-start.10 = (bf16[1024,256]{1,0:T(8,128)(2,1)}, bf16[1024,256]{1,0:T(8,128)(2,1)S(1)}, u32[]{:S(2)}) copy-start(bf16[1024,256]{1,0:T(8,128)(2,1)S(1)} %convolution_convert_fusion.1.ko_ref.vo_ref) | copy-start | bytes 1572868
  75.8 15.0 %collective-permute-start = (bf16[1024,256]{1,0:T(8,128)(2,1)S(1)}, bf16[1024,256]{1,0:T(8,128)(2,1)S(1)}, u32[]{:S(2)}, u32[]{:S(2)}) collective-permute-start(bf16[1024,256]{1,0:T(8,128)(2,1)S(1)} %convolution_convert_fusion.1.ko_ref.vo_ref), channel_id=1, source_target_pairs={{0,8},{8,16},{16,24},{24,32},{32,40},{40,48},{48,56},{56,64},{64,7... | collective-permute-start | bytes 1572872 | tf_op jit(solution)/shard_map/ppermute | solution.py:20
  90.8 6.0 %copy-start.11 = (bf16[1024,256]{1,0:T(8,128)(2,1)}, bf16[1024,256]{1,0:T(8,128)(2,1)S(1)}, u32[]{:S(2)}) copy-start(bf16[1024,256]{1,0:T(8,128)(2,1)S(1)} %collective-permute-done.kp_ref.vp_ref) | copy-start | bytes 1572868
  90.8 17.5 %collective-permute-start.1 = (bf16[1024,256]{1,0:T(8,128)(2,1)}, bf16[1024,256]{1,0:T(8,128)(2,1)}, u32[]{:S(2)}, u32[]{:S(2)}) collective-permute-start(bf16[1024,256]{1,0:T(8,128)(2,1)} %convolution_convert_fusion.ko_ref.vo_ref), channel_id=1, source_target_pairs={{0,8},{8,16},{16,24},{24,32},{32,40},{40,48},{48,56},{56,64},{64,7... | collective-permute-start | bytes 1572872 | tf_op jit(solution)/shard_map/ppermute | solution.py:20
  107.0 15.1 %collective-permute-start.2 = (bf16[1024,256]{1,0:T(8,128)(2,1)}, bf16[1024,256]{1,0:T(8,128)(2,1)}, u32[]{:S(2)}, u32[]{:S(2)}) collective-permute-start(bf16[1024,256]{1,0:T(8,128)(2,1)} %get-tuple-element.17), channel_id=1, source_target_pairs={{8,0},{16,8},{24,16},{32,24},{40,32},{48,40},{56,48},{64,56},{72,6... | collective-permute-start | bytes 1572872 | tf_op jit(solution)/shard_map/ppermute | solution.py:20
  118.4 15.7 %collective-permute-start.3 = (bf16[1024,256]{1,0:T(8,128)(2,1)}, bf16[1024,256]{1,0:T(8,128)(2,1)S(1)}, u32[]{:S(2)}, u32[]{:S(2)}) collective-permute-start(bf16[1024,256]{1,0:T(8,128)(2,1)} %get-tuple-element.19), channel_id=1, source_target_pairs={{8,0},{16,8},{24,16},{32,24},{40,32},{48,40},{56,48},{64,56},{72,6... | collective-permute-start | bytes 1572872 | tf_op jit(solution)/shard_map/ppermute | solution.py:20
  122.1 2.7 %copy-start.4 = (bf16[1024,128]{1,0:T(8,128)(2,1)S(1)}, bf16[1024,128]{1,0:T(8,128)(2,1)}, u32[]{:S(2)}) copy-start(bf16[1024,128]{1,0:T(8,128)(2,1)} %get-tuple-element.14) | copy-start | bytes 786436
  122.1 2.7 %copy-start.5 = (bf16[1024,128]{1,0:T(8,128)(2,1)S(1)}, bf16[1024,128]{1,0:T(8,128)(2,1)}, u32[]{:S(2)}) copy-start(bf16[1024,128]{1,0:T(8,128)(2,1)} %get-tuple-element.15) | copy-start | bytes 786436
  124.8 9.3 %copy-start.2 = (f32[1024,256]{1,0:T(8,128)S(1)}, f32[1024,256]{1,0:T(8,128)}, u32[]{:S(2)}) copy-start(f32[1024,256]{1,0:T(8,128)} %get-tuple-element.18) | copy-start | bytes 3145732
  137.4 0.9 copy-start.6
  137.4 1.0 copy-start.7
Sparse Core Ops, SparseCore 0:
  37.1 33.8 all-gather.1
  137.6 41.6 reduce-scatter.1
